TPU v7x, 32 devices: a whole 2x2x4 slice. The times are simulated.
32 devices in a mesh: groups: 2 (over y), span: 4 (over z), layer: 2 (over x), rep: 2 (over core).
Axes of the slice: x: 2, y: 2, z: 4, core: 2. Of those that a mesh axis runs over, the one named last changes fastest.
Arguments:
- queries: bfloat16 [4096, 2, 4096], P('groups', 'layer', 'span'), parts along dimension 0, may hold values from -6 to 6
- train_grads: bfloat16 [4096, 2, 4096], P(('groups', 'span'), 'layer'), parts along dimension 0, may hold values from -6 to 6
- precond: float32 [2, 4096], P('layer', 'span'), may hold values from 0.25 to 4
- requests: int32 [8, 6], P('groups'), parts along dimension 0, may hold values from 0 to 15, as said below
- pair_slot: int32 [8, 24], P(('groups', 'span')), parts along dimension 0, may hold values from 0 to 5
- pair_train: int32 [8, 24], P(('groups', 'span')), parts along dimension 0, may hold values from 0 to 3
- pair_count: int32 [8, 2], P(('groups', 'span')), parts along dimension 0, may hold values from 1 to 12, as said below
Outputs:
- scores: float32 [8, 3072, 128], P(('groups', 'span'), ('layer', 'rep')), parts along dimension 0
There are 2 independent parts, one for each index of `groups`. A program takes and returns all parts, laid end to end along the dimension named above; an argument that names none is the same for every part. Nothing has to cross between parts.
Inputs may be any that keep to these rules, and one draw needn't show every extreme that they name: `requests`: each row names 6 different query blocks. The live pairs of half h of shard c's list are the first pair_count[c, h] of that half's 12 slots; some half is full in every draw.
All inputs are finite; a program needn't handle non-finite values.
Results may differ from a plain program's by a relative error of at most 0.0029.
Values may be sent and summed in bfloat16 or wider, within the bound.
No kernel may reach another device: no remote copies, remote signals or barrier semaphores. Data moves between devices by JAX's collectives and lax.ppermute only.
A program may use at most 64 MiB of HBM per device.

v0:
```python
import math

import jax
import jax.numpy as jnp
from jax import lax
from jax.sharding import PartitionSpec as P


BLOCK = 128
ROW_CHUNKS = 2


def ring_reduce_scatter(x, axis_name, dim):
    n = lax.axis_size(axis_name)
    me = lax.axis_index(axis_name)

    def piece(c):
        return lax.dynamic_index_in_dim(x, c % n, axis=dim, keepdims=False)

    if n == 1:
        return piece(me)
    perm = [(i, (i + 1) % n) for i in range(n)]
    acc = piece(me - 1 + n)
    for t in range(n - 1):
        recv = lax.ppermute(acc, axis_name, perm)
        acc = recv + piece(me - 2 - t + 2 * n)
    return acc


def shards(queries, train_grads, precond, requests, pair_slot, pair_train, pair_count):
    _, l_dev, features = queries.shape
    n_span = lax.axis_size("span")
    n_rep = lax.axis_size("rep")
    n_layer = lax.axis_size("layer")
    n_train, _, d_full = train_grads.shape
    tb_dev = n_train // BLOCK
    pmax = pair_slot.shape[1]
    cap = requests.shape[1]
    phalf = pmax // pair_count.shape[1]
    half = features // n_rep
    per_dev = pmax // (n_layer * n_rep)
    rep_index = lax.axis_index("rep")
    span_index = lax.axis_index("span")
    rows = BLOCK // ROW_CHUNKS

    dests = (span_index + jnp.arange(n_span, dtype=jnp.int32)) % n_span
    sources = (span_index - jnp.arange(n_span, dtype=jnp.int32) + n_span) % n_span
    q_half = []
    t_half = []
    for layer in range(l_dev):
        q_l = lax.dynamic_slice_in_dim(queries[:, layer, :], rep_index * half, half, axis=1)
        q_l = q_l * 1
        q_half.append(q_l)
        t_l = train_grads[:, layer, :]
        for k in range(n_span):
            t_half.append(lax.dynamic_slice_in_dim(t_l, sources[k] * features + rep_index * half, half, axis=1))
    p_half = lax.dynamic_slice_in_dim(precond, rep_index * half, half, axis=1)
    train = jnp.concatenate(t_half, axis=1)
    train = jnp.concatenate([train, jnp.zeros((BLOCK, train.shape[1]), train.dtype)], axis=0)

    score_scale = 1.0 / math.sqrt(l_dev * n_layer * d_full)
    slot_row = pair_slot[0]
    train_row = pair_train[0]
    counts = pair_count[0]
    slots = jnp.arange(pmax, dtype=jnp.int32)
    live = (slots % phalf) < counts[slots // phalf]
    pick_train = jnp.where(live, train_row, tb_dev)
    row_in_block = jnp.arange(rows, dtype=jnp.int32)

    outs = []
    gate = None
    for chunk in range(ROW_CHUNKS):
        row_ids = requests[dests] * BLOCK + chunk * rows
        row_ids = row_ids[:, :, None] + row_in_block
        if gate is not None:
            row_ids, _ = lax.optimization_barrier((row_ids, prev_sent))
        sent = []
        for layer in range(l_dev):
            got = q_half[layer][row_ids]
            sent.append((got.astype(jnp.float32) * p_half[layer]).astype(jnp.bfloat16))
        prev_sent = sent
        if gate is not None:
            sent, _ = lax.optimization_barrier((sent, gate))
        pieces = []
        for layer in range(l_dev):
            for k in range(n_span):
                piece = sent[layer][k]
                if k:
                    perm = [(i, (i + k) % n_span) for i in range(n_span)]
                    piece = lax.ppermute(piece, "span", perm)
                pieces.append(piece)
        gate = pieces
        arrived = jnp.concatenate(pieces, axis=-1).reshape(cap * rows, -1)
        combos = lax.dot_general(
            arrived,
            train,
            (((1,), (1,)), ((), ())),
            preferred_element_type=jnp.float32,
        ).reshape(cap, rows, tb_dev + 1, BLOCK)
        partial = combos.at[slot_row, :, pick_train, :].get(mode="promise_in_bounds") * score_scale
        partial = partial.reshape(n_layer, n_rep, per_dev, rows, BLOCK)
        partial = ring_reduce_scatter(partial, "rep", 1)
        partial = ring_reduce_scatter(partial, "layer", 0)
        outs.append(partial)
    summed = jnp.concatenate(outs, axis=1).reshape(per_dev * BLOCK, BLOCK)
    return summed[None]


def solution(mesh):
    placed = (
        P("groups", "layer", "span"),
        P(("groups", "span"), "layer", None),
        P("layer", "span"),
        P("groups", None),
        P(("groups", "span"), None),
        P(("groups", "span"), None),
        P(("groups", "span"), None),
    )

    return jax.shard_map(
        shards,
        mesh=mesh,
        in_specs=placed,
        out_specs=P(("groups", "span"), ("layer", "rep"), None),
        check_vma=False,
    )
```

profile of v0, /device:TPU:0, one launch (start us, length us, event | category | flops | bytes accessed | tf_op | source)
XLA Modules:
  0.0 106.7 jit_solution(17801448492555659408)
XLA Ops:
  0.0 0.0 copy-start
  0.0 1.2 %gather_fusion = s32[4,6]{1,0:T(4,128)S(1)} fusion(s32[4,6]{1,0:T(4,128)} %param.10, s32[1024]{0:T(1024)S(1)} %pad_clamp_fusion.2), kind=kCustom, calls=%fused_computation | custom fusion | bytes 208 | tf_op jit(solution)/shard_map/gather | solution.py:73
  1.3 0.1 compare_select_fusion.1
  1.4 0.1 reshape.246
  1.4 1.7 %dynamic-slice_bitcast_fusion = bf16[2048,512]{1,0:T(8,128)(2,1)S(1)} fusion(bf16[2048,1,1024]{2,0,1:T(8,128)(2,1)} %param.7, s32[]{:T(128)S(6)} %select_n.170), kind=kLoop, calls=%fused_computation.17 | loop fusion | bytes 4194308 | tf_op jit(solution)/shard_map/dynamic_slice | solution.py:51
  3.2 0.0 copy-done
  3.2 5.4 %gather_fusion.1 = bf16[1536,512]{1,0:T(8,128)(2,1)} fusion(bf16[2048,512]{1,0:T(8,128)(2,1)S(1)} %dynamic-slice_bitcast_fusion, s32[2048]{0:T(1024)S(1)} %pad_clamp_fusion.1), kind=kCustom, calls=%fused_computation.1 | custom fusion | bytes 3151872 | tf_op jit(solution)/shard_map/gather | solution.py:79
  8.6 0.0 copy-start.3
  8.6 1.7 %fusion.5 = bf16[4,6,64,512]{3,2,1,0:T(8,128)(2,1)S(1)} fusion(bf16[4,6,64,512]{3,2,1,0:T(8,128)(2,1)} %bitcast.88, f32[512]{0:T(512)S(1)} %bitcast.95), kind=kLoop, calls=%fused_computation.13 | loop fusion | flops 2359296 | bytes 3147776 | tf_op jit(solution)/shard_map/convert_element_type | solution.py:80
  10.4 0.9 slice_bitcast_fusion.3
  11.2 3.1 %collective-permute-start = (bf16[6,64,512]{2,1,0:T(8,128)(2,1)}, bf16[6,64,512]{2,1,0:T(8,128)(2,1)}, u32[]{:S(2)}, u32[]{:S(2)}) collective-permute-start(bf16[6,64,512]{2,1,0:T(8,128)(2,1)} %get-tuple-element.16), channel_id=1, source_target_pairs={{0,4},{4,8},{8,12},{12,0},{1,5},{5,9},{9,13},{13,1},{2,6},{6,10},{... | collective-permute-start | bytes 1179656 | tf_op jit(solution)/shard_map/ppermute | solution.py:90
  14.3 2.6 %collective-permute-start.1 = (bf16[6,64,512]{2,1,0:T(8,128)(2,1)S(1)}, bf16[6,64,512]{2,1,0:T(8,128)(2,1)}, u32[]{:S(2)}, u32[]{:S(2)}) collective-permute-start(bf16[6,64,512]{2,1,0:T(8,128)(2,1)S(1)} %get-tuple-element.15), channel_id=1, source_target_pairs={{0,8},{4,12},{8,0},{12,4},{1,9},{5,13},{9,1},{13,5},{2,10},{6,14},... | collective-permute-start | bytes 1179656 | tf_op jit(solution)/shard_map/ppermute | solution.py:90
  16.9 1.3 %collective-permute-start.2 = (bf16[6,64,512]{2,1,0:T(8,128)(2,1)S(1)}, bf16[6,64,512]{2,1,0:T(8,128)(2,1)}, u32[]{:S(2)}, u32[]{:S(2)}) collective-permute-start(bf16[6,64,512]{2,1,0:T(8,128)(2,1)S(1)} %get-tuple-element.14), channel_id=1, source_target_pairs={{0,12},{4,0},{8,4},{12,8},{1,13},{5,1},{9,5},{13,9},{2,14},{6,2},{... | collective-permute-start | bytes 1179656 | tf_op jit(solution)/shard_map/ppermute | solution.py:90
  18.2 0.7 fusion.35
  21.4 0.1 iota_add_fusion
  21.5 0.1 reshape.269
  21.6 0.0 copy-done.3
  21.6 0.6 fusion.34
  22.1 1.7 %dynamic-slice_bitcast_fusion.4 = (bf16[512,512]{1,0:T(8,128)(2,1)S(1)}, bf16[512,512]{1,0:T(8,128)(2,1)S(1)}, bf16[512,512]{1,0:T(8,128)(2,1)S(1)}, bf16[512,512]{1,0:T(8,128)(2,1)S(1)}) fusion(bf16[512,1,4096]{2,0,1:T(8,128)(2,1)} %param.8, s32[]{:T(128)S(6)} %select_n.175, s32[]{:T(128)S(6)} %select_n.176, s32[]{:T(128)S(6)} %select_n.178, s32[]{:T(128)S(6)} %select_n.177), kind=kLoop, calls=%fused_computation.37 | loop fusion | bytes 4194320 | tf_op jit(solution)/shard_map/dynamic_slice | solution.py:56
  23.8 0.0 copy-start.4
  23.8 0.0 copy-start.5
  23.8 4.3 %fusion.8 = bf16[640,2048]{1,0:T(8,128)(2,1)} fusion(bf16[512,512]{1,0:T(8,128)(2,1)S(1)} %get-tuple-element.11, bf16[512,512]{1,0:T(8,128)(2,1)S(1)} %get-tuple-element.12, bf16[512,512]{1,0:T(8,128)(2,1)S(1)} %get-tuple-element.10, bf16[512,512]{1,0:T(8,128)(2,1)S(1)} %get-tuple-element.9), kind=kLoop, calls=%fused_computation.16 | loop fusion | flops 17039360 | bytes 4718592 | tf_op jit(solution)/shard_map/concatenate | solution.py:58
  28.2 0.0 copy-done.4
  28.2 0.0 copy-done.5
  28.2 1.2 %fusion.31 = s32[24]{0:T(128)S(1)} fusion(s32[1,24]{1,0:T(1,128)S(1)} %copy-done.4, s32[1,24]{1,0:T(1,128)S(1)} %copy-done.5, s32[]{:T(128)} %bitcast.22, s32[]{:T(128)} %bitcast.21), kind=kLoop, calls=%fused_computation.90 | loop fusion | flops 720 | bytes 296 | tf_op jit(solution)/shard_map/concatenate | solution.py:100
  29.4 5.4 %gather_fusion.3 = bf16[1536,512]{1,0:T(8,128)(2,1)} fusion(bf16[2048,512]{1,0:T(8,128)(2,1)S(1)} %dynamic-slice_bitcast_fusion, s32[2048]{0:T(1024)S(1)} %pad_clamp_fusion), kind=kCustom, calls=%fused_computation.3 | custom fusion | bytes 3151872 | tf_op jit(solution)/shard_map/gather | solution.py:79
  34.8 0.0 copy-start.1
  34.8 1.9 %fusion.4 = bf16[4,6,64,512]{3,2,1,0:T(8,128)(2,1)S(1)} fusion(bf16[4,6,64,512]{3,2,1,0:T(8,128)(2,1)} %bitcast.87, f32[512]{0:T(512)S(1)} %bitcast.96), kind=kLoop, calls=%fused_computation.11 | loop fusion | flops 2359296 | bytes 3147776 | tf_op jit(solution)/shard_map/convert_element_type | solution.py:80
  36.7 0.0 collective-permute-done
  36.7 6.0 %collective-permute-done.1 = bf16[6,64,512]{2,1,0:T(8,128)(2,1)} collective-permute-done((bf16[6,64,512]{2,1,0:T(8,128)(2,1)S(1)}, bf16[6,64,512]{2,1,0:T(8,128)(2,1)}, u32[]{:S(2)}, u32[]{:S(2)}) %collective-permute-start.1) | collective-permute-done | bytes 393248 | tf_op jit(solution)/shard_map/ppermute | solution.py:90
  42.7 0.0 collective-permute-done.2
  42.7 1.0 slice_bitcast_fusion.7
  43.8 9.9 %collective-permute-start.7 = (bf16[6,64,512]{2,1,0:T(8,128)(2,1)}, bf16[6,64,512]{2,1,0:T(8,128)(2,1)}, u32[]{:S(2)}, u32[]{:S(2)}) collective-permute-start(bf16[6,64,512]{2,1,0:T(8,128)(2,1)} %get-tuple-element.18), channel_id=1, source_target_pairs={{0,12},{4,0},{8,4},{12,8},{1,13},{5,1},{9,5},{13,9},{2,14},{6,2},{... | collective-permute-start | bytes 1179656 | tf_op jit(solution)/shard_map/ppermute | solution.py:90
  53.7 0.4 collective-permute-start.6
  54.1 0.1 collective-permute-start.5
  54.3 0.0 copy-done.1
  54.3 2.6 %fusion.9 = f32[6,64,5,128]{3,1,2,0:T(8,128)S(1)} fusion(bf16[5,128,2048,1]{2,1,0,3:T(8,128)(2,1)S(1)} %bitcast.94, bf16[6,64,512]{2,1,0:T(8,128)(2,1)} %collective-permute-done.2, bf16[6,64,512]{2,1,0:T(8,128)(2,1)} %collective-permute-done.1, bf16[6,64,512]{2,1,0:T(8,128)(2,1)} %collective-permute-done, bf16[6,64,512]{2,1,0:T(8,128)(2,1)S(1)} %get-tuple-element.13), kind=kOutput, calls=%fused_computation.19 | convolution fusion | flops 1012924416 | bytes 5177344 | tf_op jit(solution)/shard_map/dot_general | solution.py:94
  56.9 0.0 copy-start.2
  56.9 0.7 gather_fusion.2
  57.6 0.1 broadcast_multiply_fusion.1
  57.7 0.8 dynamic-slice_bitcast_fusion.6
  58.5 0.0 collective-permute-start.3
  58.5 5.1 %collective-permute-done.7 = bf16[6,64,512]{2,1,0:T(8,128)(2,1)} collective-permute-done((bf16[6,64,512]{2,1,0:T(8,128)(2,1)}, bf16[6,64,512]{2,1,0:T(8,128)(2,1)}, u32[]{:S(2)}, u32[]{:S(2)}) %collective-permute-start.7) | collective-permute-done | bytes 393248 | tf_op jit(solution)/shard_map/ppermute | solution.py:90
  63.6 25.2 %collective-permute-done.6 = bf16[6,64,512]{2,1,0:T(8,128)(2,1)} collective-permute-done((bf16[6,64,512]{2,1,0:T(8,128)(2,1)}, bf16[6,64,512]{2,1,0:T(8,128)(2,1)}, u32[]{:S(2)}, u32[]{:S(2)}) %collective-permute-start.6) | collective-permute-done | bytes 393248 | tf_op jit(solution)/shard_map/ppermute | solution.py:90
  88.8 0.0 collective-permute-done.5
  88.8 0.0 copy-done.2
  88.8 3.5 %fusion.16 = f32[6,64,5,128]{3,1,2,0:T(8,128)S(1)} fusion(bf16[5,128,2048,1]{2,1,0,3:T(8,128)(2,1)} %bitcast.93, bf16[6,64,512]{2,1,0:T(8,128)(2,1)} %collective-permute-done.7, bf16[6,64,512]{2,1,0:T(8,128)(2,1)} %collective-permute-done.6, bf16[6,64,512]{2,1,0:T(8,128)(2,1)} %collective-permute-done.5, bf16[6,64,512]{2,1,0:T(8,128)(2,1)S(1)} %copy-done.2), kind=kOutput, calls=%fused_computation.27 | convolution fusion | flops 1012924416 | bytes 5177344 | tf_op jit(solution)/shard_map/dot_general | solution.py:94
  92.3 0.7 gather_fusion.4
  93.0 0.1 broadcast_multiply_fusion
  93.1 0.1 collective-permute-start.8
  93.2 0.0 collective-permute-done.3
  93.2 1.1 %bitcast_add_fusion.1 = f32[2,6,64,128]{3,2,1,0:T(8,128)S(1)} fusion(f32[2,6,64,128]{3,2,1,0:T(8,128)} %collective-permute-done.3, f32[2,2,6,64,128]{4,3,2,1,0:T(8,128)S(1)} %bitcast.90, s32[]{:T(128)S(6)} %select_n.188), kind=kLoop, calls=%fused_computation.44 | loop fusion | flops 98304 | bytes 1179652 | tf_op jit(solution)/shard_map/add | solution.py:26
  94.3 1.6 %collective-permute-start.4 = (f32[6,64,128]{2,1,0:T(8,128)S(1)}, f32[6,64,128]{2,1,0:T(8,128)S(1)}, u32[]{:S(2)}, u32[]{:S(2)}) collective-permute-start(f32[6,64,128]{2,1,0:T(8,128)S(1)} %dynamic-slice_bitcast_fusion.8), channel_id=1, source_target_pairs={{0,2},{2,0},{1,3},{3,1},{4,6},{6,4},{5,7},{7,5},{8,10},{10,8},{9,1... | collective-permute-start | bytes 589832 | tf_op jit(solution)/shard_map/ppermute | solution.py:25
  95.9 0.0 collective-permute-done.8
  96.0 0.6 collective-permute-start.9
  96.6 5.6 %collective-permute-done.4 = f32[6,64,128]{2,1,0:T(8,128)S(1)} collective-permute-done((f32[6,64,128]{2,1,0:T(8,128)S(1)}, f32[6,64,128]{2,1,0:T(8,128)S(1)}, u32[]{:S(2)}, u32[]{:S(2)}) %collective-permute-start.4) | collective-permute-done | bytes 196640 | tf_op jit(solution)/shard_map/ppermute | solution.py:25
  102.2 3.7 %collective-permute-done.9 = f32[6,64,128]{2,1,0:T(8,128)S(1)} collective-permute-done((f32[6,64,128]{2,1,0:T(8,128)S(1)}, f32[6,64,128]{2,1,0:T(8,128)S(1)}, u32[]{:S(2)}, u32[]{:S(2)}) %collective-permute-start.9) | collective-permute-done | bytes 196640 | tf_op jit(solution)/shard_map/ppermute | solution.py:25
  105.9 0.8 pad_maximum_fusion
  (14 shorter events, 0.3 us)
Async XLA Ops:
  0.0 3.2 %copy-start = (f32[1,1024]{1,0:T(1,128)S(1)}, f32[1,1024]{1,0:T(1,128)}, u32[]{:S(2)}) copy-start(f32[1,1024]{1,0:T(1,128)} %param.9) | copy-start | bytes 12292
  8.6 13.0 %copy-start.3 = (s32[1,2]{1,0:T(1,128)S(1)}, s32[1,2]{1,0:T(1,128)}, u32[]{:S(2)}) copy-start(s32[1,2]{1,0:T(1,128)} %param.13) | copy-start | bytes 28
  11.2 25.4 %collective-permute-start = (bf16[6,64,512]{2,1,0:T(8,128)(2,1)}, bf16[6,64,512]{2,1,0:T(8,128)(2,1)}, u32[]{:S(2)}, u32[]{:S(2)}) collective-permute-start(bf16[6,64,512]{2,1,0:T(8,128)(2,1)} %get-tuple-element.16), channel_id=1, source_target_pairs={{0,4},{4,8},{8,12},{12,0},{1,5},{5,9},{9,13},{13,1},{2,6},{6,10},{... | collective-permute-start | bytes 1179656 | tf_op jit(solution)/shard_map/ppermute | solution.py:90
  14.3 28.4 %collective-permute-start.1 = (bf16[6,64,512]{2,1,0:T(8,128)(2,1)S(1)}, bf16[6,64,512]{2,1,0:T(8,128)(2,1)}, u32[]{:S(2)}, u32[]{:S(2)}) collective-permute-start(bf16[6,64,512]{2,1,0:T(8,128)(2,1)S(1)} %get-tuple-element.15), channel_id=1, source_target_pairs={{0,8},{4,12},{8,0},{12,4},{1,9},{5,13},{9,1},{13,5},{2,10},{6,14},... | collective-permute-start | bytes 1179656 | tf_op jit(solution)/shard_map/ppermute | solution.py:90
  16.9 25.9 %collective-permute-start.2 = (bf16[6,64,512]{2,1,0:T(8,128)(2,1)S(1)}, bf16[6,64,512]{2,1,0:T(8,128)(2,1)}, u32[]{:S(2)}, u32[]{:S(2)}) collective-permute-start(bf16[6,64,512]{2,1,0:T(8,128)(2,1)S(1)} %get-tuple-element.14), channel_id=1, source_target_pairs={{0,12},{4,0},{8,4},{12,8},{1,13},{5,1},{9,5},{13,9},{2,14},{6,2},{... | collective-permute-start | bytes 1179656 | tf_op jit(solution)/shard_map/ppermute | solution.py:90
  23.8 4.4 %copy-start.4 = (s32[1,24]{1,0:T(1,128)S(1)}, s32[1,24]{1,0:T(1,128)}, u32[]{:S(2)}) copy-start(s32[1,24]{1,0:T(1,128)} %param.12) | copy-start | bytes 292
  23.8 4.3 %copy-start.5 = (s32[1,24]{1,0:T(1,128)S(1)}, s32[1,24]{1,0:T(1,128)}, u32[]{:S(2)}) copy-start(s32[1,24]{1,0:T(1,128)} %param.11) | copy-start | bytes 292
  34.8 19.5 %copy-start.1 = (bf16[640,2048]{1,0:T(8,128)(2,1)S(1)}, bf16[640,2048]{1,0:T(8,128)(2,1)}, u32[]{:S(2)}) copy-start(bf16[640,2048]{1,0:T(8,128)(2,1)} %fusion.8) | copy-start | bytes 7864324
  43.8 19.8 %collective-permute-start.7 = (bf16[6,64,512]{2,1,0:T(8,128)(2,1)}, bf16[6,64,512]{2,1,0:T(8,128)(2,1)}, u32[]{:S(2)}, u32[]{:S(2)}) collective-permute-start(bf16[6,64,512]{2,1,0:T(8,128)(2,1)} %get-tuple-element.18), channel_id=1, source_target_pairs={{0,12},{4,0},{8,4},{12,8},{1,13},{5,1},{9,5},{13,9},{2,14},{6,2},{... | collective-permute-start | bytes 1179656 | tf_op jit(solution)/shard_map/ppermute | solution.py:90
  53.7 35.0 %collective-permute-start.6 = (bf16[6,64,512]{2,1,0:T(8,128)(2,1)}, bf16[6,64,512]{2,1,0:T(8,128)(2,1)}, u32[]{:S(2)}, u32[]{:S(2)}) collective-permute-start(bf16[6,64,512]{2,1,0:T(8,128)(2,1)} %get-tuple-element.19), channel_id=1, source_target_pairs={{0,8},{4,12},{8,0},{12,4},{1,9},{5,13},{9,1},{13,5},{2,10},{6,14},... | collective-permute-start | bytes 1179656 | tf_op jit(solution)/shard_map/ppermute | solution.py:90
  54.1 34.6 %collective-permute-start.5 = (bf16[6,64,512]{2,1,0:T(8,128)(2,1)S(1)}, bf16[6,64,512]{2,1,0:T(8,128)(2,1)}, u32[]{:S(2)}, u32[]{:S(2)}) collective-permute-start(bf16[6,64,512]{2,1,0:T(8,128)(2,1)S(1)} %get-tuple-element.20), channel_id=1, source_target_pairs={{0,4},{4,8},{8,12},{12,0},{1,5},{5,9},{9,13},{13,1},{2,6},{6,10},{... | collective-permute-start | bytes 1179656 | tf_op jit(solution)/shard_map/ppermute | solution.py:90
  56.9 31.8 %copy-start.2 = (bf16[6,64,512]{2,1,0:T(8,128)(2,1)S(1)}, bf16[6,64,512]{2,1,0:T(8,128)(2,1)}, u32[]{:S(2)}) copy-start(bf16[6,64,512]{2,1,0:T(8,128)(2,1)} %get-tuple-element.17) | copy-start | bytes 1179652
  58.5 34.7 %collective-permute-start.3 = (f32[2,6,64,128]{3,2,1,0:T(8,128)}, f32[2,6,64,128]{3,2,1,0:T(8,128)}, u32[]{:S(2)}, u32[]{:S(2)}) collective-permute-start(f32[2,6,64,128]{3,2,1,0:T(8,128)} %dynamic-slice_bitcast_fusion.6), channel_id=1, source_target_pairs={{0,1},{1,0},{2,3},{3,2},{4,5},{5,4},{6,7},{7,6},{8,9},{9,8},{10,11... | collective-permute-start | bytes 1179656 | tf_op jit(solution)/shard_map/ppermute | solution.py:25
  93.1 2.8 %collective-permute-start.8 = (f32[2,6,64,128]{3,2,1,0:T(8,128)S(1)}, f32[2,6,64,128]{3,2,1,0:T(8,128)S(1)}, u32[]{:S(2)}, u32[]{:S(2)}) collective-permute-start(f32[2,6,64,128]{3,2,1,0:T(8,128)S(1)} %dynamic-slice_bitcast_fusion.5), channel_id=1, source_target_pairs={{0,1},{1,0},{2,3},{3,2},{4,5},{5,4},{6,7},{7,6},{8,9},{9,8},{10,11... | collective-permute-start | bytes 1179656 | tf_op jit(solution)/shard_map/ppermute | solution.py:25
  94.3 7.8 %collective-permute-start.4 = (f32[6,64,128]{2,1,0:T(8,128)S(1)}, f32[6,64,128]{2,1,0:T(8,128)S(1)}, u32[]{:S(2)}, u32[]{:S(2)}) collective-permute-start(f32[6,64,128]{2,1,0:T(8,128)S(1)} %dynamic-slice_bitcast_fusion.8), channel_id=1, source_target_pairs={{0,2},{2,0},{1,3},{3,1},{4,6},{6,4},{5,7},{7,5},{8,10},{10,8},{9,1... | collective-permute-start | bytes 589832 | tf_op jit(solution)/shard_map/ppermute | solution.py:25
  96.0 9.9 %collective-permute-start.9 = (f32[6,64,128]{2,1,0:T(8,128)S(1)}, f32[6,64,128]{2,1,0:T(8,128)S(1)}, u32[]{:S(2)}, u32[]{:S(2)}) collective-permute-start(f32[6,64,128]{2,1,0:T(8,128)S(1)} %dynamic-slice_bitcast_fusion.7), channel_id=1, source_target_pairs={{0,2},{2,0},{1,3},{3,1},{4,6},{6,4},{5,7},{7,5},{8,10},{10,8},{9,1... | collective-permute-start | bytes 589832 | tf_op jit(solution)/shard_map/ppermute | solution.py:25
where the time goes:
time: 107 us
  waiting for transfers between devices  45.5 us (43%)
  local copies, waits for them, and re-layouts  21 us (20%)
  starting transfers between devices  19.7 us (18%)
  other arithmetic  11.5 us (11%)
  matrix products  6.16 us (6%)
  between operations  2.78 us (3%)
    ppermute x6, waiting for transfers between devices, shards(): piece = lax.ppermute(piece, 'span', perm)  36.3 us
    ppermute x6, starting transfers between devices, shards(): piece = lax.ppermute(piece, 'span', perm)  17.5 us
    gather x2, local copies, waits for them, and re-layouts, shards(): got = q_half[layer][row_ids]  10.8 us
    ppermute x4, waiting for transfers between devices, ring_reduce_scatter(): recv = lax.ppermute(acc, axis_name, perm)  9.26 us
    dot_general x2, matrix products, shards(): lax.dot_general(arrived, train, (((1,), (1,)), ((), ())), preferred_eleme...  6.16 us
    concatenate x1, other arithmetic, shards(): train = jnp.concatenate(t_half, axis=1)  4.32 us
    convert_element_type x2, other arithmetic, shards(): sent.append((got.astype(jnp.float32) * p_half[layer]).astype(jnp.bfloat16))  3.64 us
    ppermute x4, starting transfers between devices, ring_reduce_scatter(): recv = lax.ppermute(acc, axis_name, perm)  2.23 us
  transfers between devices with their start and end apart: 10, of which 5 were waited for; matrix products, arithmetic and copies ran while one was open for 24% of the time, Pallas kernels for 0%

commit v1 on v0

--- a/solution.py
+++ b/solution.py
@@ -7,7 +7,7 @@
 
 
 BLOCK = 128
-ROW_CHUNKS = 2
+ROW_SPLIT = (80, 48)
 
 
 def ring_reduce_scatter(x, axis_name, dim):
@@ -41,7 +41,6 @@
     per_dev = pmax // (n_layer * n_rep)
     rep_index = lax.axis_index("rep")
     span_index = lax.axis_index("span")
-    rows = BLOCK // ROW_CHUNKS
 
     dests = (span_index + jnp.arange(n_span, dtype=jnp.int32)) % n_span
     sources = (span_index - jnp.arange(n_span, dtype=jnp.int32) + n_span) % n_span
@@ -65,13 +64,14 @@
     slots = jnp.arange(pmax, dtype=jnp.int32)
     live = (slots % phalf) < counts[slots // phalf]
     pick_train = jnp.where(live, train_row, tb_dev)
-    row_in_block = jnp.arange(rows, dtype=jnp.int32)
 
     outs = []
     gate = None
-    for chunk in range(ROW_CHUNKS):
-        row_ids = requests[dests] * BLOCK + chunk * rows
-        row_ids = row_ids[:, :, None] + row_in_block
+    row_start = 0
+    for rows in ROW_SPLIT:
+        row_ids = requests[dests] * BLOCK + row_start
+        row_ids = row_ids[:, :, None] + jnp.arange(rows, dtype=jnp.int32)
+        row_start += rows
         if gate is not None:
             row_ids, _ = lax.optimization_barrier((row_ids, prev_sent))
         sent = []

time: 107 us -> 108 us (level)
  other arithmetic: 11.5 us -> 7.98 us
  starting transfers between devices: 19.7 us -> 22.5 us
  waiting for transfers between devices: 45.5 us -> 47.5 us
    ppermute x6, starting transfers between devices: 17.5 us -> 19.7 us  [shards(): piece = lax.ppermute(piece, 'span', perm)]
    convert_element_type x2, other arithmetic: 3.64 us -> 2.21 us  [shards(): sent.append((got.astype(jnp.float32) * p_half[layer]).astype(jnp.bfloat16))]
    ppermute x6, waiting for transfers between devices: 36.3 us -> 37.7 us  [shards(): piece = lax.ppermute(piece, 'span', perm)]
    concatenate x1, other arithmetic: 4.32 us -> 3.23 us  [shards(): train = jnp.concatenate(t_half, axis=1)]
  transfers between devices with their start and end apart: 10 -> 10, of which waited for: 5 -> 6; matrix products, arithmetic and copies ran while one was open for 24% -> 15% of each run, Pallas kernels for 0% -> 0%
where the time goes in v1:
time: 108 us; the launch traced here: 107 us
  waiting for transfers between devices  47.5 us (44%)
  starting transfers between devices  22.5 us (21%)
  local copies, waits for them, and re-layouts  20.4 us (19%)
  other arithmetic  7.98 us (7%)
  matrix products  6.18 us (6%)
  between operations  2.8 us (3%)
    ppermute x6, waiting for transfers between devices, shards(): piece = lax.ppermute(piece, 'span', perm)  37.7 us
    ppermute x6, starting transfers between devices, shards(): piece = lax.ppermute(piece, 'span', perm)  19.7 us
    gather x2, local copies, waits for them, and re-layouts, shards(): got = q_half[layer][row_ids]  11 us
    ppermute x4, waiting for transfers between devices, ring_reduce_scatter(): recv = lax.ppermute(acc, axis_name, perm)  9.78 us
    dot_general x2, matrix products, shards(): lax.dot_general(arrived, train, (((1,), (1,)), ((), ())), preferred_eleme...  6.18 us
    concatenate x1, other arithmetic, shards(): train = jnp.concatenate(t_half, axis=1)  3.23 us
    ppermute x4, starting transfers between devices, ring_reduce_scatter(): recv = lax.ppermute(acc, axis_name, perm)  2.82 us
    convert_element_type x2, other arithmetic, shards(): sent.append((got.astype(jnp.float32) * p_half[layer]).astype(jnp.bfloat16))  2.21 us
  transfers between devices with their start and end apart: 10, of which 6 were waited for; matrix products, arithmetic and copies ran while one was open for 15% of the time, Pallas kernels for 0%

profile of v1, /device:TPU:0, one launch (start us, length us, event | category | flops | bytes accessed | tf_op | source)
XLA Modules:
  0.0 107.4 jit_solution(12593059842318295827)
XLA Ops:
  0.0 0.0 copy-start
  0.0 1.2 %gather_fusion = s32[4,6]{1,0:T(4,128)S(1)} fusion(s32[4,6]{1,0:T(4,128)} %param.10, s32[1024]{0:T(1024)S(1)} %pad_clamp_fusion.2), kind=kCustom, calls=%fused_computation | custom fusion | bytes 208 | tf_op jit(solution)/shard_map/gather | solution.py:72
  1.3 0.1 compare_select_fusion.1
  1.4 0.1 reshape.246
  1.5 1.7 %dynamic-slice_bitcast_fusion = bf16[2048,512]{1,0:T(8,128)(2,1)S(1)} fusion(bf16[2048,1,1024]{2,0,1:T(8,128)(2,1)} %param.7, s32[]{:T(128)S(6)} %select_n.172), kind=kLoop, calls=%fused_computation.17 | loop fusion | bytes 4194308 | tf_op jit(solution)/shard_map/dynamic_slice | solution.py:50
  3.2 0.0 copy-done
  3.2 6.8 %gather_fusion.1 = bf16[1920,512]{1,0:T(8,128)(2,1)} fusion(bf16[2048,512]{1,0:T(8,128)(2,1)S(1)} %dynamic-slice_bitcast_fusion, s32[2048]{0:T(1024)S(1)} %pad_clamp_fusion.1), kind=kCustom, calls=%fused_computation.1 | custom fusion | bytes 3939840 | tf_op jit(solution)/shard_map/gather | solution.py:79
  10.0 2.0 %fusion.4 = bf16[4,6,80,512]{3,2,1,0:T(8,128)(2,1)S(1)} fusion(bf16[4,6,80,512]{3,2,1,0:T(8,128)(2,1)} %bitcast.87, f32[512]{0:T(512)S(1)} %bitcast.95), kind=kLoop, calls=%fused_computation.11 | loop fusion | flops 2949120 | bytes 3934208 | tf_op jit(solution)/shard_map/convert_element_type | solution.py:80
  12.0 1.4 %slice_bitcast_fusion.3 = (bf16[6,80,512]{2,1,0:T(8,128)(2,1)}, bf16[6,80,512]{2,1,0:T(8,128)(2,1)}, bf16[6,80,512]{2,1,0:T(8,128)(2,1)}, bf16[6,80,512]{2,1,0:T(8,128)(2,1)}) fusion(bf16[4,6,80,512]{3,2,1,0:T(8,128)(2,1)S(1)} %fusion.4), kind=kLoop, calls=%fused_computation.41 | loop fusion | bytes 3932160 | tf_op jit(solution)/shard_map/concatenate | solution.py:93
  13.3 3.1 %collective-permute-start = (bf16[6,80,512]{2,1,0:T(8,128)(2,1)}, bf16[6,80,512]{2,1,0:T(8,128)(2,1)}, u32[]{:S(2)}, u32[]{:S(2)}) collective-permute-start(bf16[6,80,512]{2,1,0:T(8,128)(2,1)} %get-tuple-element.16), channel_id=1, source_target_pairs={{0,4},{4,8},{8,12},{12,0},{1,5},{5,9},{9,13},{13,1},{2,6},{6,10},{... | collective-permute-start | bytes 1474568 | tf_op jit(solution)/shard_map/ppermute | solution.py:90
  16.4 2.6 %collective-permute-start.1 = (bf16[6,80,512]{2,1,0:T(8,128)(2,1)}, bf16[6,80,512]{2,1,0:T(8,128)(2,1)}, u32[]{:S(2)}, u32[]{:S(2)}) collective-permute-start(bf16[6,80,512]{2,1,0:T(8,128)(2,1)} %get-tuple-element.15), channel_id=1, source_target_pairs={{0,8},{4,12},{8,0},{12,4},{1,9},{5,13},{9,1},{13,5},{2,10},{6,14},... | collective-permute-start | bytes 1474568 | tf_op jit(solution)/shard_map/ppermute | solution.py:90
  19.0 1.3 %collective-permute-start.2 = (bf16[6,80,512]{2,1,0:T(8,128)(2,1)}, bf16[6,80,512]{2,1,0:T(8,128)(2,1)}, u32[]{:S(2)}, u32[]{:S(2)}) collective-permute-start(bf16[6,80,512]{2,1,0:T(8,128)(2,1)} %get-tuple-element.14), channel_id=1, source_target_pairs={{0,12},{4,0},{8,4},{12,8},{1,13},{5,1},{9,5},{13,9},{2,14},{6,2},{... | collective-permute-start | bytes 1474568 | tf_op jit(solution)/shard_map/ppermute | solution.py:90
  20.3 0.7 fusion.35
  23.5 0.1 iota_add_fusion
  23.6 0.1 reshape.269
  23.7 4.2 %gather_fusion.3 = bf16[1152,512]{1,0:T(8,128)(2,1)S(1)} fusion(bf16[2048,512]{1,0:T(8,128)(2,1)S(1)} %dynamic-slice_bitcast_fusion, s32[2048]{0:T(1024)S(1)} %pad_clamp_fusion), kind=kCustom, calls=%fused_computation.3 | custom fusion | bytes 2363904 | tf_op jit(solution)/shard_map/gather | solution.py:79
  27.9 0.0 copy-start.3
  28.0 0.0 copy-start.4
  28.0 0.0 copy-start.5
  28.0 0.2 fusion.8
  28.2 0.4 copy-done.3
  28.6 0.6 fusion.34
  29.2 0.0 copy-done.4
  29.2 0.0 copy-done.5
  29.2 1.3 %fusion.31 = s32[24]{0:T(128)S(1)} fusion(s32[1,24]{1,0:T(1,128)S(1)} %copy-done.4, s32[1,24]{1,0:T(1,128)S(1)} %copy-done.5, s32[]{:T(128)} %bitcast.22, s32[]{:T(128)} %bitcast.21), kind=kLoop, calls=%fused_computation.90 | loop fusion | flops 720 | bytes 296 | tf_op jit(solution)/shard_map/concatenate | solution.py:100
  30.5 1.7 %dynamic-slice_bitcast_fusion.4 = (bf16[512,512]{1,0:T(8,128)(2,1)S(1)}, bf16[512,512]{1,0:T(8,128)(2,1)S(1)}, bf16[512,512]{1,0:T(8,128)(2,1)S(1)}, bf16[512,512]{1,0:T(8,128)(2,1)S(1)}) fusion(bf16[512,1,4096]{2,0,1:T(8,128)(2,1)} %param.8, s32[]{:T(128)S(6)} %select_n.177, s32[]{:T(128)S(6)} %select_n.178, s32[]{:T(128)S(6)} %select_n.180, s32[]{:T(128)S(6)} %select_n.179), kind=kLoop, calls=%fused_computation.37 | loop fusion | bytes 4194320 | tf_op jit(solution)/shard_map/dynamic_slice | solution.py:55
  32.2 3.2 %fusion.7 = bf16[640,2048]{1,0:T(8,128)(2,1)S(1)} fusion(bf16[512,512]{1,0:T(8,128)(2,1)S(1)} %get-tuple-element.11, bf16[512,512]{1,0:T(8,128)(2,1)S(1)} %get-tuple-element.12, bf16[512,512]{1,0:T(8,128)(2,1)S(1)} %get-tuple-element.10, bf16[512,512]{1,0:T(8,128)(2,1)S(1)} %get-tuple-element.9), kind=kLoop, calls=%fused_computation.14 | loop fusion | flops 17039360 | bytes 4718592 | tf_op jit(solution)/shard_map/concatenate | solution.py:57
  35.4 0.0 copy-start.1
  35.4 0.0 copy-start.2
  35.4 0.0 collective-permute-done
  35.4 15.7 %collective-permute-done.1 = bf16[6,80,512]{2,1,0:T(8,128)(2,1)} collective-permute-done((bf16[6,80,512]{2,1,0:T(8,128)(2,1)}, bf16[6,80,512]{2,1,0:T(8,128)(2,1)}, u32[]{:S(2)}, u32[]{:S(2)}) %collective-permute-start.1) | collective-permute-done | bytes 491552 | tf_op jit(solution)/shard_map/ppermute | solution.py:90
  51.1 0.0 collective-permute-done.2
  51.1 0.1 slice_bitcast_fusion.7
  51.2 12.1 %collective-permute-start.7 = (bf16[6,48,512]{2,1,0:T(8,128)(2,1)S(1)}, bf16[6,48,512]{2,1,0:T(8,128)(2,1)}, u32[]{:S(2)}, u32[]{:S(2)}) collective-permute-start(bf16[6,48,512]{2,1,0:T(8,128)(2,1)S(1)} %get-tuple-element.18), channel_id=1, source_target_pairs={{0,12},{4,0},{8,4},{12,8},{1,13},{5,1},{9,5},{13,9},{2,14},{6,2},{... | collective-permute-start | bytes 884744 | tf_op jit(solution)/shard_map/ppermute | solution.py:90
  63.3 0.4 collective-permute-start.6
  63.7 0.2 collective-permute-start.5
  63.9 0.0 copy-done.1
  63.9 0.0 copy-done.2
  64.0 3.0 %fusion.9 = f32[6,80,5,128]{3,1,2,0:T(8,128)S(1)} fusion(bf16[5,128,2048,1]{2,1,0,3:T(8,128)(2,1)S(1)} %bitcast.91, bf16[6,80,512]{2,1,0:T(8,128)(2,1)} %collective-permute-done.2, bf16[6,80,512]{2,1,0:T(8,128)(2,1)} %collective-permute-done.1, bf16[6,80,512]{2,1,0:T(8,128)(2,1)} %collective-permute-done, bf16[6,80,512]{2,1,0:T(8,128)(2,1)S(1)} %copy-done.2), kind=kOutput, calls=%fused_computation.19 | convolution fusion | flops 1266155520 | bytes 5816320 | tf_op jit(solution)/shard_map/dot_general | solution.py:94
  67.0 0.7 gather_fusion.2
  67.7 3.0 %collective-permute-done.7 = bf16[6,48,512]{2,1,0:T(8,128)(2,1)} collective-permute-done((bf16[6,48,512]{2,1,0:T(8,128)(2,1)S(1)}, bf16[6,48,512]{2,1,0:T(8,128)(2,1)}, u32[]{:S(2)}, u32[]{:S(2)}) %collective-permute-start.7) | collective-permute-done | bytes 294944 | tf_op jit(solution)/shard_map/ppermute | solution.py:90
  70.7 19.0 %collective-permute-done.6 = bf16[6,48,512]{2,1,0:T(8,128)(2,1)} collective-permute-done((bf16[6,48,512]{2,1,0:T(8,128)(2,1)S(1)}, bf16[6,48,512]{2,1,0:T(8,128)(2,1)}, u32[]{:S(2)}, u32[]{:S(2)}) %collective-permute-start.6) | collective-permute-done | bytes 294944 | tf_op jit(solution)/shard_map/ppermute | solution.py:90
  89.7 0.0 collective-permute-done.5
  89.7 3.1 %fusion.16 = f32[6,48,5,128]{3,1,2,0:T(8,128)S(1)} fusion(bf16[5,128,2048,1]{2,1,0,3:T(8,128)(2,1)} %bitcast.92, bf16[6,48,512]{2,1,0:T(8,128)(2,1)} %collective-permute-done.7, bf16[6,48,512]{2,1,0:T(8,128)(2,1)} %collective-permute-done.6, bf16[6,48,512]{2,1,0:T(8,128)(2,1)} %collective-permute-done.5, bf16[6,48,512]{2,1,0:T(8,128)(2,1)S(1)} %get-tuple-element.17), kind=kOutput, calls=%fused_computation.27 | convolution fusion | flops 759693312 | bytes 4538368 | tf_op jit(solution)/shard_map/dot_general | solution.py:94
  92.8 0.7 gather_fusion.4
  93.5 0.1 broadcast_multiply_fusion.1
  93.6 0.1 collective-permute-start.8
  93.7 0.1 broadcast_multiply_fusion
  93.9 0.6 collective-permute-start.3
  94.4 0.9 collective-permute-done.8
  95.4 1.6 %collective-permute-start.9 = (f32[6,48,128]{2,1,0:T(8,128)S(1)}, f32[6,48,128]{2,1,0:T(8,128)S(1)}, u32[]{:S(2)}, u32[]{:S(2)}) collective-permute-start(f32[6,48,128]{2,1,0:T(8,128)S(1)} %dynamic-slice_bitcast_fusion.8), channel_id=1, source_target_pairs={{0,2},{2,0},{1,3},{3,1},{4,6},{6,4},{5,7},{7,5},{8,10},{10,8},{9,1... | collective-permute-start | bytes 442376 | tf_op jit(solution)/shard_map/ppermute | solution.py:25
  96.9 0.0 collective-permute-done.3
  96.9 0.1 bitcast_add_fusion
  97.0 0.6 collective-permute-start.4
  97.6 4.5 %collective-permute-done.9 = f32[6,48,128]{2,1,0:T(8,128)S(1)} collective-permute-done((f32[6,48,128]{2,1,0:T(8,128)S(1)}, f32[6,48,128]{2,1,0:T(8,128)S(1)}, u32[]{:S(2)}, u32[]{:S(2)}) %collective-permute-start.9) | collective-permute-done | bytes 147488 | tf_op jit(solution)/shard_map/ppermute | solution.py:25
  102.2 4.4 %collective-permute-done.4 = f32[6,80,128]{2,1,0:T(8,128)S(1)} collective-permute-done((f32[6,80,128]{2,1,0:T(8,128)S(1)}, f32[6,80,128]{2,1,0:T(8,128)S(1)}, u32[]{:S(2)}, u32[]{:S(2)}) %collective-permute-start.4) | collective-permute-done | bytes 245792 | tf_op jit(solution)/shard_map/ppermute | solution.py:25
  106.6 0.8 pad_maximum_fusion
  (15 shorter events, 0.3 us)
Async XLA Ops:
  0.0 3.2 %copy-start = (f32[1,1024]{1,0:T(1,128)S(1)}, f32[1,1024]{1,0:T(1,128)}, u32[]{:S(2)}) copy-start(f32[1,1024]{1,0:T(1,128)} %param.9) | copy-start | bytes 12292
  13.3 22.1 %collective-permute-start = (bf16[6,80,512]{2,1,0:T(8,128)(2,1)}, bf16[6,80,512]{2,1,0:T(8,128)(2,1)}, u32[]{:S(2)}, u32[]{:S(2)}) collective-permute-start(bf16[6,80,512]{2,1,0:T(8,128)(2,1)} %get-tuple-element.16), channel_id=1, source_target_pairs={{0,4},{4,8},{8,12},{12,0},{1,5},{5,9},{9,13},{13,1},{2,6},{6,10},{... | collective-permute-start | bytes 1474568 | tf_op jit(solution)/shard_map/ppermute | solution.py:90
  16.4 34.8 %collective-permute-start.1 = (bf16[6,80,512]{2,1,0:T(8,128)(2,1)}, bf16[6,80,512]{2,1,0:T(8,128)(2,1)}, u32[]{:S(2)}, u32[]{:S(2)}) collective-permute-start(bf16[6,80,512]{2,1,0:T(8,128)(2,1)} %get-tuple-element.15), channel_id=1, source_target_pairs={{0,8},{4,12},{8,0},{12,4},{1,9},{5,13},{9,1},{13,5},{2,10},{6,14},... | collective-permute-start | bytes 1474568 | tf_op jit(solution)/shard_map/ppermute | solution.py:90
  19.0 32.2 %collective-permute-start.2 = (bf16[6,80,512]{2,1,0:T(8,128)(2,1)}, bf16[6,80,512]{2,1,0:T(8,128)(2,1)}, u32[]{:S(2)}, u32[]{:S(2)}) collective-permute-start(bf16[6,80,512]{2,1,0:T(8,128)(2,1)} %get-tuple-element.14), channel_id=1, source_target_pairs={{0,12},{4,0},{8,4},{12,8},{1,13},{5,1},{9,5},{13,9},{2,14},{6,2},{... | collective-permute-start | bytes 1474568 | tf_op jit(solution)/shard_map/ppermute | solution.py:90
  27.9 0.7 copy-start.3
  28.0 1.2 %copy-start.4 = (s32[1,24]{1,0:T(1,128)S(1)}, s32[1,24]{1,0:T(1,128)}, u32[]{:S(2)}) copy-start(s32[1,24]{1,0:T(1,128)} %param.12) | copy-start | bytes 292
  28.0 1.2 %copy-start.5 = (s32[1,24]{1,0:T(1,128)S(1)}, s32[1,24]{1,0:T(1,128)}, u32[]{:S(2)}) copy-start(s32[1,24]{1,0:T(1,128)} %param.11) | copy-start | bytes 292
  35.4 28.5 %copy-start.1 = (bf16[640,2048]{1,0:T(8,128)(2,1)}, bf16[640,2048]{1,0:T(8,128)(2,1)S(1)}, u32[]{:S(2)}) copy-start(bf16[640,2048]{1,0:T(8,128)(2,1)S(1)} %fusion.7) | copy-start | bytes 7864324
  35.4 28.5 %copy-start.2 = (bf16[6,80,512]{2,1,0:T(8,128)(2,1)S(1)}, bf16[6,80,512]{2,1,0:T(8,128)(2,1)}, u32[]{:S(2)}) copy-start(bf16[6,80,512]{2,1,0:T(8,128)(2,1)} %get-tuple-element.13) | copy-start | bytes 1474564
  51.2 19.5 %collective-permute-start.7 = (bf16[6,48,512]{2,1,0:T(8,128)(2,1)S(1)}, bf16[6,48,512]{2,1,0:T(8,128)(2,1)}, u32[]{:S(2)}, u32[]{:S(2)}) collective-permute-start(bf16[6,48,512]{2,1,0:T(8,128)(2,1)S(1)} %get-tuple-element.18), channel_id=1, source_target_pairs={{0,12},{4,0},{8,4},{12,8},{1,13},{5,1},{9,5},{13,9},{2,14},{6,2},{... | collective-permute-start | bytes 884744 | tf_op jit(solution)/shard_map/ppermute | solution.py:90
  63.3 26.4 %collective-permute-start.6 = (bf16[6,48,512]{2,1,0:T(8,128)(2,1)S(1)}, bf16[6,48,512]{2,1,0:T(8,128)(2,1)}, u32[]{:S(2)}, u32[]{:S(2)}) collective-permute-start(bf16[6,48,512]{2,1,0:T(8,128)(2,1)S(1)} %get-tuple-element.19), channel_id=1, source_target_pairs={{0,8},{4,12},{8,0},{12,4},{1,9},{5,13},{9,1},{13,5},{2,10},{6,14},... | collective-permute-start | bytes 884744 | tf_op jit(solution)/shard_map/ppermute | solution.py:90
  63.7 26.0 %collective-permute-start.5 = (bf16[6,48,512]{2,1,0:T(8,128)(2,1)S(1)}, bf16[6,48,512]{2,1,0:T(8,128)(2,1)}, u32[]{:S(2)}, u32[]{:S(2)}) collective-permute-start(bf16[6,48,512]{2,1,0:T(8,128)(2,1)S(1)} %get-tuple-element.20), channel_id=1, source_target_pairs={{0,4},{4,8},{8,12},{12,0},{1,5},{5,9},{9,13},{13,1},{2,6},{6,10},{... | collective-permute-start | bytes 884744 | tf_op jit(solution)/shard_map/ppermute | solution.py:90
  93.6 1.6 %collective-permute-start.8 = (f32[2,6,48,128]{3,2,1,0:T(8,128)S(1)}, f32[2,6,48,128]{3,2,1,0:T(8,128)S(1)}, u32[]{:S(2)}, u32[]{:S(2)}) collective-permute-start(f32[2,6,48,128]{3,2,1,0:T(8,128)S(1)} %dynamic-slice_bitcast_fusion.6), channel_id=1, source_target_pairs={{0,1},{1,0},{2,3},{3,2},{4,5},{5,4},{6,7},{7,6},{8,9},{9,8},{10,11... | collective-permute-start | bytes 884744 | tf_op jit(solution)/shard_map/ppermute | solution.py:25
  93.9 3.1 %collective-permute-start.3 = (f32[2,6,80,128]{3,2,1,0:T(8,128)S(1)}, f32[2,6,80,128]{3,2,1,0:T(8,128)S(1)}, u32[]{:S(2)}, u32[]{:S(2)}) collective-permute-start(f32[2,6,80,128]{3,2,1,0:T(8,128)S(1)} %dynamic-slice_bitcast_fusion.5), channel_id=1, source_target_pairs={{0,1},{1,0},{2,3},{3,2},{4,5},{5,4},{6,7},{7,6},{8,9},{9,8},{10,11... | collective-permute-start | bytes 1474568 | tf_op jit(solution)/shard_map/ppermute | solution.py:25
  95.4 6.8 %collective-permute-start.9 = (f32[6,48,128]{2,1,0:T(8,128)S(1)}, f32[6,48,128]{2,1,0:T(8,128)S(1)}, u32[]{:S(2)}, u32[]{:S(2)}) collective-permute-start(f32[6,48,128]{2,1,0:T(8,128)S(1)} %dynamic-slice_bitcast_fusion.8), channel_id=1, source_target_pairs={{0,2},{2,0},{1,3},{3,1},{4,6},{6,4},{5,7},{7,5},{8,10},{10,8},{9,1... | collective-permute-start | bytes 442376 | tf_op jit(solution)/shard_map/ppermute | solution.py:25
  97.0 9.6 %collective-permute-start.4 = (f32[6,80,128]{2,1,0:T(8,128)S(1)}, f32[6,80,128]{2,1,0:T(8,128)S(1)}, u32[]{:S(2)}, u32[]{:S(2)}) collective-permute-start(f32[6,80,128]{2,1,0:T(8,128)S(1)} %dynamic-slice_bitcast_fusion.7), channel_id=1, source_target_pairs={{0,2},{2,0},{1,3},{3,1},{4,6},{6,4},{5,7},{7,5},{8,10},{10,8},{9,1... | collective-permute-start | bytes 737288 | tf_op jit(solution)/shard_map/ppermute | solution.py:25

commit v2 on v1

--- a/solution.py
+++ b/solution.py
@@ -28,7 +28,7 @@
 
 
 def shards(queries, train_grads, precond, requests, pair_slot, pair_train, pair_count):
-    _, l_dev, features = queries.shape
+    n_query, l_dev, features = queries.shape
     n_span = lax.axis_size("span")
     n_rep = lax.axis_size("rep")
     n_layer = lax.axis_size("layer")
@@ -69,15 +69,16 @@
     gate = None
     row_start = 0
     for rows in ROW_SPLIT:
-        row_ids = requests[dests] * BLOCK + row_start
-        row_ids = row_ids[:, :, None] + jnp.arange(rows, dtype=jnp.int32)
-        row_start += rows
+        block_ids = requests[dests].reshape(-1)
         if gate is not None:
-            row_ids, _ = lax.optimization_barrier((row_ids, prev_sent))
+            block_ids, _ = lax.optimization_barrier((block_ids, prev_sent))
         sent = []
         for layer in range(l_dev):
-            got = q_half[layer][row_ids]
+            q3 = q_half[layer].reshape(n_query // BLOCK, BLOCK, half)
+            got = jnp.take(q3[:, row_start:row_start + rows], block_ids, axis=0)
+            got = got.reshape(n_span, cap, rows, half)
             sent.append((got.astype(jnp.float32) * p_half[layer]).astype(jnp.bfloat16))
+        row_start += rows
         prev_sent = sent
         if gate is not None:
             sent, _ = lax.optimization_barrier((sent, gate))

time: 108 us -> 105 us (0.972)
  local copies, waits for them, and re-layouts: 20.4 us -> 13.3 us
  waiting for transfers between devices: 47.5 us -> 49.6 us
  other arithmetic: 7.98 us -> 9.42 us
    gather x3, local copies, waits for them, and re-layouts: 12.3 us -> 3.9 us  [the longest x2 2.65 us: shards(): got = jnp.take(q3[:, row_start:row_start + rows], block_ids, axis=0)]
    ppermute x6, waiting for transfers between devices: 37.7 us -> 39.6 us  [shards(): piece = lax.ppermute(piece, 'span', perm)]
    concatenate x1, other arithmetic: 3.23 us -> 4.32 us  [shards(): train = jnp.concatenate(t_half, axis=1)]
  transfers between devices with their start and end apart: 10 -> 10, of which waited for: 6 -> 6; matrix products, arithmetic and copies ran while one was open for 15% -> 14% of each run, Pallas kernels for 0% -> 0%
where the time goes in v2:
time: 105 us
  waiting for transfers between devices  49.6 us (47%)
  starting transfers between devices  22.3 us (21%)
  local copies, waits for them, and re-layouts  13.3 us (13%)
  other arithmetic  9.42 us (9%)
  matrix products  7.06 us (7%)
  between operations  2.84 us (3%)
    ppermute x6, waiting for transfers between devices, shards(): piece = lax.ppermute(piece, 'span', perm)  39.6 us
    ppermute x6, starting transfers between devices, shards(): piece = lax.ppermute(piece, 'span', perm)  19.6 us
    ppermute x4, waiting for transfers between devices, ring_reduce_scatter(): recv = lax.ppermute(acc, axis_name, perm)  9.99 us
    dot_general x2, matrix products, shards(): lax.dot_general(arrived, train, (((1,), (1,)), ((), ())), preferred_eleme...  7.06 us
    concatenate x1, other arithmetic, shards(): train = jnp.concatenate(t_half, axis=1)  4.32 us
    ppermute x4, starting transfers between devices, ring_reduce_scatter(): recv = lax.ppermute(acc, axis_name, perm)  2.77 us
    gather x2, local copies, waits for them, and re-layouts, shards(): got = jnp.take(q3[:, row_start:row_start + rows], block_ids, axis=0)  2.65 us
    convert_element_type x2, other arithmetic, shards(): sent.append((got.astype(jnp.float32) * p_half[layer]).astype(jnp.bfloat16))  2.64 us
  transfers between devices with their start and end apart: 10, of which 6 were waited for; matrix products, arithmetic and copies ran while one was open for 14% of the time, Pallas kernels for 0%

profile of v2, /device:TPU:0, one launch (start us, length us, event | category | flops | bytes accessed | tf_op | source)
XLA Modules:
  0.0 104.6 jit_solution(18346072689621495458)
XLA Ops:
  0.0 0.0 copy-start
  0.0 1.2 %gather_fusion = s32[4,6]{1,0:T(4,128)S(1)} fusion(s32[4,6]{1,0:T(4,128)} %param.10, s32[1024]{0:T(1024)S(1)} %pad_clamp_fusion.2), kind=kCustom, calls=%fused_computation | custom fusion | bytes 208 | tf_op jit(solution)/shard_map/gather | solution.py:72
  1.3 0.1 reshape.273
  1.4 0.0 copy-done
  1.4 1.7 %constant_dynamic-slice_fusion.1 = bf16[2048,1,512]{2,0,1:T(8,128)(2,1)S(1)} fusion(bf16[2048,1,1024]{2,0,1:T(8,128)(2,1)} %param.7, s32[]{:T(128)S(6)} %select_n.192), kind=kLoop, calls=%fused_computation.59 | loop fusion | bytes 4194308 | tf_op jit(solution)/shard_map/dynamic_slice | solution.py:50
  3.1 0.1 slice.72
  3.3 2.0 %gather_fusion.1 = bf16[24,80,512]{2,1,0:T(8,128)(2,1)} fusion(bf16[16,80,512]{2,1,0:T(8,128)(2,1)S(1)} %slice.72, s32[1024]{0:T(1024)S(1)} %pad_clamp_fusion.1), kind=kCustom, calls=%fused_computation.1 | custom fusion | bytes 3932256 | tf_op jit(solution)/shard_map/jit(_take)/gather | solution.py:78
  5.3 2.2 %multiply_convert_fusion = bf16[4,6,80,512]{3,2,1,0:T(8,128)(2,1)S(1)} fusion(f32[512]{0:T(512)S(1)} %bitcast.92, bf16[4,6,80,512]{3,2,1,0:T(8,128)(2,1)} %bitcast.86, pred[4,6]{1,0:T(4,128)(4,1)S(1)} %compare_and_fusion.1), kind=kLoop, calls=%fused_computation.10 | loop fusion | flops 3932160 | bytes 3934232 | tf_op jit(solution)/shard_map/convert_element_type | solution.py:80
  7.5 0.0 copy-start.1
  7.6 1.1 %slice_bitcast_fusion.3 = (bf16[6,80,512]{2,1,0:T(8,128)(2,1)S(1)}, bf16[6,80,512]{2,1,0:T(8,128)(2,1)}, bf16[6,80,512]{2,1,0:T(8,128)(2,1)}, bf16[6,80,512]{2,1,0:T(8,128)(2,1)}) fusion(bf16[4,6,80,512]{3,2,1,0:T(8,128)(2,1)S(1)} %multiply_convert_fusion), kind=kLoop, calls=%fused_computation.38 | loop fusion | bytes 3932160 | tf_op jit(solution)/shard_map/concatenate | solution.py:94
  8.7 3.1 %collective-permute-start = (bf16[6,80,512]{2,1,0:T(8,128)(2,1)}, bf16[6,80,512]{2,1,0:T(8,128)(2,1)}, u32[]{:S(2)}, u32[]{:S(2)}) collective-permute-start(bf16[6,80,512]{2,1,0:T(8,128)(2,1)} %get-tuple-element.16), channel_id=1, source_target_pairs={{0,4},{4,8},{8,12},{12,0},{1,5},{5,9},{9,13},{13,1},{2,6},{6,10},{... | collective-permute-start | bytes 1474568 | tf_op jit(solution)/shard_map/ppermute | solution.py:91
  11.8 2.6 %collective-permute-start.1 = (bf16[6,80,512]{2,1,0:T(8,128)(2,1)}, bf16[6,80,512]{2,1,0:T(8,128)(2,1)}, u32[]{:S(2)}, u32[]{:S(2)}) collective-permute-start(bf16[6,80,512]{2,1,0:T(8,128)(2,1)} %get-tuple-element.15), channel_id=1, source_target_pairs={{0,8},{4,12},{8,0},{12,4},{1,9},{5,13},{9,1},{13,5},{2,10},{6,14},... | collective-permute-start | bytes 1474568 | tf_op jit(solution)/shard_map/ppermute | solution.py:91
  14.3 1.3 %collective-permute-start.2 = (bf16[6,80,512]{2,1,0:T(8,128)(2,1)}, bf16[6,80,512]{2,1,0:T(8,128)(2,1)}, u32[]{:S(2)}, u32[]{:S(2)}) collective-permute-start(bf16[6,80,512]{2,1,0:T(8,128)(2,1)} %get-tuple-element.14), channel_id=1, source_target_pairs={{0,12},{4,0},{8,4},{12,8},{1,13},{5,1},{9,5},{13,9},{2,14},{6,2},{... | collective-permute-start | bytes 1474568 | tf_op jit(solution)/shard_map/ppermute | solution.py:91
  15.7 0.7 fusion.34
  19.0 0.1 slice.77
  19.0 0.1 reshape.274
  19.2 0.1 broadcast_in_dim.39
  19.3 0.0 copy-done.1
  19.3 0.6 fusion.33
  19.9 0.0 copy-start.2
  19.9 0.0 copy-start.3
  19.9 0.6 gather_fusion.3
  20.5 0.4 multiply_convert_fusion.1
  20.9 0.0 copy-done.2
  20.9 0.0 copy-done.3
  20.9 1.4 %fusion.30 = s32[24]{0:T(128)S(1)} fusion(s32[1,24]{1,0:T(1,128)S(1)} %copy-done.2, s32[1,24]{1,0:T(1,128)S(1)} %copy-done.3, s32[]{:T(128)} %bitcast.23, s32[]{:T(128)} %bitcast.22), kind=kLoop, calls=%fused_computation.89 | loop fusion | flops 720 | bytes 296 | tf_op jit(solution)/shard_map/concatenate | solution.py:101
  22.3 1.7 %dynamic-slice_bitcast_fusion.3 = (bf16[512,512]{1,0:T(8,128)(2,1)S(1)}, bf16[512,512]{1,0:T(8,128)(2,1)S(1)}, bf16[512,512]{1,0:T(8,128)(2,1)S(1)}, bf16[512,512]{1,0:T(8,128)(2,1)S(1)}) fusion(bf16[512,1,4096]{2,0,1:T(8,128)(2,1)} %param.8, s32[]{:T(128)S(6)} %select_n.196, s32[]{:T(128)S(6)} %select_n.197, s32[]{:T(128)S(6)} %select_n.199, s32[]{:T(128)S(6)} %select_n.198), kind=kLoop, calls=%fused_computation.34 | loop fusion | bytes 4194320 | tf_op jit(solution)/shard_map/dynamic_slice | solution.py:55
  24.0 4.3 %fusion.6 = bf16[640,2048]{1,0:T(8,128)(2,1)} fusion(bf16[512,512]{1,0:T(8,128)(2,1)S(1)} %get-tuple-element.11, bf16[512,512]{1,0:T(8,128)(2,1)S(1)} %get-tuple-element.12, bf16[512,512]{1,0:T(8,128)(2,1)S(1)} %get-tuple-element.10, bf16[512,512]{1,0:T(8,128)(2,1)S(1)} %get-tuple-element.9), kind=kLoop, calls=%fused_computation.13 | loop fusion | flops 17039360 | bytes 4718592 | tf_op jit(solution)/shard_map/concatenate | solution.py:57
  28.3 0.0 collective-permute-done
  28.3 18.2 %collective-permute-done.1 = bf16[6,80,512]{2,1,0:T(8,128)(2,1)} collective-permute-done((bf16[6,80,512]{2,1,0:T(8,128)(2,1)}, bf16[6,80,512]{2,1,0:T(8,128)(2,1)}, u32[]{:S(2)}, u32[]{:S(2)}) %collective-permute-start.1) | collective-permute-done | bytes 491552 | tf_op jit(solution)/shard_map/ppermute | solution.py:91
  46.5 0.0 collective-permute-done.2
  46.5 0.9 slice_bitcast_fusion.7
  47.4 12.0 %collective-permute-start.7 = (bf16[6,48,512]{2,1,0:T(8,128)(2,1)}, bf16[6,48,512]{2,1,0:T(8,128)(2,1)}, u32[]{:S(2)}, u32[]{:S(2)}) collective-permute-start(bf16[6,48,512]{2,1,0:T(8,128)(2,1)} %get-tuple-element.18), channel_id=1, source_target_pairs={{0,12},{4,0},{8,4},{12,8},{1,13},{5,1},{9,5},{13,9},{2,14},{6,2},{... | collective-permute-start | bytes 884744 | tf_op jit(solution)/shard_map/ppermute | solution.py:91
  59.5 0.4 collective-permute-start.6
  59.9 0.1 collective-permute-start.5
  60.0 3.9 %fusion.7 = f32[6,80,5,128]{3,1,2,0:T(8,128)S(1)} fusion(bf16[5,128,2048,1]{2,1,0,3:T(8,128)(2,1)} %bitcast.20, bf16[6,80,512]{2,1,0:T(8,128)(2,1)} %collective-permute-done.2, bf16[6,80,512]{2,1,0:T(8,128)(2,1)} %collective-permute-done.1, bf16[6,80,512]{2,1,0:T(8,128)(2,1)} %collective-permute-done, bf16[6,80,512]{2,1,0:T(8,128)(2,1)S(1)} %get-tuple-element.13), kind=kOutput, calls=%fused_computation.16 | convolution fusion | flops 1266155520 | bytes 5816320 | tf_op jit(solution)/shard_map/dot_general | solution.py:95
  64.0 0.7 gather_fusion.2
  64.7 2.6 %collective-permute-done.7 = bf16[6,48,512]{2,1,0:T(8,128)(2,1)} collective-permute-done((bf16[6,48,512]{2,1,0:T(8,128)(2,1)}, bf16[6,48,512]{2,1,0:T(8,128)(2,1)}, u32[]{:S(2)}, u32[]{:S(2)}) %collective-permute-start.7) | collective-permute-done | bytes 294944 | tf_op jit(solution)/shard_map/ppermute | solution.py:91
  67.2 18.9 %collective-permute-done.6 = bf16[6,48,512]{2,1,0:T(8,128)(2,1)} collective-permute-done((bf16[6,48,512]{2,1,0:T(8,128)(2,1)}, bf16[6,48,512]{2,1,0:T(8,128)(2,1)}, u32[]{:S(2)}, u32[]{:S(2)}) %collective-permute-start.6) | collective-permute-done | bytes 294944 | tf_op jit(solution)/shard_map/ppermute | solution.py:91
  86.1 0.0 collective-permute-done.5
  86.1 3.1 %fusion.14 = f32[6,48,5,128]{3,1,2,0:T(8,128)S(1)} fusion(bf16[5,128,2048,1]{2,1,0,3:T(8,128)(2,1)} %bitcast.20, bf16[6,48,512]{2,1,0:T(8,128)(2,1)} %collective-permute-done.7, bf16[6,48,512]{2,1,0:T(8,128)(2,1)} %collective-permute-done.6, bf16[6,48,512]{2,1,0:T(8,128)(2,1)} %collective-permute-done.5, bf16[6,48,512]{2,1,0:T(8,128)(2,1)S(1)} %get-tuple-element.17), kind=kOutput, calls=%fused_computation.24 | convolution fusion | flops 759693312 | bytes 4538368 | tf_op jit(solution)/shard_map/dot_general | solution.py:95
  89.2 0.7 gather_fusion.4
  89.9 0.1 broadcast_multiply_fusion.1
  90.0 0.7 dynamic-slice_bitcast_fusion.5
  90.7 0.0 collective-permute-start.8
  90.7 0.1 broadcast_multiply_fusion
  90.9 0.6 collective-permute-start.3
  91.4 1.1 %collective-permute-done.8 = f32[2,6,48,128]{3,2,1,0:T(8,128)S(1)} collective-permute-done((f32[2,6,48,128]{3,2,1,0:T(8,128)}, f32[2,6,48,128]{3,2,1,0:T(8,128)S(1)}, u32[]{:S(2)}, u32[]{:S(2)}) %collective-permute-start.8) | collective-permute-done | bytes 294944 | tf_op jit(solution)/shard_map/ppermute | solution.py:25
  92.6 1.6 %collective-permute-start.9 = (f32[6,48,128]{2,1,0:T(8,128)S(1)}, f32[6,48,128]{2,1,0:T(8,128)S(1)}, u32[]{:S(2)}, u32[]{:S(2)}) collective-permute-start(f32[6,48,128]{2,1,0:T(8,128)S(1)} %dynamic-slice_bitcast_fusion.7), channel_id=1, source_target_pairs={{0,2},{2,0},{1,3},{3,1},{4,6},{6,4},{5,7},{7,5},{8,10},{10,8},{9,1... | collective-permute-start | bytes 442376 | tf_op jit(solution)/shard_map/ppermute | solution.py:25
  94.1 0.0 collective-permute-done.3
  94.1 0.1 bitcast_add_fusion
  94.2 0.6 collective-permute-start.4
  94.9 4.5 %collective-permute-done.9 = f32[6,48,128]{2,1,0:T(8,128)S(1)} collective-permute-done((f32[6,48,128]{2,1,0:T(8,128)S(1)}, f32[6,48,128]{2,1,0:T(8,128)S(1)}, u32[]{:S(2)}, u32[]{:S(2)}) %collective-permute-start.9) | collective-permute-done | bytes 147488 | tf_op jit(solution)/shard_map/ppermute | solution.py:25
  99.4 4.4 %collective-permute-done.4 = f32[6,80,128]{2,1,0:T(8,128)S(1)} collective-permute-done((f32[6,80,128]{2,1,0:T(8,128)S(1)}, f32[6,80,128]{2,1,0:T(8,128)S(1)}, u32[]{:S(2)}, u32[]{:S(2)}) %collective-permute-start.4) | collective-permute-done | bytes 245792 | tf_op jit(solution)/shard_map/ppermute | solution.py:25
  103.8 0.8 pad_maximum_fusion
  (16 shorter events, 0.2 us)
Async XLA Ops:
  0.0 1.4 %copy-start = (f32[1,1024]{1,0:T(1,128)S(1)}, f32[1,1024]{1,0:T(1,128)}, u32[]{:S(2)}) copy-start(f32[1,1024]{1,0:T(1,128)} %param.9) | copy-start | bytes 12292
  7.5 11.7 %copy-start.1 = (s32[1,2]{1,0:T(1,128)S(1)}, s32[1,2]{1,0:T(1,128)}, u32[]{:S(2)}) copy-start(s32[1,2]{1,0:T(1,128)} %param.13) | copy-start | bytes 28
  8.7 19.6 %collective-permute-start = (bf16[6,80,512]{2,1,0:T(8,128)(2,1)}, bf16[6,80,512]{2,1,0:T(8,128)(2,1)}, u32[]{:S(2)}, u32[]{:S(2)}) collective-permute-start(bf16[6,80,512]{2,1,0:T(8,128)(2,1)} %get-tuple-element.16), channel_id=1, source_target_pairs={{0,4},{4,8},{8,12},{12,0},{1,5},{5,9},{9,13},{13,1},{2,6},{6,10},{... | collective-permute-start | bytes 1474568 | tf_op jit(solution)/shard_map/ppermute | solution.py:91
  11.8 34.8 %collective-permute-start.1 = (bf16[6,80,512]{2,1,0:T(8,128)(2,1)}, bf16[6,80,512]{2,1,0:T(8,128)(2,1)}, u32[]{:S(2)}, u32[]{:S(2)}) collective-permute-start(bf16[6,80,512]{2,1,0:T(8,128)(2,1)} %get-tuple-element.15), channel_id=1, source_target_pairs={{0,8},{4,12},{8,0},{12,4},{1,9},{5,13},{9,1},{13,5},{2,10},{6,14},... | collective-permute-start | bytes 1474568 | tf_op jit(solution)/shard_map/ppermute | solution.py:91
  14.3 32.2 %collective-permute-start.2 = (bf16[6,80,512]{2,1,0:T(8,128)(2,1)}, bf16[6,80,512]{2,1,0:T(8,128)(2,1)}, u32[]{:S(2)}, u32[]{:S(2)}) collective-permute-start(bf16[6,80,512]{2,1,0:T(8,128)(2,1)} %get-tuple-element.14), channel_id=1, source_target_pairs={{0,12},{4,0},{8,4},{12,8},{1,13},{5,1},{9,5},{13,9},{2,14},{6,2},{... | collective-permute-start | bytes 1474568 | tf_op jit(solution)/shard_map/ppermute | solution.py:91
  19.9 1.1 %copy-start.2 = (s32[1,24]{1,0:T(1,128)S(1)}, s32[1,24]{1,0:T(1,128)}, u32[]{:S(2)}) copy-start(s32[1,24]{1,0:T(1,128)} %param.12) | copy-start | bytes 292
  19.9 1.1 %copy-start.3 = (s32[1,24]{1,0:T(1,128)S(1)}, s32[1,24]{1,0:T(1,128)}, u32[]{:S(2)}) copy-start(s32[1,24]{1,0:T(1,128)} %param.11) | copy-start | bytes 292
  47.4 19.8 %collective-permute-start.7 = (bf16[6,48,512]{2,1,0:T(8,128)(2,1)}, bf16[6,48,512]{2,1,0:T(8,128)(2,1)}, u32[]{:S(2)}, u32[]{:S(2)}) collective-permute-start(bf16[6,48,512]{2,1,0:T(8,128)(2,1)} %get-tuple-element.18), channel_id=1, source_target_pairs={{0,12},{4,0},{8,4},{12,8},{1,13},{5,1},{9,5},{13,9},{2,14},{6,2},{... | collective-permute-start | bytes 884744 | tf_op jit(solution)/shard_map/ppermute | solution.py:91
  59.5 26.6 %collective-permute-start.6 = (bf16[6,48,512]{2,1,0:T(8,128)(2,1)}, bf16[6,48,512]{2,1,0:T(8,128)(2,1)}, u32[]{:S(2)}, u32[]{:S(2)}) collective-permute-start(bf16[6,48,512]{2,1,0:T(8,128)(2,1)} %get-tuple-element.19), channel_id=1, source_target_pairs={{0,8},{4,12},{8,0},{12,4},{1,9},{5,13},{9,1},{13,5},{2,10},{6,14},... | collective-permute-start | bytes 884744 | tf_op jit(solution)/shard_map/ppermute | solution.py:91
  59.9 26.2 %collective-permute-start.5 = (bf16[6,48,512]{2,1,0:T(8,128)(2,1)}, bf16[6,48,512]{2,1,0:T(8,128)(2,1)}, u32[]{:S(2)}, u32[]{:S(2)}) collective-permute-start(bf16[6,48,512]{2,1,0:T(8,128)(2,1)} %get-tuple-element.20), channel_id=1, source_target_pairs={{0,4},{4,8},{8,12},{12,0},{1,5},{5,9},{9,13},{13,1},{2,6},{6,10},{... | collective-permute-start | bytes 884744 | tf_op jit(solution)/shard_map/ppermute | solution.py:91
  90.7 1.8 %collective-permute-start.8 = (f32[2,6,48,128]{3,2,1,0:T(8,128)}, f32[2,6,48,128]{3,2,1,0:T(8,128)S(1)}, u32[]{:S(2)}, u32[]{:S(2)}) collective-permute-start(f32[2,6,48,128]{3,2,1,0:T(8,128)} %dynamic-slice_bitcast_fusion.5), channel_id=1, source_target_pairs={{0,1},{1,0},{2,3},{3,2},{4,5},{5,4},{6,7},{7,6},{8,9},{9,8},{10,11... | collective-permute-start | bytes 884744 | tf_op jit(solution)/shard_map/ppermute | solution.py:25
  90.9 3.3 %collective-permute-start.3 = (f32[2,6,80,128]{3,2,1,0:T(8,128)S(1)}, f32[2,6,80,128]{3,2,1,0:T(8,128)S(1)}, u32[]{:S(2)}, u32[]{:S(2)}) collective-permute-start(f32[2,6,80,128]{3,2,1,0:T(8,128)S(1)} %dynamic-slice_bitcast_fusion.4), channel_id=1, source_target_pairs={{0,1},{1,0},{2,3},{3,2},{4,5},{5,4},{6,7},{7,6},{8,9},{9,8},{10,11... | collective-permute-start | bytes 1474568 | tf_op jit(solution)/shard_map/ppermute | solution.py:25
  92.6 6.8 %collective-permute-start.9 = (f32[6,48,128]{2,1,0:T(8,128)S(1)}, f32[6,48,128]{2,1,0:T(8,128)S(1)}, u32[]{:S(2)}, u32[]{:S(2)}) collective-permute-start(f32[6,48,128]{2,1,0:T(8,128)S(1)} %dynamic-slice_bitcast_fusion.7), channel_id=1, source_target_pairs={{0,2},{2,0},{1,3},{3,1},{4,6},{6,4},{5,7},{7,5},{8,10},{10,8},{9,1... | collective-permute-start | bytes 442376 | tf_op jit(solution)/shard_map/ppermute | solution.py:25
  94.2 9.6 %collective-permute-start.4 = (f32[6,80,128]{2,1,0:T(8,128)S(1)}, f32[6,80,128]{2,1,0:T(8,128)S(1)}, u32[]{:S(2)}, u32[]{:S(2)}) collective-permute-start(f32[6,80,128]{2,1,0:T(8,128)S(1)} %dynamic-slice_bitcast_fusion.6), channel_id=1, source_target_pairs={{0,2},{2,0},{1,3},{3,1},{4,6},{6,4},{5,7},{7,5},{8,10},{10,8},{9,1... | collective-permute-start | bytes 737288 | tf_op jit(solution)/shard_map/ppermute | solution.py:25

commit v3 on v2

--- a/solution.py
+++ b/solution.py
@@ -7,7 +7,8 @@
 
 
 BLOCK = 128
-ROW_SPLIT = (80, 48)
+ROW_SPLIT = (96, 32)
+GATE = True
 
 
 def ring_reduce_scatter(x, axis_name, dim):
@@ -80,7 +81,7 @@
             sent.append((got.astype(jnp.float32) * p_half[layer]).astype(jnp.bfloat16))
         row_start += rows
         prev_sent = sent
-        if gate is not None:
+        if GATE and gate is not None:
             sent, _ = lax.optimization_barrier((sent, gate))
         pieces = []
         for layer in range(l_dev):

time: 105 us -> 106 us (level)
  waiting for transfers between devices: 49.6 us -> 45.7 us
  local copies, waits for them, and re-layouts: 13.3 us -> 16.9 us
  starting transfers between devices: 22.3 us -> 24.1 us
  other arithmetic: 9.42 us -> 8.34 us
    ppermute x6, waiting for transfers between devices: 39.6 us -> 35.3 us  [shards(): piece = lax.ppermute(piece, 'span', perm)]
    gather x2, local copies, waits for them, and re-layouts: 1.37 us -> 3.73 us  [shards(): combos.at[slot_row, :, pick_train, :].get(mode='promise_in_bounds')]
    ppermute x6, starting transfers between devices: 19.6 us -> 21.8 us  [shards(): piece = lax.ppermute(piece, 'span', perm)]
    unnamed x8 -> x18, local copies, waits for them, and re-layouts: 0.02 us -> 1.37 us
    concatenate x1, other arithmetic: 4.32 us -> 3.24 us  [shards(): train = jnp.concatenate(t_half, axis=1)]
  transfers between devices with their start and end apart: 10 -> 10, of which waited for: 6 -> 6; matrix products, arithmetic and copies ran while one was open for 14% -> 20% of each run, Pallas kernels for 0% -> 0%
where the time goes in v3:
time: 106 us; the launch traced here: 105 us
  waiting for transfers between devices  45.7 us (43%)
  starting transfers between devices  24.1 us (23%)
  local copies, waits for them, and re-layouts  16.9 us (16%)
  other arithmetic  8.34 us (8%)
  matrix products  7.32 us (7%)
  between operations  2.82 us (3%)
    ppermute x6, waiting for transfers between devices, shards(): piece = lax.ppermute(piece, 'span', perm)  35.3 us
    ppermute x6, starting transfers between devices, shards(): piece = lax.ppermute(piece, 'span', perm)  21.8 us
    ppermute x4, waiting for transfers between devices, ring_reduce_scatter(): recv = lax.ppermute(acc, axis_name, perm)  10.3 us
    dot_general x2, matrix products, shards(): lax.dot_general(arrived, train, (((1,), (1,)), ((), ())), preferred_eleme...  7.32 us
    gather x2, local copies, waits for them, and re-layouts, shards(): combos.at[slot_row, :, pick_train, :].get(mode='promise_in_bounds')  3.73 us
    concatenate x1, other arithmetic, shards(): train = jnp.concatenate(t_half, axis=1)  3.24 us
    gather x2, local copies, waits for them, and re-layouts, shards(): got = jnp.take(q3[:, row_start:row_start + rows], block_ids, axis=0)  2.81 us
    convert_element_type x2, other arithmetic, shards(): sent.append((got.astype(jnp.float32) * p_half[layer]).astype(jnp.bfloat16))  2.67 us
  transfers between devices with their start and end apart: 10, of which 6 were waited for; matrix products, arithmetic and copies ran while one was open for 20% of the time, Pallas kernels for 0%

profile of v3, /device:TPU:0, one launch (start us, length us, event | category | flops | bytes accessed | tf_op | source)
XLA Modules:
  0.0 105.2 jit_solution(65713701262772887)
XLA Ops:
  0.0 0.0 copy-start
  0.0 1.2 %gather_fusion = s32[4,6]{1,0:T(4,128)S(1)} fusion(s32[4,6]{1,0:T(4,128)} %param.10, s32[1024]{0:T(1024)S(1)} %pad_clamp_fusion.2), kind=kCustom, calls=%fused_computation | custom fusion | bytes 208 | tf_op jit(solution)/shard_map/gather | solution.py:73
  1.3 0.1 reshape.273
  1.4 0.0 copy-done
  1.4 1.7 %constant_dynamic-slice_fusion.1 = bf16[2048,1,512]{2,0,1:T(8,128)(2,1)S(1)} fusion(bf16[2048,1,1024]{2,0,1:T(8,128)(2,1)} %param.7, s32[]{:T(128)S(6)} %select_n.192), kind=kLoop, calls=%fused_computation.59 | loop fusion | bytes 4194308 | tf_op jit(solution)/shard_map/dynamic_slice | solution.py:51
  3.1 0.0 copy-start.1
  3.1 1.3 %copy-done.1 = bf16[2048,1,512]{2,0,1:T(8,128)(2,1)} copy-done((bf16[2048,1,512]{2,0,1:T(8,128)(2,1)}, bf16[2048,1,512]{2,0,1:T(8,128)(2,1)S(1)}, u32[]{:S(2)}) %copy-start.1) | copy-done | bytes 2097176
  4.5 0.1 slice.72
  4.7 2.2 %gather_fusion.1 = bf16[24,96,512]{2,1,0:T(8,128)(2,1)} fusion(bf16[16,96,512]{2,1,0:T(8,128)(2,1)S(1)} %slice.72, s32[1024]{0:T(1024)S(1)} %pad_clamp_fusion.1), kind=kCustom, calls=%fused_computation.1 | custom fusion | bytes 4718688 | tf_op jit(solution)/shard_map/jit(_take)/gather | solution.py:79
  6.9 2.4 %multiply_convert_fusion = bf16[4,6,96,512]{3,2,1,0:T(8,128)(2,1)S(1)} fusion(f32[512]{0:T(512)S(1)} %bitcast.94, bf16[4,6,96,512]{3,2,1,0:T(8,128)(2,1)} %bitcast.84, pred[4,6]{1,0:T(4,128)(4,1)S(1)} %compare_and_fusion.1), kind=kLoop, calls=%fused_computation.10 | loop fusion | flops 4718592 | bytes 4720664 | tf_op jit(solution)/shard_map/convert_element_type | solution.py:81
  9.3 0.0 copy-start.5
  9.3 1.5 %slice_bitcast_fusion.3 = (bf16[6,96,512]{2,1,0:T(8,128)(2,1)}, bf16[6,96,512]{2,1,0:T(8,128)(2,1)}, bf16[6,96,512]{2,1,0:T(8,128)(2,1)}, bf16[6,96,512]{2,1,0:T(8,128)(2,1)}) fusion(bf16[4,6,96,512]{3,2,1,0:T(8,128)(2,1)S(1)} %multiply_convert_fusion), kind=kLoop, calls=%fused_computation.34 | loop fusion | bytes 4718592 | tf_op jit(solution)/shard_map/concatenate | solution.py:95
  10.8 0.0 copy-start.6
  10.8 0.0 copy-start.7
  10.8 3.1 %collective-permute-start = (bf16[6,96,512]{2,1,0:T(8,128)(2,1)}, bf16[6,96,512]{2,1,0:T(8,128)(2,1)S(1)}, u32[]{:S(2)}, u32[]{:S(2)}) collective-permute-start(bf16[6,96,512]{2,1,0:T(8,128)(2,1)} %get-tuple-element.16), channel_id=1, source_target_pairs={{0,4},{4,8},{8,12},{12,0},{1,5},{5,9},{9,13},{13,1},{2,6},{6,10},{... | collective-permute-start | bytes 1769480 | tf_op jit(solution)/shard_map/ppermute | solution.py:92
  13.8 2.6 %collective-permute-start.1 = (bf16[6,96,512]{2,1,0:T(8,128)(2,1)}, bf16[6,96,512]{2,1,0:T(8,128)(2,1)}, u32[]{:S(2)}, u32[]{:S(2)}) collective-permute-start(bf16[6,96,512]{2,1,0:T(8,128)(2,1)} %get-tuple-element.15), channel_id=1, source_target_pairs={{0,8},{4,12},{8,0},{12,4},{1,9},{5,13},{9,1},{13,5},{2,10},{6,14},... | collective-permute-start | bytes 1769480 | tf_op jit(solution)/shard_map/ppermute | solution.py:92
  16.4 1.3 %collective-permute-start.2 = (bf16[6,96,512]{2,1,0:T(8,128)(2,1)}, bf16[6,96,512]{2,1,0:T(8,128)(2,1)}, u32[]{:S(2)}, u32[]{:S(2)}) collective-permute-start(bf16[6,96,512]{2,1,0:T(8,128)(2,1)} %get-tuple-element.14), channel_id=1, source_target_pairs={{0,12},{4,0},{8,4},{12,8},{1,13},{5,1},{9,5},{13,9},{2,14},{6,2},{... | collective-permute-start | bytes 1769480 | tf_op jit(solution)/shard_map/ppermute | solution.py:92
  17.8 0.6 fusion.34
  20.9 1.1 %slice.77 = bf16[16,32,512]{2,1,0:T(8,128)(2,1)S(1)} slice(bf16[16,128,512]{2,1,0:T(8,128)(2,1)} %bitcast.86), slice={[0:16], [96:128], [0:512]} | slice | bytes 1048576 | tf_op jit(solution)/shard_map/slice | solution.py:79
  22.0 0.1 reshape.274
  22.1 0.1 broadcast_in_dim.39
  22.2 0.0 copy-done.5
  22.2 0.6 fusion.33
  22.8 0.6 gather_fusion.3
  23.4 0.3 multiply_convert_fusion.1
  23.6 0.0 copy-done.6
  23.6 0.0 copy-done.7
  23.6 1.3 %fusion.30 = s32[24]{0:T(128)S(1)} fusion(s32[1,24]{1,0:T(1,128)S(1)} %copy-done.6, s32[1,24]{1,0:T(1,128)S(1)} %copy-done.7, s32[]{:T(128)} %bitcast.23, s32[]{:T(128)} %bitcast.22), kind=kLoop, calls=%fused_computation.89 | loop fusion | flops 720 | bytes 296 | tf_op jit(solution)/shard_map/concatenate | solution.py:102
  24.9 1.7 %dynamic-slice_bitcast_fusion.4 = (bf16[512,512]{1,0:T(8,128)(2,1)S(1)}, bf16[512,512]{1,0:T(8,128)(2,1)S(1)}, bf16[512,512]{1,0:T(8,128)(2,1)S(1)}, bf16[512,512]{1,0:T(8,128)(2,1)S(1)}) fusion(bf16[512,1,4096]{2,0,1:T(8,128)(2,1)} %param.8, s32[]{:T(128)S(6)} %select_n.196, s32[]{:T(128)S(6)} %select_n.197, s32[]{:T(128)S(6)} %select_n.199, s32[]{:T(128)S(6)} %select_n.198), kind=kLoop, calls=%fused_computation.41 | loop fusion | bytes 4194320 | tf_op jit(solution)/shard_map/dynamic_slice | solution.py:56
  26.6 0.0 copy-start.4
  26.6 3.2 %fusion.6 = bf16[640,2048]{1,0:T(8,128)(2,1)S(1)} fusion(bf16[512,512]{1,0:T(8,128)(2,1)S(1)} %get-tuple-element.11, bf16[512,512]{1,0:T(8,128)(2,1)S(1)} %get-tuple-element.12, bf16[512,512]{1,0:T(8,128)(2,1)S(1)} %get-tuple-element.10, bf16[512,512]{1,0:T(8,128)(2,1)S(1)} %get-tuple-element.9), kind=kLoop, calls=%fused_computation.13 | loop fusion | flops 17039360 | bytes 4718592 | tf_op jit(solution)/shard_map/concatenate | solution.py:58
  29.9 0.0 copy-start.2
  29.9 0.5 collective-permute-done
  30.4 0.0 copy-start.8
  30.4 24.5 %collective-permute-done.1 = bf16[6,96,512]{2,1,0:T(8,128)(2,1)} collective-permute-done((bf16[6,96,512]{2,1,0:T(8,128)(2,1)}, bf16[6,96,512]{2,1,0:T(8,128)(2,1)}, u32[]{:S(2)}, u32[]{:S(2)}) %collective-permute-start.1) | collective-permute-done | bytes 589856 | tf_op jit(solution)/shard_map/ppermute | solution.py:92
  54.9 0.0 copy-done.8
  54.9 0.0 collective-permute-done.2
  54.9 0.1 slice_bitcast_fusion.7
  55.0 14.2 %collective-permute-start.7 = (bf16[6,32,512]{2,1,0:T(8,128)(2,1)S(1)}, bf16[6,32,512]{2,1,0:T(8,128)(2,1)S(1)}, u32[]{:S(2)}, u32[]{:S(2)}) collective-permute-start(bf16[6,32,512]{2,1,0:T(8,128)(2,1)S(1)} %get-tuple-element.18), channel_id=1, source_target_pairs={{0,12},{4,0},{8,4},{12,8},{1,13},{5,1},{9,5},{13,9},{2,14},{6,2},{... | collective-permute-start | bytes 589832 | tf_op jit(solution)/shard_map/ppermute | solution.py:92
  69.2 0.4 collective-permute-start.6
  69.6 0.2 collective-permute-start.5
  69.8 0.0 copy-done.2
  69.8 0.0 copy-done.4
  69.8 4.6 %fusion.7 = f32[6,96,5,128]{3,1,2,0:T(8,128)} fusion(bf16[5,128,2048,1]{2,1,0,3:T(8,128)(2,1)S(1)} %bitcast.90, bf16[6,96,512]{2,1,0:T(8,128)(2,1)} %collective-permute-done.2, bf16[6,96,512]{2,1,0:T(8,128)(2,1)} %collective-permute-done.1, bf16[6,96,512]{2,1,0:T(8,128)(2,1)} %copy-done.8, bf16[6,96,512]{2,1,0:T(8,128)(2,1)S(1)} %copy-done.4), kind=kOutput, calls=%fused_computation.15 | convolution fusion | flops 1519386624 | bytes 6455296 | tf_op jit(solution)/shard_map/dot_general | solution.py:96
  74.4 2.0 %gather_fusion.2 = f32[24,96,128]{2,1,0:T(8,128)S(1)} fusion(f32[6,96,5,128]{3,1,2,0:T(8,128)} %fusion.7, s32[24]{0:T(128)S(1)} %fusion.30), kind=kCustom, calls=%fused_computation.2 | custom fusion | bytes 2359488 | tf_op jit(solution)/shard_map/gather | solution.py:102
  76.4 0.0 copy-start.3
  76.4 0.1 broadcast_multiply_fusion
  76.6 0.1 collective-permute-start.3
  76.7 0.0 collective-permute-done.7
  76.7 10.3 %collective-permute-done.6 = bf16[6,32,512]{2,1,0:T(8,128)(2,1)S(1)} collective-permute-done((bf16[6,32,512]{2,1,0:T(8,128)(2,1)S(1)}, bf16[6,32,512]{2,1,0:T(8,128)(2,1)S(1)}, u32[]{:S(2)}, u32[]{:S(2)}) %collective-permute-start.6) | collective-permute-done | bytes 196640 | tf_op jit(solution)/shard_map/ppermute | solution.py:92
  87.0 0.0 collective-permute-done.5
  87.0 0.0 copy-done.3
  87.0 2.8 %fusion.14 = f32[6,32,5,128]{3,1,2,0:T(8,128)} fusion(bf16[5,128,2048,1]{2,1,0,3:T(8,128)(2,1)S(1)} %bitcast.91, bf16[6,32,512]{2,1,0:T(8,128)(2,1)S(1)} %collective-permute-done.7, bf16[6,32,512]{2,1,0:T(8,128)(2,1)S(1)} %collective-permute-done.6, bf16[6,32,512]{2,1,0:T(8,128)(2,1)} %collective-permute-done.5, bf16[6,32,512]{2,1,0:T(8,128)(2,1)S(1)} %get-tuple-element.17), kind=kOutput, calls=%fused_computation.24 | convolution fusion | flops 506462208 | bytes 3899392 | tf_op jit(solution)/shard_map/dot_general | solution.py:96
  89.8 1.7 %gather_fusion.4 = f32[24,32,128]{2,1,0:T(8,128)S(1)} fusion(f32[6,32,5,128]{3,1,2,0:T(8,128)} %fusion.14, s32[24]{0:T(128)S(1)} %fusion.30), kind=kCustom, calls=%fused_computation.4 | custom fusion | bytes 786624 | tf_op jit(solution)/shard_map/gather | solution.py:102
  91.6 0.1 collective-permute-start.8
  91.7 1.4 %collective-permute-done.8 = f32[2,6,32,128]{3,2,1,0:T(8,128)S(1)} collective-permute-done((f32[2,6,32,128]{3,2,1,0:T(8,128)S(1)}, f32[2,6,32,128]{3,2,1,0:T(8,128)S(1)}, u32[]{:S(2)}, u32[]{:S(2)}) %collective-permute-start.8) | collective-permute-done | bytes 196640 | tf_op jit(solution)/shard_map/ppermute | solution.py:26
  93.1 1.6 %collective-permute-start.9 = (f32[6,32,128]{2,1,0:T(8,128)S(1)}, f32[6,32,128]{2,1,0:T(8,128)S(1)}, u32[]{:S(2)}, u32[]{:S(2)}) collective-permute-start(f32[6,32,128]{2,1,0:T(8,128)S(1)} %dynamic-slice_bitcast_fusion.7), channel_id=1, source_target_pairs={{0,2},{2,0},{1,3},{3,1},{4,6},{6,4},{5,7},{7,5},{8,10},{10,8},{9,1... | collective-permute-start | bytes 294920 | tf_op jit(solution)/shard_map/ppermute | solution.py:26
  94.7 0.0 collective-permute-done.3
  94.7 0.1 bitcast_add_fusion
  94.8 0.6 collective-permute-start.4
  95.4 3.3 %collective-permute-done.9 = f32[6,32,128]{2,1,0:T(8,128)S(1)} collective-permute-done((f32[6,32,128]{2,1,0:T(8,128)S(1)}, f32[6,32,128]{2,1,0:T(8,128)S(1)}, u32[]{:S(2)}, u32[]{:S(2)}) %collective-permute-start.9) | collective-permute-done | bytes 98336 | tf_op jit(solution)/shard_map/ppermute | solution.py:26
  98.8 5.6 %collective-permute-done.4 = f32[6,96,128]{2,1,0:T(8,128)S(1)} collective-permute-done((f32[6,96,128]{2,1,0:T(8,128)S(1)}, f32[6,96,128]{2,1,0:T(8,128)S(1)}, u32[]{:S(2)}, u32[]{:S(2)}) %collective-permute-start.4) | collective-permute-done | bytes 294944 | tf_op jit(solution)/shard_map/ppermute | solution.py:26
  104.4 0.8 pad_maximum_fusion
  (18 shorter events, 0.3 us)
Async XLA Ops:
  0.0 1.4 %copy-start = (f32[1,1024]{1,0:T(1,128)S(1)}, f32[1,1024]{1,0:T(1,128)}, u32[]{:S(2)}) copy-start(f32[1,1024]{1,0:T(1,128)} %param.9) | copy-start | bytes 12292
  3.1 1.3 %copy-start.1 = (bf16[2048,1,512]{2,0,1:T(8,128)(2,1)}, bf16[2048,1,512]{2,0,1:T(8,128)(2,1)S(1)}, u32[]{:S(2)}) copy-start(bf16[2048,1,512]{2,0,1:T(8,128)(2,1)S(1)} %constant_dynamic-slice_fusion.1) | copy-start | bytes 6291460
  9.3 12.9 %copy-start.5 = (s32[1,2]{1,0:T(1,128)S(1)}, s32[1,2]{1,0:T(1,128)}, u32[]{:S(2)}) copy-start(s32[1,2]{1,0:T(1,128)} %param.13) | copy-start | bytes 28
  10.8 12.9 %copy-start.6 = (s32[1,24]{1,0:T(1,128)S(1)}, s32[1,24]{1,0:T(1,128)}, u32[]{:S(2)}) copy-start(s32[1,24]{1,0:T(1,128)} %param.12) | copy-start | bytes 292
  10.8 12.9 %copy-start.7 = (s32[1,24]{1,0:T(1,128)S(1)}, s32[1,24]{1,0:T(1,128)}, u32[]{:S(2)}) copy-start(s32[1,24]{1,0:T(1,128)} %param.11) | copy-start | bytes 292
  10.8 19.6 %collective-permute-start = (bf16[6,96,512]{2,1,0:T(8,128)(2,1)}, bf16[6,96,512]{2,1,0:T(8,128)(2,1)S(1)}, u32[]{:S(2)}, u32[]{:S(2)}) collective-permute-start(bf16[6,96,512]{2,1,0:T(8,128)(2,1)} %get-tuple-element.16), channel_id=1, source_target_pairs={{0,4},{4,8},{8,12},{12,0},{1,5},{5,9},{9,13},{13,1},{2,6},{6,10},{... | collective-permute-start | bytes 1769480 | tf_op jit(solution)/shard_map/ppermute | solution.py:92
  13.8 41.1 %collective-permute-start.1 = (bf16[6,96,512]{2,1,0:T(8,128)(2,1)}, bf16[6,96,512]{2,1,0:T(8,128)(2,1)}, u32[]{:S(2)}, u32[]{:S(2)}) collective-permute-start(bf16[6,96,512]{2,1,0:T(8,128)(2,1)} %get-tuple-element.15), channel_id=1, source_target_pairs={{0,8},{4,12},{8,0},{12,4},{1,9},{5,13},{9,1},{13,5},{2,10},{6,14},... | collective-permute-start | bytes 1769480 | tf_op jit(solution)/shard_map/ppermute | solution.py:92
  16.4 38.5 %collective-permute-start.2 = (bf16[6,96,512]{2,1,0:T(8,128)(2,1)}, bf16[6,96,512]{2,1,0:T(8,128)(2,1)}, u32[]{:S(2)}, u32[]{:S(2)}) collective-permute-start(bf16[6,96,512]{2,1,0:T(8,128)(2,1)} %get-tuple-element.14), channel_id=1, source_target_pairs={{0,12},{4,0},{8,4},{12,8},{1,13},{5,1},{9,5},{13,9},{2,14},{6,2},{... | collective-permute-start | bytes 1769480 | tf_op jit(solution)/shard_map/ppermute | solution.py:92
  26.6 43.2 %copy-start.4 = (bf16[6,96,512]{2,1,0:T(8,128)(2,1)S(1)}, bf16[6,96,512]{2,1,0:T(8,128)(2,1)}, u32[]{:S(2)}) copy-start(bf16[6,96,512]{2,1,0:T(8,128)(2,1)} %get-tuple-element.13) | copy-start | bytes 1769476
  29.9 39.9 %copy-start.2 = (bf16[640,2048]{1,0:T(8,128)(2,1)}, bf16[640,2048]{1,0:T(8,128)(2,1)S(1)}, u32[]{:S(2)}) copy-start(bf16[640,2048]{1,0:T(8,128)(2,1)S(1)} %fusion.6) | copy-start | bytes 7864324
  30.4 24.5 %copy-start.8 = (bf16[6,96,512]{2,1,0:T(8,128)(2,1)}, bf16[6,96,512]{2,1,0:T(8,128)(2,1)S(1)}, u32[]{:S(2)}) copy-start(bf16[6,96,512]{2,1,0:T(8,128)(2,1)S(1)} %collective-permute-done) | copy-start | bytes 1769476
  55.0 21.7 %collective-permute-start.7 = (bf16[6,32,512]{2,1,0:T(8,128)(2,1)S(1)}, bf16[6,32,512]{2,1,0:T(8,128)(2,1)S(1)}, u32[]{:S(2)}, u32[]{:S(2)}) collective-permute-start(bf16[6,32,512]{2,1,0:T(8,128)(2,1)S(1)} %get-tuple-element.18), channel_id=1, source_target_pairs={{0,12},{4,0},{8,4},{12,8},{1,13},{5,1},{9,5},{13,9},{2,14},{6,2},{... | collective-permute-start | bytes 589832 | tf_op jit(solution)/shard_map/ppermute | solution.py:92
  69.2 17.9 %collective-permute-start.6 = (bf16[6,32,512]{2,1,0:T(8,128)(2,1)S(1)}, bf16[6,32,512]{2,1,0:T(8,128)(2,1)S(1)}, u32[]{:S(2)}, u32[]{:S(2)}) collective-permute-start(bf16[6,32,512]{2,1,0:T(8,128)(2,1)S(1)} %get-tuple-element.19), channel_id=1, source_target_pairs={{0,8},{4,12},{8,0},{12,4},{1,9},{5,13},{9,1},{13,5},{2,10},{6,14},... | collective-permute-start | bytes 589832 | tf_op jit(solution)/shard_map/ppermute | solution.py:92
  69.6 17.4 %collective-permute-start.5 = (bf16[6,32,512]{2,1,0:T(8,128)(2,1)S(1)}, bf16[6,32,512]{2,1,0:T(8,128)(2,1)}, u32[]{:S(2)}, u32[]{:S(2)}) collective-permute-start(bf16[6,32,512]{2,1,0:T(8,128)(2,1)S(1)} %get-tuple-element.20), channel_id=1, source_target_pairs={{0,4},{4,8},{8,12},{12,0},{1,5},{5,9},{9,13},{13,1},{2,6},{6,10},{... | collective-permute-start | bytes 589832 | tf_op jit(solution)/shard_map/ppermute | solution.py:92
  76.4 10.6 %copy-start.3 = (bf16[640,2048]{1,0:T(8,128)(2,1)S(1)}, bf16[640,2048]{1,0:T(8,128)(2,1)}, u32[]{:S(2)}) copy-start(bf16[640,2048]{1,0:T(8,128)(2,1)} %copy-done.2) | copy-start | bytes 7864324
  76.6 18.1 %collective-permute-start.3 = (f32[2,6,96,128]{3,2,1,0:T(8,128)S(1)}, f32[2,6,96,128]{3,2,1,0:T(8,128)S(1)}, u32[]{:S(2)}, u32[]{:S(2)}) collective-permute-start(f32[2,6,96,128]{3,2,1,0:T(8,128)S(1)} %dynamic-slice_bitcast_fusion), channel_id=1, source_target_pairs={{0,1},{1,0},{2,3},{3,2},{4,5},{5,4},{6,7},{7,6},{8,9},{9,8},{10,11... | collective-permute-start | bytes 1769480 | tf_op jit(solution)/shard_map/ppermute | solution.py:26
  91.6 1.5 %collective-permute-start.8 = (f32[2,6,32,128]{3,2,1,0:T(8,128)S(1)}, f32[2,6,32,128]{3,2,1,0:T(8,128)S(1)}, u32[]{:S(2)}, u32[]{:S(2)}) collective-permute-start(f32[2,6,32,128]{3,2,1,0:T(8,128)S(1)} %dynamic-slice_bitcast_fusion.6), channel_id=1, source_target_pairs={{0,1},{1,0},{2,3},{3,2},{4,5},{5,4},{6,7},{7,6},{8,9},{9,8},{10,11... | collective-permute-start | bytes 589832 | tf_op jit(solution)/shard_map/ppermute | solution.py:26
  93.1 5.6 %collective-permute-start.9 = (f32[6,32,128]{2,1,0:T(8,128)S(1)}, f32[6,32,128]{2,1,0:T(8,128)S(1)}, u32[]{:S(2)}, u32[]{:S(2)}) collective-permute-start(f32[6,32,128]{2,1,0:T(8,128)S(1)} %dynamic-slice_bitcast_fusion.7), channel_id=1, source_target_pairs={{0,2},{2,0},{1,3},{3,1},{4,6},{6,4},{5,7},{7,5},{8,10},{10,8},{9,1... | collective-permute-start | bytes 294920 | tf_op jit(solution)/shard_map/ppermute | solution.py:26
  94.8 9.6 %collective-permute-start.4 = (f32[6,96,128]{2,1,0:T(8,128)S(1)}, f32[6,96,128]{2,1,0:T(8,128)S(1)}, u32[]{:S(2)}, u32[]{:S(2)}) collective-permute-start(f32[6,96,128]{2,1,0:T(8,128)S(1)} %dynamic-slice_bitcast_fusion.5), channel_id=1, source_target_pairs={{0,2},{2,0},{1,3},{3,1},{4,6},{6,4},{5,7},{7,5},{8,10},{10,8},{9,1... | collective-permute-start | bytes 884744 | tf_op jit(solution)/shard_map/ppermute | solution.py:26

commit v4 on v3

--- a/solution.py
+++ b/solution.py
@@ -7,8 +7,8 @@
 
 
 BLOCK = 128
-ROW_SPLIT = (96, 32)
-GATE = True
+ROW_SPLIT = (24, 40)
+GATE = False
 
 
 def ring_reduce_scatter(x, axis_name, dim):
@@ -38,24 +38,19 @@
     pmax = pair_slot.shape[1]
     cap = requests.shape[1]
     phalf = pmax // pair_count.shape[1]
-    half = features // n_rep
     per_dev = pmax // (n_layer * n_rep)
     rep_index = lax.axis_index("rep")
     span_index = lax.axis_index("span")
+    own_rows = BLOCK // n_rep
 
     dests = (span_index + jnp.arange(n_span, dtype=jnp.int32)) % n_span
     sources = (span_index - jnp.arange(n_span, dtype=jnp.int32) + n_span) % n_span
-    q_half = []
-    t_half = []
+    t_parts = []
     for layer in range(l_dev):
-        q_l = lax.dynamic_slice_in_dim(queries[:, layer, :], rep_index * half, half, axis=1)
-        q_l = q_l * 1
-        q_half.append(q_l)
         t_l = train_grads[:, layer, :]
         for k in range(n_span):
-            t_half.append(lax.dynamic_slice_in_dim(t_l, sources[k] * features + rep_index * half, half, axis=1))
-    p_half = lax.dynamic_slice_in_dim(precond, rep_index * half, half, axis=1)
-    train = jnp.concatenate(t_half, axis=1)
+            t_parts.append(lax.dynamic_slice_in_dim(t_l, sources[k] * features, features, axis=1))
+    train = jnp.concatenate(t_parts, axis=1)
     train = jnp.concatenate([train, jnp.zeros((BLOCK, train.shape[1]), train.dtype)], axis=0)
 
     score_scale = 1.0 / math.sqrt(l_dev * n_layer * d_full)
@@ -75,10 +70,10 @@
             block_ids, _ = lax.optimization_barrier((block_ids, prev_sent))
         sent = []
         for layer in range(l_dev):
-            q3 = q_half[layer].reshape(n_query // BLOCK, BLOCK, half)
-            got = jnp.take(q3[:, row_start:row_start + rows], block_ids, axis=0)
-            got = got.reshape(n_span, cap, rows, half)
-            sent.append((got.astype(jnp.float32) * p_half[layer]).astype(jnp.bfloat16))
+            q3 = queries[:, layer, :].reshape(n_query // BLOCK, BLOCK, features)
+            q3 = lax.dynamic_slice_in_dim(q3, rep_index * own_rows + row_start, rows, axis=1)
+            got = jnp.take(q3, block_ids, axis=0).reshape(n_span, cap, rows, features)
+            sent.append((got.astype(jnp.float32) * precond[layer]).astype(jnp.bfloat16))
         row_start += rows
         prev_sent = sent
         if GATE and gate is not None:
@@ -101,10 +96,19 @@
         ).reshape(cap, rows, tb_dev + 1, BLOCK)
         partial = combos.at[slot_row, :, pick_train, :].get(mode="promise_in_bounds") * score_scale
         partial = partial.reshape(n_layer, n_rep, per_dev, rows, BLOCK)
-        partial = ring_reduce_scatter(partial, "rep", 1)
         partial = ring_reduce_scatter(partial, "layer", 0)
-        outs.append(partial)
-    summed = jnp.concatenate(outs, axis=1).reshape(per_dev * BLOCK, BLOCK)
+        got_rows = [lax.dynamic_index_in_dim(partial, rep_index, axis=0, keepdims=False)]
+        for k in range(1, n_rep):
+            perm = [(i, (i + k) % n_rep) for i in range(n_rep)]
+            send = lax.dynamic_index_in_dim(partial, (rep_index + k) % n_rep, axis=0, keepdims=False)
+            got_rows.append(lax.ppermute(send, "rep", perm))
+        by_owner = jnp.stack(got_rows, axis=0)
+        owner_order = (rep_index - jnp.arange(n_rep, dtype=jnp.int32) + n_rep) % n_rep
+        order = jnp.argsort(owner_order)
+        by_owner = jnp.take(by_owner, order, axis=0)
+        outs.append(by_owner)
+    summed = jnp.concatenate(outs, axis=2)
+    summed = jnp.transpose(summed, (1, 0, 2, 3)).reshape(per_dev * BLOCK, BLOCK)
     return summed[None]
 
 

time: 106 us -> 92.7 us (0.87)
  the two profiles are of different devices: /device:TPU:0 before, /device:TPU:9 now
where the time goes in v4:
time: 92.7 us; the launch traced here: 92.4 us
  waiting for transfers between devices  40.5 us (44%)
  other arithmetic  15.6 us (17%)
  local copies, waits for them, and re-layouts  14 us (15%)
  starting transfers between devices  11.8 us (13%)
  matrix products  7.52 us (8%)
  between operations  2.92 us (3%)
    ppermute x6, waiting for transfers between devices, shards(): piece = lax.ppermute(piece, 'span', perm)  31.6 us
    concatenate x1, other arithmetic, shards(): train = jnp.concatenate(t_parts, axis=1)  12.1 us
    dot_general x2, matrix products, shards(): lax.dot_general(arrived, train, (((1,), (1,)), ((), ())), preferred_eleme...  7.52 us
    ppermute x2, waiting for transfers between devices, ring_reduce_scatter(): recv = lax.ppermute(acc, axis_name, perm)  7.07 us
    ppermute x6, starting transfers between devices, shards(): piece = lax.ppermute(piece, 'span', perm)  7.03 us
    dynamic_slice x1, local copies, waits for them, and re-layouts, shards(): lax.dynamic_slice_in_dim(t_l, sources[k] * features, features, axis=1)  2.64 us
    dynamic_slice x2, local copies, waits for them, and re-layouts, shards(): lax.dynamic_slice_in_dim(q3, rep_index * own_rows + row_start, rows, axis=1)  2.62 us
    ppermute x2, starting transfers between devices, ring_reduce_scatter(): recv = lax.ppermute(acc, axis_name, perm)  2.55 us
  transfers between devices with their start and end apart: 10, of which 7 were waited for; matrix products, arithmetic and copies ran while one was open for 28% of the time, Pallas kernels for 0%

profile of v4, /device:TPU:9, one launch (start us, length us, event | category | flops | bytes accessed | tf_op | source)
XLA Modules:
  0.0 92.4 jit_solution(69302994015152632)
XLA Ops:
  0.0 0.0 copy-start
  0.0 0.0 copy-start.3
  0.0 0.7 copy-done
  0.7 0.6 gather_fusion
  1.2 0.1 reshape.271
  1.4 1.2 %constant_dynamic-slice_fusion.3 = bf16[16,24,1024]{2,1,0:T(8,128)(2,1)S(1)} fusion(bf16[16,128,1024]{2,1,0:T(8,128)(2,1)} %bitcast.92, s32[]{:T(128)S(6)} %select_n.213), kind=kLoop, calls=%fused_computation.66 | loop fusion | bytes 1572868 | tf_op jit(solution)/shard_map/dynamic_slice | solution.py:74
  2.6 0.6 gather_fusion.1
  3.2 0.0 copy-done.3
  3.2 0.4 multiply_convert_fusion.1
  3.6 1.0 %slice_bitcast_fusion.7 = (bf16[6,24,1024]{2,1,0:T(8,128)(2,1)}, bf16[6,24,1024]{2,1,0:T(8,128)(2,1)}, bf16[6,24,1024]{2,1,0:T(8,128)(2,1)}, bf16[6,24,1024]{2,1,0:T(8,128)(2,1)}) fusion(bf16[4,6,24,1024]{3,2,1,0:T(8,128)(2,1)S(1)} %multiply_convert_fusion.1), kind=kLoop, calls=%fused_computation.45 | loop fusion | bytes 2359296 | tf_op jit(solution)/shard_map/concatenate | solution.py:90
  4.7 1.3 %collective-permute-start = (bf16[6,24,1024]{2,1,0:T(8,128)(2,1)}, bf16[6,24,1024]{2,1,0:T(8,128)(2,1)}, u32[]{:S(2)}, u32[]{:S(2)}) collective-permute-start(bf16[6,24,1024]{2,1,0:T(8,128)(2,1)} %get-tuple-element.20), channel_id=1, source_target_pairs={{0,4},{4,8},{8,12},{12,0},{1,5},{5,9},{9,13},{13,1},{2,6},{6,10},{... | collective-permute-start | bytes 884744 | tf_op jit(solution)/shard_map/ppermute | solution.py:87
  6.0 1.0 %collective-permute-start.1 = (bf16[6,24,1024]{2,1,0:T(8,128)(2,1)}, bf16[6,24,1024]{2,1,0:T(8,128)(2,1)}, u32[]{:S(2)}, u32[]{:S(2)}) collective-permute-start(bf16[6,24,1024]{2,1,0:T(8,128)(2,1)} %get-tuple-element.19), channel_id=1, source_target_pairs={{0,8},{4,12},{8,0},{12,4},{1,9},{5,13},{9,1},{13,5},{2,10},{6,14},... | collective-permute-start | bytes 884744 | tf_op jit(solution)/shard_map/ppermute | solution.py:87
  7.0 1.5 %collective-permute-start.2 = (bf16[6,24,1024]{2,1,0:T(8,128)(2,1)}, bf16[6,24,1024]{2,1,0:T(8,128)(2,1)}, u32[]{:S(2)}, u32[]{:S(2)}) collective-permute-start(bf16[6,24,1024]{2,1,0:T(8,128)(2,1)} %get-tuple-element.18), channel_id=1, source_target_pairs={{0,12},{4,0},{8,4},{12,8},{1,13},{5,1},{9,5},{13,9},{2,14},{6,2},{... | collective-permute-start | bytes 884744 | tf_op jit(solution)/shard_map/ppermute | solution.py:87
  8.5 0.1 reshape.272
  8.6 1.4 %constant_dynamic-slice_fusion.1 = bf16[16,40,1024]{2,1,0:T(8,128)(2,1)S(1)} fusion(bf16[16,128,1024]{2,1,0:T(8,128)(2,1)} %bitcast.93, s32[]{:T(128)S(6)} %select_n.236), kind=kLoop, calls=%fused_computation.64 | loop fusion | bytes 2621444 | tf_op jit(solution)/shard_map/dynamic_slice | solution.py:74
  10.0 0.1 broadcast_in_dim.65
  10.1 0.7 gather_fusion.4
  10.8 0.7 multiply_convert_fusion
  11.5 0.2 slice_bitcast_fusion.3
  11.6 0.1 collective-permute-start.5
  11.7 3.1 %collective-permute-start.6 = (bf16[6,40,1024]{2,1,0:T(8,128)(2,1)S(1)}, bf16[6,40,1024]{2,1,0:T(8,128)(2,1)}, u32[]{:S(2)}, u32[]{:S(2)}) collective-permute-start(bf16[6,40,1024]{2,1,0:T(8,128)(2,1)S(1)} %get-tuple-element.15), channel_id=1, source_target_pairs={{0,8},{4,12},{8,0},{12,4},{1,9},{5,13},{9,1},{13,5},{2,10},{6,14},... | collective-permute-start | bytes 1474568 | tf_op jit(solution)/shard_map/ppermute | solution.py:87
  14.9 0.7 fusion.35
  18.1 0.6 sort.19
  18.8 2.6 %dynamic-slice_bitcast_fusion.3 = (bf16[512,1024]{1,0:T(8,128)(2,1)S(1)}, bf16[512,1024]{1,0:T(8,128)(2,1)S(1)}, bf16[512,1024]{1,0:T(8,128)(2,1)S(1)}, bf16[512,1024]{1,0:T(8,128)(2,1)S(1)}) fusion(bf16[512,1,4096]{2,0,1:T(8,128)(2,1)} %param.8, s32[]{:T(128)S(6)} %select_n.217, s32[]{:T(128)S(6)} %select_n.218, s32[]{:T(128)S(6)} %select_n.220, ...), kind=kLoop, calls=%fused_computation.36 | loop fusion | bytes 8388624 | tf_op jit(solution)/shard_map/dynamic_slice | solution.py:52
  21.4 0.0 copy-start.4
  21.4 0.0 copy-start.5
  21.4 0.0 copy-start.6
  21.4 0.0 copy-start.2
  21.5 12.1 %fusion.6 = bf16[640,4096]{1,0:T(8,128)(2,1)S(1)} fusion(bf16[512,1024]{1,0:T(8,128)(2,1)S(1)} %get-tuple-element.11, bf16[512,1024]{1,0:T(8,128)(2,1)S(1)} %get-tuple-element.12, bf16[512,1024]{1,0:T(8,128)(2,1)S(1)} %get-tuple-element.10, bf16[512,1024]{1,0:T(8,128)(2,1)S(1)} %get-tuple-element.9), kind=kLoop, calls=%fused_computation.14 | loop fusion | flops 34078720 | bytes 9437184 | tf_op jit(solution)/shard_map/concatenate | solution.py:53
  33.6 0.0 copy-done.4
  33.6 0.0 copy-start.1
  33.6 0.7 fusion.34
  34.3 0.0 copy-done.5
  34.3 0.0 copy-done.6
  34.3 1.3 %fusion.31 = s32[24]{0:T(128)S(1)} fusion(s32[1,24]{1,0:T(1,128)S(1)} %copy-done.5, s32[1,24]{1,0:T(1,128)S(1)} %copy-done.6, s32[]{:T(128)} %bitcast.23, s32[]{:T(128)} %bitcast.22), kind=kLoop, calls=%fused_computation.102 | loop fusion | flops 720 | bytes 296 | tf_op jit(solution)/shard_map/concatenate | solution.py:97
  35.6 0.0 collective-permute-done
  35.6 0.1 collective-permute-start.7
  35.7 0.0 collective-permute-done.1
  35.7 19.1 %collective-permute-done.2 = bf16[6,24,1024]{2,1,0:T(8,128)(2,1)} collective-permute-done((bf16[6,24,1024]{2,1,0:T(8,128)(2,1)}, bf16[6,24,1024]{2,1,0:T(8,128)(2,1)}, u32[]{:S(2)}, u32[]{:S(2)}) %collective-permute-start.2) | collective-permute-done | bytes 294944 | tf_op jit(solution)/shard_map/ppermute | solution.py:87
  54.8 0.0 copy-done.1
  54.8 0.0 copy-done.2
  54.8 2.9 %fusion.14 = f32[6,24,5,128]{3,1,2,0:T(8,128)S(1)} fusion(bf16[5,128,4096,1]{2,1,0,3:T(8,128)(2,1)S(1)} %bitcast.85, bf16[6,24,1024]{2,1,0:T(8,128)(2,1)} %collective-permute-done.2, bf16[6,24,1024]{2,1,0:T(8,128)(2,1)} %collective-permute-done.1, bf16[6,24,1024]{2,1,0:T(8,128)(2,1)} %collective-permute-done, bf16[6,24,1024]{2,1,0:T(8,128)(2,1)S(1)} %copy-done.2), kind=kOutput, calls=%fused_computation.26 | convolution fusion | flops 759693312 | bytes 6791168 | tf_op jit(solution)/shard_map/dot_general | solution.py:91
  57.8 0.7 gather_fusion.2
  58.5 1.3 %collective-permute-start.3 = (f32[2,6,24,128]{3,2,1,0:T(8,128)S(1)}, f32[2,6,24,128]{3,2,1,0:T(8,128)S(1)}, u32[]{:S(2)}, u32[]{:S(2)}) collective-permute-start(f32[2,6,24,128]{3,2,1,0:T(8,128)S(1)} %dynamic-slice_bitcast_fusion.5), channel_id=1, source_target_pairs={{0,2},{2,0},{1,3},{3,1},{4,6},{6,4},{5,7},{7,5},{8,10},{10,8},{9,1... | collective-permute-start | bytes 442376 | tf_op jit(solution)/shard_map/ppermute | solution.py:26
  59.8 3.6 %collective-permute-done.3 = f32[2,6,24,128]{3,2,1,0:T(8,128)S(1)} collective-permute-done((f32[2,6,24,128]{3,2,1,0:T(8,128)S(1)}, f32[2,6,24,128]{3,2,1,0:T(8,128)S(1)}, u32[]{:S(2)}, u32[]{:S(2)}) %collective-permute-start.3) | collective-permute-done | bytes 147488 | tf_op jit(solution)/shard_map/ppermute | solution.py:26
  63.4 0.0 collective-permute-done.5
  63.4 9.6 %collective-permute-done.6 = bf16[6,40,1024]{2,1,0:T(8,128)(2,1)} collective-permute-done((bf16[6,40,1024]{2,1,0:T(8,128)(2,1)S(1)}, bf16[6,40,1024]{2,1,0:T(8,128)(2,1)}, u32[]{:S(2)}, u32[]{:S(2)}) %collective-permute-start.6) | collective-permute-done | bytes 491552 | tf_op jit(solution)/shard_map/ppermute | solution.py:87
  73.0 2.9 %collective-permute-done.7 = bf16[6,40,1024]{2,1,0:T(8,128)(2,1)} collective-permute-done((bf16[6,40,1024]{2,1,0:T(8,128)(2,1)S(1)}, bf16[6,40,1024]{2,1,0:T(8,128)(2,1)}, u32[]{:S(2)}, u32[]{:S(2)}) %collective-permute-start.7) | collective-permute-done | bytes 491552 | tf_op jit(solution)/shard_map/ppermute | solution.py:87
  75.9 4.6 %fusion.7 = f32[6,40,5,128]{3,1,2,0:T(8,128)S(1)} fusion(bf16[5,128,4096,1]{2,1,0,3:T(8,128)(2,1)} %bitcast.86, bf16[6,40,1024]{2,1,0:T(8,128)(2,1)} %collective-permute-done.7, bf16[6,40,1024]{2,1,0:T(8,128)(2,1)} %collective-permute-done.6, bf16[6,40,1024]{2,1,0:T(8,128)(2,1)S(1)} %collective-permute-done.5, bf16[6,40,1024]{2,1,0:T(8,128)(2,1)S(1)} %get-tuple-element.13), kind=kOutput, calls=%fused_computation.18 | convolution fusion | flops 1266155520 | bytes 7823360 | tf_op jit(solution)/shard_map/dot_general | solution.py:91
  80.5 0.7 gather_fusion.5
  81.3 1.3 %collective-permute-start.8 = (f32[2,6,40,128]{3,2,1,0:T(8,128)S(1)}, f32[2,6,40,128]{3,2,1,0:T(8,128)S(1)}, u32[]{:S(2)}, u32[]{:S(2)}) collective-permute-start(f32[2,6,40,128]{3,2,1,0:T(8,128)S(1)} %dynamic-slice_bitcast_fusion.4), channel_id=1, source_target_pairs={{0,2},{2,0},{1,3},{3,1},{4,6},{6,4},{5,7},{7,5},{8,10},{10,8},{9,1... | collective-permute-start | bytes 737288 | tf_op jit(solution)/shard_map/ppermute | solution.py:26
  82.6 0.8 collective-permute-start.4
  83.4 0.9 collective-permute-done.4
  84.4 0.6 gather_fusion.3
  84.9 3.5 %collective-permute-done.8 = f32[2,6,40,128]{3,2,1,0:T(8,128)S(1)} collective-permute-done((f32[2,6,40,128]{3,2,1,0:T(8,128)S(1)}, f32[2,6,40,128]{3,2,1,0:T(8,128)S(1)}, u32[]{:S(2)}, u32[]{:S(2)}) %collective-permute-start.8) | collective-permute-done | bytes 245792 | tf_op jit(solution)/shard_map/ppermute | solution.py:26
  88.5 1.4 %collective-permute-start.9 = (f32[6,40,128]{2,1,0:T(8,128)S(1)}, f32[6,40,128]{2,1,0:T(8,128)S(1)}, u32[]{:S(2)}, u32[]{:S(2)}) collective-permute-start(f32[6,40,128]{2,1,0:T(8,128)S(1)} %get-tuple-element.22), channel_id=1, source_target_pairs={{0,1},{1,0},{2,3},{3,2},{4,5},{5,4},{6,7},{7,6},{8,9},{9,8},{10,11... | collective-permute-start | bytes 368648 | tf_op jit(solution)/shard_map/ppermute | solution.py:104
  89.9 0.1 broadcast_select_fusion.1
  90.0 0.9 collective-permute-done.9
  90.9 0.6 gather_fusion.6
  91.4 0.1 broadcast_select_fusion
  91.6 0.8 copy.8
  (25 shorter events, 0.4 us)
Async XLA Ops:
  0.0 0.7 copy-start
  0.0 3.2 %copy-start.3 = (f32[1,1024]{1,0:T(1,128)S(1)}, f32[1,1024]{1,0:T(1,128)}, u32[]{:S(2)}) copy-start(f32[1,1024]{1,0:T(1,128)} %param.9) | copy-start | bytes 12292
  4.7 31.0 %collective-permute-start = (bf16[6,24,1024]{2,1,0:T(8,128)(2,1)}, bf16[6,24,1024]{2,1,0:T(8,128)(2,1)}, u32[]{:S(2)}, u32[]{:S(2)}) collective-permute-start(bf16[6,24,1024]{2,1,0:T(8,128)(2,1)} %get-tuple-element.20), channel_id=1, source_target_pairs={{0,4},{4,8},{8,12},{12,0},{1,5},{5,9},{9,13},{13,1},{2,6},{6,10},{... | collective-permute-start | bytes 884744 | tf_op jit(solution)/shard_map/ppermute | solution.py:87
  6.0 29.7 %collective-permute-start.1 = (bf16[6,24,1024]{2,1,0:T(8,128)(2,1)}, bf16[6,24,1024]{2,1,0:T(8,128)(2,1)}, u32[]{:S(2)}, u32[]{:S(2)}) collective-permute-start(bf16[6,24,1024]{2,1,0:T(8,128)(2,1)} %get-tuple-element.19), channel_id=1, source_target_pairs={{0,8},{4,12},{8,0},{12,4},{1,9},{5,13},{9,1},{13,5},{2,10},{6,14},... | collective-permute-start | bytes 884744 | tf_op jit(solution)/shard_map/ppermute | solution.py:87
  7.0 47.8 %collective-permute-start.2 = (bf16[6,24,1024]{2,1,0:T(8,128)(2,1)}, bf16[6,24,1024]{2,1,0:T(8,128)(2,1)}, u32[]{:S(2)}, u32[]{:S(2)}) collective-permute-start(bf16[6,24,1024]{2,1,0:T(8,128)(2,1)} %get-tuple-element.18), channel_id=1, source_target_pairs={{0,12},{4,0},{8,4},{12,8},{1,13},{5,1},{9,5},{13,9},{2,14},{6,2},{... | collective-permute-start | bytes 884744 | tf_op jit(solution)/shard_map/ppermute | solution.py:87
  11.6 51.8 %collective-permute-start.5 = (bf16[6,40,1024]{2,1,0:T(8,128)(2,1)S(1)}, bf16[6,40,1024]{2,1,0:T(8,128)(2,1)S(1)}, u32[]{:S(2)}, u32[]{:S(2)}) collective-permute-start(bf16[6,40,1024]{2,1,0:T(8,128)(2,1)S(1)} %get-tuple-element.16), channel_id=1, source_target_pairs={{0,4},{4,8},{8,12},{12,0},{1,5},{5,9},{9,13},{13,1},{2,6},{6,10},{... | collective-permute-start | bytes 1474568 | tf_op jit(solution)/shard_map/ppermute | solution.py:87
  11.7 61.3 %collective-permute-start.6 = (bf16[6,40,1024]{2,1,0:T(8,128)(2,1)S(1)}, bf16[6,40,1024]{2,1,0:T(8,128)(2,1)}, u32[]{:S(2)}, u32[]{:S(2)}) collective-permute-start(bf16[6,40,1024]{2,1,0:T(8,128)(2,1)S(1)} %get-tuple-element.15), channel_id=1, source_target_pairs={{0,8},{4,12},{8,0},{12,4},{1,9},{5,13},{9,1},{13,5},{2,10},{6,14},... | collective-permute-start | bytes 1474568 | tf_op jit(solution)/shard_map/ppermute | solution.py:87
  21.4 12.2 %copy-start.4 = (s32[1,2]{1,0:T(1,128)S(1)}, s32[1,2]{1,0:T(1,128)}, u32[]{:S(2)}) copy-start(s32[1,2]{1,0:T(1,128)} %param.13) | copy-start | bytes 28
  21.4 12.9 %copy-start.5 = (s32[1,24]{1,0:T(1,128)S(1)}, s32[1,24]{1,0:T(1,128)}, u32[]{:S(2)}) copy-start(s32[1,24]{1,0:T(1,128)} %param.12) | copy-start | bytes 292
  21.4 12.9 %copy-start.6 = (s32[1,24]{1,0:T(1,128)S(1)}, s32[1,24]{1,0:T(1,128)}, u32[]{:S(2)}) copy-start(s32[1,24]{1,0:T(1,128)} %param.11) | copy-start | bytes 292
  21.4 33.4 %copy-start.2 = (bf16[6,24,1024]{2,1,0:T(8,128)(2,1)S(1)}, bf16[6,24,1024]{2,1,0:T(8,128)(2,1)}, u32[]{:S(2)}) copy-start(bf16[6,24,1024]{2,1,0:T(8,128)(2,1)} %get-tuple-element.17) | copy-start | bytes 884740
  33.6 21.2 %copy-start.1 = (bf16[640,4096]{1,0:T(8,128)(2,1)}, bf16[640,4096]{1,0:T(8,128)(2,1)S(1)}, u32[]{:S(2)}) copy-start(bf16[640,4096]{1,0:T(8,128)(2,1)S(1)} %fusion.6) | copy-start | bytes 15728644
  35.6 40.3 %collective-permute-start.7 = (bf16[6,40,1024]{2,1,0:T(8,128)(2,1)S(1)}, bf16[6,40,1024]{2,1,0:T(8,128)(2,1)}, u32[]{:S(2)}, u32[]{:S(2)}) collective-permute-start(bf16[6,40,1024]{2,1,0:T(8,128)(2,1)S(1)} %get-tuple-element.14), channel_id=1, source_target_pairs={{0,12},{4,0},{8,4},{12,8},{1,13},{5,1},{9,5},{13,9},{2,14},{6,2},{... | collective-permute-start | bytes 1474568 | tf_op jit(solution)/shard_map/ppermute | solution.py:87
  58.5 4.9 %collective-permute-start.3 = (f32[2,6,24,128]{3,2,1,0:T(8,128)S(1)}, f32[2,6,24,128]{3,2,1,0:T(8,128)S(1)}, u32[]{:S(2)}, u32[]{:S(2)}) collective-permute-start(f32[2,6,24,128]{3,2,1,0:T(8,128)S(1)} %dynamic-slice_bitcast_fusion.5), channel_id=1, source_target_pairs={{0,2},{2,0},{1,3},{3,1},{4,6},{6,4},{5,7},{7,5},{8,10},{10,8},{9,1... | collective-permute-start | bytes 442376 | tf_op jit(solution)/shard_map/ppermute | solution.py:26
  81.3 7.1 %collective-permute-start.8 = (f32[2,6,40,128]{3,2,1,0:T(8,128)S(1)}, f32[2,6,40,128]{3,2,1,0:T(8,128)S(1)}, u32[]{:S(2)}, u32[]{:S(2)}) collective-permute-start(f32[2,6,40,128]{3,2,1,0:T(8,128)S(1)} %dynamic-slice_bitcast_fusion.4), channel_id=1, source_target_pairs={{0,2},{2,0},{1,3},{3,1},{4,6},{6,4},{5,7},{7,5},{8,10},{10,8},{9,1... | collective-permute-start | bytes 737288 | tf_op jit(solution)/shard_map/ppermute | solution.py:26
  82.6 1.8 %collective-permute-start.4 = (f32[6,24,128]{2,1,0:T(8,128)S(1)}, f32[6,24,128]{2,1,0:T(8,128)S(1)}, u32[]{:S(2)}, u32[]{:S(2)}) collective-permute-start(f32[6,24,128]{2,1,0:T(8,128)S(1)} %get-tuple-element.24), channel_id=1, source_target_pairs={{0,1},{1,0},{2,3},{3,2},{4,5},{5,4},{6,7},{7,6},{8,9},{9,8},{10,11... | collective-permute-start | bytes 221192 | tf_op jit(solution)/shard_map/ppermute | solution.py:104
  88.5 2.4 %collective-permute-start.9 = (f32[6,40,128]{2,1,0:T(8,128)S(1)}, f32[6,40,128]{2,1,0:T(8,128)S(1)}, u32[]{:S(2)}, u32[]{:S(2)}) collective-permute-start(f32[6,40,128]{2,1,0:T(8,128)S(1)} %get-tuple-element.22), channel_id=1, source_target_pairs={{0,1},{1,0},{2,3},{3,2},{4,5},{5,4},{6,7},{7,6},{8,9},{9,8},{10,11... | collective-permute-start | bytes 368648 | tf_op jit(solution)/shard_map/ppermute | solution.py:104

commit v5 on v4

--- a/solution.py
+++ b/solution.py
@@ -87,13 +87,21 @@
                     piece = lax.ppermute(piece, "span", perm)
                 pieces.append(piece)
         gate = pieces
-        arrived = jnp.concatenate(pieces, axis=-1).reshape(cap * rows, -1)
-        combos = lax.dot_general(
-            arrived,
-            train,
-            (((1,), (1,)), ((), ())),
-            preferred_element_type=jnp.float32,
-        ).reshape(cap, rows, tb_dev + 1, BLOCK)
+        dims = (((1,), (1,)), ((), ()))
+        local = jnp.concatenate([pieces[layer * n_span] for layer in range(l_dev)], axis=-1)
+        local_train = jnp.concatenate(
+            [train[:, layer * n_span * features:(layer * n_span + 1) * features] for layer in range(l_dev)],
+            axis=1,
+        )
+        combos = lax.dot_general(local.reshape(cap * rows, -1), local_train, dims, preferred_element_type=jnp.float32)
+        remote = [p for i, p in enumerate(pieces) if i % n_span]
+        remote_train = jnp.concatenate(
+            [train[:, (layer * n_span + 1) * features:(layer + 1) * n_span * features] for layer in range(l_dev)],
+            axis=1,
+        )
+        arrived = jnp.concatenate(remote, axis=-1).reshape(cap * rows, -1)
+        combos = combos + lax.dot_general(arrived, remote_train, dims, preferred_element_type=jnp.float32)
+        combos = combos.reshape(cap, rows, tb_dev + 1, BLOCK)
         partial = combos.at[slot_row, :, pick_train, :].get(mode="promise_in_bounds") * score_scale
         partial = partial.reshape(n_layer, n_rep, per_dev, rows, BLOCK)
         partial = ring_reduce_scatter(partial, "layer", 0)

time: 92.7 us -> 96.4 us (1.040)
  waiting for transfers between devices: 40.5 us -> 34.2 us
  local copies, waits for them, and re-layouts: 14 us -> 18 us
  other arithmetic: 15.6 us -> 18.6 us
  matrix products: 7.52 us -> 10.5 us
    ppermute x6, waiting for transfers between devices: 31.6 us -> 25.3 us  [shards(): piece = lax.ppermute(piece, 'span', perm)]
    dot_general x2 -> x4, matrix products: 7.52 us -> 10.5 us  [the longest x2 7.2 us: shards(): lax.dot_general(arrived, remote_train, dims, preferred_element_type=jnp.f...]
    unnamed x14 -> x10, local copies, waits for them, and re-layouts: 0.69 us -> 2.97 us
    squeeze x0 -> x2, local copies, waits for them, and re-layouts: none -> 2 us  [shards(): piece = sent[layer][k]]
    select_n x2, other arithmetic: 0.01 us -> 1.97 us  [shards(): got = jnp.take(q3, block_ids, axis=0).reshape(n_span, cap, rows, features)]
    concatenate x2 -> x0, local copies, waits for them, and re-layouts: 1.21 us -> none  [shards(): arrived = jnp.concatenate(pieces, axis=-1).reshape(cap * rows, -1)]
    concatenate x1 -> x2, other arithmetic: 1.31 us -> 2.32 us  [shards(): arrived = jnp.concatenate(remote, axis=-1).reshape(cap * rows, -1)]
  transfers between devices with their start and end apart: 10 -> 10, of which waited for: 7 -> 7; matrix products, arithmetic and copies ran while one was open for 28% -> 31% of each run, Pallas kernels for 0% -> 0%
where the time goes in v5:
time: 96.4 us; the launch traced here: 96 us
  waiting for transfers between devices  34.2 us (35%)
  other arithmetic  18.6 us (19%)
  local copies, waits for them, and re-layouts  18 us (19%)
  starting transfers between devices  11.7 us (12%)
  matrix products  10.5 us (11%)
  between operations  2.91 us (3%)
    ppermute x6, waiting for transfers between devices, shards(): piece = lax.ppermute(piece, 'span', perm)  25.3 us
    concatenate x1, other arithmetic, shards(): train = jnp.concatenate(t_parts, axis=1)  12.2 us
    dot_general x2, matrix products, shards(): lax.dot_general(arrived, remote_train, dims, preferred_element_type=jnp.f...  7.2 us
    ppermute x2, waiting for transfers between devices, ring_reduce_scatter(): recv = lax.ppermute(acc, axis_name, perm)  7.07 us
    ppermute x6, starting transfers between devices, shards(): piece = lax.ppermute(piece, 'span', perm)  6.93 us
    dot_general x2, matrix products, shards(): lax.dot_general(local.reshape(cap * rows, -1), local_train, dims, preferr...  3.34 us
    unnamed x10, local copies, waits for them, and re-layouts  2.97 us
    dynamic_slice x1, local copies, waits for them, and re-layouts, shards(): lax.dynamic_slice_in_dim(t_l, sources[k] * features, features, axis=1)  2.64 us
  transfers between devices with their start and end apart: 10, of which 7 were waited for; matrix products, arithmetic and copies ran while one was open for 31% of the time, Pallas kernels for 0%

profile of v5, /device:TPU:9, one launch (start us, length us, event | category | flops | bytes accessed | tf_op | source)
XLA Modules:
  0.0 96.0 jit_solution(13145713200015914042)
XLA Ops:
  0.0 0.0 copy-start
  0.0 0.7 copy-done
  0.7 0.6 gather_fusion
  1.2 0.1 reshape.249
  1.3 1.3 %fusion.32 = (s32[1,1]{1,0:T(1,128)}, s32[1,1]{1,0:T(1,128)}) fusion(s32[1,2]{1,0:T(1,128)} %param.13), kind=kLoop, calls=%fused_computation.97 | loop fusion | bytes 16 | tf_op jit(solution)/shard_map/gather | solution.py:61
  2.7 2.0 %fusion.25 = (s32[24]{0:T(128)S(1)}, s32[24]{0:T(128)S(1)}) fusion(s32[24,1]{0,1:T(1,128)S(1)} %reshape.249, s32[1,24]{1,0:T(1,128)} %param.12, s32[]{:T(128)} %bitcast.20, s32[]{:T(128)} %bitcast.19, s32[1,24]{1,0:T(1,128)} %param.11), kind=kLoop, calls=%fused_computation.90 | loop fusion | flops 792 | bytes 488 | tf_op jit(solution)/shard_map/jit(_take)/jit(_where)/select_n | solution.py:75
  4.6 1.2 %constant_dynamic-slice_fusion.3 = bf16[16,24,1024]{2,1,0:T(8,128)(2,1)S(1)} fusion(bf16[16,128,1024]{2,1,0:T(8,128)(2,1)} %bitcast.80, s32[]{:T(128)S(6)} %select_n.213), kind=kLoop, calls=%fused_computation.60 | loop fusion | bytes 1572868 | tf_op jit(solution)/shard_map/dynamic_slice | solution.py:74
  5.8 0.6 gather_fusion.1
  6.5 0.0 copy-done.3
  6.5 0.4 multiply_convert_fusion.1
  6.9 1.0 %slice_bitcast_fusion.5 = (bf16[6,24,1024]{2,1,0:T(8,128)(2,1)}, bf16[6,24,1024]{2,1,0:T(8,128)(2,1)}, bf16[6,24,1024]{2,1,0:T(8,128)(2,1)}, bf16[1,6,24,1024]{3,2,1,0:T(8,128)(2,1)}) fusion(bf16[4,6,24,1024]{3,2,1,0:T(8,128)(2,1)S(1)} %multiply_convert_fusion.1), kind=kLoop, calls=%fused_computation.39 | loop fusion | bytes 2359296 | tf_op jit(solution)/shard_map/squeeze | solution.py:84
  7.9 1.3 %collective-permute-start = (bf16[6,24,1024]{2,1,0:T(8,128)(2,1)}, bf16[6,24,1024]{2,1,0:T(8,128)(2,1)}, u32[]{:S(2)}, u32[]{:S(2)}) collective-permute-start(bf16[6,24,1024]{2,1,0:T(8,128)(2,1)} %get-tuple-element.17), channel_id=1, source_target_pairs={{0,4},{4,8},{8,12},{12,0},{1,5},{5,9},{9,13},{13,1},{2,6},{6,10},{... | collective-permute-start | bytes 884744 | tf_op jit(solution)/shard_map/ppermute | solution.py:87
  9.2 1.0 %collective-permute-start.1 = (bf16[6,24,1024]{2,1,0:T(8,128)(2,1)}, bf16[6,24,1024]{2,1,0:T(8,128)(2,1)}, u32[]{:S(2)}, u32[]{:S(2)}) collective-permute-start(bf16[6,24,1024]{2,1,0:T(8,128)(2,1)} %get-tuple-element.19), channel_id=1, source_target_pairs={{0,8},{4,12},{8,0},{12,4},{1,9},{5,13},{9,1},{13,5},{2,10},{6,14},... | collective-permute-start | bytes 884744 | tf_op jit(solution)/shard_map/ppermute | solution.py:87
  10.3 1.5 %collective-permute-start.2 = (bf16[6,24,1024]{2,1,0:T(8,128)(2,1)}, bf16[6,24,1024]{2,1,0:T(8,128)(2,1)}, u32[]{:S(2)}, u32[]{:S(2)}) collective-permute-start(bf16[6,24,1024]{2,1,0:T(8,128)(2,1)} %get-tuple-element.18), channel_id=1, source_target_pairs={{0,12},{4,0},{8,4},{12,8},{1,13},{5,1},{9,5},{13,9},{2,14},{6,2},{... | collective-permute-start | bytes 884744 | tf_op jit(solution)/shard_map/ppermute | solution.py:87
  11.7 0.1 reshape.252
  11.8 1.4 %constant_dynamic-slice_fusion.1 = bf16[16,40,1024]{2,1,0:T(8,128)(2,1)S(1)} fusion(bf16[16,128,1024]{2,1,0:T(8,128)(2,1)} %bitcast.81, s32[]{:T(128)S(6)} %select_n.236), kind=kLoop, calls=%fused_computation.58 | loop fusion | bytes 2621444 | tf_op jit(solution)/shard_map/dynamic_slice | solution.py:74
  13.3 0.1 broadcast_in_dim.65
  13.3 0.7 gather_fusion.4
  14.0 0.7 multiply_convert_fusion
  14.7 1.0 %slice_bitcast_fusion.2 = (bf16[6,40,1024]{2,1,0:T(8,128)(2,1)}, bf16[6,40,1024]{2,1,0:T(8,128)(2,1)S(1)}, bf16[6,40,1024]{2,1,0:T(8,128)(2,1)S(1)}, bf16[1,6,40,1024]{3,2,1,0:T(8,128)(2,1)S(1)}) fusion(bf16[4,6,40,1024]{3,2,1,0:T(8,128)(2,1)S(1)} %multiply_convert_fusion), kind=kLoop, calls=%fused_computation.35 | loop fusion | bytes 3932160 | tf_op jit(solution)/shard_map/squeeze | solution.py:84
  15.7 0.0 collective-permute-start.5
  15.7 3.1 %collective-permute-start.6 = (bf16[6,40,1024]{2,1,0:T(8,128)(2,1)S(1)}, bf16[6,40,1024]{2,1,0:T(8,128)(2,1)S(1)}, u32[]{:S(2)}, u32[]{:S(2)}) collective-permute-start(bf16[6,40,1024]{2,1,0:T(8,128)(2,1)S(1)} %get-tuple-element.15), channel_id=1, source_target_pairs={{0,8},{4,12},{8,0},{12,4},{1,9},{5,13},{9,1},{13,5},{2,10},{6,14},... | collective-permute-start | bytes 1474568 | tf_op jit(solution)/shard_map/ppermute | solution.py:87
  18.9 0.6 fusion.33
  22.1 2.6 %dynamic-slice_bitcast_fusion.3 = (bf16[512,1024]{1,0:T(8,128)(2,1)S(1)}, bf16[512,1024]{1,0:T(8,128)(2,1)S(1)}, bf16[512,1024]{1,0:T(8,128)(2,1)S(1)}, bf16[512,1024]{1,0:T(8,128)(2,1)S(1)}) fusion(bf16[512,1,4096]{2,0,1:T(8,128)(2,1)} %param.8, s32[]{:T(128)S(6)} %select_n.217, s32[]{:T(128)S(6)} %select_n.218, s32[]{:T(128)S(6)} %select_n.220, ...), kind=kLoop, calls=%fused_computation.31 | loop fusion | bytes 8388624 | tf_op jit(solution)/shard_map/dynamic_slice | solution.py:52
  24.8 0.0 copy-start.2
  24.8 12.2 %fusion.6 = bf16[640,4096]{1,0:T(8,128)(2,1)S(1)} fusion(bf16[512,1024]{1,0:T(8,128)(2,1)S(1)} %get-tuple-element.11, bf16[512,1024]{1,0:T(8,128)(2,1)S(1)} %get-tuple-element.12, bf16[512,1024]{1,0:T(8,128)(2,1)S(1)} %get-tuple-element.10, bf16[512,1024]{1,0:T(8,128)(2,1)S(1)} %get-tuple-element.9), kind=kLoop, calls=%fused_computation.14 | loop fusion | flops 34078720 | bytes 9437184 | tf_op jit(solution)/shard_map/concatenate | solution.py:53
  36.9 0.0 copy-start.1
  37.0 2.3 %copy-done.1 = bf16[640,4096]{1,0:T(8,128)(2,1)} copy-done((bf16[640,4096]{1,0:T(8,128)(2,1)}, bf16[640,4096]{1,0:T(8,128)(2,1)S(1)}, u32[]{:S(2)}) %copy-start.1) | copy-done | bytes 5242904
  39.3 0.0 copy-done.2
  39.3 0.6 fusion.19
  39.8 0.6 sort.19
  40.4 2.8 %fusion.17 = f32[240,640]{1,0:T(8,128)} fusion(bf16[240,1024]{1,0:T(8,128)(2,1)S(1)} %bitcast.83, bf16[640,4096]{1,0:T(8,128)(2,1)} %copy-done.1), kind=kOutput, calls=%fused_computation.24 | convolution fusion | flops 314572800 | bytes 2416640 | tf_op jit(solution)/shard_map/dot_general | solution.py:96
  43.2 0.0 collective-permute-done
  43.2 0.0 collective-permute-start.7
  43.2 0.0 collective-permute-done.1
  43.2 14.9 %collective-permute-done.2 = bf16[6,24,1024]{2,1,0:T(8,128)(2,1)} collective-permute-done((bf16[6,24,1024]{2,1,0:T(8,128)(2,1)}, bf16[6,24,1024]{2,1,0:T(8,128)(2,1)}, u32[]{:S(2)}, u32[]{:S(2)}) %collective-permute-start.2) | collective-permute-done | bytes 294944 | tf_op jit(solution)/shard_map/ppermute | solution.py:87
  58.1 1.2 %pad_maximum_fusion.1 = bf16[6,24,3072]{2,1,0:T(8,128)(2,1)S(1)} fusion(bf16[6,24,1024]{2,1,0:T(8,128)(2,1)} %collective-permute-done.2, bf16[6,24,1024]{2,1,0:T(8,128)(2,1)} %collective-permute-done.1, bf16[6,24,1024]{2,1,0:T(8,128)(2,1)} %collective-permute-done), kind=kLoop, calls=%fused_computation.32 | loop fusion | flops 2654208 | bytes 1769472 | tf_op jit(solution)/shard_map/concatenate | solution.py:102
  59.3 3.6 %fusion.14 = f32[144,640]{1,0:T(8,128)S(1)} fusion(f32[144,640]{1,0:T(8,128)S(1)} %fusion.19, bf16[144,3072]{1,0:T(8,128)(2,1)S(1)} %bitcast.82, bf16[640,4096]{1,0:T(8,128)(2,1)} %copy-done.1), kind=kOutput, calls=%fused_computation.23 | convolution fusion | flops 566323200 | bytes 5554176 | tf_op jit(solution)/shard_map/dot_general | solution.py:103
  62.9 0.1 reshape.251
  63.0 0.1 copy.12
  63.0 0.0 copy-start.4
  63.0 0.7 gather_fusion.2
  63.8 1.3 %collective-permute-start.3 = (f32[2,6,24,128]{3,2,1,0:T(8,128)S(1)}, f32[2,6,24,128]{3,2,1,0:T(8,128)S(1)}, u32[]{:S(2)}, u32[]{:S(2)}) collective-permute-start(f32[2,6,24,128]{3,2,1,0:T(8,128)S(1)} %dynamic-slice_bitcast_fusion.5), channel_id=1, source_target_pairs={{0,2},{2,0},{1,3},{3,1},{4,6},{6,4},{5,7},{7,5},{8,10},{10,8},{9,1... | collective-permute-start | bytes 442376 | tf_op jit(solution)/shard_map/ppermute | solution.py:26
  65.1 3.6 %collective-permute-done.3 = f32[2,6,24,128]{3,2,1,0:T(8,128)S(1)} collective-permute-done((f32[2,6,24,128]{3,2,1,0:T(8,128)S(1)}, f32[2,6,24,128]{3,2,1,0:T(8,128)S(1)}, u32[]{:S(2)}, u32[]{:S(2)}) %collective-permute-start.3) | collective-permute-done | bytes 147488 | tf_op jit(solution)/shard_map/ppermute | solution.py:26
  68.7 0.0 collective-permute-done.5
  68.7 7.6 %collective-permute-done.6 = bf16[6,40,1024]{2,1,0:T(8,128)(2,1)S(1)} collective-permute-done((bf16[6,40,1024]{2,1,0:T(8,128)(2,1)S(1)}, bf16[6,40,1024]{2,1,0:T(8,128)(2,1)S(1)}, u32[]{:S(2)}, u32[]{:S(2)}) %collective-permute-start.6) | collective-permute-done | bytes 491552 | tf_op jit(solution)/shard_map/ppermute | solution.py:87
  76.3 2.9 %collective-permute-done.7 = bf16[6,40,1024]{2,1,0:T(8,128)(2,1)} collective-permute-done((bf16[6,40,1024]{2,1,0:T(8,128)(2,1)S(1)}, bf16[6,40,1024]{2,1,0:T(8,128)(2,1)}, u32[]{:S(2)}, u32[]{:S(2)}) %collective-permute-start.7) | collective-permute-done | bytes 491552 | tf_op jit(solution)/shard_map/ppermute | solution.py:87
  79.2 1.1 %pad_maximum_fusion = bf16[6,40,3072]{2,1,0:T(8,128)(2,1)S(1)} fusion(bf16[6,40,1024]{2,1,0:T(8,128)(2,1)} %collective-permute-done.7, bf16[6,40,1024]{2,1,0:T(8,128)(2,1)S(1)} %collective-permute-done.6, bf16[6,40,1024]{2,1,0:T(8,128)(2,1)S(1)} %collective-permute-done.5), kind=kLoop, calls=%fused_computation.21 | loop fusion | flops 4423680 | bytes 2949120 | tf_op jit(solution)/shard_map/concatenate | solution.py:102
  80.3 0.0 copy-done.4
  80.3 3.6 %fusion.11 = f32[240,640]{1,0:T(8,128)S(1)} fusion(f32[240,640]{1,0:T(8,128)S(1)} %copy-done.4, bf16[240,3072]{1,0:T(8,128)(2,1)S(1)} %bitcast.77, bf16[640,4096]{1,0:T(8,128)(2,1)} %copy-done.1), kind=kOutput, calls=%fused_computation.22 | convolution fusion | flops 943872000 | bytes 6635520 | tf_op jit(solution)/shard_map/dot_general | solution.py:103
  83.9 0.1 reshape.254
  84.0 0.1 copy.13
  84.2 0.7 gather_fusion.5
  84.9 1.3 %collective-permute-start.8 = (f32[2,6,40,128]{3,2,1,0:T(8,128)S(1)}, f32[2,6,40,128]{3,2,1,0:T(8,128)S(1)}, u32[]{:S(2)}, u32[]{:S(2)}) collective-permute-start(f32[2,6,40,128]{3,2,1,0:T(8,128)S(1)} %dynamic-slice_bitcast_fusion.4), channel_id=1, source_target_pairs={{0,2},{2,0},{1,3},{3,1},{4,6},{6,4},{5,7},{7,5},{8,10},{10,8},{9,1... | collective-permute-start | bytes 737288 | tf_op jit(solution)/shard_map/ppermute | solution.py:26
  86.2 0.8 collective-permute-start.4
  87.1 0.9 collective-permute-done.4
  88.0 0.6 gather_fusion.3
  88.6 3.5 %collective-permute-done.8 = f32[2,6,40,128]{3,2,1,0:T(8,128)S(1)} collective-permute-done((f32[2,6,40,128]{3,2,1,0:T(8,128)S(1)}, f32[2,6,40,128]{3,2,1,0:T(8,128)S(1)}, u32[]{:S(2)}, u32[]{:S(2)}) %collective-permute-start.8) | collective-permute-done | bytes 245792 | tf_op jit(solution)/shard_map/ppermute | solution.py:26
  92.1 1.4 %collective-permute-start.9 = (f32[6,40,128]{2,1,0:T(8,128)S(1)}, f32[6,40,128]{2,1,0:T(8,128)S(1)}, u32[]{:S(2)}, u32[]{:S(2)}) collective-permute-start(f32[6,40,128]{2,1,0:T(8,128)S(1)} %get-tuple-element.22), channel_id=1, source_target_pairs={{0,1},{1,0},{2,3},{3,2},{4,5},{5,4},{6,7},{7,6},{8,9},{9,8},{10,11... | collective-permute-start | bytes 368648 | tf_op jit(solution)/shard_map/ppermute | solution.py:112
  93.5 0.1 broadcast_select_fusion.1
  93.6 0.9 collective-permute-done.9
  94.5 0.6 gather_fusion.6
  95.1 0.1 broadcast_select_fusion
  95.2 0.8 copy.14
  (25 shorter events, 0.4 us)
Async XLA Ops:
  0.0 0.7 copy-start
  0.0 6.5 %copy-start.3 = (f32[1,1024]{1,0:T(1,128)S(1)}, f32[1,1024]{1,0:T(1,128)}, u32[]{:S(2)}) copy-start(f32[1,1024]{1,0:T(1,128)} %param.9) | copy-start | bytes 12292
  7.9 35.3 %collective-permute-start = (bf16[6,24,1024]{2,1,0:T(8,128)(2,1)}, bf16[6,24,1024]{2,1,0:T(8,128)(2,1)}, u32[]{:S(2)}, u32[]{:S(2)}) collective-permute-start(bf16[6,24,1024]{2,1,0:T(8,128)(2,1)} %get-tuple-element.17), channel_id=1, source_target_pairs={{0,4},{4,8},{8,12},{12,0},{1,5},{5,9},{9,13},{13,1},{2,6},{6,10},{... | collective-permute-start | bytes 884744 | tf_op jit(solution)/shard_map/ppermute | solution.py:87
  9.2 34.0 %collective-permute-start.1 = (bf16[6,24,1024]{2,1,0:T(8,128)(2,1)}, bf16[6,24,1024]{2,1,0:T(8,128)(2,1)}, u32[]{:S(2)}, u32[]{:S(2)}) collective-permute-start(bf16[6,24,1024]{2,1,0:T(8,128)(2,1)} %get-tuple-element.19), channel_id=1, source_target_pairs={{0,8},{4,12},{8,0},{12,4},{1,9},{5,13},{9,1},{13,5},{2,10},{6,14},... | collective-permute-start | bytes 884744 | tf_op jit(solution)/shard_map/ppermute | solution.py:87
  10.3 47.8 %collective-permute-start.2 = (bf16[6,24,1024]{2,1,0:T(8,128)(2,1)}, bf16[6,24,1024]{2,1,0:T(8,128)(2,1)}, u32[]{:S(2)}, u32[]{:S(2)}) collective-permute-start(bf16[6,24,1024]{2,1,0:T(8,128)(2,1)} %get-tuple-element.18), channel_id=1, source_target_pairs={{0,12},{4,0},{8,4},{12,8},{1,13},{5,1},{9,5},{13,9},{2,14},{6,2},{... | collective-permute-start | bytes 884744 | tf_op jit(solution)/shard_map/ppermute | solution.py:87
  15.7 53.0 %collective-permute-start.5 = (bf16[6,40,1024]{2,1,0:T(8,128)(2,1)}, bf16[6,40,1024]{2,1,0:T(8,128)(2,1)S(1)}, u32[]{:S(2)}, u32[]{:S(2)}) collective-permute-start(bf16[6,40,1024]{2,1,0:T(8,128)(2,1)} %get-tuple-element.13), channel_id=1, source_target_pairs={{0,4},{4,8},{8,12},{12,0},{1,5},{5,9},{9,13},{13,1},{2,6},{6,10},{... | collective-permute-start | bytes 1474568 | tf_op jit(solution)/shard_map/ppermute | solution.py:87
  15.7 60.6 %collective-permute-start.6 = (bf16[6,40,1024]{2,1,0:T(8,128)(2,1)S(1)}, bf16[6,40,1024]{2,1,0:T(8,128)(2,1)S(1)}, u32[]{:S(2)}, u32[]{:S(2)}) collective-permute-start(bf16[6,40,1024]{2,1,0:T(8,128)(2,1)S(1)} %get-tuple-element.15), channel_id=1, source_target_pairs={{0,8},{4,12},{8,0},{12,4},{1,9},{5,13},{9,1},{13,5},{2,10},{6,14},... | collective-permute-start | bytes 1474568 | tf_op jit(solution)/shard_map/ppermute | solution.py:87
  24.8 14.5 %copy-start.2 = (bf16[1,6,24,1024]{3,2,1,0:T(8,128)(2,1)S(1)}, bf16[1,6,24,1024]{3,2,1,0:T(8,128)(2,1)}, u32[]{:S(2)}) copy-start(bf16[1,6,24,1024]{3,2,1,0:T(8,128)(2,1)} %get-tuple-element.20) | copy-start | bytes 884740
  36.9 2.3 %copy-start.1 = (bf16[640,4096]{1,0:T(8,128)(2,1)}, bf16[640,4096]{1,0:T(8,128)(2,1)S(1)}, u32[]{:S(2)}) copy-start(bf16[640,4096]{1,0:T(8,128)(2,1)S(1)} %fusion.6) | copy-start | bytes 15728644
  43.2 35.9 %collective-permute-start.7 = (bf16[6,40,1024]{2,1,0:T(8,128)(2,1)S(1)}, bf16[6,40,1024]{2,1,0:T(8,128)(2,1)}, u32[]{:S(2)}, u32[]{:S(2)}) collective-permute-start(bf16[6,40,1024]{2,1,0:T(8,128)(2,1)S(1)} %get-tuple-element.14), channel_id=1, source_target_pairs={{0,12},{4,0},{8,4},{12,8},{1,13},{5,1},{9,5},{13,9},{2,14},{6,2},{... | collective-permute-start | bytes 1474568 | tf_op jit(solution)/shard_map/ppermute | solution.py:87
  63.0 17.3 %copy-start.4 = (f32[240,640]{1,0:T(8,128)S(1)}, f32[240,640]{1,0:T(8,128)}, u32[]{:S(2)}) copy-start(f32[240,640]{1,0:T(8,128)} %fusion.17) | copy-start | bytes 1843204
  63.8 4.9 %collective-permute-start.3 = (f32[2,6,24,128]{3,2,1,0:T(8,128)S(1)}, f32[2,6,24,128]{3,2,1,0:T(8,128)S(1)}, u32[]{:S(2)}, u32[]{:S(2)}) collective-permute-start(f32[2,6,24,128]{3,2,1,0:T(8,128)S(1)} %dynamic-slice_bitcast_fusion.5), channel_id=1, source_target_pairs={{0,2},{2,0},{1,3},{3,1},{4,6},{6,4},{5,7},{7,5},{8,10},{10,8},{9,1... | collective-permute-start | bytes 442376 | tf_op jit(solution)/shard_map/ppermute | solution.py:26
  84.9 7.1 %collective-permute-start.8 = (f32[2,6,40,128]{3,2,1,0:T(8,128)S(1)}, f32[2,6,40,128]{3,2,1,0:T(8,128)S(1)}, u32[]{:S(2)}, u32[]{:S(2)}) collective-permute-start(f32[2,6,40,128]{3,2,1,0:T(8,128)S(1)} %dynamic-slice_bitcast_fusion.4), channel_id=1, source_target_pairs={{0,2},{2,0},{1,3},{3,1},{4,6},{6,4},{5,7},{7,5},{8,10},{10,8},{9,1... | collective-permute-start | bytes 737288 | tf_op jit(solution)/shard_map/ppermute | solution.py:26
  86.2 1.8 %collective-permute-start.4 = (f32[6,24,128]{2,1,0:T(8,128)S(1)}, f32[6,24,128]{2,1,0:T(8,128)S(1)}, u32[]{:S(2)}, u32[]{:S(2)}) collective-permute-start(f32[6,24,128]{2,1,0:T(8,128)S(1)} %get-tuple-element.24), channel_id=1, source_target_pairs={{0,1},{1,0},{2,3},{3,2},{4,5},{5,4},{6,7},{7,6},{8,9},{9,8},{10,11... | collective-permute-start | bytes 221192 | tf_op jit(solution)/shard_map/ppermute | solution.py:112
  92.1 2.4 %collective-permute-start.9 = (f32[6,40,128]{2,1,0:T(8,128)S(1)}, f32[6,40,128]{2,1,0:T(8,128)S(1)}, u32[]{:S(2)}, u32[]{:S(2)}) collective-permute-start(f32[6,40,128]{2,1,0:T(8,128)S(1)} %get-tuple-element.22), channel_id=1, source_target_pairs={{0,1},{1,0},{2,3},{3,2},{4,5},{5,4},{6,7},{7,6},{8,9},{9,8},{10,11... | collective-permute-start | bytes 368648 | tf_op jit(solution)/shard_map/ppermute | solution.py:112

commit v6 on v4

--- a/solution.py
+++ b/solution.py
@@ -7,8 +7,8 @@
 
 
 BLOCK = 128
-ROW_SPLIT = (24, 40)
-GATE = False
+ROW_SPLIT = (24, 32, 8)
+GATE_FROM = {2: 0}
 
 
 def ring_reduce_scatter(x, axis_name, dim):
@@ -63,8 +63,9 @@
 
     outs = []
     gate = None
+    arrivals = []
     row_start = 0
-    for rows in ROW_SPLIT:
+    for chunk, rows in enumerate(ROW_SPLIT):
         block_ids = requests[dests].reshape(-1)
         if gate is not None:
             block_ids, _ = lax.optimization_barrier((block_ids, prev_sent))
@@ -76,8 +77,8 @@
             sent.append((got.astype(jnp.float32) * precond[layer]).astype(jnp.bfloat16))
         row_start += rows
         prev_sent = sent
-        if GATE and gate is not None:
-            sent, _ = lax.optimization_barrier((sent, gate))
+        if chunk in GATE_FROM:
+            sent, _ = lax.optimization_barrier((sent, arrivals[GATE_FROM[chunk]]))
         pieces = []
         for layer in range(l_dev):
             for k in range(n_span):
@@ -87,6 +88,7 @@
                     piece = lax.ppermute(piece, "span", perm)
                 pieces.append(piece)
         gate = pieces
+        arrivals.append(pieces)
         arrived = jnp.concatenate(pieces, axis=-1).reshape(cap * rows, -1)
         combos = lax.dot_general(
             arrived,

time: 92.7 us -> 100 us (1.079)
  the two profiles are of different devices: /device:TPU:9 before, /device:TPU:0 now
where the time goes in v6:
time: 100 us; the launch traced here: 99.7 us
  starting transfers between devices  44.1 us (44%)
  other arithmetic  17 us (17%)
  local copies, waits for them, and re-layouts  16.4 us (16%)
  matrix products  13.5 us (14%)
  waiting for transfers between devices  5.5 us (6%)
  between operations  3.09 us (3%)
    ppermute x9, starting transfers between devices, shards(): piece = lax.ppermute(piece, 'span', perm)  39.8 us
    dot_general x3, matrix products, shards(): lax.dot_general(arrived, train, (((1,), (1,)), ((), ())), preferred_eleme...  13.5 us
    concatenate x1, other arithmetic, shards(): train = jnp.concatenate(t_parts, axis=1)  13.3 us
    ppermute x3, starting transfers between devices, ring_reduce_scatter(): recv = lax.ppermute(acc, axis_name, perm)  3.64 us
    dynamic_slice x3, local copies, waits for them, and re-layouts, shards(): lax.dynamic_slice_in_dim(q3, rep_index * own_rows + row_start, rows, axis=1)  3.49 us
    dynamic_slice x1, local copies, waits for them, and re-layouts, shards(): lax.dynamic_slice_in_dim(t_l, sources[k] * features, features, axis=1)  2.63 us
    ppermute x3, waiting for transfers between devices, ring_reduce_scatter(): recv = lax.ppermute(acc, axis_name, perm)  2.26 us
    gather x3, local copies, waits for them, and re-layouts, shards(): combos.at[slot_row, :, pick_train, :].get(mode='promise_in_bounds')  2.04 us
  transfers between devices with their start and end apart: 15, of which 4 were waited for; matrix products, arithmetic and copies ran while one was open for 41% of the time, Pallas kernels for 0%

profile of v6, /device:TPU:0, one launch (start us, length us, event | category | flops | bytes accessed | tf_op | source)
XLA Modules:
  0.0 99.7 jit_solution(4872972010685832617)
XLA Ops:
  0.0 0.7 copy-done
  0.7 0.6 gather_fusion
  1.2 0.1 reshape.302
  1.4 1.2 %constant_dynamic-slice_fusion.5 = bf16[16,24,1024]{2,1,0:T(8,128)(2,1)S(1)} fusion(bf16[16,128,1024]{2,1,0:T(8,128)(2,1)} %bitcast.117, s32[]{:T(128)S(6)} %select_n.248), kind=kLoop, calls=%fused_computation.86 | loop fusion | bytes 1572868 | tf_op jit(solution)/shard_map/dynamic_slice | solution.py:75
  2.6 0.6 gather_fusion.1
  3.2 0.4 multiply_convert_fusion.1
  3.6 0.8 slice_bitcast_fusion.7
  4.4 3.1 %collective-permute-start = (bf16[6,24,1024]{2,1,0:T(8,128)(2,1)}, bf16[6,24,1024]{2,1,0:T(8,128)(2,1)}, u32[]{:S(2)}, u32[]{:S(2)}) collective-permute-start(bf16[6,24,1024]{2,1,0:T(8,128)(2,1)} %get-tuple-element.24), channel_id=1, source_target_pairs={{0,4},{4,8},{8,12},{12,0},{1,5},{5,9},{9,13},{13,1},{2,6},{6,10},{... | collective-permute-start | bytes 884744 | tf_op jit(solution)/shard_map/ppermute | solution.py:88
  7.5 2.6 %collective-permute-start.1 = (bf16[6,24,1024]{2,1,0:T(8,128)(2,1)S(1)}, bf16[6,24,1024]{2,1,0:T(8,128)(2,1)}, u32[]{:S(2)}, u32[]{:S(2)}) collective-permute-start(bf16[6,24,1024]{2,1,0:T(8,128)(2,1)S(1)} %get-tuple-element.23), channel_id=1, source_target_pairs={{0,8},{4,12},{8,0},{12,4},{1,9},{5,13},{9,1},{13,5},{2,10},{6,14},... | collective-permute-start | bytes 884744 | tf_op jit(solution)/shard_map/ppermute | solution.py:88
  10.1 1.3 %collective-permute-start.2 = (bf16[6,24,1024]{2,1,0:T(8,128)(2,1)S(1)}, bf16[6,24,1024]{2,1,0:T(8,128)(2,1)}, u32[]{:S(2)}, u32[]{:S(2)}) collective-permute-start(bf16[6,24,1024]{2,1,0:T(8,128)(2,1)S(1)} %get-tuple-element.22), channel_id=1, source_target_pairs={{0,12},{4,0},{8,4},{12,8},{1,13},{5,1},{9,5},{13,9},{2,14},{6,2},{... | collective-permute-start | bytes 884744 | tf_op jit(solution)/shard_map/ppermute | solution.py:88
  11.4 0.1 reshape.303
  11.5 1.3 %constant_dynamic-slice_fusion.3 = bf16[16,32,1024]{2,1,0:T(8,128)(2,1)S(1)} fusion(bf16[16,128,1024]{2,1,0:T(8,128)(2,1)} %bitcast.118, s32[]{:T(128)S(6)} %select_n.271), kind=kLoop, calls=%fused_computation.84 | loop fusion | bytes 2097156 | tf_op jit(solution)/shard_map/dynamic_slice | solution.py:75
  12.9 0.1 broadcast_in_dim.92
  13.0 0.6 gather_fusion.4
  13.6 0.0 copy-start.2
  13.6 0.5 multiply_convert_fusion
  14.2 0.2 slice_bitcast_fusion.3
  14.3 0.5 collective-permute-start.7
  14.8 1.7 %collective-permute-start.6 = (bf16[6,32,1024]{2,1,0:T(8,128)(2,1)S(1)}, bf16[6,32,1024]{2,1,0:T(8,128)(2,1)}, u32[]{:S(2)}, u32[]{:S(2)}) collective-permute-start(bf16[6,32,1024]{2,1,0:T(8,128)(2,1)S(1)} %get-tuple-element.19), channel_id=1, source_target_pairs={{0,8},{4,12},{8,0},{12,4},{1,9},{5,13},{9,1},{13,5},{2,10},{6,14},... | collective-permute-start | bytes 1179656 | tf_op jit(solution)/shard_map/ppermute | solution.py:88
  16.5 0.7 fusion.43
  19.9 0.7 sort.21
  20.6 1.0 constant_dynamic-slice_fusion.1
  21.6 0.6 fusion.42
  22.2 2.6 %dynamic-slice_bitcast_fusion.3 = (bf16[512,1024]{1,0:T(8,128)(2,1)S(1)}, bf16[512,1024]{1,0:T(8,128)(2,1)S(1)}, bf16[512,1024]{1,0:T(8,128)(2,1)S(1)}, bf16[512,1024]{1,0:T(8,128)(2,1)S(1)}) fusion(bf16[512,1,4096]{2,0,1:T(8,128)(2,1)} %param.8, s32[]{:T(128)S(6)} %select_n.252, s32[]{:T(128)S(6)} %select_n.253, s32[]{:T(128)S(6)} %select_n.255, ...), kind=kLoop, calls=%fused_computation.39 | loop fusion | bytes 8388624 | tf_op jit(solution)/shard_map/dynamic_slice | solution.py:52
  24.8 0.0 copy-start.3
  24.8 0.0 copy-start.4
  24.9 13.3 %fusion.6 = bf16[640,4096]{1,0:T(8,128)(2,1)} fusion(bf16[512,1024]{1,0:T(8,128)(2,1)S(1)} %get-tuple-element.15, bf16[512,1024]{1,0:T(8,128)(2,1)S(1)} %get-tuple-element.16, bf16[512,1024]{1,0:T(8,128)(2,1)S(1)} %get-tuple-element.14, bf16[512,1024]{1,0:T(8,128)(2,1)S(1)} %get-tuple-element.13), kind=kLoop, calls=%fused_computation.17 | loop fusion | flops 34078720 | bytes 9437184 | tf_op jit(solution)/shard_map/concatenate | solution.py:53
  38.2 1.3 %fusion.38 = s32[24]{0:T(128)S(1)} fusion(s32[1,24]{1,0:T(1,128)S(1)} %copy-done.3, s32[1,24]{1,0:T(1,128)S(1)} %copy-done.4, s32[]{:T(128)} %bitcast.23, s32[]{:T(128)} %bitcast.22), kind=kLoop, calls=%fused_computation.129 | loop fusion | flops 720 | bytes 296 | tf_op jit(solution)/shard_map/concatenate | solution.py:99
  39.6 0.1 broadcast_in_dim.98
  39.7 0.6 gather_fusion.7
  40.3 0.2 multiply_convert_fusion.2
  40.4 0.0 collective-permute-done
  40.4 0.0 collective-permute-done.1
  40.4 0.0 collective-permute-done.2
  40.5 15.0 %collective-permute-start.12 = (bf16[6,8,1024]{2,1,0:T(8,128)(2,1)S(1)}, bf16[6,8,1024]{2,1,0:T(8,128)(2,1)S(1)}, u32[]{:S(2)}, u32[]{:S(2)}) collective-permute-start(bf16[6,8,1024]{2,1,0:T(8,128)(2,1)S(1)} %get-tuple-element.26), channel_id=1, source_target_pairs={{0,12},{4,0},{8,4},{12,8},{1,13},{5,1},{9,5},{13,9},{2,14},{6,2},{... | collective-permute-start | bytes 294920 | tf_op jit(solution)/shard_map/ppermute | solution.py:88
  55.5 0.0 collective-permute-start.11
  55.5 0.6 collective-permute-start.10
  56.1 4.6 %fusion.14 = f32[6,24,5,128]{3,1,2,0:T(8,128)S(1)} fusion(bf16[5,128,4096,1]{2,1,0,3:T(8,128)(2,1)} %bitcast.108, bf16[6,24,1024]{2,1,0:T(8,128)(2,1)} %collective-permute-done.2, bf16[6,24,1024]{2,1,0:T(8,128)(2,1)} %collective-permute-done.1, bf16[6,24,1024]{2,1,0:T(8,128)(2,1)} %collective-permute-done, bf16[6,24,1024]{2,1,0:T(8,128)(2,1)S(1)} %get-tuple-element.21), kind=kOutput, calls=%fused_computation.29 | convolution fusion | flops 759693312 | bytes 6791168 | tf_op jit(solution)/shard_map/dot_general | solution.py:93
  60.7 0.7 gather_fusion.2
  61.5 15.0 %collective-permute-start.5 = (bf16[6,32,1024]{2,1,0:T(8,128)(2,1)S(1)}, bf16[6,32,1024]{2,1,0:T(8,128)(2,1)}, u32[]{:S(2)}, u32[]{:S(2)}) collective-permute-start(bf16[6,32,1024]{2,1,0:T(8,128)(2,1)S(1)} %get-tuple-element.20), channel_id=1, source_target_pairs={{0,4},{4,8},{8,12},{12,0},{1,5},{5,9},{9,13},{13,1},{2,6},{6,10},{... | collective-permute-start | bytes 1179656 | tf_op jit(solution)/shard_map/ppermute | solution.py:88
  76.5 1.4 %collective-permute-done.11 = bf16[6,8,1024]{2,1,0:T(8,128)(2,1)S(1)} collective-permute-done((bf16[6,8,1024]{2,1,0:T(8,128)(2,1)S(1)}, bf16[6,8,1024]{2,1,0:T(8,128)(2,1)S(1)}, u32[]{:S(2)}, u32[]{:S(2)}) %collective-permute-start.11) | collective-permute-done | bytes 98336 | tf_op jit(solution)/shard_map/ppermute | solution.py:88
  77.9 1.5 %collective-permute-start.3 = (f32[2,6,24,128]{3,2,1,0:T(8,128)S(1)}, f32[2,6,24,128]{3,2,1,0:T(8,128)S(1)}, u32[]{:S(2)}, u32[]{:S(2)}) collective-permute-start(f32[2,6,24,128]{3,2,1,0:T(8,128)S(1)} %dynamic-slice_bitcast_fusion.5), channel_id=1, source_target_pairs={{0,2},{2,0},{1,3},{3,1},{4,6},{6,4},{5,7},{7,5},{8,10},{10,8},{9,1... | collective-permute-start | bytes 442376 | tf_op jit(solution)/shard_map/ppermute | solution.py:26
  79.4 0.0 collective-permute-done.10
  79.4 4.2 %fusion.21 = f32[6,8,5,128]{3,1,2,0:T(8,128)S(1)} fusion(bf16[5,128,4096,1]{2,1,0,3:T(8,128)(2,1)} %bitcast.109, bf16[6,8,1024]{2,1,0:T(8,128)(2,1)S(1)} %collective-permute-done.12, bf16[6,8,1024]{2,1,0:T(8,128)(2,1)S(1)} %collective-permute-done.11, bf16[6,8,1024]{2,1,0:T(8,128)(2,1)} %collective-permute-done.10, ...), kind=kOutput, calls=%fused_computation.46 | convolution fusion | flops 253231104 | bytes 5758976 | tf_op jit(solution)/shard_map/dot_general | solution.py:93
  83.6 0.7 gather_fusion.8
  84.3 0.6 collective-permute-start.13
  85.0 4.7 %fusion.7 = f32[6,32,5,128]{3,1,2,0:T(8,128)S(1)} fusion(bf16[5,128,4096,1]{2,1,0,3:T(8,128)(2,1)} %bitcast.110, bf16[6,32,1024]{2,1,0:T(8,128)(2,1)} %collective-permute-done.7, bf16[6,32,1024]{2,1,0:T(8,128)(2,1)} %collective-permute-done.6, bf16[6,32,1024]{2,1,0:T(8,128)(2,1)} %collective-permute-done.5, bf16[6,32,1024]{2,1,0:T(8,128)(2,1)S(1)} %get-tuple-element.17), kind=kOutput, calls=%fused_computation.21 | convolution fusion | flops 1012924416 | bytes 7307264 | tf_op jit(solution)/shard_map/dot_general | solution.py:93
  89.7 0.7 gather_fusion.5
  90.5 1.5 %collective-permute-start.8 = (f32[2,6,32,128]{3,2,1,0:T(8,128)S(1)}, f32[2,6,32,128]{3,2,1,0:T(8,128)S(1)}, u32[]{:S(2)}, u32[]{:S(2)}) collective-permute-start(f32[2,6,32,128]{3,2,1,0:T(8,128)S(1)} %dynamic-slice_bitcast_fusion.4), channel_id=1, source_target_pairs={{0,2},{2,0},{1,3},{3,1},{4,6},{6,4},{5,7},{7,5},{8,10},{10,8},{9,1... | collective-permute-start | bytes 589832 | tf_op jit(solution)/shard_map/ppermute | solution.py:26
  92.0 0.0 collective-permute-done.13
  92.1 0.1 collective-permute-start.14
  92.2 0.5 collective-permute-start.4
  92.8 0.6 collective-permute-done.14
  93.3 0.6 gather_fusion.9
  93.9 0.1 broadcast_select_fusion.2
  94.0 0.0 collective-permute-done.4
  94.0 0.6 gather_fusion.3
  94.5 2.3 %collective-permute-done.8 = f32[2,6,32,128]{3,2,1,0:T(8,128)S(1)} collective-permute-done((f32[2,6,32,128]{3,2,1,0:T(8,128)S(1)}, f32[2,6,32,128]{3,2,1,0:T(8,128)S(1)}, u32[]{:S(2)}, u32[]{:S(2)}) %collective-permute-start.8) | collective-permute-done | bytes 196640 | tf_op jit(solution)/shard_map/ppermute | solution.py:26
  96.9 0.1 collective-permute-start.9
  96.9 0.1 broadcast_select_fusion.1
  97.0 1.2 %collective-permute-done.9 = f32[6,32,128]{2,1,0:T(8,128)S(1)} collective-permute-done((f32[6,32,128]{2,1,0:T(8,128)S(1)}, f32[6,32,128]{2,1,0:T(8,128)S(1)}, u32[]{:S(2)}, u32[]{:S(2)}) %collective-permute-start.9) | collective-permute-done | bytes 98336 | tf_op jit(solution)/shard_map/ppermute | solution.py:106
  98.2 0.6 gather_fusion.6
  98.8 0.1 broadcast_select_fusion
  98.9 0.8 copy.8
  (45 shorter events, 0.5 us)
Async XLA Ops:
  0.0 0.7 copy-start
  0.0 3.2 %copy-start.1 = (f32[1,1024]{1,0:T(1,128)S(1)}, f32[1,1024]{1,0:T(1,128)}, u32[]{:S(2)}) copy-start(f32[1,1024]{1,0:T(1,128)} %param.9) | copy-start | bytes 12292
  4.4 36.0 %collective-permute-start = (bf16[6,24,1024]{2,1,0:T(8,128)(2,1)}, bf16[6,24,1024]{2,1,0:T(8,128)(2,1)}, u32[]{:S(2)}, u32[]{:S(2)}) collective-permute-start(bf16[6,24,1024]{2,1,0:T(8,128)(2,1)} %get-tuple-element.24), channel_id=1, source_target_pairs={{0,4},{4,8},{8,12},{12,0},{1,5},{5,9},{9,13},{13,1},{2,6},{6,10},{... | collective-permute-start | bytes 884744 | tf_op jit(solution)/shard_map/ppermute | solution.py:88
  7.5 32.9 %collective-permute-start.1 = (bf16[6,24,1024]{2,1,0:T(8,128)(2,1)S(1)}, bf16[6,24,1024]{2,1,0:T(8,128)(2,1)}, u32[]{:S(2)}, u32[]{:S(2)}) collective-permute-start(bf16[6,24,1024]{2,1,0:T(8,128)(2,1)S(1)} %get-tuple-element.23), channel_id=1, source_target_pairs={{0,8},{4,12},{8,0},{12,4},{1,9},{5,13},{9,1},{13,5},{2,10},{6,14},... | collective-permute-start | bytes 884744 | tf_op jit(solution)/shard_map/ppermute | solution.py:88
  10.1 30.4 %collective-permute-start.2 = (bf16[6,24,1024]{2,1,0:T(8,128)(2,1)S(1)}, bf16[6,24,1024]{2,1,0:T(8,128)(2,1)}, u32[]{:S(2)}, u32[]{:S(2)}) collective-permute-start(bf16[6,24,1024]{2,1,0:T(8,128)(2,1)S(1)} %get-tuple-element.22), channel_id=1, source_target_pairs={{0,12},{4,0},{8,4},{12,8},{1,13},{5,1},{9,5},{13,9},{2,14},{6,2},{... | collective-permute-start | bytes 884744 | tf_op jit(solution)/shard_map/ppermute | solution.py:88
  13.6 7.9 %copy-start.2 = (s32[1,2]{1,0:T(1,128)S(1)}, s32[1,2]{1,0:T(1,128)}, u32[]{:S(2)}) copy-start(s32[1,2]{1,0:T(1,128)} %param.13) | copy-start | bytes 28
  14.3 70.6 %collective-permute-start.7 = (bf16[6,32,1024]{2,1,0:T(8,128)(2,1)S(1)}, bf16[6,32,1024]{2,1,0:T(8,128)(2,1)}, u32[]{:S(2)}, u32[]{:S(2)}) collective-permute-start(bf16[6,32,1024]{2,1,0:T(8,128)(2,1)S(1)} %get-tuple-element.18), channel_id=1, source_target_pairs={{0,12},{4,0},{8,4},{12,8},{1,13},{5,1},{9,5},{13,9},{2,14},{6,2},{... | collective-permute-start | bytes 1179656 | tf_op jit(solution)/shard_map/ppermute | solution.py:88
  14.8 70.1 %collective-permute-start.6 = (bf16[6,32,1024]{2,1,0:T(8,128)(2,1)S(1)}, bf16[6,32,1024]{2,1,0:T(8,128)(2,1)}, u32[]{:S(2)}, u32[]{:S(2)}) collective-permute-start(bf16[6,32,1024]{2,1,0:T(8,128)(2,1)S(1)} %get-tuple-element.19), channel_id=1, source_target_pairs={{0,8},{4,12},{8,0},{12,4},{1,9},{5,13},{9,1},{13,5},{2,10},{6,14},... | collective-permute-start | bytes 1179656 | tf_op jit(solution)/shard_map/ppermute | solution.py:88
  24.8 13.4 %copy-start.3 = (s32[1,24]{1,0:T(1,128)S(1)}, s32[1,24]{1,0:T(1,128)}, u32[]{:S(2)}) copy-start(s32[1,24]{1,0:T(1,128)} %param.12) | copy-start | bytes 292
  24.8 13.4 %copy-start.4 = (s32[1,24]{1,0:T(1,128)S(1)}, s32[1,24]{1,0:T(1,128)}, u32[]{:S(2)}) copy-start(s32[1,24]{1,0:T(1,128)} %param.11) | copy-start | bytes 292
  40.5 21.0 %collective-permute-start.12 = (bf16[6,8,1024]{2,1,0:T(8,128)(2,1)S(1)}, bf16[6,8,1024]{2,1,0:T(8,128)(2,1)S(1)}, u32[]{:S(2)}, u32[]{:S(2)}) collective-permute-start(bf16[6,8,1024]{2,1,0:T(8,128)(2,1)S(1)} %get-tuple-element.26), channel_id=1, source_target_pairs={{0,12},{4,0},{8,4},{12,8},{1,13},{5,1},{9,5},{13,9},{2,14},{6,2},{... | collective-permute-start | bytes 294920 | tf_op jit(solution)/shard_map/ppermute | solution.py:88
  55.5 22.4 %collective-permute-start.11 = (bf16[6,8,1024]{2,1,0:T(8,128)(2,1)S(1)}, bf16[6,8,1024]{2,1,0:T(8,128)(2,1)S(1)}, u32[]{:S(2)}, u32[]{:S(2)}) collective-permute-start(bf16[6,8,1024]{2,1,0:T(8,128)(2,1)S(1)} %get-tuple-element.27), channel_id=1, source_target_pairs={{0,8},{4,12},{8,0},{12,4},{1,9},{5,13},{9,1},{13,5},{2,10},{6,14},... | collective-permute-start | bytes 294920 | tf_op jit(solution)/shard_map/ppermute | solution.py:88
  55.5 23.9 %collective-permute-start.10 = (bf16[6,8,1024]{2,1,0:T(8,128)(2,1)S(1)}, bf16[6,8,1024]{2,1,0:T(8,128)(2,1)}, u32[]{:S(2)}, u32[]{:S(2)}) collective-permute-start(bf16[6,8,1024]{2,1,0:T(8,128)(2,1)S(1)} %get-tuple-element.28), channel_id=1, source_target_pairs={{0,4},{4,8},{8,12},{12,0},{1,5},{5,9},{9,13},{13,1},{2,6},{6,10},{... | collective-permute-start | bytes 294920 | tf_op jit(solution)/shard_map/ppermute | solution.py:88
  61.5 23.5 %collective-permute-start.5 = (bf16[6,32,1024]{2,1,0:T(8,128)(2,1)S(1)}, bf16[6,32,1024]{2,1,0:T(8,128)(2,1)}, u32[]{:S(2)}, u32[]{:S(2)}) collective-permute-start(bf16[6,32,1024]{2,1,0:T(8,128)(2,1)S(1)} %get-tuple-element.20), channel_id=1, source_target_pairs={{0,4},{4,8},{8,12},{12,0},{1,5},{5,9},{9,13},{13,1},{2,6},{6,10},{... | collective-permute-start | bytes 1179656 | tf_op jit(solution)/shard_map/ppermute | solution.py:88
  77.9 14.2 %collective-permute-start.3 = (f32[2,6,24,128]{3,2,1,0:T(8,128)S(1)}, f32[2,6,24,128]{3,2,1,0:T(8,128)S(1)}, u32[]{:S(2)}, u32[]{:S(2)}) collective-permute-start(f32[2,6,24,128]{3,2,1,0:T(8,128)S(1)} %dynamic-slice_bitcast_fusion.5), channel_id=1, source_target_pairs={{0,2},{2,0},{1,3},{3,1},{4,6},{6,4},{5,7},{7,5},{8,10},{10,8},{9,1... | collective-permute-start | bytes 442376 | tf_op jit(solution)/shard_map/ppermute | solution.py:26
  84.3 7.7 %collective-permute-start.13 = (f32[2,6,8,128]{3,2,1,0:T(8,128)S(1)}, f32[2,6,8,128]{3,2,1,0:T(8,128)S(1)}, u32[]{:S(2)}, u32[]{:S(2)}) collective-permute-start(f32[2,6,8,128]{3,2,1,0:T(8,128)S(1)} %dynamic-slice_bitcast_fusion.8), channel_id=1, source_target_pairs={{0,2},{2,0},{1,3},{3,1},{4,6},{6,4},{5,7},{7,5},{8,10},{10,8},{9,1... | collective-permute-start | bytes 147464 | tf_op jit(solution)/shard_map/ppermute | solution.py:26
  90.5 6.3 %collective-permute-start.8 = (f32[2,6,32,128]{3,2,1,0:T(8,128)S(1)}, f32[2,6,32,128]{3,2,1,0:T(8,128)S(1)}, u32[]{:S(2)}, u32[]{:S(2)}) collective-permute-start(f32[2,6,32,128]{3,2,1,0:T(8,128)S(1)} %dynamic-slice_bitcast_fusion.4), channel_id=1, source_target_pairs={{0,2},{2,0},{1,3},{3,1},{4,6},{6,4},{5,7},{7,5},{8,10},{10,8},{9,1... | collective-permute-start | bytes 589832 | tf_op jit(solution)/shard_map/ppermute | solution.py:26
  92.1 1.3 %collective-permute-start.14 = (f32[6,8,128]{2,1,0:T(8,128)S(1)}, f32[6,8,128]{2,1,0:T(8,128)S(1)}, u32[]{:S(2)}, u32[]{:S(2)}) collective-permute-start(f32[6,8,128]{2,1,0:T(8,128)S(1)} %get-tuple-element.34), channel_id=1, source_target_pairs={{0,1},{1,0},{2,3},{3,2},{4,5},{5,4},{6,7},{7,6},{8,9},{9,8},{10,11... | collective-permute-start | bytes 73736 | tf_op jit(solution)/shard_map/ppermute | solution.py:106
  92.2 1.8 %collective-permute-start.4 = (f32[6,24,128]{2,1,0:T(8,128)S(1)}, f32[6,24,128]{2,1,0:T(8,128)S(1)}, u32[]{:S(2)}, u32[]{:S(2)}) collective-permute-start(f32[6,24,128]{2,1,0:T(8,128)S(1)} %get-tuple-element.32), channel_id=1, source_target_pairs={{0,1},{1,0},{2,3},{3,2},{4,5},{5,4},{6,7},{7,6},{8,9},{9,8},{10,11... | collective-permute-start | bytes 221192 | tf_op jit(solution)/shard_map/ppermute | solution.py:106
  96.9 1.4 %collective-permute-start.9 = (f32[6,32,128]{2,1,0:T(8,128)S(1)}, f32[6,32,128]{2,1,0:T(8,128)S(1)}, u32[]{:S(2)}, u32[]{:S(2)}) collective-permute-start(f32[6,32,128]{2,1,0:T(8,128)S(1)} %get-tuple-element.30), channel_id=1, source_target_pairs={{0,1},{1,0},{2,3},{3,2},{4,5},{5,4},{6,7},{7,6},{8,9},{9,8},{10,11... | collective-permute-start | bytes 294920 | tf_op jit(solution)/shard_map/ppermute | solution.py:106

commit v7 on v6

--- a/solution.py
+++ b/solution.py
@@ -7,7 +7,7 @@
 
 
 BLOCK = 128
-ROW_SPLIT = (24, 32, 8)
+ROW_SPLIT = (8, 40, 16)
 GATE_FROM = {2: 0}
 
 
@@ -51,7 +51,6 @@
         for k in range(n_span):
             t_parts.append(lax.dynamic_slice_in_dim(t_l, sources[k] * features, features, axis=1))
     train = jnp.concatenate(t_parts, axis=1)
-    train = jnp.concatenate([train, jnp.zeros((BLOCK, train.shape[1]), train.dtype)], axis=0)
 
     score_scale = 1.0 / math.sqrt(l_dev * n_layer * d_full)
     slot_row = pair_slot[0]
@@ -59,7 +58,6 @@
     counts = pair_count[0]
     slots = jnp.arange(pmax, dtype=jnp.int32)
     live = (slots % phalf) < counts[slots // phalf]
-    pick_train = jnp.where(live, train_row, tb_dev)
 
     outs = []
     gate = None
@@ -73,7 +71,7 @@
         for layer in range(l_dev):
             q3 = queries[:, layer, :].reshape(n_query // BLOCK, BLOCK, features)
             q3 = lax.dynamic_slice_in_dim(q3, rep_index * own_rows + row_start, rows, axis=1)
-            got = jnp.take(q3, block_ids, axis=0).reshape(n_span, cap, rows, features)
+            got = jnp.take(q3, block_ids, axis=0, mode="clip").reshape(n_span, cap, rows, features)
             sent.append((got.astype(jnp.float32) * precond[layer]).astype(jnp.bfloat16))
         row_start += rows
         prev_sent = sent
@@ -95,8 +93,9 @@
             train,
             (((1,), (1,)), ((), ())),
             preferred_element_type=jnp.float32,
-        ).reshape(cap, rows, tb_dev + 1, BLOCK)
-        partial = combos.at[slot_row, :, pick_train, :].get(mode="promise_in_bounds") * score_scale
+        ).reshape(cap, rows, tb_dev, BLOCK)
+        partial = combos.at[slot_row, :, train_row, :].get(mode="promise_in_bounds") * score_scale
+        partial = jnp.where(live[:, None, None], partial, 0.0)
         partial = partial.reshape(n_layer, n_rep, per_dev, rows, BLOCK)
         partial = ring_reduce_scatter(partial, "layer", 0)
         got_rows = [lax.dynamic_index_in_dim(partial, rep_index, axis=0, keepdims=False)]
@@ -107,7 +106,7 @@
         by_owner = jnp.stack(got_rows, axis=0)
         owner_order = (rep_index - jnp.arange(n_rep, dtype=jnp.int32) + n_rep) % n_rep
         order = jnp.argsort(owner_order)
-        by_owner = jnp.take(by_owner, order, axis=0)
+        by_owner = jnp.take(by_owner, order, axis=0, mode="clip")
         outs.append(by_owner)
     summed = jnp.concatenate(outs, axis=2)
     summed = jnp.transpose(summed, (1, 0, 2, 3)).reshape(per_dev * BLOCK, BLOCK)

time: 100 us -> 101 us (1.010)
  other arithmetic: 17 us -> 4.73 us
  waiting for transfers between devices: 5.5 us -> 12.4 us
  starting transfers between devices: 44.1 us -> 50.8 us
  matrix products: 13.5 us -> 9.32 us
  local copies, waits for them, and re-layouts: 16.4 us -> 20.2 us
    concatenate x2 -> x1, other arithmetic: 14.7 us -> 0.01 us  [shards(): combos.at[slot_row, :, train_row, :].get(mode='promise_in_bounds')]
    ppermute x9, starting transfers between devices: 39.8 us -> 46 us  [shards(): piece = lax.ppermute(piece, 'span', perm)]
    ppermute x9, waiting for transfers between devices: 1.47 us -> 6.16 us  [shards(): piece = lax.ppermute(piece, 'span', perm)]
    dot_general x3, matrix products: 13.5 us -> 9.32 us  [shards(): lax.dot_general(arrived, train, (((1,), (1,)), ((), ())), preferred_eleme...]
    ppermute x3, waiting for transfers between devices: 2.26 us -> 6.27 us  [ring_reduce_scatter(): recv = lax.ppermute(acc, axis_name, perm)]
    ppermute x3, waiting for transfers between devices: 1.77 us -> 0.01 us  [shards(): got_rows.append(lax.ppermute(send, 'rep', perm))]
    unnamed x10 -> x18, local copies, waits for them, and re-layouts: 0.68 us -> 1.97 us
    gather x4 -> x5, other arithmetic: 0.02 us -> 1.29 us  [the longest x1 1.27 us: shards(): live = slots % phalf < counts[slots // phalf]]
  transfers between devices with their start and end apart: 15 -> 15, of which waited for: 4 -> 4; matrix products, arithmetic and copies ran while one was open for 41% -> 27% of each run, Pallas kernels for 0% -> 0%
where the time goes in v7:
time: 101 us; the launch traced here: 100 us
  starting transfers between devices  50.8 us (50%)
  local copies, waits for them, and re-layouts  20.2 us (20%)
  waiting for transfers between devices  12.4 us (12%)
  matrix products  9.32 us (9%)
  other arithmetic  4.73 us (5%)
  between operations  3.01 us (3%)
    ppermute x9, starting transfers between devices, shards(): piece = lax.ppermute(piece, 'span', perm)  46 us
    dot_general x3, matrix products, shards(): lax.dot_general(arrived, train, (((1,), (1,)), ((), ())), preferred_eleme...  9.32 us
    ppermute x3, waiting for transfers between devices, ring_reduce_scatter(): recv = lax.ppermute(acc, axis_name, perm)  6.27 us
    ppermute x9, waiting for transfers between devices, shards(): piece = lax.ppermute(piece, 'span', perm)  6.16 us
    ppermute x3, starting transfers between devices, ring_reduce_scatter(): recv = lax.ppermute(acc, axis_name, perm)  4.67 us
    dynamic_slice x3, local copies, waits for them, and re-layouts, shards(): lax.dynamic_slice_in_dim(q3, rep_index * own_rows + row_start, rows, axis=1)  3.47 us
    gather x3, local copies, waits for them, and re-layouts, shards(): combos.at[slot_row, :, train_row, :].get(mode='promise_in_bounds')  3.05 us
    dynamic_slice x1, local copies, waits for them, and re-layouts, shards(): lax.dynamic_slice_in_dim(t_l, sources[k] * features, features, axis=1)  2.62 us
  transfers between devices with their start and end apart: 15, of which 4 were waited for; matrix products, arithmetic and copies ran while one was open for 27% of the time, Pallas kernels for 0%

profile of v7, /device:TPU:0, one launch (start us, length us, event | category | flops | bytes accessed | tf_op | source)
XLA Modules:
  0.0 100.5 jit_solution(10700032266037399963)
XLA Ops:
  0.0 0.7 copy-done
  0.7 0.6 gather_fusion
  1.2 0.1 reshape.305
  1.3 1.0 constant_dynamic-slice_fusion.9
  2.3 0.6 gather_fusion.1
  2.9 0.0 copy-start.5
  2.9 0.8 fusion.16
  3.7 0.7 slice_bitcast_fusion.11
  4.4 5.1 %collective-permute-start.2 = (bf16[6,8,1024]{2,1,0:T(8,128)(2,1)}, bf16[6,8,1024]{2,1,0:T(8,128)(2,1)}, u32[]{:S(2)}, u32[]{:S(2)}) collective-permute-start(bf16[6,8,1024]{2,1,0:T(8,128)(2,1)} %get-tuple-element.26), channel_id=1, source_target_pairs={{0,12},{4,0},{8,4},{12,8},{1,13},{5,1},{9,5},{13,9},{2,14},{6,2},{... | collective-permute-start | bytes 294920 | tf_op jit(solution)/shard_map/ppermute | solution.py:86
  9.5 0.0 collective-permute-start.1
  9.5 1.0 %collective-permute-start = (bf16[6,8,1024]{2,1,0:T(8,128)(2,1)S(1)}, bf16[6,8,1024]{2,1,0:T(8,128)(2,1)}, u32[]{:S(2)}, u32[]{:S(2)}) collective-permute-start(bf16[6,8,1024]{2,1,0:T(8,128)(2,1)S(1)} %get-tuple-element.28), channel_id=1, source_target_pairs={{0,4},{4,8},{8,12},{12,0},{1,5},{5,9},{9,13},{13,1},{2,6},{6,10},{... | collective-permute-start | bytes 294920 | tf_op jit(solution)/shard_map/ppermute | solution.py:86
  10.5 1.4 %constant_dynamic-slice_fusion.3 = bf16[16,40,1024]{2,1,0:T(8,128)(2,1)S(1)} fusion(bf16[16,128,1024]{2,1,0:T(8,128)(2,1)} %bitcast.118, s32[]{:T(128)S(6)} %select_n.206), kind=kLoop, calls=%fused_computation.75 | loop fusion | bytes 2621444 | tf_op jit(solution)/shard_map/dynamic_slice | solution.py:73
  12.0 0.7 gather_fusion.4
  12.6 0.0 copy-start.6
  12.7 0.5 fusion
  13.2 0.0 copy-start.7
  13.2 0.0 copy-start.8
  13.2 1.3 %slice_bitcast_fusion.3 = (bf16[6,40,1024]{2,1,0:T(8,128)(2,1)}, bf16[6,40,1024]{2,1,0:T(8,128)(2,1)}, bf16[6,40,1024]{2,1,0:T(8,128)(2,1)}, bf16[6,40,1024]{2,1,0:T(8,128)(2,1)}) fusion(bf16[4,6,40,1024]{3,2,1,0:T(8,128)(2,1)S(1)} %fusion), kind=kLoop, calls=%fused_computation.36 | loop fusion | bytes 3932160 | tf_op jit(solution)/shard_map/concatenate | solution.py:90
  14.5 2.8 %collective-permute-start.7 = (bf16[6,40,1024]{2,1,0:T(8,128)(2,1)}, bf16[6,40,1024]{2,1,0:T(8,128)(2,1)}, u32[]{:S(2)}, u32[]{:S(2)}) collective-permute-start(bf16[6,40,1024]{2,1,0:T(8,128)(2,1)} %get-tuple-element.18), channel_id=1, source_target_pairs={{0,12},{4,0},{8,4},{12,8},{1,13},{5,1},{9,5},{13,9},{2,14},{6,2},{... | collective-permute-start | bytes 1474568 | tf_op jit(solution)/shard_map/ppermute | solution.py:86
  17.3 1.1 %collective-permute-start.6 = (bf16[6,40,1024]{2,1,0:T(8,128)(2,1)}, bf16[6,40,1024]{2,1,0:T(8,128)(2,1)}, u32[]{:S(2)}, u32[]{:S(2)}) collective-permute-start(bf16[6,40,1024]{2,1,0:T(8,128)(2,1)} %get-tuple-element.19), channel_id=1, source_target_pairs={{0,8},{4,12},{8,0},{12,4},{1,9},{5,13},{9,1},{13,5},{2,10},{6,14},... | collective-permute-start | bytes 1474568 | tf_op jit(solution)/shard_map/ppermute | solution.py:86
  18.5 0.7 fusion.40
  21.7 0.6 fusion.39
  22.3 1.3 %fusion.25 = s32[24]{0:T(128)S(1)} fusion(s32[]{:T(128)} %bitcast.1, s32[]{:T(128)} %bitcast), kind=kLoop, calls=%fused_computation.107 | loop fusion | flops 312 | bytes 104 | tf_op jit(solution)/shard_map/gather | solution.py:60
  23.5 0.1 gather.44
  23.7 1.1 %constant_dynamic-slice_fusion.1 = bf16[16,16,1024]{2,1,0:T(8,128)(2,1)S(1)} fusion(bf16[16,128,1024]{2,1,0:T(8,128)(2,1)} %bitcast.119, s32[]{:T(128)S(6)} %select_n.208), kind=kLoop, calls=%fused_computation.73 | loop fusion | bytes 1048580 | tf_op jit(solution)/shard_map/dynamic_slice | solution.py:73
  24.8 0.6 gather_fusion.7
  25.4 0.2 fusion.8
  25.6 0.6 sort.21
  26.2 2.6 %constant_dynamic-slice_fusion.8 = (bf16[512,1,1024]{2,0,1:T(8,128)(2,1)S(1)}, bf16[512,1,1024]{2,0,1:T(8,128)(2,1)S(1)}, bf16[512,1,1024]{2,0,1:T(8,128)(2,1)S(1)}, bf16[512,1,1024]{2,0,1:T(8,128)(2,1)S(1)}) fusion(bf16[512,1,4096]{2,0,1:T(8,128)(2,1)} %param.8, s32[]{:T(128)S(6)} %select_n.191, s32[]{:T(128)S(6)} %select_n.192, s32[]{:T(128)S(6)} %select_n.194, ...), kind=kLoop, calls=%fused_computation.80 | loop fusion | bytes 8388624 | tf_op jit(solution)/shard_map/dynamic_slice | solution.py:52
  28.9 0.0 collective-permute-done.2
  28.9 0.0 collective-permute-done.1
  28.9 0.9 copy-done.1
  29.8 0.4 copy-done.3
  30.2 2.3 %fusion.17 = f32[6,8,4,128]{3,1,2,0:T(8,128)S(1)} fusion(bf16[6,8,1024]{2,1,0:T(8,128)(2,1)} %collective-permute-done.2, bf16[6,8,1024]{2,1,0:T(8,128)(2,1)} %collective-permute-done.1, bf16[6,8,1024]{2,1,0:T(8,128)(2,1)} %collective-permute-done, bf16[6,8,1024]{2,1,0:T(8,128)(2,1)S(1)} %get-tuple-element.25, bf16[4,128,1024]{2,1,0:T(8,128)(2,1)S(1)} %bitcast.111, ...), kind=kOutput, calls=%fused_computation.38 | convolution fusion | flops 219676672 | bytes 4685824 | tf_op jit(solution)/shard_map/dot_general | solution.py:91
  32.6 0.7 gather_fusion.2
  33.3 0.1 broadcast_select_fusion.2
  33.4 1.6 %collective-permute-start.3 = (f32[2,6,8,128]{3,2,1,0:T(8,128)S(1)}, f32[2,6,8,128]{3,2,1,0:T(8,128)S(1)}, u32[]{:S(2)}, u32[]{:S(2)}) collective-permute-start(f32[2,6,8,128]{3,2,1,0:T(8,128)S(1)} %dynamic-slice_bitcast_fusion.4), channel_id=1, source_target_pairs={{0,2},{2,0},{1,3},{3,1},{4,6},{6,4},{5,7},{7,5},{8,10},{10,8},{9,1... | collective-permute-start | bytes 147464 | tf_op jit(solution)/shard_map/ppermute | solution.py:26
  34.9 0.1 slice_bitcast_fusion.7
  35.0 1.0 collective-permute-start.12
  35.9 18.0 %collective-permute-start.11 = (bf16[6,16,1024]{2,1,0:T(8,128)(2,1)S(1)}, bf16[6,16,1024]{2,1,0:T(8,128)(2,1)S(1)}, u32[]{:S(2)}, u32[]{:S(2)}) collective-permute-start(bf16[6,16,1024]{2,1,0:T(8,128)(2,1)S(1)} %get-tuple-element.23), channel_id=1, source_target_pairs={{0,8},{4,12},{8,0},{12,4},{1,9},{5,13},{9,1},{13,5},{2,10},{6,14},... | collective-permute-start | bytes 589832 | tf_op jit(solution)/shard_map/ppermute | solution.py:86
  54.0 0.0 collective-permute-done.3
  54.0 1.9 %collective-permute-start.10 = (bf16[6,16,1024]{2,1,0:T(8,128)(2,1)S(1)}, bf16[6,16,1024]{2,1,0:T(8,128)(2,1)S(1)}, u32[]{:S(2)}, u32[]{:S(2)}) collective-permute-start(bf16[6,16,1024]{2,1,0:T(8,128)(2,1)S(1)} %get-tuple-element.24), channel_id=1, source_target_pairs={{0,4},{4,8},{8,12},{12,0},{1,5},{5,9},{9,13},{13,1},{2,6},{6,10},{... | collective-permute-start | bytes 589832 | tf_op jit(solution)/shard_map/ppermute | solution.py:86
  56.0 0.6 constant_dynamic-slice_fusion.4
  56.6 4.0 %collective-permute-done.12 = bf16[6,16,1024]{2,1,0:T(8,128)(2,1)S(1)} collective-permute-done((bf16[6,16,1024]{2,1,0:T(8,128)(2,1)S(1)}, bf16[6,16,1024]{2,1,0:T(8,128)(2,1)S(1)}, u32[]{:S(2)}, u32[]{:S(2)}) %collective-permute-start.12) | collective-permute-done | bytes 196640 | tf_op jit(solution)/shard_map/ppermute | solution.py:86
  60.6 15.0 %collective-permute-start.5 = (bf16[6,40,1024]{2,1,0:T(8,128)(2,1)}, bf16[6,40,1024]{2,1,0:T(8,128)(2,1)}, u32[]{:S(2)}, u32[]{:S(2)}) collective-permute-start(bf16[6,40,1024]{2,1,0:T(8,128)(2,1)} %get-tuple-element.20), channel_id=1, source_target_pairs={{0,4},{4,8},{8,12},{12,0},{1,5},{5,9},{9,13},{13,1},{2,6},{6,10},{... | collective-permute-start | bytes 1474568 | tf_op jit(solution)/shard_map/ppermute | solution.py:86
  75.6 1.9 %collective-permute-done.11 = bf16[6,16,1024]{2,1,0:T(8,128)(2,1)S(1)} collective-permute-done((bf16[6,16,1024]{2,1,0:T(8,128)(2,1)S(1)}, bf16[6,16,1024]{2,1,0:T(8,128)(2,1)S(1)}, u32[]{:S(2)}, u32[]{:S(2)}) %collective-permute-start.11) | collective-permute-done | bytes 196640 | tf_op jit(solution)/shard_map/ppermute | solution.py:86
  77.5 0.0 collective-permute-start.4
  77.5 3.1 %fusion.9 = f32[6,16,4,128]{3,1,2,0:T(8,128)S(1)} fusion(bf16[6,16,1024]{2,1,0:T(8,128)(2,1)S(1)} %collective-permute-done.12, bf16[6,16,1024]{2,1,0:T(8,128)(2,1)S(1)} %collective-permute-done.11, bf16[6,16,1024]{2,1,0:T(8,128)(2,1)S(1)} %collective-permute-done.10, bf16[6,16,1024]{2,1,0:T(8,128)(2,1)S(1)} %get-tuple-element.21, ...), kind=kOutput, calls=%fused_computation.24 | convolution fusion | flops 422576128 | bytes 5177344 | tf_op jit(solution)/shard_map/dot_general | solution.py:91
  80.6 0.7 gather_fusion.8
  81.3 0.1 broadcast_select_fusion.1
  81.5 1.6 %collective-permute-start.13 = (f32[2,6,16,128]{3,2,1,0:T(8,128)S(1)}, f32[2,6,16,128]{3,2,1,0:T(8,128)S(1)}, u32[]{:S(2)}, u32[]{:S(2)}) collective-permute-start(f32[2,6,16,128]{3,2,1,0:T(8,128)S(1)} %dynamic-slice_bitcast_fusion.2), channel_id=1, source_target_pairs={{0,2},{2,0},{1,3},{3,1},{4,6},{6,4},{5,7},{7,5},{8,10},{10,8},{9,1... | collective-permute-start | bytes 294920 | tf_op jit(solution)/shard_map/ppermute | solution.py:26
  83.0 0.2 collective-permute-done.5
  83.2 3.9 %fusion.1 = f32[6,40,4,128]{3,1,2,0:T(8,128)} fusion(bf16[6,40,1024]{2,1,0:T(8,128)(2,1)} %collective-permute-done.7, bf16[6,40,1024]{2,1,0:T(8,128)(2,1)} %collective-permute-done.6, bf16[6,40,1024]{2,1,0:T(8,128)(2,1)} %collective-permute-done.5, bf16[6,40,1024]{2,1,0:T(8,128)(2,1)} %get-tuple-element.17, bf16[4,128,1024]{2,1,0:T(8,128)(2,1)S(1)} %bitcast.113, ...), kind=kOutput, calls=%fused_computation.14 | convolution fusion | flops 1031274496 | bytes 6651904 | tf_op jit(solution)/shard_map/dot_general | solution.py:91
  87.2 1.7 %gather_fusion.5 = f32[24,40,128]{2,1,0:T(8,128)S(1)} fusion(f32[6,40,4,128]{3,1,2,0:T(8,128)} %fusion.1, s32[24]{0:T(128)S(1)} %fusion.35), kind=kCustom, calls=%fused_computation.5 | custom fusion | bytes 983232 | tf_op jit(solution)/shard_map/gather | solution.py:97
  88.9 0.1 broadcast_select_fusion
  89.1 1.6 %collective-permute-start.8 = (f32[2,6,40,128]{3,2,1,0:T(8,128)S(1)}, f32[2,6,40,128]{3,2,1,0:T(8,128)S(1)}, u32[]{:S(2)}, u32[]{:S(2)}) collective-permute-start(f32[2,6,40,128]{3,2,1,0:T(8,128)S(1)} %dynamic-slice_bitcast_fusion), channel_id=1, source_target_pairs={{0,2},{2,0},{1,3},{3,1},{4,6},{6,4},{5,7},{7,5},{8,10},{10,8},{9,1... | collective-permute-start | bytes 737288 | tf_op jit(solution)/shard_map/ppermute | solution.py:26
  90.7 0.1 collective-permute-start.14
  90.7 6.3 %collective-permute-done.8 = f32[2,6,40,128]{3,2,1,0:T(8,128)S(1)} collective-permute-done((f32[2,6,40,128]{3,2,1,0:T(8,128)S(1)}, f32[2,6,40,128]{3,2,1,0:T(8,128)S(1)}, u32[]{:S(2)}, u32[]{:S(2)}) %collective-permute-start.8) | collective-permute-done | bytes 245792 | tf_op jit(solution)/shard_map/ppermute | solution.py:26
  97.1 0.1 collective-permute-start.9
  97.2 0.7 pad_maximum_fusion.2
  97.9 0.6 gather_fusion.3
  98.5 0.6 gather_fusion.9
  99.1 0.6 gather_fusion.6
  99.7 0.8 copy.8
  (44 shorter events, 0.4 us)
Async XLA Ops:
  0.0 0.7 copy-start
  2.9 9.8 %copy-start.5 = (f32[1,1024]{1,0:T(1,128)S(1)}, f32[1,1024]{1,0:T(1,128)}, u32[]{:S(2)}) copy-start(f32[1,1024]{1,0:T(1,128)} %param.9) | copy-start | bytes 12292
  4.4 24.5 %collective-permute-start.2 = (bf16[6,8,1024]{2,1,0:T(8,128)(2,1)}, bf16[6,8,1024]{2,1,0:T(8,128)(2,1)}, u32[]{:S(2)}, u32[]{:S(2)}) collective-permute-start(bf16[6,8,1024]{2,1,0:T(8,128)(2,1)} %get-tuple-element.26), channel_id=1, source_target_pairs={{0,12},{4,0},{8,4},{12,8},{1,13},{5,1},{9,5},{13,9},{2,14},{6,2},{... | collective-permute-start | bytes 294920 | tf_op jit(solution)/shard_map/ppermute | solution.py:86
  9.5 19.4 %collective-permute-start.1 = (bf16[6,8,1024]{2,1,0:T(8,128)(2,1)}, bf16[6,8,1024]{2,1,0:T(8,128)(2,1)}, u32[]{:S(2)}, u32[]{:S(2)}) collective-permute-start(bf16[6,8,1024]{2,1,0:T(8,128)(2,1)} %get-tuple-element.27), channel_id=1, source_target_pairs={{0,8},{4,12},{8,0},{12,4},{1,9},{5,13},{9,1},{13,5},{2,10},{6,14},... | collective-permute-start | bytes 294920 | tf_op jit(solution)/shard_map/ppermute | solution.py:86
  9.5 19.4 %collective-permute-start = (bf16[6,8,1024]{2,1,0:T(8,128)(2,1)S(1)}, bf16[6,8,1024]{2,1,0:T(8,128)(2,1)}, u32[]{:S(2)}, u32[]{:S(2)}) collective-permute-start(bf16[6,8,1024]{2,1,0:T(8,128)(2,1)S(1)} %get-tuple-element.28), channel_id=1, source_target_pairs={{0,4},{4,8},{8,12},{12,0},{1,5},{5,9},{9,13},{13,1},{2,6},{6,10},{... | collective-permute-start | bytes 294920 | tf_op jit(solution)/shard_map/ppermute | solution.py:86
  12.6 9.0 %copy-start.6 = (s32[1,2]{1,0:T(1,128)S(1)}, s32[1,2]{1,0:T(1,128)}, u32[]{:S(2)}) copy-start(s32[1,2]{1,0:T(1,128)} %param.13) | copy-start | bytes 28
  13.2 12.4 %copy-start.7 = (s32[1,24]{1,0:T(1,128)S(1)}, s32[1,24]{1,0:T(1,128)}, u32[]{:S(2)}) copy-start(s32[1,24]{1,0:T(1,128)} %param.12) | copy-start | bytes 292
  13.2 12.4 %copy-start.8 = (s32[1,24]{1,0:T(1,128)S(1)}, s32[1,24]{1,0:T(1,128)}, u32[]{:S(2)}) copy-start(s32[1,24]{1,0:T(1,128)} %param.11) | copy-start | bytes 292
  14.5 68.5 %collective-permute-start.7 = (bf16[6,40,1024]{2,1,0:T(8,128)(2,1)}, bf16[6,40,1024]{2,1,0:T(8,128)(2,1)}, u32[]{:S(2)}, u32[]{:S(2)}) collective-permute-start(bf16[6,40,1024]{2,1,0:T(8,128)(2,1)} %get-tuple-element.18), channel_id=1, source_target_pairs={{0,12},{4,0},{8,4},{12,8},{1,13},{5,1},{9,5},{13,9},{2,14},{6,2},{... | collective-permute-start | bytes 1474568 | tf_op jit(solution)/shard_map/ppermute | solution.py:86
  17.3 65.7 %collective-permute-start.6 = (bf16[6,40,1024]{2,1,0:T(8,128)(2,1)}, bf16[6,40,1024]{2,1,0:T(8,128)(2,1)}, u32[]{:S(2)}, u32[]{:S(2)}) collective-permute-start(bf16[6,40,1024]{2,1,0:T(8,128)(2,1)} %get-tuple-element.19), channel_id=1, source_target_pairs={{0,8},{4,12},{8,0},{12,4},{1,9},{5,13},{9,1},{13,5},{2,10},{6,14},... | collective-permute-start | bytes 1474568 | tf_op jit(solution)/shard_map/ppermute | solution.py:86
  28.9 1.0 copy-start.1
  28.9 1.3 %copy-start.3 = (bf16[512,1,1024]{2,0,1:T(8,128)(2,1)}, bf16[512,1,1024]{2,0,1:T(8,128)(2,1)S(1)}, u32[]{:S(2)}) copy-start(bf16[512,1,1024]{2,0,1:T(8,128)(2,1)S(1)} %get-tuple-element.16) | copy-start | bytes 3145732
  33.4 20.6 %collective-permute-start.3 = (f32[2,6,8,128]{3,2,1,0:T(8,128)S(1)}, f32[2,6,8,128]{3,2,1,0:T(8,128)S(1)}, u32[]{:S(2)}, u32[]{:S(2)}) collective-permute-start(f32[2,6,8,128]{3,2,1,0:T(8,128)S(1)} %dynamic-slice_bitcast_fusion.4), channel_id=1, source_target_pairs={{0,2},{2,0},{1,3},{3,1},{4,6},{6,4},{5,7},{7,5},{8,10},{10,8},{9,1... | collective-permute-start | bytes 147464 | tf_op jit(solution)/shard_map/ppermute | solution.py:26
  35.0 25.6 %collective-permute-start.12 = (bf16[6,16,1024]{2,1,0:T(8,128)(2,1)S(1)}, bf16[6,16,1024]{2,1,0:T(8,128)(2,1)S(1)}, u32[]{:S(2)}, u32[]{:S(2)}) collective-permute-start(bf16[6,16,1024]{2,1,0:T(8,128)(2,1)S(1)} %get-tuple-element.22), channel_id=1, source_target_pairs={{0,12},{4,0},{8,4},{12,8},{1,13},{5,1},{9,5},{13,9},{2,14},{6,2},{... | collective-permute-start | bytes 589832 | tf_op jit(solution)/shard_map/ppermute | solution.py:86
  35.9 41.6 %collective-permute-start.11 = (bf16[6,16,1024]{2,1,0:T(8,128)(2,1)S(1)}, bf16[6,16,1024]{2,1,0:T(8,128)(2,1)S(1)}, u32[]{:S(2)}, u32[]{:S(2)}) collective-permute-start(bf16[6,16,1024]{2,1,0:T(8,128)(2,1)S(1)} %get-tuple-element.23), channel_id=1, source_target_pairs={{0,8},{4,12},{8,0},{12,4},{1,9},{5,13},{9,1},{13,5},{2,10},{6,14},... | collective-permute-start | bytes 589832 | tf_op jit(solution)/shard_map/ppermute | solution.py:86
  54.0 23.5 %collective-permute-start.10 = (bf16[6,16,1024]{2,1,0:T(8,128)(2,1)S(1)}, bf16[6,16,1024]{2,1,0:T(8,128)(2,1)S(1)}, u32[]{:S(2)}, u32[]{:S(2)}) collective-permute-start(bf16[6,16,1024]{2,1,0:T(8,128)(2,1)S(1)} %get-tuple-element.24), channel_id=1, source_target_pairs={{0,4},{4,8},{8,12},{12,0},{1,5},{5,9},{9,13},{13,1},{2,6},{6,10},{... | collective-permute-start | bytes 589832 | tf_op jit(solution)/shard_map/ppermute | solution.py:86
  60.6 22.7 %collective-permute-start.5 = (bf16[6,40,1024]{2,1,0:T(8,128)(2,1)}, bf16[6,40,1024]{2,1,0:T(8,128)(2,1)}, u32[]{:S(2)}, u32[]{:S(2)}) collective-permute-start(bf16[6,40,1024]{2,1,0:T(8,128)(2,1)} %get-tuple-element.20), channel_id=1, source_target_pairs={{0,4},{4,8},{8,12},{12,0},{1,5},{5,9},{9,13},{13,1},{2,6},{6,10},{... | collective-permute-start | bytes 1474568 | tf_op jit(solution)/shard_map/ppermute | solution.py:86
  77.5 19.6 %collective-permute-start.4 = (f32[6,8,128]{2,1,0:T(8,128)}, f32[6,8,128]{2,1,0:T(8,128)}, u32[]{:S(2)}, u32[]{:S(2)}) collective-permute-start(f32[6,8,128]{2,1,0:T(8,128)} %get-tuple-element.34), channel_id=1, source_target_pairs={{0,1},{1,0},{2,3},{3,2},{4,5},{5,4},{6,7},{7,6},{8,9},{9,8},{10,11... | collective-permute-start | bytes 73736 | tf_op jit(solution)/shard_map/ppermute | solution.py:105
  77.5 5.7 %copy-start.2 = (bf16[512,1,1024]{2,0,1:T(8,128)(2,1)S(1)}, bf16[512,1,1024]{2,0,1:T(8,128)(2,1)}, u32[]{:S(2)}) copy-start(bf16[512,1,1024]{2,0,1:T(8,128)(2,1)} %copy-done.1) | copy-start | bytes 3145732
  81.5 9.2 %collective-permute-start.13 = (f32[2,6,16,128]{3,2,1,0:T(8,128)S(1)}, f32[2,6,16,128]{3,2,1,0:T(8,128)S(1)}, u32[]{:S(2)}, u32[]{:S(2)}) collective-permute-start(f32[2,6,16,128]{3,2,1,0:T(8,128)S(1)} %dynamic-slice_bitcast_fusion.2), channel_id=1, source_target_pairs={{0,2},{2,0},{1,3},{3,1},{4,6},{6,4},{5,7},{7,5},{8,10},{10,8},{9,1... | collective-permute-start | bytes 294920 | tf_op jit(solution)/shard_map/ppermute | solution.py:26
  87.2 10.0 %copy-start.4 = (f32[1,6,8,128]{3,2,1,0:T(8,128)S(1)}, f32[1,6,8,128]{3,2,1,0:T(8,128)}, u32[]{:S(2)}) copy-start(f32[1,6,8,128]{3,2,1,0:T(8,128)} %get-tuple-element.33) | copy-start | bytes 73732
  89.1 8.0 %collective-permute-start.8 = (f32[2,6,40,128]{3,2,1,0:T(8,128)S(1)}, f32[2,6,40,128]{3,2,1,0:T(8,128)S(1)}, u32[]{:S(2)}, u32[]{:S(2)}) collective-permute-start(f32[2,6,40,128]{3,2,1,0:T(8,128)S(1)} %dynamic-slice_bitcast_fusion), channel_id=1, source_target_pairs={{0,2},{2,0},{1,3},{3,1},{4,6},{6,4},{5,7},{7,5},{8,10},{10,8},{9,1... | collective-permute-start | bytes 737288 | tf_op jit(solution)/shard_map/ppermute | solution.py:26
  90.7 7.8 %collective-permute-start.14 = (f32[6,16,128]{2,1,0:T(8,128)S(1)}, f32[6,16,128]{2,1,0:T(8,128)S(1)}, u32[]{:S(2)}, u32[]{:S(2)}) collective-permute-start(f32[6,16,128]{2,1,0:T(8,128)S(1)} %get-tuple-element.32), channel_id=1, source_target_pairs={{0,1},{1,0},{2,3},{3,2},{4,5},{5,4},{6,7},{7,6},{8,9},{9,8},{10,11... | collective-permute-start | bytes 147464 | tf_op jit(solution)/shard_map/ppermute | solution.py:105
  97.1 2.0 %collective-permute-start.9 = (f32[6,40,128]{2,1,0:T(8,128)S(1)}, f32[6,40,128]{2,1,0:T(8,128)S(1)}, u32[]{:S(2)}, u32[]{:S(2)}) collective-permute-start(f32[6,40,128]{2,1,0:T(8,128)S(1)} %get-tuple-element.30), channel_id=1, source_target_pairs={{0,1},{1,0},{2,3},{3,2},{4,5},{5,4},{6,7},{7,6},{8,9},{9,8},{10,11... | collective-permute-start | bytes 368648 | tf_op jit(solution)/shard_map/ppermute | solution.py:105

commit v8 on v6

--- a/solution.py
+++ b/solution.py
@@ -7,7 +7,7 @@
 
 
 BLOCK = 128
-ROW_SPLIT = (24, 32, 8)
+ROW_SPLIT = (8, 24, 32)
 GATE_FROM = {2: 0}
 
 
@@ -61,7 +61,7 @@
     live = (slots % phalf) < counts[slots // phalf]
     pick_train = jnp.where(live, train_row, tb_dev)
 
-    outs = []
+    out_buf = jnp.zeros((per_dev, BLOCK, BLOCK), jnp.float32)
     gate = None
     arrivals = []
     row_start = 0
@@ -104,14 +104,10 @@
             perm = [(i, (i + k) % n_rep) for i in range(n_rep)]
             send = lax.dynamic_index_in_dim(partial, (rep_index + k) % n_rep, axis=0, keepdims=False)
             got_rows.append(lax.ppermute(send, "rep", perm))
-        by_owner = jnp.stack(got_rows, axis=0)
-        owner_order = (rep_index - jnp.arange(n_rep, dtype=jnp.int32) + n_rep) % n_rep
-        order = jnp.argsort(owner_order)
-        by_owner = jnp.take(by_owner, order, axis=0)
-        outs.append(by_owner)
-    summed = jnp.concatenate(outs, axis=2)
-    summed = jnp.transpose(summed, (1, 0, 2, 3)).reshape(per_dev * BLOCK, BLOCK)
-    return summed[None]
+        for k, got in enumerate(got_rows):
+            owner = (rep_index - k + n_rep) % n_rep
+            out_buf = lax.dynamic_update_slice(out_buf, got, (0, owner * own_rows + row_start - rows, 0))
+    return out_buf.reshape(per_dev * BLOCK, BLOCK)[None]
 
 
 def solution(mesh):

time: 100 us -> 99 us (0.990)
  starting transfers between devices: 44.1 us -> 21.8 us
  waiting for transfers between devices: 5.5 us -> 27.7 us
    ppermute x9, starting transfers between devices: 39.8 us -> 17.1 us  [shards(): piece = lax.ppermute(piece, 'span', perm)]
    ppermute x9, waiting for transfers between devices: 1.47 us -> 17.6 us  [shards(): piece = lax.ppermute(piece, 'span', perm)]
    ppermute x3, waiting for transfers between devices: 2.26 us -> 8.87 us  [ring_reduce_scatter(): recv = lax.ppermute(acc, axis_name, perm)]
    gather x3 -> x0, local copies, waits for them, and re-layouts: 1.67 us -> none  [shards(): by_owner = jnp.take(by_owner, order, axis=0)]
where the time goes in v8:
time: 99 us; the launch traced here: 98.5 us
  waiting for transfers between devices  27.7 us (28%)
  starting transfers between devices  21.8 us (22%)
  other arithmetic  16.7 us (17%)
  local copies, waits for them, and re-layouts  15.6 us (16%)
  matrix products  13.6 us (14%)
  between operations  3.01 us (3%)
    ppermute x9, waiting for transfers between devices, shards(): piece = lax.ppermute(piece, 'span', perm)  17.6 us
    ppermute x9, starting transfers between devices, shards(): piece = lax.ppermute(piece, 'span', perm)  17.1 us
    dot_general x3, matrix products, shards(): lax.dot_general(arrived, train, (((1,), (1,)), ((), ())), preferred_eleme...  13.6 us
    concatenate x1, other arithmetic, shards(): train = jnp.concatenate(t_parts, axis=1)  13.4 us
    ppermute x3, waiting for transfers between devices, ring_reduce_scatter(): recv = lax.ppermute(acc, axis_name, perm)  8.87 us
    ppermute x3, starting transfers between devices, ring_reduce_scatter(): recv = lax.ppermute(acc, axis_name, perm)  4.62 us
    dynamic_slice x3, local copies, waits for them, and re-layouts, shards(): lax.dynamic_slice_in_dim(q3, rep_index * own_rows + row_start, rows, axis=1)  3.49 us
    dynamic_slice x1, local copies, waits for them, and re-layouts, shards(): lax.dynamic_slice_in_dim(t_l, sources[k] * features, features, axis=1)  2.64 us
  transfers between devices with their start and end apart: 15, of which 4 were waited for; matrix products, arithmetic and copies ran while one was open for 41% of the time, Pallas kernels for 0%

profile of v8, /device:TPU:0, one launch (start us, length us, event | category | flops | bytes accessed | tf_op | source)
XLA Modules:
  0.0 98.5 jit_solution(904418500659143336)
XLA Ops:
  0.0 0.7 copy-done
  0.7 0.6 gather_fusion
  1.2 0.1 reshape.297
  1.4 1.0 constant_dynamic-slice_fusion.2
  2.3 0.0 copy-start.2
  2.4 0.6 gather_fusion.1
  2.9 0.9 multiply_convert_fusion.2
  3.8 0.7 slice_bitcast_fusion.11
  4.5 5.1 %collective-permute-start.2 = (bf16[6,8,1024]{2,1,0:T(8,128)(2,1)}, bf16[6,8,1024]{2,1,0:T(8,128)(2,1)}, u32[]{:S(2)}, u32[]{:S(2)}) collective-permute-start(bf16[6,8,1024]{2,1,0:T(8,128)(2,1)} %get-tuple-element.24), channel_id=1, source_target_pairs={{0,12},{4,0},{8,4},{12,8},{1,13},{5,1},{9,5},{13,9},{2,14},{6,2},{... | collective-permute-start | bytes 294920 | tf_op jit(solution)/shard_map/ppermute | solution.py:88
  9.6 0.0 collective-permute-start.1
  9.6 1.0 %collective-permute-start = (bf16[6,8,1024]{2,1,0:T(8,128)(2,1)}, bf16[6,8,1024]{2,1,0:T(8,128)(2,1)}, u32[]{:S(2)}, u32[]{:S(2)}) collective-permute-start(bf16[6,8,1024]{2,1,0:T(8,128)(2,1)} %get-tuple-element.26), channel_id=1, source_target_pairs={{0,4},{4,8},{8,12},{12,0},{1,5},{5,9},{9,13},{13,1},{2,6},{6,10},{... | collective-permute-start | bytes 294920 | tf_op jit(solution)/shard_map/ppermute | solution.py:88
  10.6 0.1 reshape.298
  10.7 1.2 %constant_dynamic-slice_fusion.1 = bf16[16,24,1024]{2,1,0:T(8,128)(2,1)S(1)} fusion(bf16[16,128,1024]{2,1,0:T(8,128)(2,1)} %bitcast.119, s32[]{:T(128)S(6)} %select_n.272), kind=kLoop, calls=%fused_computation.76 | loop fusion | bytes 1572868 | tf_op jit(solution)/shard_map/dynamic_slice | solution.py:75
  11.9 0.1 broadcast_in_dim.60
  12.0 0.6 gather_fusion.3
  12.7 0.4 multiply_convert_fusion.1
  13.1 0.9 slice_bitcast_fusion.7
  14.0 2.8 %collective-permute-start.7 = (bf16[6,24,1024]{2,1,0:T(8,128)(2,1)}, bf16[6,24,1024]{2,1,0:T(8,128)(2,1)}, u32[]{:S(2)}, u32[]{:S(2)}) collective-permute-start(bf16[6,24,1024]{2,1,0:T(8,128)(2,1)} %get-tuple-element.20), channel_id=1, source_target_pairs={{0,12},{4,0},{8,4},{12,8},{1,13},{5,1},{9,5},{13,9},{2,14},{6,2},{... | collective-permute-start | bytes 884744 | tf_op jit(solution)/shard_map/ppermute | solution.py:88
  16.8 1.1 %collective-permute-start.6 = (bf16[6,24,1024]{2,1,0:T(8,128)(2,1)}, bf16[6,24,1024]{2,1,0:T(8,128)(2,1)}, u32[]{:S(2)}, u32[]{:S(2)}) collective-permute-start(bf16[6,24,1024]{2,1,0:T(8,128)(2,1)} %get-tuple-element.21), channel_id=1, source_target_pairs={{0,8},{4,12},{8,0},{12,4},{1,9},{5,13},{9,1},{13,5},{2,10},{6,14},... | collective-permute-start | bytes 884744 | tf_op jit(solution)/shard_map/ppermute | solution.py:88
  18.0 0.7 fusion.42
  21.2 0.6 fusion.41
  21.8 1.3 %constant_dynamic-slice_fusion = bf16[16,32,1024]{2,1,0:T(8,128)(2,1)S(1)} fusion(bf16[16,128,1024]{2,1,0:T(8,128)(2,1)} %bitcast.120, s32[]{:T(128)S(6)} %select_n.277), kind=kLoop, calls=%fused_computation.74 | loop fusion | bytes 2097156 | tf_op jit(solution)/shard_map/dynamic_slice | solution.py:75
  23.1 0.1 broadcast_in_dim.64
  23.2 0.6 gather_fusion.5
  23.9 0.6 multiply_convert_fusion
  24.4 2.6 %dynamic-slice_bitcast_fusion.3 = (bf16[512,1024]{1,0:T(8,128)(2,1)S(1)}, bf16[512,1024]{1,0:T(8,128)(2,1)S(1)}, bf16[512,1024]{1,0:T(8,128)(2,1)S(1)}, bf16[512,1024]{1,0:T(8,128)(2,1)S(1)}) fusion(bf16[512,1,4096]{2,0,1:T(8,128)(2,1)} %param.8, s32[]{:T(128)S(6)} %select_n.251, s32[]{:T(128)S(6)} %select_n.252, s32[]{:T(128)S(6)} %select_n.254, ...), kind=kLoop, calls=%fused_computation.36 | loop fusion | bytes 8388624 | tf_op jit(solution)/shard_map/dynamic_slice | solution.py:52
  27.1 0.0 copy-start.4
  27.1 0.0 copy-start.5
  27.1 13.4 %fusion.6 = bf16[640,4096]{1,0:T(8,128)(2,1)} fusion(bf16[512,1024]{1,0:T(8,128)(2,1)S(1)} %get-tuple-element.13, bf16[512,1024]{1,0:T(8,128)(2,1)S(1)} %get-tuple-element.14, bf16[512,1024]{1,0:T(8,128)(2,1)S(1)} %get-tuple-element.12, bf16[512,1024]{1,0:T(8,128)(2,1)S(1)} %get-tuple-element.11), kind=kLoop, calls=%fused_computation.14 | loop fusion | flops 34078720 | bytes 9437184 | tf_op jit(solution)/shard_map/concatenate | solution.py:53
  40.5 1.2 %fusion.37 = s32[24]{0:T(128)S(1)} fusion(s32[1,24]{1,0:T(1,128)S(1)} %copy-done.4, s32[1,24]{1,0:T(1,128)S(1)} %copy-done.5, s32[]{:T(128)} %bitcast.23, s32[]{:T(128)} %bitcast.22), kind=kLoop, calls=%fused_computation.115 | loop fusion | flops 720 | bytes 296 | tf_op jit(solution)/shard_map/concatenate | solution.py:99
  41.8 0.0 collective-permute-done.2
  41.8 0.1 collective-permute-start.5
  41.9 0.0 collective-permute-done.1
  41.9 0.0 collective-permute-done
  41.9 4.3 %fusion.21 = f32[6,8,5,128]{3,1,2,0:T(8,128)S(1)} fusion(bf16[5,128,4096,1]{2,1,0,3:T(8,128)(2,1)} %bitcast.109, bf16[6,8,1024]{2,1,0:T(8,128)(2,1)} %collective-permute-done.2, bf16[6,8,1024]{2,1,0:T(8,128)(2,1)} %collective-permute-done.1, bf16[6,8,1024]{2,1,0:T(8,128)(2,1)} %collective-permute-done, bf16[6,8,1024]{2,1,0:T(8,128)(2,1)S(1)} %get-tuple-element.23), kind=kOutput, calls=%fused_computation.39 | convolution fusion | flops 253231104 | bytes 5758976 | tf_op jit(solution)/shard_map/dot_general | solution.py:93
  46.2 0.7 gather_fusion.2
  46.9 1.6 %collective-permute-start.3 = (f32[2,6,8,128]{3,2,1,0:T(8,128)S(1)}, f32[2,6,8,128]{3,2,1,0:T(8,128)S(1)}, u32[]{:S(2)}, u32[]{:S(2)}) collective-permute-start(f32[2,6,8,128]{3,2,1,0:T(8,128)S(1)} %dynamic-slice_bitcast_fusion.8), channel_id=1, source_target_pairs={{0,2},{2,0},{1,3},{3,1},{4,6},{6,4},{5,7},{7,5},{8,10},{10,8},{9,1... | collective-permute-start | bytes 147464 | tf_op jit(solution)/shard_map/ppermute | solution.py:26
  48.5 0.2 slice_bitcast_fusion.3
  48.7 3.8 %collective-permute-start.12 = (bf16[6,32,1024]{2,1,0:T(8,128)(2,1)S(1)}, bf16[6,32,1024]{2,1,0:T(8,128)(2,1)}, u32[]{:S(2)}, u32[]{:S(2)}) collective-permute-start(bf16[6,32,1024]{2,1,0:T(8,128)(2,1)S(1)} %get-tuple-element.16), channel_id=1, source_target_pairs={{0,12},{4,0},{8,4},{12,8},{1,13},{5,1},{9,5},{13,9},{2,14},{6,2},{... | collective-permute-start | bytes 1179656 | tf_op jit(solution)/shard_map/ppermute | solution.py:88
  52.5 0.0 collective-permute-done.3
  52.5 0.4 collective-permute-start.11
  52.9 0.0 collective-permute-done.7
  52.9 2.8 %collective-permute-start.10 = (bf16[6,32,1024]{2,1,0:T(8,128)(2,1)S(1)}, bf16[6,32,1024]{2,1,0:T(8,128)(2,1)}, u32[]{:S(2)}, u32[]{:S(2)}) collective-permute-start(bf16[6,32,1024]{2,1,0:T(8,128)(2,1)S(1)} %get-tuple-element.18), channel_id=1, source_target_pairs={{0,4},{4,8},{8,12},{12,0},{1,5},{5,9},{9,13},{13,1},{2,6},{6,10},{... | collective-permute-start | bytes 1179656 | tf_op jit(solution)/shard_map/ppermute | solution.py:88
  55.7 0.0 collective-permute-done.6
  55.7 0.0 collective-permute-start.4
  55.7 0.0 collective-permute-done.5
  55.7 4.6 %fusion.14 = f32[6,24,5,128]{3,1,2,0:T(8,128)S(1)} fusion(bf16[5,128,4096,1]{2,1,0,3:T(8,128)(2,1)} %bitcast.110, bf16[6,24,1024]{2,1,0:T(8,128)(2,1)} %collective-permute-done.7, bf16[6,24,1024]{2,1,0:T(8,128)(2,1)} %collective-permute-done.6, bf16[6,24,1024]{2,1,0:T(8,128)(2,1)} %collective-permute-done.5, bf16[6,24,1024]{2,1,0:T(8,128)(2,1)S(1)} %get-tuple-element.19), kind=kOutput, calls=%fused_computation.26 | convolution fusion | flops 759693312 | bytes 6791168 | tf_op jit(solution)/shard_map/dot_general | solution.py:93
  60.3 0.7 gather_fusion.4
  61.1 1.6 %collective-permute-start.8 = (f32[2,6,24,128]{3,2,1,0:T(8,128)S(1)}, f32[2,6,24,128]{3,2,1,0:T(8,128)S(1)}, u32[]{:S(2)}, u32[]{:S(2)}) collective-permute-start(f32[2,6,24,128]{3,2,1,0:T(8,128)S(1)} %dynamic-slice_bitcast_fusion.5), channel_id=1, source_target_pairs={{0,2},{2,0},{1,3},{3,1},{4,6},{6,4},{5,7},{7,5},{8,10},{10,8},{9,1... | collective-permute-start | bytes 442376 | tf_op jit(solution)/shard_map/ppermute | solution.py:26
  62.7 0.0 collective-permute-done.4
  62.7 4.7 %collective-permute-done.8 = f32[2,6,24,128]{3,2,1,0:T(8,128)S(1)} collective-permute-done((f32[2,6,24,128]{3,2,1,0:T(8,128)S(1)}, f32[2,6,24,128]{3,2,1,0:T(8,128)S(1)}, u32[]{:S(2)}, u32[]{:S(2)}) %collective-permute-start.8) | collective-permute-done | bytes 147488 | tf_op jit(solution)/shard_map/ppermute | solution.py:26
  67.4 0.1 collective-permute-start.9
  67.5 0.0 collective-permute-done.12
  67.5 17.6 %collective-permute-done.11 = bf16[6,32,1024]{2,1,0:T(8,128)(2,1)} collective-permute-done((bf16[6,32,1024]{2,1,0:T(8,128)(2,1)S(1)}, bf16[6,32,1024]{2,1,0:T(8,128)(2,1)}, u32[]{:S(2)}, u32[]{:S(2)}) %collective-permute-start.11) | collective-permute-done | bytes 393248 | tf_op jit(solution)/shard_map/ppermute | solution.py:88
  85.0 0.0 collective-permute-done.10
  85.1 4.7 %fusion.7 = f32[6,32,5,128]{3,1,2,0:T(8,128)S(1)} fusion(bf16[5,128,4096,1]{2,1,0,3:T(8,128)(2,1)} %bitcast.111, bf16[6,32,1024]{2,1,0:T(8,128)(2,1)} %collective-permute-done.12, bf16[6,32,1024]{2,1,0:T(8,128)(2,1)} %collective-permute-done.11, bf16[6,32,1024]{2,1,0:T(8,128)(2,1)} %collective-permute-done.10, bf16[6,32,1024]{2,1,0:T(8,128)(2,1)S(1)} %get-tuple-element.15), kind=kOutput, calls=%fused_computation.18 | convolution fusion | flops 1012924416 | bytes 7307264 | tf_op jit(solution)/shard_map/dot_general | solution.py:93
  89.8 0.7 gather_fusion.6
  90.6 1.5 %collective-permute-start.13 = (f32[2,6,32,128]{3,2,1,0:T(8,128)S(1)}, f32[2,6,32,128]{3,2,1,0:T(8,128)S(1)}, u32[]{:S(2)}, u32[]{:S(2)}) collective-permute-start(f32[2,6,32,128]{3,2,1,0:T(8,128)S(1)} %dynamic-slice_bitcast_fusion.4), channel_id=1, source_target_pairs={{0,2},{2,0},{1,3},{3,1},{4,6},{6,4},{5,7},{7,5},{8,10},{10,8},{9,1... | collective-permute-start | bytes 589832 | tf_op jit(solution)/shard_map/ppermute | solution.py:26
  92.1 0.0 collective-permute-done.9
  92.1 4.2 %collective-permute-done.13 = f32[2,6,32,128]{3,2,1,0:T(8,128)S(1)} collective-permute-done((f32[2,6,32,128]{3,2,1,0:T(8,128)S(1)}, f32[2,6,32,128]{3,2,1,0:T(8,128)S(1)}, u32[]{:S(2)}, u32[]{:S(2)}) %collective-permute-start.13) | collective-permute-done | bytes 196640 | tf_op jit(solution)/shard_map/ppermute | solution.py:26
  96.4 0.1 collective-permute-start.14
  96.5 1.3 %collective-permute-done.14 = f32[6,32,128]{2,1,0:T(8,128)S(1)} collective-permute-done((f32[6,32,128]{2,1,0:T(8,128)S(1)}, f32[6,32,128]{2,1,0:T(8,128)S(1)}, u32[]{:S(2)}, u32[]{:S(2)}) %collective-permute-start.14) | collective-permute-done | bytes 98336 | tf_op jit(solution)/shard_map/ppermute | solution.py:106
  97.7 0.0 copy-start.1
  97.8 0.7 copy-done.1
  (37 shorter events, 0.4 us)
Async XLA Ops:
  0.0 0.7 copy-start
  2.3 10.3 %copy-start.2 = (f32[1,1024]{1,0:T(1,128)S(1)}, f32[1,1024]{1,0:T(1,128)}, u32[]{:S(2)}) copy-start(f32[1,1024]{1,0:T(1,128)} %param.9) | copy-start | bytes 12292
  4.5 37.3 %collective-permute-start.2 = (bf16[6,8,1024]{2,1,0:T(8,128)(2,1)}, bf16[6,8,1024]{2,1,0:T(8,128)(2,1)}, u32[]{:S(2)}, u32[]{:S(2)}) collective-permute-start(bf16[6,8,1024]{2,1,0:T(8,128)(2,1)} %get-tuple-element.24), channel_id=1, source_target_pairs={{0,12},{4,0},{8,4},{12,8},{1,13},{5,1},{9,5},{13,9},{2,14},{6,2},{... | collective-permute-start | bytes 294920 | tf_op jit(solution)/shard_map/ppermute | solution.py:88
  9.6 32.3 %collective-permute-start.1 = (bf16[6,8,1024]{2,1,0:T(8,128)(2,1)}, bf16[6,8,1024]{2,1,0:T(8,128)(2,1)}, u32[]{:S(2)}, u32[]{:S(2)}) collective-permute-start(bf16[6,8,1024]{2,1,0:T(8,128)(2,1)} %get-tuple-element.25), channel_id=1, source_target_pairs={{0,8},{4,12},{8,0},{12,4},{1,9},{5,13},{9,1},{13,5},{2,10},{6,14},... | collective-permute-start | bytes 294920 | tf_op jit(solution)/shard_map/ppermute | solution.py:88
  9.6 32.3 %collective-permute-start = (bf16[6,8,1024]{2,1,0:T(8,128)(2,1)}, bf16[6,8,1024]{2,1,0:T(8,128)(2,1)}, u32[]{:S(2)}, u32[]{:S(2)}) collective-permute-start(bf16[6,8,1024]{2,1,0:T(8,128)(2,1)} %get-tuple-element.26), channel_id=1, source_target_pairs={{0,4},{4,8},{8,12},{12,0},{1,5},{5,9},{9,13},{13,1},{2,6},{6,10},{... | collective-permute-start | bytes 294920 | tf_op jit(solution)/shard_map/ppermute | solution.py:88
  12.0 9.1 %copy-start.3 = (s32[1,2]{1,0:T(1,128)S(1)}, s32[1,2]{1,0:T(1,128)}, u32[]{:S(2)}) copy-start(s32[1,2]{1,0:T(1,128)} %param.13) | copy-start | bytes 28
  14.0 38.9 %collective-permute-start.7 = (bf16[6,24,1024]{2,1,0:T(8,128)(2,1)}, bf16[6,24,1024]{2,1,0:T(8,128)(2,1)}, u32[]{:S(2)}, u32[]{:S(2)}) collective-permute-start(bf16[6,24,1024]{2,1,0:T(8,128)(2,1)} %get-tuple-element.20), channel_id=1, source_target_pairs={{0,12},{4,0},{8,4},{12,8},{1,13},{5,1},{9,5},{13,9},{2,14},{6,2},{... | collective-permute-start | bytes 884744 | tf_op jit(solution)/shard_map/ppermute | solution.py:88
  16.8 38.9 %collective-permute-start.6 = (bf16[6,24,1024]{2,1,0:T(8,128)(2,1)}, bf16[6,24,1024]{2,1,0:T(8,128)(2,1)}, u32[]{:S(2)}, u32[]{:S(2)}) collective-permute-start(bf16[6,24,1024]{2,1,0:T(8,128)(2,1)} %get-tuple-element.21), channel_id=1, source_target_pairs={{0,8},{4,12},{8,0},{12,4},{1,9},{5,13},{9,1},{13,5},{2,10},{6,14},... | collective-permute-start | bytes 884744 | tf_op jit(solution)/shard_map/ppermute | solution.py:88
  27.1 13.4 %copy-start.4 = (s32[1,24]{1,0:T(1,128)S(1)}, s32[1,24]{1,0:T(1,128)}, u32[]{:S(2)}) copy-start(s32[1,24]{1,0:T(1,128)} %param.12) | copy-start | bytes 292
  27.1 13.4 %copy-start.5 = (s32[1,24]{1,0:T(1,128)S(1)}, s32[1,24]{1,0:T(1,128)}, u32[]{:S(2)}) copy-start(s32[1,24]{1,0:T(1,128)} %param.11) | copy-start | bytes 292
  41.8 13.9 %collective-permute-start.5 = (bf16[6,24,1024]{2,1,0:T(8,128)(2,1)}, bf16[6,24,1024]{2,1,0:T(8,128)(2,1)}, u32[]{:S(2)}, u32[]{:S(2)}) collective-permute-start(bf16[6,24,1024]{2,1,0:T(8,128)(2,1)} %get-tuple-element.22), channel_id=1, source_target_pairs={{0,4},{4,8},{8,12},{12,0},{1,5},{5,9},{9,13},{13,1},{2,6},{6,10},{... | collective-permute-start | bytes 884744 | tf_op jit(solution)/shard_map/ppermute | solution.py:88
  46.9 5.6 %collective-permute-start.3 = (f32[2,6,8,128]{3,2,1,0:T(8,128)S(1)}, f32[2,6,8,128]{3,2,1,0:T(8,128)S(1)}, u32[]{:S(2)}, u32[]{:S(2)}) collective-permute-start(f32[2,6,8,128]{3,2,1,0:T(8,128)S(1)} %dynamic-slice_bitcast_fusion.8), channel_id=1, source_target_pairs={{0,2},{2,0},{1,3},{3,1},{4,6},{6,4},{5,7},{7,5},{8,10},{10,8},{9,1... | collective-permute-start | bytes 147464 | tf_op jit(solution)/shard_map/ppermute | solution.py:26
  48.7 18.8 %collective-permute-start.12 = (bf16[6,32,1024]{2,1,0:T(8,128)(2,1)S(1)}, bf16[6,32,1024]{2,1,0:T(8,128)(2,1)}, u32[]{:S(2)}, u32[]{:S(2)}) collective-permute-start(bf16[6,32,1024]{2,1,0:T(8,128)(2,1)S(1)} %get-tuple-element.16), channel_id=1, source_target_pairs={{0,12},{4,0},{8,4},{12,8},{1,13},{5,1},{9,5},{13,9},{2,14},{6,2},{... | collective-permute-start | bytes 1179656 | tf_op jit(solution)/shard_map/ppermute | solution.py:88
  52.5 32.5 %collective-permute-start.11 = (bf16[6,32,1024]{2,1,0:T(8,128)(2,1)S(1)}, bf16[6,32,1024]{2,1,0:T(8,128)(2,1)}, u32[]{:S(2)}, u32[]{:S(2)}) collective-permute-start(bf16[6,32,1024]{2,1,0:T(8,128)(2,1)S(1)} %get-tuple-element.17), channel_id=1, source_target_pairs={{0,8},{4,12},{8,0},{12,4},{1,9},{5,13},{9,1},{13,5},{2,10},{6,14},... | collective-permute-start | bytes 1179656 | tf_op jit(solution)/shard_map/ppermute | solution.py:88
  52.9 32.1 %collective-permute-start.10 = (bf16[6,32,1024]{2,1,0:T(8,128)(2,1)S(1)}, bf16[6,32,1024]{2,1,0:T(8,128)(2,1)}, u32[]{:S(2)}, u32[]{:S(2)}) collective-permute-start(bf16[6,32,1024]{2,1,0:T(8,128)(2,1)S(1)} %get-tuple-element.18), channel_id=1, source_target_pairs={{0,4},{4,8},{8,12},{12,0},{1,5},{5,9},{9,13},{13,1},{2,6},{6,10},{... | collective-permute-start | bytes 1179656 | tf_op jit(solution)/shard_map/ppermute | solution.py:88
  55.7 7.0 %collective-permute-start.4 = (f32[6,8,128]{2,1,0:T(8,128)S(1)}, f32[6,8,128]{2,1,0:T(8,128)S(1)}, u32[]{:S(2)}, u32[]{:S(2)}) collective-permute-start(f32[6,8,128]{2,1,0:T(8,128)S(1)} %dynamic-slice_bitcast_fusion.9), channel_id=1, source_target_pairs={{0,1},{1,0},{2,3},{3,2},{4,5},{5,4},{6,7},{7,6},{8,9},{9,8},{10,11... | collective-permute-start | bytes 73736 | tf_op jit(solution)/shard_map/ppermute | solution.py:106
  61.1 6.3 %collective-permute-start.8 = (f32[2,6,24,128]{3,2,1,0:T(8,128)S(1)}, f32[2,6,24,128]{3,2,1,0:T(8,128)S(1)}, u32[]{:S(2)}, u32[]{:S(2)}) collective-permute-start(f32[2,6,24,128]{3,2,1,0:T(8,128)S(1)} %dynamic-slice_bitcast_fusion.5), channel_id=1, source_target_pairs={{0,2},{2,0},{1,3},{3,1},{4,6},{6,4},{5,7},{7,5},{8,10},{10,8},{9,1... | collective-permute-start | bytes 442376 | tf_op jit(solution)/shard_map/ppermute | solution.py:26
  67.4 24.7 %collective-permute-start.9 = (f32[6,24,128]{2,1,0:T(8,128)S(1)}, f32[6,24,128]{2,1,0:T(8,128)S(1)}, u32[]{:S(2)}, u32[]{:S(2)}) collective-permute-start(f32[6,24,128]{2,1,0:T(8,128)S(1)} %dynamic-slice_bitcast_fusion.7), channel_id=1, source_target_pairs={{0,1},{1,0},{2,3},{3,2},{4,5},{5,4},{6,7},{7,6},{8,9},{9,8},{10,11... | collective-permute-start | bytes 221192 | tf_op jit(solution)/shard_map/ppermute | solution.py:106
  90.6 5.7 %collective-permute-start.13 = (f32[2,6,32,128]{3,2,1,0:T(8,128)S(1)}, f32[2,6,32,128]{3,2,1,0:T(8,128)S(1)}, u32[]{:S(2)}, u32[]{:S(2)}) collective-permute-start(f32[2,6,32,128]{3,2,1,0:T(8,128)S(1)} %dynamic-slice_bitcast_fusion.4), channel_id=1, source_target_pairs={{0,2},{2,0},{1,3},{3,1},{4,6},{6,4},{5,7},{7,5},{8,10},{10,8},{9,1... | collective-permute-start | bytes 589832 | tf_op jit(solution)/shard_map/ppermute | solution.py:26
  96.4 1.4 %collective-permute-start.14 = (f32[6,32,128]{2,1,0:T(8,128)S(1)}, f32[6,32,128]{2,1,0:T(8,128)S(1)}, u32[]{:S(2)}, u32[]{:S(2)}) collective-permute-start(f32[6,32,128]{2,1,0:T(8,128)S(1)} %dynamic-slice_bitcast_fusion.6), channel_id=1, source_target_pairs={{0,1},{1,0},{2,3},{3,2},{4,5},{5,4},{6,7},{7,6},{8,9},{9,8},{10,11... | collective-permute-start | bytes 294920 | tf_op jit(solution)/shard_map/ppermute | solution.py:106
  97.7 0.7 copy-start.1

commit v9 on v8

--- a/solution.py
+++ b/solution.py
@@ -51,7 +51,6 @@
         for k in range(n_span):
             t_parts.append(lax.dynamic_slice_in_dim(t_l, sources[k] * features, features, axis=1))
     train = jnp.concatenate(t_parts, axis=1)
-    train = jnp.concatenate([train, jnp.zeros((BLOCK, train.shape[1]), train.dtype)], axis=0)
 
     score_scale = 1.0 / math.sqrt(l_dev * n_layer * d_full)
     slot_row = pair_slot[0]
@@ -59,7 +58,6 @@
     counts = pair_count[0]
     slots = jnp.arange(pmax, dtype=jnp.int32)
     live = (slots % phalf) < counts[slots // phalf]
-    pick_train = jnp.where(live, train_row, tb_dev)
 
     out_buf = jnp.zeros((per_dev, BLOCK, BLOCK), jnp.float32)
     gate = None
@@ -73,7 +71,7 @@
         for layer in range(l_dev):
             q3 = queries[:, layer, :].reshape(n_query // BLOCK, BLOCK, features)
             q3 = lax.dynamic_slice_in_dim(q3, rep_index * own_rows + row_start, rows, axis=1)
-            got = jnp.take(q3, block_ids, axis=0).reshape(n_span, cap, rows, features)
+            got = jnp.take(q3, block_ids, axis=0, mode="clip").reshape(n_span, cap, rows, features)
             sent.append((got.astype(jnp.float32) * precond[layer]).astype(jnp.bfloat16))
         row_start += rows
         prev_sent = sent
@@ -95,8 +93,9 @@
             train,
             (((1,), (1,)), ((), ())),
             preferred_element_type=jnp.float32,
-        ).reshape(cap, rows, tb_dev + 1, BLOCK)
-        partial = combos.at[slot_row, :, pick_train, :].get(mode="promise_in_bounds") * score_scale
+        ).reshape(cap, rows, tb_dev, BLOCK)
+        partial = combos.at[slot_row, :, train_row, :].get(mode="promise_in_bounds") * score_scale
+        partial = jnp.where(live[:, None, None], partial, 0.0)
         partial = partial.reshape(n_layer, n_rep, per_dev, rows, BLOCK)
         partial = ring_reduce_scatter(partial, "layer", 0)
         got_rows = [lax.dynamic_index_in_dim(partial, rep_index, axis=0, keepdims=False)]

time: 99 us -> 89.1 us (0.90)
  the two profiles are of different devices: /device:TPU:0 before, /device:TPU:11 now
where the time goes in v9:
time: 89.1 us; the launch traced here: 88.7 us
  waiting for transfers between devices  41.8 us (47%)
  local copies, waits for them, and re-layouts  17 us (19%)
  starting transfers between devices  13.7 us (15%)
  matrix products  9.42 us (11%)
  other arithmetic  3.92 us (4%)
  between operations  2.85 us (3%)
    ppermute x9, waiting for transfers between devices, shards(): piece = lax.ppermute(piece, 'span', perm)  28.7 us
    ppermute x3, waiting for transfers between devices, ring_reduce_scatter(): recv = lax.ppermute(acc, axis_name, perm)  12.2 us
    dot_general x3, matrix products, shards(): lax.dot_general(arrived, train, (((1,), (1,)), ((), ())), preferred_eleme...  9.42 us
    ppermute x9, starting transfers between devices, shards(): piece = lax.ppermute(piece, 'span', perm)  7.25 us
    ppermute x3, starting transfers between devices, shards(): got_rows.append(lax.ppermute(send, 'rep', perm))  5.51 us
    dynamic_slice x1, local copies, waits for them, and re-layouts, shards(): lax.dynamic_slice_in_dim(t_l, sources[k] * features, features, axis=1)  3.91 us
    dynamic_slice x3, local copies, waits for them, and re-layouts, shards(): lax.dynamic_slice_in_dim(q3, rep_index * own_rows + row_start, rows, axis=1)  3.48 us
    concatenate x3, local copies, waits for them, and re-layouts, shards(): arrived = jnp.concatenate(pieces, axis=-1).reshape(cap * rows, -1)  2.11 us
  transfers between devices with their start and end apart: 15, of which 9 were waited for; matrix products, arithmetic and copies ran while one was open for 29% of the time, Pallas kernels for 0%

profile of v9, /device:TPU:11, one launch (start us, length us, event | category | flops | bytes accessed | tf_op | source)
XLA Modules:
  0.0 88.7 jit_solution(6907456083685587074)
XLA Ops:
  0.0 0.7 copy-done
  0.7 0.6 gather_fusion
  1.2 0.1 reshape.305
  1.3 1.0 %constant_dynamic-slice_fusion.6 = bf16[16,8,1024]{2,1,0:T(8,128)(2,1)S(1)} fusion(bf16[16,128,1024]{2,1,0:T(8,128)(2,1)} %bitcast.119, s32[]{:T(128)S(6)} %select_n.209), kind=kLoop, calls=%fused_computation.77 | loop fusion | bytes 524292 | tf_op jit(solution)/shard_map/dynamic_slice | solution.py:73
  2.3 0.0 copy-start.6
  2.3 0.6 gather_fusion.1
  2.9 0.8 fusion.16
  3.7 1.3 %collective-permute-start = (bf16[6,8,1024]{2,1,0:T(8,128)(2,1)S(1)}, bf16[6,8,1024]{2,1,0:T(8,128)(2,1)}, u32[]{:S(2)}, u32[]{:S(2)}) collective-permute-start(bf16[6,8,1024]{2,1,0:T(8,128)(2,1)S(1)} %get-tuple-element.26), channel_id=1, source_target_pairs={{0,4},{4,8},{8,12},{12,0},{1,5},{5,9},{9,13},{13,1},{2,6},{6,10},{... | collective-permute-start | bytes 294920 | tf_op jit(solution)/shard_map/ppermute | solution.py:86
  5.1 1.1 %collective-permute-start.1 = (bf16[6,8,1024]{2,1,0:T(8,128)(2,1)S(1)}, bf16[6,8,1024]{2,1,0:T(8,128)(2,1)}, u32[]{:S(2)}, u32[]{:S(2)}) collective-permute-start(bf16[6,8,1024]{2,1,0:T(8,128)(2,1)S(1)} %get-tuple-element.25), channel_id=1, source_target_pairs={{0,8},{4,12},{8,0},{12,4},{1,9},{5,13},{9,1},{13,5},{2,10},{6,14},... | collective-permute-start | bytes 294920 | tf_op jit(solution)/shard_map/ppermute | solution.py:86
  6.2 1.4 %collective-permute-start.2 = (bf16[6,8,1024]{2,1,0:T(8,128)(2,1)S(1)}, bf16[6,8,1024]{2,1,0:T(8,128)(2,1)}, u32[]{:S(2)}, u32[]{:S(2)}) collective-permute-start(bf16[6,8,1024]{2,1,0:T(8,128)(2,1)S(1)} %get-tuple-element.24), channel_id=1, source_target_pairs={{0,12},{4,0},{8,4},{12,8},{1,13},{5,1},{9,5},{13,9},{2,14},{6,2},{... | collective-permute-start | bytes 294920 | tf_op jit(solution)/shard_map/ppermute | solution.py:86
  7.5 1.2 %constant_dynamic-slice_fusion.1 = bf16[16,24,1024]{2,1,0:T(8,128)(2,1)S(1)} fusion(bf16[16,128,1024]{2,1,0:T(8,128)(2,1)} %bitcast.120, s32[]{:T(128)S(6)} %select_n.230), kind=kLoop, calls=%fused_computation.71 | loop fusion | bytes 1572868 | tf_op jit(solution)/shard_map/dynamic_slice | solution.py:73
  8.7 0.6 gather_fusion.3
  9.4 0.3 fusion.1
  9.7 1.0 %slice_bitcast_fusion.7 = (bf16[6,24,1024]{2,1,0:T(8,128)(2,1)}, bf16[6,24,1024]{2,1,0:T(8,128)(2,1)}, bf16[6,24,1024]{2,1,0:T(8,128)(2,1)}, bf16[6,24,1024]{2,1,0:T(8,128)(2,1)}) fusion(bf16[4,6,24,1024]{3,2,1,0:T(8,128)(2,1)S(1)} %fusion.1), kind=kLoop, calls=%fused_computation.45 | loop fusion | bytes 2359296 | tf_op jit(solution)/shard_map/concatenate | solution.py:90
  10.7 0.1 collective-permute-start.5
  10.8 3.1 %collective-permute-start.6 = (bf16[6,24,1024]{2,1,0:T(8,128)(2,1)}, bf16[6,24,1024]{2,1,0:T(8,128)(2,1)}, u32[]{:S(2)}, u32[]{:S(2)}) collective-permute-start(bf16[6,24,1024]{2,1,0:T(8,128)(2,1)} %get-tuple-element.21), channel_id=1, source_target_pairs={{0,8},{4,12},{8,0},{12,4},{1,9},{5,13},{9,1},{13,5},{2,10},{6,14},... | collective-permute-start | bytes 884744 | tf_op jit(solution)/shard_map/ppermute | solution.py:86
  13.9 0.6 fusion.39
  16.9 1.3 %constant_dynamic-slice_fusion = bf16[16,32,1024]{2,1,0:T(8,128)(2,1)S(1)} fusion(bf16[16,128,1024]{2,1,0:T(8,128)(2,1)} %bitcast.121, s32[]{:T(128)S(6)} %select_n.234), kind=kLoop, calls=%fused_computation.68 | loop fusion | bytes 2097156 | tf_op jit(solution)/shard_map/dynamic_slice | solution.py:73
  18.3 0.0 copy-start.7
  18.3 0.0 copy-start.8
  18.3 0.6 gather_fusion.5
  19.0 0.4 fusion
  19.4 0.6 fusion.38
  20.0 1.3 %fusion.25 = s32[24]{0:T(128)S(1)} fusion(s32[]{:T(128)} %bitcast.1, s32[]{:T(128)} %bitcast), kind=kLoop, calls=%fused_computation.99 | loop fusion | flops 312 | bytes 104 | tf_op jit(solution)/shard_map/gather | solution.py:60
  21.3 0.1 gather.32
  21.4 0.7 fusion.34
  22.1 3.9 %constant_dynamic-slice_fusion.5 = (bf16[512,1,1024]{2,0,1:T(8,128)(2,1)S(1)}, bf16[512,1,1024]{2,0,1:T(8,128)(2,1)}, bf16[512,1,1024]{2,0,1:T(8,128)(2,1)}, bf16[512,1,1024]{2,0,1:T(8,128)(2,1)}) fusion(bf16[512,1,4096]{2,0,1:T(8,128)(2,1)} %param.8, s32[]{:T(128)S(6)} %select_n.213, s32[]{:T(128)S(6)} %select_n.214, s32[]{:T(128)S(6)} %select_n.216, ...), kind=kLoop, calls=%fused_computation.76 | loop fusion | bytes 8388624 | tf_op jit(solution)/shard_map/dynamic_slice | solution.py:52
  26.0 0.0 collective-permute-done
  26.0 0.0 collective-permute-start.7
  26.0 0.0 collective-permute-done.1
  26.0 2.4 %collective-permute-done.2 = bf16[6,8,1024]{2,1,0:T(8,128)(2,1)} collective-permute-done((bf16[6,8,1024]{2,1,0:T(8,128)(2,1)S(1)}, bf16[6,8,1024]{2,1,0:T(8,128)(2,1)}, u32[]{:S(2)}, u32[]{:S(2)}) %collective-permute-start.2) | collective-permute-done | bytes 98336 | tf_op jit(solution)/shard_map/ppermute | solution.py:86
  28.4 3.0 %fusion.17 = f32[6,8,4,128]{3,1,2,0:T(8,128)S(1)} fusion(bf16[6,8,1024]{2,1,0:T(8,128)(2,1)} %collective-permute-done.2, bf16[6,8,1024]{2,1,0:T(8,128)(2,1)} %collective-permute-done.1, bf16[6,8,1024]{2,1,0:T(8,128)(2,1)} %collective-permute-done, bf16[6,8,1024]{2,1,0:T(8,128)(2,1)S(1)} %get-tuple-element.23, bf16[4,128,1024]{2,1,0:T(8,128)(2,1)} %bitcast.113, ...), kind=kOutput, calls=%fused_computation.31 | convolution fusion | flops 219676672 | bytes 4685824 | tf_op jit(solution)/shard_map/dot_general | solution.py:91
  31.4 0.7 gather_fusion.2
  32.2 0.1 broadcast_select_fusion.2
  32.3 0.3 collective-permute-start.3
  32.6 1.0 %slice_bitcast_fusion.3 = (bf16[6,32,1024]{2,1,0:T(8,128)(2,1)S(1)}, bf16[6,32,1024]{2,1,0:T(8,128)(2,1)S(1)}, bf16[6,32,1024]{2,1,0:T(8,128)(2,1)}, bf16[6,32,1024]{2,1,0:T(8,128)(2,1)}) fusion(bf16[4,6,32,1024]{3,2,1,0:T(8,128)(2,1)S(1)} %fusion), kind=kLoop, calls=%fused_computation.41 | loop fusion | bytes 3145728 | tf_op jit(solution)/shard_map/concatenate | solution.py:90
  33.7 0.0 collective-permute-start.10
  33.7 2.0 %collective-permute-done.3 = f32[2,6,8,128]{3,2,1,0:T(8,128)S(1)} collective-permute-done((f32[2,6,8,128]{3,2,1,0:T(8,128)S(1)}, f32[2,6,8,128]{3,2,1,0:T(8,128)S(1)}, u32[]{:S(2)}, u32[]{:S(2)}) %collective-permute-start.3) | collective-permute-done | bytes 49184 | tf_op jit(solution)/shard_map/ppermute | solution.py:26
  35.7 0.0 collective-permute-start.11
  35.8 0.0 collective-permute-done.5
  35.8 0.3 collective-permute-start.12
  36.0 2.4 %collective-permute-done.6 = bf16[6,24,1024]{2,1,0:T(8,128)(2,1)} collective-permute-done((bf16[6,24,1024]{2,1,0:T(8,128)(2,1)}, bf16[6,24,1024]{2,1,0:T(8,128)(2,1)}, u32[]{:S(2)}, u32[]{:S(2)}) %collective-permute-start.6) | collective-permute-done | bytes 294944 | tf_op jit(solution)/shard_map/ppermute | solution.py:86
  38.4 2.6 %collective-permute-start.4 = (f32[6,8,128]{2,1,0:T(8,128)S(1)}, f32[6,8,128]{2,1,0:T(8,128)S(1)}, u32[]{:S(2)}, u32[]{:S(2)}) collective-permute-start(f32[6,8,128]{2,1,0:T(8,128)S(1)} %dynamic-slice_bitcast_fusion.5), channel_id=1, source_target_pairs={{0,1},{1,0},{2,3},{3,2},{4,5},{5,4},{6,7},{7,6},{8,9},{9,8},{10,11... | collective-permute-start | bytes 73736 | tf_op jit(solution)/shard_map/ppermute | solution.py:105
  41.0 17.0 %collective-permute-done.7 = bf16[6,24,1024]{2,1,0:T(8,128)(2,1)} collective-permute-done((bf16[6,24,1024]{2,1,0:T(8,128)(2,1)}, bf16[6,24,1024]{2,1,0:T(8,128)(2,1)}, u32[]{:S(2)}, u32[]{:S(2)}) %collective-permute-start.7) | collective-permute-done | bytes 294944 | tf_op jit(solution)/shard_map/ppermute | solution.py:86
  58.0 2.7 %fusion.9 = f32[6,24,4,128]{3,1,2,0:T(8,128)S(1)} fusion(bf16[6,24,1024]{2,1,0:T(8,128)(2,1)} %collective-permute-done.7, bf16[6,24,1024]{2,1,0:T(8,128)(2,1)} %collective-permute-done.6, bf16[6,24,1024]{2,1,0:T(8,128)(2,1)} %collective-permute-done.5, bf16[6,24,1024]{2,1,0:T(8,128)(2,1)S(1)} %copy-done.5, bf16[4,128,1024]{2,1,0:T(8,128)(2,1)S(1)} %bitcast.115, ...), kind=kOutput, calls=%fused_computation.21 | convolution fusion | flops 625475584 | bytes 5668864 | tf_op jit(solution)/shard_map/dot_general | solution.py:91
  60.7 0.7 gather_fusion.4
  61.4 0.1 broadcast_select_fusion.1
  61.5 0.3 collective-permute-start.8
  61.9 0.0 collective-permute-done.4
  61.9 4.5 %collective-permute-done.8 = f32[2,6,24,128]{3,2,1,0:T(8,128)S(1)} collective-permute-done((f32[2,6,24,128]{3,2,1,0:T(8,128)S(1)}, f32[2,6,24,128]{3,2,1,0:T(8,128)S(1)}, u32[]{:S(2)}, u32[]{:S(2)}) %collective-permute-start.8) | collective-permute-done | bytes 147488 | tf_op jit(solution)/shard_map/ppermute | solution.py:26
  66.4 1.5 %collective-permute-start.9 = (f32[6,24,128]{2,1,0:T(8,128)S(1)}, f32[6,24,128]{2,1,0:T(8,128)S(1)}, u32[]{:S(2)}, u32[]{:S(2)}) collective-permute-start(f32[6,24,128]{2,1,0:T(8,128)S(1)} %dynamic-slice_bitcast_fusion.3), channel_id=1, source_target_pairs={{0,1},{1,0},{2,3},{3,2},{4,5},{5,4},{6,7},{7,6},{8,9},{9,8},{10,11... | collective-permute-start | bytes 221192 | tf_op jit(solution)/shard_map/ppermute | solution.py:105
  68.0 0.0 collective-permute-done.10
  68.0 4.1 %collective-permute-done.11 = bf16[6,32,1024]{2,1,0:T(8,128)(2,1)} collective-permute-done((bf16[6,32,1024]{2,1,0:T(8,128)(2,1)}, bf16[6,32,1024]{2,1,0:T(8,128)(2,1)}, u32[]{:S(2)}, u32[]{:S(2)}) %collective-permute-start.11) | collective-permute-done | bytes 393248 | tf_op jit(solution)/shard_map/ppermute | solution.py:86
  72.1 2.7 %collective-permute-done.12 = bf16[6,32,1024]{2,1,0:T(8,128)(2,1)} collective-permute-done((bf16[6,32,1024]{2,1,0:T(8,128)(2,1)S(1)}, bf16[6,32,1024]{2,1,0:T(8,128)(2,1)}, u32[]{:S(2)}, u32[]{:S(2)}) %collective-permute-start.12) | collective-permute-done | bytes 393248 | tf_op jit(solution)/shard_map/ppermute | solution.py:86
  74.8 3.8 %fusion.2 = f32[6,32,4,128]{3,1,2,0:T(8,128)S(1)} fusion(bf16[6,32,1024]{2,1,0:T(8,128)(2,1)} %collective-permute-done.12, bf16[6,32,1024]{2,1,0:T(8,128)(2,1)} %collective-permute-done.11, bf16[6,32,1024]{2,1,0:T(8,128)(2,1)} %collective-permute-done.10, bf16[6,32,1024]{2,1,0:T(8,128)(2,1)S(1)} %get-tuple-element.15, bf16[4,128,1024]{2,1,0:T(8,128)(2,1)} %bitcast.114, ...), kind=kOutput, calls=%fused_computation.13 | convolution fusion | flops 828375040 | bytes 6160384 | tf_op jit(solution)/shard_map/dot_general | solution.py:91
  78.6 0.7 gather_fusion.6
  79.3 0.1 broadcast_select_fusion
  79.5 0.3 collective-permute-start.13
  79.8 0.0 collective-permute-done.9
  79.8 5.7 %collective-permute-done.13 = f32[2,6,32,128]{3,2,1,0:T(8,128)S(1)} collective-permute-done((f32[2,6,32,128]{3,2,1,0:T(8,128)S(1)}, f32[2,6,32,128]{3,2,1,0:T(8,128)S(1)}, u32[]{:S(2)}, u32[]{:S(2)}) %collective-permute-start.13) | collective-permute-done | bytes 196640 | tf_op jit(solution)/shard_map/ppermute | solution.py:26
  85.6 1.4 %collective-permute-start.14 = (f32[6,32,128]{2,1,0:T(8,128)S(1)}, f32[6,32,128]{2,1,0:T(8,128)S(1)}, u32[]{:S(2)}, u32[]{:S(2)}) collective-permute-start(f32[6,32,128]{2,1,0:T(8,128)S(1)} %dynamic-slice_bitcast_fusion.2), channel_id=1, source_target_pairs={{0,1},{1,0},{2,3},{3,2},{4,5},{5,4},{6,7},{7,6},{8,9},{9,8},{10,11... | collective-permute-start | bytes 294920 | tf_op jit(solution)/shard_map/ppermute | solution.py:105
  87.0 0.9 %collective-permute-done.14 = f32[6,32,128]{2,1,0:T(8,128)S(1)} collective-permute-done((f32[6,32,128]{2,1,0:T(8,128)S(1)}, f32[6,32,128]{2,1,0:T(8,128)S(1)}, u32[]{:S(2)}, u32[]{:S(2)}) %collective-permute-start.14) | collective-permute-done | bytes 98336 | tf_op jit(solution)/shard_map/ppermute | solution.py:105
  87.9 0.0 copy-start.4
  88.0 0.7 copy-done.4
  (39 shorter events, 0.4 us)
Async XLA Ops:
  0.0 0.7 copy-start
  2.3 7.1 %copy-start.6 = (f32[1,1024]{1,0:T(1,128)S(1)}, f32[1,1024]{1,0:T(1,128)}, u32[]{:S(2)}) copy-start(f32[1,1024]{1,0:T(1,128)} %param.9) | copy-start | bytes 12292
  3.7 22.3 %collective-permute-start = (bf16[6,8,1024]{2,1,0:T(8,128)(2,1)S(1)}, bf16[6,8,1024]{2,1,0:T(8,128)(2,1)}, u32[]{:S(2)}, u32[]{:S(2)}) collective-permute-start(bf16[6,8,1024]{2,1,0:T(8,128)(2,1)S(1)} %get-tuple-element.26), channel_id=1, source_target_pairs={{0,4},{4,8},{8,12},{12,0},{1,5},{5,9},{9,13},{13,1},{2,6},{6,10},{... | collective-permute-start | bytes 294920 | tf_op jit(solution)/shard_map/ppermute | solution.py:86
  5.1 20.9 %collective-permute-start.1 = (bf16[6,8,1024]{2,1,0:T(8,128)(2,1)S(1)}, bf16[6,8,1024]{2,1,0:T(8,128)(2,1)}, u32[]{:S(2)}, u32[]{:S(2)}) collective-permute-start(bf16[6,8,1024]{2,1,0:T(8,128)(2,1)S(1)} %get-tuple-element.25), channel_id=1, source_target_pairs={{0,8},{4,12},{8,0},{12,4},{1,9},{5,13},{9,1},{13,5},{2,10},{6,14},... | collective-permute-start | bytes 294920 | tf_op jit(solution)/shard_map/ppermute | solution.py:86
  6.2 22.3 %collective-permute-start.2 = (bf16[6,8,1024]{2,1,0:T(8,128)(2,1)S(1)}, bf16[6,8,1024]{2,1,0:T(8,128)(2,1)}, u32[]{:S(2)}, u32[]{:S(2)}) collective-permute-start(bf16[6,8,1024]{2,1,0:T(8,128)(2,1)S(1)} %get-tuple-element.24), channel_id=1, source_target_pairs={{0,12},{4,0},{8,4},{12,8},{1,13},{5,1},{9,5},{13,9},{2,14},{6,2},{... | collective-permute-start | bytes 294920 | tf_op jit(solution)/shard_map/ppermute | solution.py:86
  10.7 25.0 %collective-permute-start.5 = (bf16[6,24,1024]{2,1,0:T(8,128)(2,1)}, bf16[6,24,1024]{2,1,0:T(8,128)(2,1)}, u32[]{:S(2)}, u32[]{:S(2)}) collective-permute-start(bf16[6,24,1024]{2,1,0:T(8,128)(2,1)} %get-tuple-element.22), channel_id=1, source_target_pairs={{0,4},{4,8},{8,12},{12,0},{1,5},{5,9},{9,13},{13,1},{2,6},{6,10},{... | collective-permute-start | bytes 884744 | tf_op jit(solution)/shard_map/ppermute | solution.py:86
  10.8 27.6 %collective-permute-start.6 = (bf16[6,24,1024]{2,1,0:T(8,128)(2,1)}, bf16[6,24,1024]{2,1,0:T(8,128)(2,1)}, u32[]{:S(2)}, u32[]{:S(2)}) collective-permute-start(bf16[6,24,1024]{2,1,0:T(8,128)(2,1)} %get-tuple-element.21), channel_id=1, source_target_pairs={{0,8},{4,12},{8,0},{12,4},{1,9},{5,13},{9,1},{13,5},{2,10},{6,14},... | collective-permute-start | bytes 884744 | tf_op jit(solution)/shard_map/ppermute | solution.py:86
  18.3 1.1 %copy-start.7 = (s32[1,2]{1,0:T(1,128)S(1)}, s32[1,2]{1,0:T(1,128)}, u32[]{:S(2)}) copy-start(s32[1,2]{1,0:T(1,128)} %param.13) | copy-start | bytes 28
  18.3 3.1 %copy-start.8 = (s32[1,24]{1,0:T(1,128)S(1)}, s32[1,24]{1,0:T(1,128)}, u32[]{:S(2)}) copy-start(s32[1,24]{1,0:T(1,128)} %param.12) | copy-start | bytes 292
  26.0 32.0 %collective-permute-start.7 = (bf16[6,24,1024]{2,1,0:T(8,128)(2,1)}, bf16[6,24,1024]{2,1,0:T(8,128)(2,1)}, u32[]{:S(2)}, u32[]{:S(2)}) collective-permute-start(bf16[6,24,1024]{2,1,0:T(8,128)(2,1)} %get-tuple-element.20), channel_id=1, source_target_pairs={{0,12},{4,0},{8,4},{12,8},{1,13},{5,1},{9,5},{13,9},{2,14},{6,2},{... | collective-permute-start | bytes 884744 | tf_op jit(solution)/shard_map/ppermute | solution.py:86
  32.1 25.9 %copy-start.1 = (bf16[512,1,1024]{2,0,1:T(8,128)(2,1)S(1)}, bf16[512,1,1024]{2,0,1:T(8,128)(2,1)}, u32[]{:S(2)}) copy-start(bf16[512,1,1024]{2,0,1:T(8,128)(2,1)} %get-tuple-element.12) | copy-start | bytes 3145732
  32.1 25.8 %copy-start.2 = (bf16[512,1,1024]{2,0,1:T(8,128)(2,1)S(1)}, bf16[512,1,1024]{2,0,1:T(8,128)(2,1)}, u32[]{:S(2)}) copy-start(bf16[512,1,1024]{2,0,1:T(8,128)(2,1)} %get-tuple-element.13) | copy-start | bytes 3145732
  32.1 25.8 %copy-start.3 = (bf16[512,1,1024]{2,0,1:T(8,128)(2,1)S(1)}, bf16[512,1,1024]{2,0,1:T(8,128)(2,1)}, u32[]{:S(2)}) copy-start(bf16[512,1,1024]{2,0,1:T(8,128)(2,1)} %get-tuple-element.14) | copy-start | bytes 3145732
  32.2 25.8 %copy-start.5 = (bf16[6,24,1024]{2,1,0:T(8,128)(2,1)S(1)}, bf16[6,24,1024]{2,1,0:T(8,128)(2,1)}, u32[]{:S(2)}) copy-start(bf16[6,24,1024]{2,1,0:T(8,128)(2,1)} %get-tuple-element.19) | copy-start | bytes 884740
  32.3 3.4 %collective-permute-start.3 = (f32[2,6,8,128]{3,2,1,0:T(8,128)S(1)}, f32[2,6,8,128]{3,2,1,0:T(8,128)S(1)}, u32[]{:S(2)}, u32[]{:S(2)}) collective-permute-start(f32[2,6,8,128]{3,2,1,0:T(8,128)S(1)} %dynamic-slice_bitcast_fusion.4), channel_id=1, source_target_pairs={{0,2},{2,0},{1,3},{3,1},{4,6},{6,4},{5,7},{7,5},{8,10},{10,8},{9,1... | collective-permute-start | bytes 147464 | tf_op jit(solution)/shard_map/ppermute | solution.py:26
  33.7 34.3 %collective-permute-start.10 = (bf16[6,32,1024]{2,1,0:T(8,128)(2,1)}, bf16[6,32,1024]{2,1,0:T(8,128)(2,1)}, u32[]{:S(2)}, u32[]{:S(2)}) collective-permute-start(bf16[6,32,1024]{2,1,0:T(8,128)(2,1)} %get-tuple-element.18), channel_id=1, source_target_pairs={{0,4},{4,8},{8,12},{12,0},{1,5},{5,9},{9,13},{13,1},{2,6},{6,10},{... | collective-permute-start | bytes 1179656 | tf_op jit(solution)/shard_map/ppermute | solution.py:86
  35.7 36.4 %collective-permute-start.11 = (bf16[6,32,1024]{2,1,0:T(8,128)(2,1)}, bf16[6,32,1024]{2,1,0:T(8,128)(2,1)}, u32[]{:S(2)}, u32[]{:S(2)}) collective-permute-start(bf16[6,32,1024]{2,1,0:T(8,128)(2,1)} %get-tuple-element.17), channel_id=1, source_target_pairs={{0,8},{4,12},{8,0},{12,4},{1,9},{5,13},{9,1},{13,5},{2,10},{6,14},... | collective-permute-start | bytes 1179656 | tf_op jit(solution)/shard_map/ppermute | solution.py:86
  35.8 39.1 %collective-permute-start.12 = (bf16[6,32,1024]{2,1,0:T(8,128)(2,1)S(1)}, bf16[6,32,1024]{2,1,0:T(8,128)(2,1)}, u32[]{:S(2)}, u32[]{:S(2)}) collective-permute-start(bf16[6,32,1024]{2,1,0:T(8,128)(2,1)S(1)} %get-tuple-element.16), channel_id=1, source_target_pairs={{0,12},{4,0},{8,4},{12,8},{1,13},{5,1},{9,5},{13,9},{2,14},{6,2},{... | collective-permute-start | bytes 1179656 | tf_op jit(solution)/shard_map/ppermute | solution.py:86
  38.4 23.5 %collective-permute-start.4 = (f32[6,8,128]{2,1,0:T(8,128)S(1)}, f32[6,8,128]{2,1,0:T(8,128)S(1)}, u32[]{:S(2)}, u32[]{:S(2)}) collective-permute-start(f32[6,8,128]{2,1,0:T(8,128)S(1)} %dynamic-slice_bitcast_fusion.5), channel_id=1, source_target_pairs={{0,1},{1,0},{2,3},{3,2},{4,5},{5,4},{6,7},{7,6},{8,9},{9,8},{10,11... | collective-permute-start | bytes 73736 | tf_op jit(solution)/shard_map/ppermute | solution.py:105
  61.5 4.9 %collective-permute-start.8 = (f32[2,6,24,128]{3,2,1,0:T(8,128)S(1)}, f32[2,6,24,128]{3,2,1,0:T(8,128)S(1)}, u32[]{:S(2)}, u32[]{:S(2)}) collective-permute-start(f32[2,6,24,128]{3,2,1,0:T(8,128)S(1)} %dynamic-slice_bitcast_fusion.1), channel_id=1, source_target_pairs={{0,2},{2,0},{1,3},{3,1},{4,6},{6,4},{5,7},{7,5},{8,10},{10,8},{9,1... | collective-permute-start | bytes 442376 | tf_op jit(solution)/shard_map/ppermute | solution.py:26
  66.4 13.3 %collective-permute-start.9 = (f32[6,24,128]{2,1,0:T(8,128)S(1)}, f32[6,24,128]{2,1,0:T(8,128)S(1)}, u32[]{:S(2)}, u32[]{:S(2)}) collective-permute-start(f32[6,24,128]{2,1,0:T(8,128)S(1)} %dynamic-slice_bitcast_fusion.3), channel_id=1, source_target_pairs={{0,1},{1,0},{2,3},{3,2},{4,5},{5,4},{6,7},{7,6},{8,9},{9,8},{10,11... | collective-permute-start | bytes 221192 | tf_op jit(solution)/shard_map/ppermute | solution.py:105
  79.5 6.0 %collective-permute-start.13 = (f32[2,6,32,128]{3,2,1,0:T(8,128)S(1)}, f32[2,6,32,128]{3,2,1,0:T(8,128)S(1)}, u32[]{:S(2)}, u32[]{:S(2)}) collective-permute-start(f32[2,6,32,128]{3,2,1,0:T(8,128)S(1)} %dynamic-slice_bitcast_fusion), channel_id=1, source_target_pairs={{0,2},{2,0},{1,3},{3,1},{4,6},{6,4},{5,7},{7,5},{8,10},{10,8},{9,1... | collective-permute-start | bytes 589832 | tf_op jit(solution)/shard_map/ppermute | solution.py:26
  85.6 2.4 %collective-permute-start.14 = (f32[6,32,128]{2,1,0:T(8,128)S(1)}, f32[6,32,128]{2,1,0:T(8,128)S(1)}, u32[]{:S(2)}, u32[]{:S(2)}) collective-permute-start(f32[6,32,128]{2,1,0:T(8,128)S(1)} %dynamic-slice_bitcast_fusion.2), channel_id=1, source_target_pairs={{0,1},{1,0},{2,3},{3,2},{4,5},{5,4},{6,7},{7,6},{8,9},{9,8},{10,11... | collective-permute-start | bytes 294920 | tf_op jit(solution)/shard_map/ppermute | solution.py:105
  87.9 0.7 copy-start.4

commit v10 on v9

--- a/solution.py
+++ b/solution.py
@@ -9,23 +9,6 @@
 BLOCK = 128
 ROW_SPLIT = (8, 24, 32)
 GATE_FROM = {2: 0}
-
-
-def ring_reduce_scatter(x, axis_name, dim):
-    n = lax.axis_size(axis_name)
-    me = lax.axis_index(axis_name)
-
-    def piece(c):
-        return lax.dynamic_index_in_dim(x, c % n, axis=dim, keepdims=False)
-
-    if n == 1:
-        return piece(me)
-    perm = [(i, (i + 1) % n) for i in range(n)]
-    acc = piece(me - 1 + n)
-    for t in range(n - 1):
-        recv = lax.ppermute(acc, axis_name, perm)
-        acc = recv + piece(me - 2 - t + 2 * n)
-    return acc
 
 
 def shards(queries, train_grads, precond, requests, pair_slot, pair_train, pair_count):
@@ -50,7 +33,8 @@
         t_l = train_grads[:, layer, :]
         for k in range(n_span):
             t_parts.append(lax.dynamic_slice_in_dim(t_l, sources[k] * features, features, axis=1))
-    train = jnp.concatenate(t_parts, axis=1)
+    train_local = jnp.concatenate([t_parts[layer * n_span] for layer in range(l_dev)], axis=1)
+    train_remote = jnp.concatenate([p for i, p in enumerate(t_parts) if i % n_span], axis=1)
 
     score_scale = 1.0 / math.sqrt(l_dev * n_layer * d_full)
     slot_row = pair_slot[0]
@@ -87,25 +71,30 @@
                 pieces.append(piece)
         gate = pieces
         arrivals.append(pieces)
-        arrived = jnp.concatenate(pieces, axis=-1).reshape(cap * rows, -1)
-        combos = lax.dot_general(
-            arrived,
-            train,
-            (((1,), (1,)), ((), ())),
-            preferred_element_type=jnp.float32,
-        ).reshape(cap, rows, tb_dev, BLOCK)
+        dims = (((1,), (1,)), ((), ()))
+        local = jnp.concatenate([pieces[layer * n_span] for layer in range(l_dev)], axis=-1)
+        combos = lax.dot_general(local.reshape(cap * rows, -1), train_local, dims, preferred_element_type=jnp.float32)
+        arrived = jnp.concatenate([p for i, p in enumerate(pieces) if i % n_span], axis=-1)
+        combos = combos + lax.dot_general(
+            arrived.reshape(cap * rows, -1), train_remote, dims, preferred_element_type=jnp.float32
+        )
+        combos = combos.reshape(cap, rows, tb_dev, BLOCK)
         partial = combos.at[slot_row, :, train_row, :].get(mode="promise_in_bounds") * score_scale
         partial = jnp.where(live[:, None, None], partial, 0.0)
         partial = partial.reshape(n_layer, n_rep, per_dev, rows, BLOCK)
-        partial = ring_reduce_scatter(partial, "layer", 0)
-        got_rows = [lax.dynamic_index_in_dim(partial, rep_index, axis=0, keepdims=False)]
-        for k in range(1, n_rep):
-            perm = [(i, (i + k) % n_rep) for i in range(n_rep)]
-            send = lax.dynamic_index_in_dim(partial, (rep_index + k) % n_rep, axis=0, keepdims=False)
-            got_rows.append(lax.ppermute(send, "rep", perm))
-        for k, got in enumerate(got_rows):
-            owner = (rep_index - k + n_rep) % n_rep
-            out_buf = lax.dynamic_update_slice(out_buf, got, (0, owner * own_rows + row_start - rows, 0))
+        n_group = n_layer * n_rep
+        me = lax.axis_index("layer") * n_rep + rep_index
+        flat = partial.reshape(n_group, per_dev, rows, BLOCK)
+        got = [lax.dynamic_index_in_dim(flat, me, axis=0, keepdims=False)]
+        for k in range(1, n_group):
+            perm = [(i, (i + k) % n_group) for i in range(n_group)]
+            send = lax.dynamic_index_in_dim(flat, (me + k) % n_group, axis=0, keepdims=False)
+            got.append(lax.ppermute(send, ("layer", "rep"), perm))
+        stacked = jnp.stack(got, axis=0)
+        row_owner = ((me - jnp.arange(n_group, dtype=jnp.int32) + n_group) % n_group) % n_rep
+        for h in range(n_rep):
+            rows_h = jnp.sum(jnp.where((row_owner == h)[:, None, None, None], stacked, 0.0), axis=0)
+            out_buf = lax.dynamic_update_slice(out_buf, rows_h, (0, h * own_rows + row_start - rows, 0))
     return out_buf.reshape(per_dev * BLOCK, BLOCK)[None]
 
 

time: 89.1 us -> 94 us (1.055)
  the two profiles are of different devices: /device:TPU:11 before, /device:TPU:0 now
where the time goes in v10:
time: 94 us; the launch traced here: 93.4 us
  waiting for transfers between devices  29.5 us (31%)
  starting transfers between devices  23.2 us (25%)
  local copies, waits for them, and re-layouts  18.5 us (20%)
  matrix products  12.4 us (13%)
  other arithmetic  6.58 us (7%)
  between operations  3.22 us (3%)
    ppermute x9, waiting for transfers between devices, shards(): piece = lax.ppermute(piece, 'span', perm)  22.1 us
    ppermute x9, starting transfers between devices, shards(): piece = lax.ppermute(piece, 'span', perm)  14 us
    ppermute x9, starting transfers between devices, shards(): got.append(lax.ppermute(send, ('layer', 'rep'), perm))  9.18 us
    ppermute x9, waiting for transfers between devices, shards(): got.append(lax.ppermute(send, ('layer', 'rep'), perm))  7.45 us
    dot_general x3, matrix products, shards(): lax.dot_general(local.reshape(cap * rows, -1), train_local, dims, preferr...  6.77 us
    dot_general x3, matrix products, shards(): lax.dot_general(arrived.reshape(cap * rows, -1), train_remote, dims, pref...  5.67 us
    dynamic_slice x3, local copies, waits for them, and re-layouts, shards(): lax.dynamic_slice_in_dim(q3, rep_index * own_rows + row_start, rows, axis=1)  3.48 us
    squeeze x3, local copies, waits for them, and re-layouts, shards(): piece = sent[layer][k]  3.07 us
  transfers between devices with their start and end apart: 18, of which 7 were waited for; matrix products, arithmetic and copies ran while one was open for 28% of the time, Pallas kernels for 0%

profile of v10, /device:TPU:0, one launch (start us, length us, event | category | flops | bytes accessed | tf_op | source)
XLA Modules:
  0.0 93.4 jit_solution(16508960588558009667)
XLA Ops:
  0.0 0.7 copy-done
  0.7 0.6 gather_fusion
  1.2 0.1 reshape.282
  1.3 1.0 %constant_dynamic-slice_fusion.5 = bf16[16,8,1024]{2,1,0:T(8,128)(2,1)S(1)} fusion(bf16[16,128,1024]{2,1,0:T(8,128)(2,1)} %bitcast.112, s32[]{:T(128)S(6)} %select_n.227), kind=kLoop, calls=%fused_computation.84 | loop fusion | bytes 524292 | tf_op jit(solution)/shard_map/dynamic_slice | solution.py:57
  2.3 0.6 gather_fusion.1
  2.9 0.8 fusion.12
  3.7 0.7 slice_bitcast_fusion.8
  4.4 3.1 %collective-permute-start = (bf16[6,8,1024]{2,1,0:T(8,128)(2,1)}, bf16[6,8,1024]{2,1,0:T(8,128)(2,1)}, u32[]{:S(2)}, u32[]{:S(2)}) collective-permute-start(bf16[6,8,1024]{2,1,0:T(8,128)(2,1)} %get-tuple-element.32), channel_id=1, source_target_pairs={{0,4},{4,8},{8,12},{12,0},{1,5},{5,9},{9,13},{13,1},{2,6},{6,10},{... | collective-permute-start | bytes 294920 | tf_op jit(solution)/shard_map/ppermute | solution.py:70
  7.4 2.0 %collective-permute-start.2 = (bf16[6,8,1024]{2,1,0:T(8,128)(2,1)}, bf16[6,8,1024]{2,1,0:T(8,128)(2,1)}, u32[]{:S(2)}, u32[]{:S(2)}) collective-permute-start(bf16[6,8,1024]{2,1,0:T(8,128)(2,1)} %get-tuple-element.33), channel_id=1, source_target_pairs={{0,12},{4,0},{8,4},{12,8},{1,13},{5,1},{9,5},{13,9},{2,14},{6,2},{... | collective-permute-start | bytes 294920 | tf_op jit(solution)/shard_map/ppermute | solution.py:70
  9.5 1.0 %collective-permute-start.1 = (bf16[6,8,1024]{2,1,0:T(8,128)(2,1)}, bf16[6,8,1024]{2,1,0:T(8,128)(2,1)}, u32[]{:S(2)}, u32[]{:S(2)}) collective-permute-start(bf16[6,8,1024]{2,1,0:T(8,128)(2,1)} %get-tuple-element.34), channel_id=1, source_target_pairs={{0,8},{4,12},{8,0},{12,4},{1,9},{5,13},{9,1},{13,5},{2,10},{6,14},... | collective-permute-start | bytes 294920 | tf_op jit(solution)/shard_map/ppermute | solution.py:70
  10.5 1.2 %constant_dynamic-slice_fusion.3 = bf16[16,24,1024]{2,1,0:T(8,128)(2,1)S(1)} fusion(bf16[16,128,1024]{2,1,0:T(8,128)(2,1)} %bitcast.113, s32[]{:T(128)S(6)} %select_n.247), kind=kLoop, calls=%fused_computation.80 | loop fusion | bytes 1572868 | tf_op jit(solution)/shard_map/dynamic_slice | solution.py:57
  11.7 0.6 gather_fusion.3
  12.3 0.3 fusion.1
  12.6 1.0 %slice_bitcast_fusion.5 = (bf16[6,24,1024]{2,1,0:T(8,128)(2,1)}, bf16[6,24,1024]{2,1,0:T(8,128)(2,1)}, bf16[6,24,1024]{2,1,0:T(8,128)(2,1)}, bf16[1,6,24,1024]{3,2,1,0:T(8,128)(2,1)}) fusion(bf16[4,6,24,1024]{3,2,1,0:T(8,128)(2,1)S(1)} %fusion.1), kind=kLoop, calls=%fused_computation.40 | loop fusion | bytes 2359296 | tf_op jit(solution)/shard_map/squeeze | solution.py:67
  13.7 1.6 %collective-permute-start.6 = (bf16[6,24,1024]{2,1,0:T(8,128)(2,1)}, bf16[6,24,1024]{2,1,0:T(8,128)(2,1)}, u32[]{:S(2)}, u32[]{:S(2)}) collective-permute-start(bf16[6,24,1024]{2,1,0:T(8,128)(2,1)} %get-tuple-element.24), channel_id=1, source_target_pairs={{0,4},{4,8},{8,12},{12,0},{1,5},{5,9},{9,13},{13,1},{2,6},{6,10},{... | collective-permute-start | bytes 884744 | tf_op jit(solution)/shard_map/ppermute | solution.py:70
  15.2 2.2 %collective-permute-start.8 = (bf16[6,24,1024]{2,1,0:T(8,128)(2,1)}, bf16[6,24,1024]{2,1,0:T(8,128)(2,1)}, u32[]{:S(2)}, u32[]{:S(2)}) collective-permute-start(bf16[6,24,1024]{2,1,0:T(8,128)(2,1)} %get-tuple-element.25), channel_id=1, source_target_pairs={{0,12},{4,0},{8,4},{12,8},{1,13},{5,1},{9,5},{13,9},{2,14},{6,2},{... | collective-permute-start | bytes 884744 | tf_op jit(solution)/shard_map/ppermute | solution.py:70
  17.5 0.7 fusion.38
  20.9 0.6 fusion.37
  21.5 1.3 %fusion.24 = s32[24]{0:T(128)S(1)} fusion(s32[]{:T(128)} %bitcast.1, s32[]{:T(128)} %bitcast), kind=kLoop, calls=%fused_computation.116 | loop fusion | flops 312 | bytes 104 | tf_op jit(solution)/shard_map/gather | solution.py:44
  22.8 0.1 gather.32
  22.9 1.3 %constant_dynamic-slice_fusion.1 = bf16[16,32,1024]{2,1,0:T(8,128)(2,1)S(1)} fusion(bf16[16,128,1024]{2,1,0:T(8,128)(2,1)} %bitcast.114, s32[]{:T(128)S(6)} %select_n.251), kind=kLoop, calls=%fused_computation.76 | loop fusion | bytes 2097156 | tf_op jit(solution)/shard_map/dynamic_slice | solution.py:57
  24.3 0.6 gather_fusion.5
  24.9 0.4 fusion
  25.4 1.7 %fusion.7 = f32[48,512]{1,0:T(8,128)S(1)} fusion(bf16[512,1,4096]{2,0,1:T(8,128)(2,1)} %param.8, s32[]{:T(128)S(6)} %select_n.231, bf16[4,6,8,1024]{3,2,1,0:T(8,128)(2,1)S(1)} %fusion.12), kind=kOutput, calls=%fused_computation.21 | convolution fusion | flops 50331648 | bytes 1245188 | tf_op jit(solution)/shard_map/dot_general | solution.py:76
  27.0 2.5 %fusion.5 = f32[144,512]{1,0:T(8,128)} fusion(bf16[144,1024]{1,0:T(8,128)(2,1)} %bitcast.109, bf16[512,1,4096]{2,0,1:T(8,128)(2,1)} %param.8, s32[]{:T(128)S(6)} %select_n.231), kind=kOutput, calls=%fused_computation.19 | convolution fusion | flops 150994944 | bytes 1638404 | tf_op jit(solution)/shard_map/dot_general | solution.py:76
  29.6 0.7 fusion.35
  30.2 2.2 %dynamic-slice_bitcast_fusion.2 = (bf16[512,1024]{1,0:T(8,128)(2,1)S(1)}, bf16[512,1024]{1,0:T(8,128)(2,1)S(1)}, bf16[512,1024]{1,0:T(8,128)(2,1)S(1)}) fusion(bf16[512,1,4096]{2,0,1:T(8,128)(2,1)} %param.8, s32[]{:T(128)S(6)} %select_n.232, s32[]{:T(128)S(6)} %select_n.234, s32[]{:T(128)S(6)} %select_n.233), kind=kLoop, calls=%fused_computation.25 | loop fusion | bytes 6291468 | tf_op jit(solution)/shard_map/dynamic_slice | solution.py:35
  32.5 0.2 collective-permute-start.7
  32.7 1.3 %slice_bitcast_fusion.2 = (bf16[6,32,1024]{2,1,0:T(8,128)(2,1)}, bf16[6,32,1024]{2,1,0:T(8,128)(2,1)}, bf16[6,32,1024]{2,1,0:T(8,128)(2,1)}, bf16[1,6,32,1024]{3,2,1,0:T(8,128)(2,1)S(1)}) fusion(bf16[4,6,32,1024]{3,2,1,0:T(8,128)(2,1)S(1)} %fusion), kind=kLoop, calls=%fused_computation.37 | loop fusion | bytes 3145728 | tf_op jit(solution)/shard_map/squeeze | solution.py:67
  34.0 0.2 collective-permute-start.12
  34.2 3.6 %collective-permute-start.14 = (bf16[6,32,1024]{2,1,0:T(8,128)(2,1)}, bf16[6,32,1024]{2,1,0:T(8,128)(2,1)}, u32[]{:S(2)}, u32[]{:S(2)}) collective-permute-start(bf16[6,32,1024]{2,1,0:T(8,128)(2,1)} %get-tuple-element.21), channel_id=1, source_target_pairs={{0,12},{4,0},{8,4},{12,8},{1,13},{5,1},{9,5},{13,9},{2,14},{6,2},{... | collective-permute-start | bytes 1179656 | tf_op jit(solution)/shard_map/ppermute | solution.py:70
  37.8 2.1 %fusion.2 = f32[6,8,4,128]{3,1,2,0:T(8,128)S(1)} fusion(f32[48,512]{1,0:T(8,128)S(1)} %fusion.7, bf16[6,8,1024]{2,1,0:T(8,128)(2,1)} %collective-permute-done.2, bf16[6,8,1024]{2,1,0:T(8,128)(2,1)} %collective-permute-done.1, bf16[6,8,1024]{2,1,0:T(8,128)(2,1)} %collective-permute-done, bf16[512,1024]{1,0:T(8,128)(2,1)S(1)} %get-tuple-element.18, ...), kind=kOutput, calls=%fused_computation.16 | convolution fusion | flops 161341440 | bytes 3637248 | tf_op jit(solution)/shard_map/dot_general | solution.py:78
  39.9 0.7 gather_fusion.2
  40.6 0.1 broadcast_select_fusion.2
  40.8 2.6 %fusion.3 = f32[192,512]{1,0:T(8,128)} fusion(bf16[192,1024]{1,0:T(8,128)(2,1)S(1)} %bitcast.106, bf16[512,1,4096]{2,0,1:T(8,128)(2,1)} %param.8, s32[]{:T(128)S(6)} %select_n.231), kind=kOutput, calls=%fused_computation.17 | convolution fusion | flops 201326592 | bytes 1835012 | tf_op jit(solution)/shard_map/dot_general | solution.py:76
  43.3 1.7 %collective-permute-start.4 = (f32[6,8,128]{2,1,0:T(8,128)S(1)}, f32[6,8,128]{2,1,0:T(8,128)S(1)}, u32[]{:S(2)}, u32[]{:S(2)}) collective-permute-start(f32[6,8,128]{2,1,0:T(8,128)S(1)} %get-tuple-element.41), channel_id=1, source_target_pairs={{0,2},{1,3},{2,0},{3,1},{4,6},{5,7},{6,4},{7,5},{8,10},{9,11},{10,... | collective-permute-start | bytes 73736 | tf_op jit(solution)/shard_map/ppermute | solution.py:92
  45.0 10.0 %collective-permute-done.7 = bf16[6,24,1024]{2,1,0:T(8,128)(2,1)} collective-permute-done((bf16[6,24,1024]{2,1,0:T(8,128)(2,1)S(1)}, bf16[6,24,1024]{2,1,0:T(8,128)(2,1)}, u32[]{:S(2)}, u32[]{:S(2)}) %collective-permute-start.7) | collective-permute-done | bytes 294944 | tf_op jit(solution)/shard_map/ppermute | solution.py:70
  55.0 1.2 %pad_maximum_fusion.2 = bf16[6,24,3072]{2,1,0:T(8,128)(2,1)S(1)} fusion(bf16[6,24,1024]{2,1,0:T(8,128)(2,1)} %collective-permute-done.8, bf16[6,24,1024]{2,1,0:T(8,128)(2,1)} %collective-permute-done.7, bf16[6,24,1024]{2,1,0:T(8,128)(2,1)} %collective-permute-done.6), kind=kLoop, calls=%fused_computation.26 | loop fusion | flops 2654208 | bytes 1769472 | tf_op jit(solution)/shard_map/concatenate | solution.py:77
  56.3 1.4 %convolution_add_fusion.1 = f32[144,512]{1,0:T(8,128)S(1)} fusion(f32[144,512]{1,0:T(8,128)S(1)} %copy-done.9, bf16[144,3072]{1,0:T(8,128)(2,1)S(1)} %bitcast.115, bf16[512,1024]{1,0:T(8,128)(2,1)S(1)} %copy-done.2, bf16[512,1024]{1,0:T(8,128)(2,1)S(1)} %copy-done.4, bf16[512,1024]{1,0:T(8,128)(2,1)S(1)} %get-tuple-element.17), kind=kOutput, calls=%fused_computation.14 | convolution fusion | flops 462495744 | bytes 4620288 | tf_op jit(solution)/shard_map/dot_general | solution.py:78
  57.7 0.1 reshape.257
  57.9 0.7 gather_fusion.4
  58.6 0.1 broadcast_select_fusion.1
  58.8 1.8 %collective-permute-start.11 = (f32[6,24,128]{2,1,0:T(8,128)S(1)}, f32[6,24,128]{2,1,0:T(8,128)S(1)}, u32[]{:S(2)}, u32[]{:S(2)}) collective-permute-start(f32[6,24,128]{2,1,0:T(8,128)S(1)} %get-tuple-element.36), channel_id=1, source_target_pairs={{0,3},{1,0},{2,1},{3,2},{4,7},{5,4},{6,5},{7,6},{8,11},{9,8},{10,9... | collective-permute-start | bytes 221192 | tf_op jit(solution)/shard_map/ppermute | solution.py:92
  60.8 2.0 %collective-permute-start.10 = (f32[6,24,128]{2,1,0:T(8,128)S(1)}, f32[6,24,128]{2,1,0:T(8,128)S(1)}, u32[]{:S(2)}, u32[]{:S(2)}) collective-permute-start(f32[6,24,128]{2,1,0:T(8,128)S(1)} %get-tuple-element.37), channel_id=1, source_target_pairs={{0,2},{1,3},{2,0},{3,1},{4,6},{5,7},{6,4},{7,5},{8,10},{9,11},{10,... | collective-permute-start | bytes 221192 | tf_op jit(solution)/shard_map/ppermute | solution.py:92
  62.8 0.5 collective-permute-done.11
  63.2 1.9 %collective-permute-start.9 = (f32[6,24,128]{2,1,0:T(8,128)S(1)}, f32[6,24,128]{2,1,0:T(8,128)S(1)}, u32[]{:S(2)}, u32[]{:S(2)}) collective-permute-start(f32[6,24,128]{2,1,0:T(8,128)S(1)} %get-tuple-element.38), channel_id=1, source_target_pairs={{0,1},{1,2},{2,3},{3,0},{4,5},{5,6},{6,7},{7,4},{8,9},{9,10},{10,1... | collective-permute-start | bytes 221192 | tf_op jit(solution)/shard_map/ppermute | solution.py:92
  65.2 1.0 %collective-permute-done.10 = f32[6,24,128]{2,1,0:T(8,128)S(1)} collective-permute-done((f32[6,24,128]{2,1,0:T(8,128)S(1)}, f32[6,24,128]{2,1,0:T(8,128)S(1)}, u32[]{:S(2)}, u32[]{:S(2)}) %collective-permute-start.10) | collective-permute-done | bytes 73760 | tf_op jit(solution)/shard_map/ppermute | solution.py:92
  66.1 1.0 %collective-permute-done.9 = f32[6,24,128]{2,1,0:T(8,128)S(1)} collective-permute-done((f32[6,24,128]{2,1,0:T(8,128)S(1)}, f32[6,24,128]{2,1,0:T(8,128)S(1)}, u32[]{:S(2)}, u32[]{:S(2)}) %collective-permute-start.9) | collective-permute-done | bytes 73760 | tf_op jit(solution)/shard_map/ppermute | solution.py:92
  67.2 0.1 select_reduce_fusion.2
  67.3 0.7 copy-done.7
  68.0 12.1 %collective-permute-done.13 = bf16[6,32,1024]{2,1,0:T(8,128)(2,1)S(1)} collective-permute-done((bf16[6,32,1024]{2,1,0:T(8,128)(2,1)S(1)}, bf16[6,32,1024]{2,1,0:T(8,128)(2,1)S(1)}, u32[]{:S(2)}, u32[]{:S(2)}) %collective-permute-start.13) | collective-permute-done | bytes 393248 | tf_op jit(solution)/shard_map/ppermute | solution.py:70
  80.1 1.2 %pad_maximum_fusion.1 = bf16[6,32,3072]{2,1,0:T(8,128)(2,1)S(1)} fusion(bf16[6,32,1024]{2,1,0:T(8,128)(2,1)} %collective-permute-done.14, bf16[6,32,1024]{2,1,0:T(8,128)(2,1)S(1)} %collective-permute-done.13, bf16[6,32,1024]{2,1,0:T(8,128)(2,1)} %collective-permute-done.12), kind=kLoop, calls=%fused_computation.13 | loop fusion | flops 3538944 | bytes 2359296 | tf_op jit(solution)/shard_map/concatenate | solution.py:77
  81.3 2.2 %convolution_add_fusion = f32[192,512]{1,0:T(8,128)S(1)} fusion(f32[192,512]{1,0:T(8,128)} %fusion.3, bf16[192,3072]{1,0:T(8,128)(2,1)S(1)} %bitcast.110, bf16[512,1024]{1,0:T(8,128)(2,1)S(1)} %copy-done.2, bf16[512,1024]{1,0:T(8,128)(2,1)S(1)} %copy-done.5, bf16[512,1024]{1,0:T(8,128)(2,1)S(1)} %get-tuple-element.17), kind=kOutput, calls=%fused_computation.12 | convolution fusion | flops 613515264 | bytes 5111808 | tf_op jit(solution)/shard_map/dot_general | solution.py:78
  83.6 0.1 reshape.259
  83.7 0.7 gather_fusion.6
  84.5 0.1 broadcast_select_fusion
  84.6 1.2 %collective-permute-start.17 = (f32[6,32,128]{2,1,0:T(8,128)S(1)}, f32[6,32,128]{2,1,0:T(8,128)S(1)}, u32[]{:S(2)}, u32[]{:S(2)}) collective-permute-start(f32[6,32,128]{2,1,0:T(8,128)S(1)} %get-tuple-element.29), channel_id=1, source_target_pairs={{0,3},{1,0},{2,1},{3,2},{4,7},{5,4},{6,5},{7,6},{8,11},{9,8},{10,9... | collective-permute-start | bytes 294920 | tf_op jit(solution)/shard_map/ppermute | solution.py:92
  85.8 0.5 collective-permute-start.16
  86.4 0.6 constant_dynamic-update-slice_fusion.2
  87.0 1.9 %collective-permute-done.17 = f32[6,32,128]{2,1,0:T(8,128)S(1)} collective-permute-done((f32[6,32,128]{2,1,0:T(8,128)S(1)}, f32[6,32,128]{2,1,0:T(8,128)S(1)}, u32[]{:S(2)}, u32[]{:S(2)}) %collective-permute-start.17) | collective-permute-done | bytes 98336 | tf_op jit(solution)/shard_map/ppermute | solution.py:92
  89.0 3.0 %collective-permute-done.16 = f32[6,32,128]{2,1,0:T(8,128)S(1)} collective-permute-done((f32[6,32,128]{2,1,0:T(8,128)S(1)}, f32[6,32,128]{2,1,0:T(8,128)S(1)}, u32[]{:S(2)}, u32[]{:S(2)}) %collective-permute-start.16) | collective-permute-done | bytes 98336 | tf_op jit(solution)/shard_map/ppermute | solution.py:92
  92.0 0.1 select_reduce_fusion
  92.1 0.7 constant_dynamic-update-slice_fusion.1
  92.8 0.6 constant_dynamic-update-slice_fusion
  (59 shorter events, 0.7 us)
Async XLA Ops:
  0.0 0.7 copy-start
  2.3 10.0 %copy-start.10 = (f32[1,1024]{1,0:T(1,128)S(1)}, f32[1,1024]{1,0:T(1,128)}, u32[]{:S(2)}) copy-start(f32[1,1024]{1,0:T(1,128)} %param.9) | copy-start | bytes 12292
  4.4 28.1 %collective-permute-start = (bf16[6,8,1024]{2,1,0:T(8,128)(2,1)}, bf16[6,8,1024]{2,1,0:T(8,128)(2,1)}, u32[]{:S(2)}, u32[]{:S(2)}) collective-permute-start(bf16[6,8,1024]{2,1,0:T(8,128)(2,1)} %get-tuple-element.32), channel_id=1, source_target_pairs={{0,4},{4,8},{8,12},{12,0},{1,5},{5,9},{9,13},{13,1},{2,6},{6,10},{... | collective-permute-start | bytes 294920 | tf_op jit(solution)/shard_map/ppermute | solution.py:70
  7.4 25.3 %collective-permute-start.2 = (bf16[6,8,1024]{2,1,0:T(8,128)(2,1)}, bf16[6,8,1024]{2,1,0:T(8,128)(2,1)}, u32[]{:S(2)}, u32[]{:S(2)}) collective-permute-start(bf16[6,8,1024]{2,1,0:T(8,128)(2,1)} %get-tuple-element.33), channel_id=1, source_target_pairs={{0,12},{4,0},{8,4},{12,8},{1,13},{5,1},{9,5},{13,9},{2,14},{6,2},{... | collective-permute-start | bytes 294920 | tf_op jit(solution)/shard_map/ppermute | solution.py:70
  9.5 23.2 %collective-permute-start.1 = (bf16[6,8,1024]{2,1,0:T(8,128)(2,1)}, bf16[6,8,1024]{2,1,0:T(8,128)(2,1)}, u32[]{:S(2)}, u32[]{:S(2)}) collective-permute-start(bf16[6,8,1024]{2,1,0:T(8,128)(2,1)} %get-tuple-element.34), channel_id=1, source_target_pairs={{0,8},{4,12},{8,0},{12,4},{1,9},{5,13},{9,1},{13,5},{2,10},{6,14},... | collective-permute-start | bytes 294920 | tf_op jit(solution)/shard_map/ppermute | solution.py:70
  11.7 9.2 %copy-start.11 = (s32[1,2]{1,0:T(1,128)S(1)}, s32[1,2]{1,0:T(1,128)}, u32[]{:S(2)}) copy-start(s32[1,2]{1,0:T(1,128)} %param.13) | copy-start | bytes 28
  13.7 29.7 %collective-permute-start.6 = (bf16[6,24,1024]{2,1,0:T(8,128)(2,1)}, bf16[6,24,1024]{2,1,0:T(8,128)(2,1)}, u32[]{:S(2)}, u32[]{:S(2)}) collective-permute-start(bf16[6,24,1024]{2,1,0:T(8,128)(2,1)} %get-tuple-element.24), channel_id=1, source_target_pairs={{0,4},{4,8},{8,12},{12,0},{1,5},{5,9},{9,13},{13,1},{2,6},{6,10},{... | collective-permute-start | bytes 884744 | tf_op jit(solution)/shard_map/ppermute | solution.py:70
  15.2 28.1 %collective-permute-start.8 = (bf16[6,24,1024]{2,1,0:T(8,128)(2,1)}, bf16[6,24,1024]{2,1,0:T(8,128)(2,1)}, u32[]{:S(2)}, u32[]{:S(2)}) collective-permute-start(bf16[6,24,1024]{2,1,0:T(8,128)(2,1)} %get-tuple-element.25), channel_id=1, source_target_pairs={{0,12},{4,0},{8,4},{12,8},{1,13},{5,1},{9,5},{13,9},{2,14},{6,2},{... | collective-permute-start | bytes 884744 | tf_op jit(solution)/shard_map/ppermute | solution.py:70
  24.9 4.7 %copy-start.12 = (s32[1,24]{1,0:T(1,128)S(1)}, s32[1,24]{1,0:T(1,128)}, u32[]{:S(2)}) copy-start(s32[1,24]{1,0:T(1,128)} %param.12) | copy-start | bytes 292
  30.2 2.3 %copy-start.8 = (bf16[6,24,1024]{2,1,0:T(8,128)(2,1)S(1)}, bf16[6,24,1024]{2,1,0:T(8,128)(2,1)}, u32[]{:S(2)}) copy-start(bf16[6,24,1024]{2,1,0:T(8,128)(2,1)} %get-tuple-element.26) | copy-start | bytes 884740
  32.5 5.4 %copy-start.1 = (bf16[512,1024]{1,0:T(8,128)(2,1)}, bf16[512,1024]{1,0:T(8,128)(2,1)S(1)}, u32[]{:S(2)}) copy-start(bf16[512,1024]{1,0:T(8,128)(2,1)S(1)} %get-tuple-element.18) | copy-start | bytes 3145732
  32.5 5.4 %copy-start.3 = (bf16[512,1024]{1,0:T(8,128)(2,1)}, bf16[512,1024]{1,0:T(8,128)(2,1)S(1)}, u32[]{:S(2)}) copy-start(bf16[512,1024]{1,0:T(8,128)(2,1)S(1)} %get-tuple-element.19) | copy-start | bytes 3145732
  32.5 22.5 %collective-permute-start.7 = (bf16[6,24,1024]{2,1,0:T(8,128)(2,1)S(1)}, bf16[6,24,1024]{2,1,0:T(8,128)(2,1)}, u32[]{:S(2)}, u32[]{:S(2)}) collective-permute-start(bf16[6,24,1024]{2,1,0:T(8,128)(2,1)S(1)} %copy-done.8), channel_id=1, source_target_pairs={{0,8},{4,12},{8,0},{12,4},{1,9},{5,13},{9,1},{13,5},{2,10},{6,14},... | collective-permute-start | bytes 884744 | tf_op jit(solution)/shard_map/ppermute | solution.py:70
  34.0 33.3 %collective-permute-start.12 = (bf16[6,32,1024]{2,1,0:T(8,128)(2,1)}, bf16[6,32,1024]{2,1,0:T(8,128)(2,1)}, u32[]{:S(2)}, u32[]{:S(2)}) collective-permute-start(bf16[6,32,1024]{2,1,0:T(8,128)(2,1)} %get-tuple-element.20), channel_id=1, source_target_pairs={{0,4},{4,8},{8,12},{12,0},{1,5},{5,9},{9,13},{13,1},{2,6},{6,10},{... | collective-permute-start | bytes 1179656 | tf_op jit(solution)/shard_map/ppermute | solution.py:70
  34.2 33.1 %collective-permute-start.14 = (bf16[6,32,1024]{2,1,0:T(8,128)(2,1)}, bf16[6,32,1024]{2,1,0:T(8,128)(2,1)}, u32[]{:S(2)}, u32[]{:S(2)}) collective-permute-start(bf16[6,32,1024]{2,1,0:T(8,128)(2,1)} %get-tuple-element.21), channel_id=1, source_target_pairs={{0,12},{4,0},{8,4},{12,8},{1,13},{5,1},{9,5},{13,9},{2,14},{6,2},{... | collective-permute-start | bytes 1179656 | tf_op jit(solution)/shard_map/ppermute | solution.py:70
  39.9 16.3 %copy-start.2 = (bf16[512,1024]{1,0:T(8,128)(2,1)S(1)}, bf16[512,1024]{1,0:T(8,128)(2,1)}, u32[]{:S(2)}) copy-start(bf16[512,1024]{1,0:T(8,128)(2,1)} %copy-done.1) | copy-start | bytes 3145732
  40.6 15.7 %copy-start.4 = (bf16[512,1024]{1,0:T(8,128)(2,1)S(1)}, bf16[512,1024]{1,0:T(8,128)(2,1)}, u32[]{:S(2)}) copy-start(bf16[512,1024]{1,0:T(8,128)(2,1)} %copy-done.3) | copy-start | bytes 3145732
  40.6 15.7 %copy-start.9 = (f32[144,512]{1,0:T(8,128)S(1)}, f32[144,512]{1,0:T(8,128)}, u32[]{:S(2)}) copy-start(f32[144,512]{1,0:T(8,128)} %fusion.5) | copy-start | bytes 884740
  43.3 15.4 %collective-permute-start.5 = (f32[6,8,128]{2,1,0:T(8,128)S(1)}, f32[6,8,128]{2,1,0:T(8,128)S(1)}, u32[]{:S(2)}, u32[]{:S(2)}) collective-permute-start(f32[6,8,128]{2,1,0:T(8,128)S(1)} %get-tuple-element.40), channel_id=1, source_target_pairs={{0,3},{1,0},{2,1},{3,2},{4,7},{5,4},{6,5},{7,6},{8,11},{9,8},{10,9... | collective-permute-start | bytes 73736 | tf_op jit(solution)/shard_map/ppermute | solution.py:92
  43.3 15.5 %collective-permute-start.4 = (f32[6,8,128]{2,1,0:T(8,128)S(1)}, f32[6,8,128]{2,1,0:T(8,128)S(1)}, u32[]{:S(2)}, u32[]{:S(2)}) collective-permute-start(f32[6,8,128]{2,1,0:T(8,128)S(1)} %get-tuple-element.41), channel_id=1, source_target_pairs={{0,2},{1,3},{2,0},{3,1},{4,6},{5,7},{6,4},{7,5},{8,10},{9,11},{10,... | collective-permute-start | bytes 73736 | tf_op jit(solution)/shard_map/ppermute | solution.py:92
  55.0 5.6 %collective-permute-start.3 = (f32[6,8,128]{2,1,0:T(8,128)S(1)}, f32[6,8,128]{2,1,0:T(8,128)S(1)}, u32[]{:S(2)}, u32[]{:S(2)}) collective-permute-start(f32[6,8,128]{2,1,0:T(8,128)S(1)} %get-tuple-element.42), channel_id=1, source_target_pairs={{0,1},{1,2},{2,3},{3,0},{4,5},{5,6},{6,7},{7,4},{8,9},{9,10},{10,1... | collective-permute-start | bytes 73736 | tf_op jit(solution)/shard_map/ppermute | solution.py:92
  57.7 1.0 %copy-start.6 = (bf16[6,32,1024]{2,1,0:T(8,128)(2,1)S(1)}, bf16[6,32,1024]{2,1,0:T(8,128)(2,1)}, u32[]{:S(2)}) copy-start(bf16[6,32,1024]{2,1,0:T(8,128)(2,1)} %get-tuple-element.22) | copy-start | bytes 1179652
  58.5 22.8 %copy-start.5 = (bf16[512,1024]{1,0:T(8,128)(2,1)S(1)}, bf16[512,1024]{1,0:T(8,128)(2,1)}, u32[]{:S(2)}) copy-start(bf16[512,1024]{1,0:T(8,128)(2,1)} %copy-done.3) | copy-start | bytes 3145732
  58.7 21.4 %collective-permute-start.13 = (bf16[6,32,1024]{2,1,0:T(8,128)(2,1)S(1)}, bf16[6,32,1024]{2,1,0:T(8,128)(2,1)S(1)}, u32[]{:S(2)}, u32[]{:S(2)}) collective-permute-start(bf16[6,32,1024]{2,1,0:T(8,128)(2,1)S(1)} %copy-done.6), channel_id=1, source_target_pairs={{0,8},{4,12},{8,0},{12,4},{1,9},{5,13},{9,1},{13,5},{2,10},{6,14},... | collective-permute-start | bytes 1179656 | tf_op jit(solution)/shard_map/ppermute | solution.py:70
  58.8 4.4 %collective-permute-start.11 = (f32[6,24,128]{2,1,0:T(8,128)S(1)}, f32[6,24,128]{2,1,0:T(8,128)S(1)}, u32[]{:S(2)}, u32[]{:S(2)}) collective-permute-start(f32[6,24,128]{2,1,0:T(8,128)S(1)} %get-tuple-element.36), channel_id=1, source_target_pairs={{0,3},{1,0},{2,1},{3,2},{4,7},{5,4},{6,5},{7,6},{8,11},{9,8},{10,9... | collective-permute-start | bytes 221192 | tf_op jit(solution)/shard_map/ppermute | solution.py:92
  60.8 5.4 %collective-permute-start.10 = (f32[6,24,128]{2,1,0:T(8,128)S(1)}, f32[6,24,128]{2,1,0:T(8,128)S(1)}, u32[]{:S(2)}, u32[]{:S(2)}) collective-permute-start(f32[6,24,128]{2,1,0:T(8,128)S(1)} %get-tuple-element.37), channel_id=1, source_target_pairs={{0,2},{1,3},{2,0},{3,1},{4,6},{5,7},{6,4},{7,5},{8,10},{9,11},{10,... | collective-permute-start | bytes 221192 | tf_op jit(solution)/shard_map/ppermute | solution.py:92
  63.2 3.9 %collective-permute-start.9 = (f32[6,24,128]{2,1,0:T(8,128)S(1)}, f32[6,24,128]{2,1,0:T(8,128)S(1)}, u32[]{:S(2)}, u32[]{:S(2)}) collective-permute-start(f32[6,24,128]{2,1,0:T(8,128)S(1)} %get-tuple-element.38), channel_id=1, source_target_pairs={{0,1},{1,2},{2,3},{3,0},{4,5},{5,6},{6,7},{7,4},{8,9},{9,10},{10,1... | collective-permute-start | bytes 221192 | tf_op jit(solution)/shard_map/ppermute | solution.py:92
  67.3 0.7 copy-start.7
  84.6 4.3 %collective-permute-start.17 = (f32[6,32,128]{2,1,0:T(8,128)S(1)}, f32[6,32,128]{2,1,0:T(8,128)S(1)}, u32[]{:S(2)}, u32[]{:S(2)}) collective-permute-start(f32[6,32,128]{2,1,0:T(8,128)S(1)} %get-tuple-element.29), channel_id=1, source_target_pairs={{0,3},{1,0},{2,1},{3,2},{4,7},{5,4},{6,5},{7,6},{8,11},{9,8},{10,9... | collective-permute-start | bytes 294920 | tf_op jit(solution)/shard_map/ppermute | solution.py:92
  85.8 6.2 %collective-permute-start.16 = (f32[6,32,128]{2,1,0:T(8,128)S(1)}, f32[6,32,128]{2,1,0:T(8,128)S(1)}, u32[]{:S(2)}, u32[]{:S(2)}) collective-permute-start(f32[6,32,128]{2,1,0:T(8,128)S(1)} %get-tuple-element.30), channel_id=1, source_target_pairs={{0,2},{1,3},{2,0},{3,1},{4,6},{5,7},{6,4},{7,5},{8,10},{9,11},{10,... | collective-permute-start | bytes 294920 | tf_op jit(solution)/shard_map/ppermute | solution.py:92
  86.3 5.7 %collective-permute-start.15 = (f32[6,32,128]{2,1,0:T(8,128)S(1)}, f32[6,32,128]{2,1,0:T(8,128)S(1)}, u32[]{:S(2)}, u32[]{:S(2)}) collective-permute-start(f32[6,32,128]{2,1,0:T(8,128)S(1)} %get-tuple-element.31), channel_id=1, source_target_pairs={{0,1},{1,2},{2,3},{3,0},{4,5},{5,6},{6,7},{7,4},{8,9},{9,10},{10,1... | collective-permute-start | bytes 294920 | tf_op jit(solution)/shard_map/ppermute | solution.py:92

commit v11 on v10

--- a/solution.py
+++ b/solution.py
@@ -33,8 +33,7 @@
         t_l = train_grads[:, layer, :]
         for k in range(n_span):
             t_parts.append(lax.dynamic_slice_in_dim(t_l, sources[k] * features, features, axis=1))
-    train_local = jnp.concatenate([t_parts[layer * n_span] for layer in range(l_dev)], axis=1)
-    train_remote = jnp.concatenate([p for i, p in enumerate(t_parts) if i % n_span], axis=1)
+    train = jnp.concatenate(t_parts, axis=1)
 
     score_scale = 1.0 / math.sqrt(l_dev * n_layer * d_full)
     slot_row = pair_slot[0]
@@ -71,25 +70,24 @@
                 pieces.append(piece)
         gate = pieces
         arrivals.append(pieces)
-        dims = (((1,), (1,)), ((), ()))
-        local = jnp.concatenate([pieces[layer * n_span] for layer in range(l_dev)], axis=-1)
-        combos = lax.dot_general(local.reshape(cap * rows, -1), train_local, dims, preferred_element_type=jnp.float32)
-        arrived = jnp.concatenate([p for i, p in enumerate(pieces) if i % n_span], axis=-1)
-        combos = combos + lax.dot_general(
-            arrived.reshape(cap * rows, -1), train_remote, dims, preferred_element_type=jnp.float32
-        )
-        combos = combos.reshape(cap, rows, tb_dev, BLOCK)
+        arrived = jnp.concatenate(pieces, axis=-1).reshape(cap * rows, -1)
+        combos = lax.dot_general(
+            arrived,
+            train,
+            (((1,), (1,)), ((), ())),
+            preferred_element_type=jnp.float32,
+        ).reshape(cap, rows, tb_dev, BLOCK)
         partial = combos.at[slot_row, :, train_row, :].get(mode="promise_in_bounds") * score_scale
         partial = jnp.where(live[:, None, None], partial, 0.0)
         partial = partial.reshape(n_layer, n_rep, per_dev, rows, BLOCK)
         n_group = n_layer * n_rep
         me = lax.axis_index("layer") * n_rep + rep_index
         flat = partial.reshape(n_group, per_dev, rows, BLOCK)
-        got = [lax.dynamic_index_in_dim(flat, me, axis=0, keepdims=False)]
-        for k in range(1, n_group):
+        got = [lax.dynamic_index_in_dim(flat, me, axis=0, keepdims=False)] + [None] * (n_group - 1)
+        for k in range(n_group - 1, 0, -1):
             perm = [(i, (i + k) % n_group) for i in range(n_group)]
             send = lax.dynamic_index_in_dim(flat, (me + k) % n_group, axis=0, keepdims=False)
-            got.append(lax.ppermute(send, ("layer", "rep"), perm))
+            got[k] = lax.ppermute(send, ("layer", "rep"), perm)
         stacked = jnp.stack(got, axis=0)
         row_owner = ((me - jnp.arange(n_group, dtype=jnp.int32) + n_group) % n_group) % n_rep
         for h in range(n_rep):

time: 94 us -> 90.2 us (0.960)
  waiting for transfers between devices: 29.5 us -> 37.6 us
  starting transfers between devices: 23.2 us -> 19.4 us
  other arithmetic: 6.58 us -> 3.6 us
  matrix products: 12.4 us -> 9.47 us
  local copies, waits for them, and re-layouts: 18.5 us -> 16.4 us
    ppermute x9, waiting for transfers between devices: 22.1 us -> 30 us  [shards(): piece = lax.ppermute(piece, 'span', perm)]
    ppermute x9, starting transfers between devices: 9.18 us -> 5.97 us  [shards(): got[k] = lax.ppermute(send, ('layer', 'rep'), perm)]
    squeeze x3 -> x0, local copies, waits for them, and re-layouts: 3.07 us -> none  [shards(): piece = sent[layer][k]]
    dot_general x6 -> x3, matrix products: 12.4 us -> 9.47 us  [shards(): lax.dot_general(arrived, train, (((1,), (1,)), ((), ())), preferred_eleme...]
    concatenate x0 -> x3, local copies, waits for them, and re-layouts: none -> 2.78 us  [shards(): arrived = jnp.concatenate(pieces, axis=-1).reshape(cap * rows, -1)]
    concatenate x2 -> x0, other arithmetic: 2.41 us -> none  [shards(): jnp.concatenate([p for i, p in enumerate(pieces) if i % n_span], axis=-1)]
    dynamic_update_slice x6, local copies, waits for them, and re-layouts: 1.97 us -> 0.06 us  [shards(): lax.dynamic_update_slice(out_buf, rows_h, (0, h * own_rows + row_start -...]
  transfers between devices with their start and end apart: 18 -> 18, of which waited for: 7 -> 8; matrix products, arithmetic and copies ran while one was open for 28% -> 22% of each run, Pallas kernels for 0% -> 0%
where the time goes in v11:
time: 90.2 us; the launch traced here: 89.5 us
  waiting for transfers between devices  37.6 us (42%)
  starting transfers between devices  19.4 us (22%)
  local copies, waits for them, and re-layouts  16.4 us (18%)
  matrix products  9.47 us (10%)
  other arithmetic  3.6 us (4%)
  between operations  3.08 us (3%)
    ppermute x9, waiting for transfers between devices, shards(): piece = lax.ppermute(piece, 'span', perm)  30 us
    ppermute x9, starting transfers between devices, shards(): piece = lax.ppermute(piece, 'span', perm)  13.4 us
    dot_general x3, matrix products, shards(): lax.dot_general(arrived, train, (((1,), (1,)), ((), ())), preferred_eleme...  9.47 us
    ppermute x9, waiting for transfers between devices, shards(): got[k] = lax.ppermute(send, ('layer', 'rep'), perm)  7.55 us
    ppermute x9, starting transfers between devices, shards(): got[k] = lax.ppermute(send, ('layer', 'rep'), perm)  5.97 us
    dynamic_slice x3, local copies, waits for them, and re-layouts, shards(): lax.dynamic_slice_in_dim(q3, rep_index * own_rows + row_start, rows, axis=1)  3.48 us
    concatenate x3, local copies, waits for them, and re-layouts, shards(): arrived = jnp.concatenate(pieces, axis=-1).reshape(cap * rows, -1)  2.78 us
    dynamic_slice x1, local copies, waits for them, and re-layouts, shards(): lax.dynamic_slice_in_dim(t_l, sources[k] * features, features, axis=1)  2.64 us
  transfers between devices with their start and end apart: 18, of which 8 were waited for; matrix products, arithmetic and copies ran while one was open for 22% of the time, Pallas kernels for 0%

profile of v11, /device:TPU:0, one launch (start us, length us, event | category | flops | bytes accessed | tf_op | source)
XLA Modules:
  0.0 89.5 jit_solution(18286246619118193815)
XLA Ops:
  0.0 0.7 copy-done
  0.7 0.6 gather_fusion
  1.2 0.1 reshape.333
  1.3 1.0 %constant_dynamic-slice_fusion.9 = bf16[16,8,1024]{2,1,0:T(8,128)(2,1)S(1)} fusion(bf16[16,128,1024]{2,1,0:T(8,128)(2,1)} %bitcast.122, s32[]{:T(128)S(6)} %select_n.227), kind=kLoop, calls=%fused_computation.88 | loop fusion | bytes 524292 | tf_op jit(solution)/shard_map/dynamic_slice | solution.py:56
  2.3 0.0 copy-start.6
  2.3 0.6 gather_fusion.1
  2.9 0.8 fusion.16
  3.7 0.7 slice_bitcast_fusion.11
  4.3 3.1 %collective-permute-start = (bf16[6,8,1024]{2,1,0:T(8,128)(2,1)}, bf16[6,8,1024]{2,1,0:T(8,128)(2,1)}, u32[]{:S(2)}, u32[]{:S(2)}) collective-permute-start(bf16[6,8,1024]{2,1,0:T(8,128)(2,1)} %get-tuple-element.36), channel_id=1, source_target_pairs={{0,4},{4,8},{8,12},{12,0},{1,5},{5,9},{9,13},{13,1},{2,6},{6,10},{... | collective-permute-start | bytes 294920 | tf_op jit(solution)/shard_map/ppermute | solution.py:69
  7.4 2.6 %collective-permute-start.1 = (bf16[6,8,1024]{2,1,0:T(8,128)(2,1)S(1)}, bf16[6,8,1024]{2,1,0:T(8,128)(2,1)}, u32[]{:S(2)}, u32[]{:S(2)}) collective-permute-start(bf16[6,8,1024]{2,1,0:T(8,128)(2,1)S(1)} %get-tuple-element.35), channel_id=1, source_target_pairs={{0,8},{4,12},{8,0},{12,4},{1,9},{5,13},{9,1},{13,5},{2,10},{6,14},... | collective-permute-start | bytes 294920 | tf_op jit(solution)/shard_map/ppermute | solution.py:69
  10.0 1.3 %collective-permute-start.2 = (bf16[6,8,1024]{2,1,0:T(8,128)(2,1)S(1)}, bf16[6,8,1024]{2,1,0:T(8,128)(2,1)}, u32[]{:S(2)}, u32[]{:S(2)}) collective-permute-start(bf16[6,8,1024]{2,1,0:T(8,128)(2,1)S(1)} %get-tuple-element.34), channel_id=1, source_target_pairs={{0,12},{4,0},{8,4},{12,8},{1,13},{5,1},{9,5},{13,9},{2,14},{6,2},{... | collective-permute-start | bytes 294920 | tf_op jit(solution)/shard_map/ppermute | solution.py:69
  11.3 1.2 %constant_dynamic-slice_fusion.3 = bf16[16,24,1024]{2,1,0:T(8,128)(2,1)S(1)} fusion(bf16[16,128,1024]{2,1,0:T(8,128)(2,1)} %bitcast.123, s32[]{:T(128)S(6)} %select_n.247), kind=kLoop, calls=%fused_computation.81 | loop fusion | bytes 1572868 | tf_op jit(solution)/shard_map/dynamic_slice | solution.py:56
  12.5 0.6 gather_fusion.3
  13.2 0.3 fusion.1
  13.5 1.1 %slice_bitcast_fusion.7 = (bf16[6,24,1024]{2,1,0:T(8,128)(2,1)}, bf16[6,24,1024]{2,1,0:T(8,128)(2,1)}, bf16[6,24,1024]{2,1,0:T(8,128)(2,1)}, bf16[6,24,1024]{2,1,0:T(8,128)(2,1)}) fusion(bf16[4,6,24,1024]{3,2,1,0:T(8,128)(2,1)S(1)} %fusion.1), kind=kLoop, calls=%fused_computation.48 | loop fusion | bytes 2359296 | tf_op jit(solution)/shard_map/concatenate | solution.py:73
  14.5 0.7 collective-permute-start.6
  15.2 0.3 collective-permute-start.7
  15.6 0.7 fusion.44
  18.8 1.3 %constant_dynamic-slice_fusion.1 = bf16[16,32,1024]{2,1,0:T(8,128)(2,1)S(1)} fusion(bf16[16,128,1024]{2,1,0:T(8,128)(2,1)} %bitcast.124, s32[]{:T(128)S(6)} %select_n.251), kind=kLoop, calls=%fused_computation.77 | loop fusion | bytes 2097156 | tf_op jit(solution)/shard_map/dynamic_slice | solution.py:56
  20.2 0.0 copy-start.7
  20.2 0.0 copy-start.8
  20.2 0.0 copy-start.9
  20.2 0.6 gather_fusion.5
  20.9 0.4 fusion
  21.3 0.7 fusion.43
  22.0 1.4 %fusion.28 = s32[24]{0:T(128)S(1)} fusion(s32[]{:T(128)} %bitcast.1, s32[]{:T(128)} %bitcast), kind=kLoop, calls=%fused_computation.120 | loop fusion | flops 312 | bytes 104 | tf_op jit(solution)/shard_map/gather | solution.py:43
  23.3 0.1 gather.32
  23.5 2.6 %constant_dynamic-slice_fusion.8 = (bf16[512,1,1024]{2,0,1:T(8,128)(2,1)S(1)}, bf16[512,1,1024]{2,0,1:T(8,128)(2,1)S(1)}, bf16[512,1,1024]{2,0,1:T(8,128)(2,1)S(1)}, bf16[512,1,1024]{2,0,1:T(8,128)(2,1)S(1)}) fusion(bf16[512,1,4096]{2,0,1:T(8,128)(2,1)} %param.8, s32[]{:T(128)S(6)} %select_n.231, s32[]{:T(128)S(6)} %select_n.232, s32[]{:T(128)S(6)} %select_n.234, ...), kind=kLoop, calls=%fused_computation.87 | loop fusion | bytes 8388624 | tf_op jit(solution)/shard_map/dynamic_slice | solution.py:35
  26.2 2.9 %collective-permute-start.8 = (bf16[6,24,1024]{2,1,0:T(8,128)(2,1)}, bf16[6,24,1024]{2,1,0:T(8,128)(2,1)}, u32[]{:S(2)}, u32[]{:S(2)}) collective-permute-start(bf16[6,24,1024]{2,1,0:T(8,128)(2,1)} %get-tuple-element.26), channel_id=1, source_target_pairs={{0,12},{4,0},{8,4},{12,8},{1,13},{5,1},{9,5},{13,9},{2,14},{6,2},{... | collective-permute-start | bytes 884744 | tf_op jit(solution)/shard_map/ppermute | solution.py:69
  29.1 0.0 collective-permute-done.1
  29.1 0.0 collective-permute-done.2
  29.1 1.0 %slice_bitcast_fusion.3 = (bf16[6,32,1024]{2,1,0:T(8,128)(2,1)S(1)}, bf16[6,32,1024]{2,1,0:T(8,128)(2,1)S(1)}, bf16[6,32,1024]{2,1,0:T(8,128)(2,1)}, bf16[6,32,1024]{2,1,0:T(8,128)(2,1)}) fusion(bf16[4,6,32,1024]{3,2,1,0:T(8,128)(2,1)S(1)} %fusion), kind=kLoop, calls=%fused_computation.44 | loop fusion | bytes 3145728 | tf_op jit(solution)/shard_map/concatenate | solution.py:73
  30.1 2.5 %collective-permute-start.12 = (bf16[6,32,1024]{2,1,0:T(8,128)(2,1)}, bf16[6,32,1024]{2,1,0:T(8,128)(2,1)}, u32[]{:S(2)}, u32[]{:S(2)}) collective-permute-start(bf16[6,32,1024]{2,1,0:T(8,128)(2,1)} %get-tuple-element.24), channel_id=1, source_target_pairs={{0,4},{4,8},{8,12},{12,0},{1,5},{5,9},{9,13},{13,1},{2,6},{6,10},{... | collective-permute-start | bytes 1179656 | tf_op jit(solution)/shard_map/ppermute | solution.py:69
  32.6 2.4 %fusion.17 = f32[6,8,4,128]{3,1,2,0:T(8,128)S(1)} fusion(bf16[6,8,1024]{2,1,0:T(8,128)(2,1)} %collective-permute-done.2, bf16[6,8,1024]{2,1,0:T(8,128)(2,1)} %collective-permute-done.1, bf16[6,8,1024]{2,1,0:T(8,128)(2,1)} %collective-permute-done, bf16[6,8,1024]{2,1,0:T(8,128)(2,1)S(1)} %get-tuple-element.33, bf16[4,128,1024]{2,1,0:T(8,128)(2,1)S(1)} %bitcast.116, ...), kind=kOutput, calls=%fused_computation.31 | convolution fusion | flops 219676672 | bytes 4685824 | tf_op jit(solution)/shard_map/dot_general | solution.py:74
  35.0 0.7 gather_fusion.2
  35.7 0.1 broadcast_select_fusion.2
  35.9 0.1 collective-permute-start.3
  35.9 18.9 %collective-permute-done.7 = bf16[6,24,1024]{2,1,0:T(8,128)(2,1)} collective-permute-done((bf16[6,24,1024]{2,1,0:T(8,128)(2,1)}, bf16[6,24,1024]{2,1,0:T(8,128)(2,1)}, u32[]{:S(2)}, u32[]{:S(2)}) %collective-permute-start.7) | collective-permute-done | bytes 294944 | tf_op jit(solution)/shard_map/ppermute | solution.py:69
  54.8 1.5 %collective-permute-start.4 = (f32[6,8,128]{2,1,0:T(8,128)S(1)}, f32[6,8,128]{2,1,0:T(8,128)S(1)}, u32[]{:S(2)}, u32[]{:S(2)}) collective-permute-start(f32[6,8,128]{2,1,0:T(8,128)S(1)} %get-tuple-element.43), channel_id=1, source_target_pairs={{0,2},{1,3},{2,0},{3,1},{4,6},{5,7},{6,4},{7,5},{8,10},{9,11},{10,... | collective-permute-start | bytes 73736 | tf_op jit(solution)/shard_map/ppermute | solution.py:90
  56.4 3.4 %fusion.9 = f32[6,24,4,128]{3,1,2,0:T(8,128)S(1)} fusion(bf16[6,24,1024]{2,1,0:T(8,128)(2,1)} %collective-permute-done.8, bf16[6,24,1024]{2,1,0:T(8,128)(2,1)} %collective-permute-done.7, bf16[6,24,1024]{2,1,0:T(8,128)(2,1)} %collective-permute-done.6, bf16[6,24,1024]{2,1,0:T(8,128)(2,1)S(1)} %copy-done.5, bf16[4,128,1024]{2,1,0:T(8,128)(2,1)} %bitcast.117, ...), kind=kOutput, calls=%fused_computation.21 | convolution fusion | flops 625475584 | bytes 5668864 | tf_op jit(solution)/shard_map/dot_general | solution.py:74
  59.8 0.7 gather_fusion.4
  60.5 0.1 broadcast_select_fusion.1
  60.7 0.1 collective-permute-start.14
  60.8 0.5 collective-permute-start.9
  61.3 0.1 select_reduce_fusion.4
  61.4 0.9 collective-permute-start.10
  62.3 2.3 %collective-permute-done.9 = f32[6,24,128]{2,1,0:T(8,128)S(1)} collective-permute-done((f32[6,24,128]{2,1,0:T(8,128)S(1)}, f32[6,24,128]{2,1,0:T(8,128)S(1)}, u32[]{:S(2)}, u32[]{:S(2)}) %collective-permute-start.9) | collective-permute-done | bytes 73760 | tf_op jit(solution)/shard_map/ppermute | solution.py:90
  64.6 1.9 %collective-permute-done.10 = f32[6,24,128]{2,1,0:T(8,128)S(1)} collective-permute-done((f32[6,24,128]{2,1,0:T(8,128)S(1)}, f32[6,24,128]{2,1,0:T(8,128)S(1)}, u32[]{:S(2)}, u32[]{:S(2)}) %collective-permute-start.10) | collective-permute-done | bytes 73760 | tf_op jit(solution)/shard_map/ppermute | solution.py:90
  66.5 0.0 collective-permute-done.11
  66.6 0.1 select_reduce_fusion.2
  66.7 2.9 %collective-permute-done.13 = bf16[6,32,1024]{2,1,0:T(8,128)(2,1)} collective-permute-done((bf16[6,32,1024]{2,1,0:T(8,128)(2,1)}, bf16[6,32,1024]{2,1,0:T(8,128)(2,1)}, u32[]{:S(2)}, u32[]{:S(2)}) %collective-permute-start.13) | collective-permute-done | bytes 393248 | tf_op jit(solution)/shard_map/ppermute | solution.py:69
  69.6 8.2 %collective-permute-done.14 = bf16[6,32,1024]{2,1,0:T(8,128)(2,1)S(1)} collective-permute-done((bf16[6,32,1024]{2,1,0:T(8,128)(2,1)S(1)}, bf16[6,32,1024]{2,1,0:T(8,128)(2,1)S(1)}, u32[]{:S(2)}, u32[]{:S(2)}) %collective-permute-start.14) | collective-permute-done | bytes 393248 | tf_op jit(solution)/shard_map/ppermute | solution.py:69
  77.8 3.6 %fusion.2 = f32[6,32,4,128]{3,1,2,0:T(8,128)S(1)} fusion(bf16[6,32,1024]{2,1,0:T(8,128)(2,1)S(1)} %collective-permute-done.14, bf16[6,32,1024]{2,1,0:T(8,128)(2,1)} %collective-permute-done.13, bf16[6,32,1024]{2,1,0:T(8,128)(2,1)} %collective-permute-done.12, bf16[6,32,1024]{2,1,0:T(8,128)(2,1)S(1)} %get-tuple-element.21, ...), kind=kOutput, calls=%fused_computation.13 | convolution fusion | flops 828375040 | bytes 6160384 | tf_op jit(solution)/shard_map/dot_general | solution.py:74
  81.5 0.7 gather_fusion.6
  82.2 0.1 broadcast_select_fusion
  82.4 0.1 collective-permute-start.15
  82.4 1.6 %collective-permute-start.16 = (f32[6,32,128]{2,1,0:T(8,128)S(1)}, f32[6,32,128]{2,1,0:T(8,128)S(1)}, u32[]{:S(2)}, u32[]{:S(2)}) collective-permute-start(f32[6,32,128]{2,1,0:T(8,128)S(1)} %get-tuple-element.31), channel_id=1, source_target_pairs={{0,2},{1,3},{2,0},{3,1},{4,6},{5,7},{6,4},{7,5},{8,10},{9,11},{10,... | collective-permute-start | bytes 294920 | tf_op jit(solution)/shard_map/ppermute | solution.py:90
  84.0 1.4 %collective-permute-start.17 = (f32[6,32,128]{2,1,0:T(8,128)S(1)}, f32[6,32,128]{2,1,0:T(8,128)S(1)}, u32[]{:S(2)}, u32[]{:S(2)}) collective-permute-start(f32[6,32,128]{2,1,0:T(8,128)S(1)} %get-tuple-element.30), channel_id=1, source_target_pairs={{0,3},{1,0},{2,1},{3,2},{4,7},{5,4},{6,5},{7,6},{8,11},{9,8},{10,9... | collective-permute-start | bytes 294920 | tf_op jit(solution)/shard_map/ppermute | solution.py:90
  85.4 1.5 %collective-permute-done.15 = f32[6,32,128]{2,1,0:T(8,128)S(1)} collective-permute-done((f32[6,32,128]{2,1,0:T(8,128)S(1)}, f32[6,32,128]{2,1,0:T(8,128)S(1)}, u32[]{:S(2)}, u32[]{:S(2)}) %collective-permute-start.15) | collective-permute-done | bytes 98336 | tf_op jit(solution)/shard_map/ppermute | solution.py:90
  86.8 1.3 %collective-permute-done.16 = f32[6,32,128]{2,1,0:T(8,128)S(1)} collective-permute-done((f32[6,32,128]{2,1,0:T(8,128)S(1)}, f32[6,32,128]{2,1,0:T(8,128)S(1)}, u32[]{:S(2)}, u32[]{:S(2)}) %collective-permute-start.16) | collective-permute-done | bytes 98336 | tf_op jit(solution)/shard_map/ppermute | solution.py:90
  88.2 0.5 collective-permute-done.17
  88.6 0.1 select_reduce_fusion
  88.8 0.0 copy-start.4
  88.8 0.7 copy-done.4
  (44 shorter events, 0.4 us)
Async XLA Ops:
  0.0 0.7 copy-start
  2.3 10.9 %copy-start.6 = (f32[1,1024]{1,0:T(1,128)S(1)}, f32[1,1024]{1,0:T(1,128)}, u32[]{:S(2)}) copy-start(f32[1,1024]{1,0:T(1,128)} %param.9) | copy-start | bytes 12292
  4.3 21.8 %collective-permute-start = (bf16[6,8,1024]{2,1,0:T(8,128)(2,1)}, bf16[6,8,1024]{2,1,0:T(8,128)(2,1)}, u32[]{:S(2)}, u32[]{:S(2)}) collective-permute-start(bf16[6,8,1024]{2,1,0:T(8,128)(2,1)} %get-tuple-element.36), channel_id=1, source_target_pairs={{0,4},{4,8},{8,12},{12,0},{1,5},{5,9},{9,13},{13,1},{2,6},{6,10},{... | collective-permute-start | bytes 294920 | tf_op jit(solution)/shard_map/ppermute | solution.py:69
  7.4 21.7 %collective-permute-start.1 = (bf16[6,8,1024]{2,1,0:T(8,128)(2,1)S(1)}, bf16[6,8,1024]{2,1,0:T(8,128)(2,1)}, u32[]{:S(2)}, u32[]{:S(2)}) collective-permute-start(bf16[6,8,1024]{2,1,0:T(8,128)(2,1)S(1)} %get-tuple-element.35), channel_id=1, source_target_pairs={{0,8},{4,12},{8,0},{12,4},{1,9},{5,13},{9,1},{13,5},{2,10},{6,14},... | collective-permute-start | bytes 294920 | tf_op jit(solution)/shard_map/ppermute | solution.py:69
  10.0 19.1 %collective-permute-start.2 = (bf16[6,8,1024]{2,1,0:T(8,128)(2,1)S(1)}, bf16[6,8,1024]{2,1,0:T(8,128)(2,1)}, u32[]{:S(2)}, u32[]{:S(2)}) collective-permute-start(bf16[6,8,1024]{2,1,0:T(8,128)(2,1)S(1)} %get-tuple-element.34), channel_id=1, source_target_pairs={{0,12},{4,0},{8,4},{12,8},{1,13},{5,1},{9,5},{13,9},{2,14},{6,2},{... | collective-permute-start | bytes 294920 | tf_op jit(solution)/shard_map/ppermute | solution.py:69
  14.5 21.3 %collective-permute-start.6 = (bf16[6,24,1024]{2,1,0:T(8,128)(2,1)}, bf16[6,24,1024]{2,1,0:T(8,128)(2,1)}, u32[]{:S(2)}, u32[]{:S(2)}) collective-permute-start(bf16[6,24,1024]{2,1,0:T(8,128)(2,1)} %get-tuple-element.28), channel_id=1, source_target_pairs={{0,4},{4,8},{8,12},{12,0},{1,5},{5,9},{9,13},{13,1},{2,6},{6,10},{... | collective-permute-start | bytes 884744 | tf_op jit(solution)/shard_map/ppermute | solution.py:69
  15.2 39.6 %collective-permute-start.7 = (bf16[6,24,1024]{2,1,0:T(8,128)(2,1)}, bf16[6,24,1024]{2,1,0:T(8,128)(2,1)}, u32[]{:S(2)}, u32[]{:S(2)}) collective-permute-start(bf16[6,24,1024]{2,1,0:T(8,128)(2,1)} %get-tuple-element.27), channel_id=1, source_target_pairs={{0,8},{4,12},{8,0},{12,4},{1,9},{5,13},{9,1},{13,5},{2,10},{6,14},... | collective-permute-start | bytes 884744 | tf_op jit(solution)/shard_map/ppermute | solution.py:69
  20.2 1.1 %copy-start.7 = (s32[1,2]{1,0:T(1,128)S(1)}, s32[1,2]{1,0:T(1,128)}, u32[]{:S(2)}) copy-start(s32[1,2]{1,0:T(1,128)} %param.13) | copy-start | bytes 28
  20.2 3.3 %copy-start.8 = (s32[1,24]{1,0:T(1,128)S(1)}, s32[1,24]{1,0:T(1,128)}, u32[]{:S(2)}) copy-start(s32[1,24]{1,0:T(1,128)} %param.12) | copy-start | bytes 292
  20.2 3.3 %copy-start.9 = (s32[1,24]{1,0:T(1,128)S(1)}, s32[1,24]{1,0:T(1,128)}, u32[]{:S(2)}) copy-start(s32[1,24]{1,0:T(1,128)} %param.11) | copy-start | bytes 292
  26.1 6.5 %copy-start.1 = (bf16[512,1,1024]{2,0,1:T(8,128)(2,1)}, bf16[512,1,1024]{2,0,1:T(8,128)(2,1)S(1)}, u32[]{:S(2)}) copy-start(bf16[512,1,1024]{2,0,1:T(8,128)(2,1)S(1)} %get-tuple-element.18) | copy-start | bytes 3145732
  26.1 6.5 %copy-start.2 = (bf16[512,1,1024]{2,0,1:T(8,128)(2,1)}, bf16[512,1,1024]{2,0,1:T(8,128)(2,1)S(1)}, u32[]{:S(2)}) copy-start(bf16[512,1,1024]{2,0,1:T(8,128)(2,1)S(1)} %get-tuple-element.19) | copy-start | bytes 3145732
  26.2 6.5 %copy-start.3 = (bf16[512,1,1024]{2,0,1:T(8,128)(2,1)}, bf16[512,1,1024]{2,0,1:T(8,128)(2,1)S(1)}, u32[]{:S(2)}) copy-start(bf16[512,1,1024]{2,0,1:T(8,128)(2,1)S(1)} %get-tuple-element.20) | copy-start | bytes 3145732
  26.2 30.1 %collective-permute-start.8 = (bf16[6,24,1024]{2,1,0:T(8,128)(2,1)}, bf16[6,24,1024]{2,1,0:T(8,128)(2,1)}, u32[]{:S(2)}, u32[]{:S(2)}) collective-permute-start(bf16[6,24,1024]{2,1,0:T(8,128)(2,1)} %get-tuple-element.26), channel_id=1, source_target_pairs={{0,12},{4,0},{8,4},{12,8},{1,13},{5,1},{9,5},{13,9},{2,14},{6,2},{... | collective-permute-start | bytes 884744 | tf_op jit(solution)/shard_map/ppermute | solution.py:69
  30.1 36.6 %collective-permute-start.12 = (bf16[6,32,1024]{2,1,0:T(8,128)(2,1)}, bf16[6,32,1024]{2,1,0:T(8,128)(2,1)}, u32[]{:S(2)}, u32[]{:S(2)}) collective-permute-start(bf16[6,32,1024]{2,1,0:T(8,128)(2,1)} %get-tuple-element.24), channel_id=1, source_target_pairs={{0,4},{4,8},{8,12},{12,0},{1,5},{5,9},{9,13},{13,1},{2,6},{6,10},{... | collective-permute-start | bytes 1179656 | tf_op jit(solution)/shard_map/ppermute | solution.py:69
  32.6 37.0 %collective-permute-start.13 = (bf16[6,32,1024]{2,1,0:T(8,128)(2,1)}, bf16[6,32,1024]{2,1,0:T(8,128)(2,1)}, u32[]{:S(2)}, u32[]{:S(2)}) collective-permute-start(bf16[6,32,1024]{2,1,0:T(8,128)(2,1)} %get-tuple-element.23), channel_id=1, source_target_pairs={{0,8},{4,12},{8,0},{12,4},{1,9},{5,13},{9,1},{13,5},{2,10},{6,14},... | collective-permute-start | bytes 1179656 | tf_op jit(solution)/shard_map/ppermute | solution.py:69
  32.6 23.7 %copy-start.5 = (bf16[6,24,1024]{2,1,0:T(8,128)(2,1)S(1)}, bf16[6,24,1024]{2,1,0:T(8,128)(2,1)}, u32[]{:S(2)}) copy-start(bf16[6,24,1024]{2,1,0:T(8,128)(2,1)} %get-tuple-element.25) | copy-start | bytes 884740
  35.9 24.8 %collective-permute-start.3 = (f32[6,8,128]{2,1,0:T(8,128)S(1)}, f32[6,8,128]{2,1,0:T(8,128)S(1)}, u32[]{:S(2)}, u32[]{:S(2)}) collective-permute-start(f32[6,8,128]{2,1,0:T(8,128)S(1)} %get-tuple-element.44), channel_id=1, source_target_pairs={{0,1},{1,2},{2,3},{3,0},{4,5},{5,6},{6,7},{7,4},{8,9},{9,10},{10,1... | collective-permute-start | bytes 73736 | tf_op jit(solution)/shard_map/ppermute | solution.py:90
  54.8 5.9 %collective-permute-start.4 = (f32[6,8,128]{2,1,0:T(8,128)S(1)}, f32[6,8,128]{2,1,0:T(8,128)S(1)}, u32[]{:S(2)}, u32[]{:S(2)}) collective-permute-start(f32[6,8,128]{2,1,0:T(8,128)S(1)} %get-tuple-element.43), channel_id=1, source_target_pairs={{0,2},{1,3},{2,0},{3,1},{4,6},{5,7},{6,4},{7,5},{8,10},{9,11},{10,... | collective-permute-start | bytes 73736 | tf_op jit(solution)/shard_map/ppermute | solution.py:90
  56.3 4.9 %collective-permute-start.5 = (f32[6,8,128]{2,1,0:T(8,128)S(1)}, f32[6,8,128]{2,1,0:T(8,128)S(1)}, u32[]{:S(2)}, u32[]{:S(2)}) collective-permute-start(f32[6,8,128]{2,1,0:T(8,128)S(1)} %get-tuple-element.42), channel_id=1, source_target_pairs={{0,3},{1,0},{2,1},{3,2},{4,7},{5,4},{6,5},{7,6},{8,11},{9,8},{10,9... | collective-permute-start | bytes 73736 | tf_op jit(solution)/shard_map/ppermute | solution.py:90
  60.7 17.1 %collective-permute-start.14 = (bf16[6,32,1024]{2,1,0:T(8,128)(2,1)S(1)}, bf16[6,32,1024]{2,1,0:T(8,128)(2,1)S(1)}, u32[]{:S(2)}, u32[]{:S(2)}) collective-permute-start(bf16[6,32,1024]{2,1,0:T(8,128)(2,1)S(1)} %get-tuple-element.22), channel_id=1, source_target_pairs={{0,12},{4,0},{8,4},{12,8},{1,13},{5,1},{9,5},{13,9},{2,14},{6,2},{... | collective-permute-start | bytes 1179656 | tf_op jit(solution)/shard_map/ppermute | solution.py:69
  60.8 3.8 %collective-permute-start.9 = (f32[6,24,128]{2,1,0:T(8,128)S(1)}, f32[6,24,128]{2,1,0:T(8,128)S(1)}, u32[]{:S(2)}, u32[]{:S(2)}) collective-permute-start(f32[6,24,128]{2,1,0:T(8,128)S(1)} %get-tuple-element.40), channel_id=1, source_target_pairs={{0,1},{1,2},{2,3},{3,0},{4,5},{5,6},{6,7},{7,4},{8,9},{9,10},{10,1... | collective-permute-start | bytes 221192 | tf_op jit(solution)/shard_map/ppermute | solution.py:90
  61.4 5.1 %collective-permute-start.10 = (f32[6,24,128]{2,1,0:T(8,128)S(1)}, f32[6,24,128]{2,1,0:T(8,128)S(1)}, u32[]{:S(2)}, u32[]{:S(2)}) collective-permute-start(f32[6,24,128]{2,1,0:T(8,128)S(1)} %get-tuple-element.39), channel_id=1, source_target_pairs={{0,2},{1,3},{2,0},{3,1},{4,6},{5,7},{6,4},{7,5},{8,10},{9,11},{10,... | collective-permute-start | bytes 221192 | tf_op jit(solution)/shard_map/ppermute | solution.py:90
  64.6 2.0 %collective-permute-start.11 = (f32[6,24,128]{2,1,0:T(8,128)S(1)}, f32[6,24,128]{2,1,0:T(8,128)S(1)}, u32[]{:S(2)}, u32[]{:S(2)}) collective-permute-start(f32[6,24,128]{2,1,0:T(8,128)S(1)} %get-tuple-element.38), channel_id=1, source_target_pairs={{0,3},{1,0},{2,1},{3,2},{4,7},{5,4},{6,5},{7,6},{8,11},{9,8},{10,9... | collective-permute-start | bytes 221192 | tf_op jit(solution)/shard_map/ppermute | solution.py:90
  82.4 4.5 %collective-permute-start.15 = (f32[6,32,128]{2,1,0:T(8,128)S(1)}, f32[6,32,128]{2,1,0:T(8,128)S(1)}, u32[]{:S(2)}, u32[]{:S(2)}) collective-permute-start(f32[6,32,128]{2,1,0:T(8,128)S(1)} %get-tuple-element.32), channel_id=1, source_target_pairs={{0,1},{1,2},{2,3},{3,0},{4,5},{5,6},{6,7},{7,4},{8,9},{9,10},{10,1... | collective-permute-start | bytes 294920 | tf_op jit(solution)/shard_map/ppermute | solution.py:90
  82.4 5.7 %collective-permute-start.16 = (f32[6,32,128]{2,1,0:T(8,128)S(1)}, f32[6,32,128]{2,1,0:T(8,128)S(1)}, u32[]{:S(2)}, u32[]{:S(2)}) collective-permute-start(f32[6,32,128]{2,1,0:T(8,128)S(1)} %get-tuple-element.31), channel_id=1, source_target_pairs={{0,2},{1,3},{2,0},{3,1},{4,6},{5,7},{6,4},{7,5},{8,10},{9,11},{10,... | collective-permute-start | bytes 294920 | tf_op jit(solution)/shard_map/ppermute | solution.py:90
  84.0 4.6 %collective-permute-start.17 = (f32[6,32,128]{2,1,0:T(8,128)S(1)}, f32[6,32,128]{2,1,0:T(8,128)S(1)}, u32[]{:S(2)}, u32[]{:S(2)}) collective-permute-start(f32[6,32,128]{2,1,0:T(8,128)S(1)} %get-tuple-element.30), channel_id=1, source_target_pairs={{0,3},{1,0},{2,1},{3,2},{4,7},{5,4},{6,5},{7,6},{8,11},{9,8},{10,9... | collective-permute-start | bytes 294920 | tf_op jit(solution)/shard_map/ppermute | solution.py:90
  88.8 0.7 copy-start.4

commit v12 on v11

--- a/solution.py
+++ b/solution.py
@@ -7,7 +7,7 @@
 
 
 BLOCK = 128
-ROW_SPLIT = (8, 24, 32)
+ROW_SPLIT = (8, 16, 40)
 GATE_FROM = {2: 0}
 
 
@@ -83,11 +83,11 @@
         n_group = n_layer * n_rep
         me = lax.axis_index("layer") * n_rep + rep_index
         flat = partial.reshape(n_group, per_dev, rows, BLOCK)
-        got = [lax.dynamic_index_in_dim(flat, me, axis=0, keepdims=False)] + [None] * (n_group - 1)
-        for k in range(n_group - 1, 0, -1):
+        got = [lax.dynamic_index_in_dim(flat, me, axis=0, keepdims=False)]
+        for k in range(1, n_group):
             perm = [(i, (i + k) % n_group) for i in range(n_group)]
             send = lax.dynamic_index_in_dim(flat, (me + k) % n_group, axis=0, keepdims=False)
-            got[k] = lax.ppermute(send, ("layer", "rep"), perm)
+            got.append(lax.ppermute(send, ("layer", "rep"), perm))
         stacked = jnp.stack(got, axis=0)
         row_owner = ((me - jnp.arange(n_group, dtype=jnp.int32) + n_group) % n_group) % n_rep
         for h in range(n_rep):

time: 90.2 us -> 94.1 us (1.043)
  the two profiles are of different devices: /device:TPU:0 before, /device:TPU:13 now
where the time goes in v12:
time: 94.1 us; the launch traced here: 93.4 us
  starting transfers between devices  39.4 us (42%)
  local copies, waits for them, and re-layouts  21.3 us (23%)
  waiting for transfers between devices  11.7 us (12%)
  matrix products  9.54 us (10%)
  other arithmetic  8.52 us (9%)
  between operations  2.95 us (3%)
    ppermute x9, starting transfers between devices, shards(): got.append(lax.ppermute(send, ('layer', 'rep'), perm))  29.4 us
    ppermute x9, starting transfers between devices, shards(): piece = lax.ppermute(piece, 'span', perm)  10 us
    ppermute x9, waiting for transfers between devices, shards(): got.append(lax.ppermute(send, ('layer', 'rep'), perm))  9.92 us
    dot_general x3, matrix products, shards(): lax.dot_general(arrived, train, (((1,), (1,)), ((), ())), preferred_eleme...  9.54 us
    dynamic_slice x3, local copies, waits for them, and re-layouts, shards(): lax.dynamic_slice_in_dim(q3, rep_index * own_rows + row_start, rows, axis=1)  3.47 us
    gather x3, local copies, waits for them, and re-layouts, shards(): jnp.take(q3, block_ids, axis=0, mode='clip')  3.19 us
    reduce_sum x3, other arithmetic, shards(): jnp.sum(jnp.where((row_owner == h)[:, None, None, None], stacked, 0.0), a...  3.11 us
    concatenate x3, local copies, waits for them, and re-layouts, shards(): arrived = jnp.concatenate(pieces, axis=-1).reshape(cap * rows, -1)  3.07 us
  transfers between devices with their start and end apart: 18, of which 8 were waited for; matrix products, arithmetic and copies ran while one was open for 30% of the time, Pallas kernels for 0%

profile of v12, /device:TPU:13, one launch (start us, length us, event | category | flops | bytes accessed | tf_op | source)
XLA Modules:
  0.0 93.4 jit_solution(7005098658747401728)
XLA Ops:
  0.0 0.7 copy-done
  0.7 0.6 gather_fusion
  1.2 0.1 reshape.333
  1.3 1.0 %constant_dynamic-slice_fusion.9 = bf16[16,8,1024]{2,1,0:T(8,128)(2,1)S(1)} fusion(bf16[16,128,1024]{2,1,0:T(8,128)(2,1)} %bitcast.121, s32[]{:T(128)S(6)} %select_n.227), kind=kLoop, calls=%fused_computation.88 | loop fusion | bytes 524292 | tf_op jit(solution)/shard_map/dynamic_slice | solution.py:56
  2.3 0.6 gather_fusion.1
  2.9 0.8 fusion.16
  3.7 0.7 slice_bitcast_fusion.11
  4.4 1.3 %collective-permute-start = (bf16[6,8,1024]{2,1,0:T(8,128)(2,1)}, bf16[6,8,1024]{2,1,0:T(8,128)(2,1)}, u32[]{:S(2)}, u32[]{:S(2)}) collective-permute-start(bf16[6,8,1024]{2,1,0:T(8,128)(2,1)} %get-tuple-element.36), channel_id=1, source_target_pairs={{0,4},{4,8},{8,12},{12,0},{1,5},{5,9},{9,13},{13,1},{2,6},{6,10},{... | collective-permute-start | bytes 294920 | tf_op jit(solution)/shard_map/ppermute | solution.py:69
  5.7 1.0 %collective-permute-start.1 = (bf16[6,8,1024]{2,1,0:T(8,128)(2,1)}, bf16[6,8,1024]{2,1,0:T(8,128)(2,1)}, u32[]{:S(2)}, u32[]{:S(2)}) collective-permute-start(bf16[6,8,1024]{2,1,0:T(8,128)(2,1)} %get-tuple-element.35), channel_id=1, source_target_pairs={{0,8},{4,12},{8,0},{12,4},{1,9},{5,13},{9,1},{13,5},{2,10},{6,14},... | collective-permute-start | bytes 294920 | tf_op jit(solution)/shard_map/ppermute | solution.py:69
  6.7 1.5 %collective-permute-start.2 = (bf16[6,8,1024]{2,1,0:T(8,128)(2,1)}, bf16[6,8,1024]{2,1,0:T(8,128)(2,1)}, u32[]{:S(2)}, u32[]{:S(2)}) collective-permute-start(bf16[6,8,1024]{2,1,0:T(8,128)(2,1)} %get-tuple-element.34), channel_id=1, source_target_pairs={{0,12},{4,0},{8,4},{12,8},{1,13},{5,1},{9,5},{13,9},{2,14},{6,2},{... | collective-permute-start | bytes 294920 | tf_op jit(solution)/shard_map/ppermute | solution.py:69
  8.2 1.1 %constant_dynamic-slice_fusion.3 = bf16[16,16,1024]{2,1,0:T(8,128)(2,1)S(1)} fusion(bf16[16,128,1024]{2,1,0:T(8,128)(2,1)} %bitcast.122, s32[]{:T(128)S(6)} %select_n.247), kind=kLoop, calls=%fused_computation.81 | loop fusion | bytes 1048580 | tf_op jit(solution)/shard_map/dynamic_slice | solution.py:56
  9.2 0.6 gather_fusion.3
  9.9 0.2 fusion.8
  10.1 0.8 slice_bitcast_fusion.7
  10.9 3.1 %collective-permute-start.7 = (bf16[6,16,1024]{2,1,0:T(8,128)(2,1)}, bf16[6,16,1024]{2,1,0:T(8,128)(2,1)}, u32[]{:S(2)}, u32[]{:S(2)}) collective-permute-start(bf16[6,16,1024]{2,1,0:T(8,128)(2,1)} %get-tuple-element.27), channel_id=1, source_target_pairs={{0,8},{4,12},{8,0},{12,4},{1,9},{5,13},{9,1},{13,5},{2,10},{6,14},... | collective-permute-start | bytes 589832 | tf_op jit(solution)/shard_map/ppermute | solution.py:69
  14.0 0.7 fusion.44
  17.2 1.4 %constant_dynamic-slice_fusion.1 = bf16[16,40,1024]{2,1,0:T(8,128)(2,1)S(1)} fusion(bf16[16,128,1024]{2,1,0:T(8,128)(2,1)} %bitcast.123, s32[]{:T(128)S(6)} %select_n.251), kind=kLoop, calls=%fused_computation.77 | loop fusion | bytes 2621444 | tf_op jit(solution)/shard_map/dynamic_slice | solution.py:56
  18.7 0.0 copy-start.8
  18.7 0.0 copy-start.9
  18.7 0.0 copy-start.10
  18.7 2.0 %gather_fusion.5 = bf16[24,40,1024]{2,1,0:T(8,128)(2,1)} fusion(bf16[16,40,1024]{2,1,0:T(8,128)(2,1)S(1)} %constant_dynamic-slice_fusion.1, s32[1024]{0:T(1024)S(1)} %pad_clamp_fusion), kind=kCustom, calls=%fused_computation.5 | custom fusion | bytes 3932256 | tf_op jit(solution)/shard_map/jit(_take)/gather | solution.py:57
  20.7 2.1 %fusion = bf16[4,6,40,1024]{3,2,1,0:T(8,128)(2,1)S(1)} fusion(bf16[4,6,40,1024]{3,2,1,0:T(8,128)(2,1)} %bitcast.105, f32[1024]{0:T(1024)S(1)} %bitcast.134), kind=kLoop, calls=%fused_computation.9 | loop fusion | flops 2949120 | bytes 3936256 | tf_op jit(solution)/shard_map/convert_element_type | solution.py:58
  22.8 0.7 fusion.43
  23.5 1.3 %fusion.28 = s32[24]{0:T(128)S(1)} fusion(s32[]{:T(128)} %bitcast.1, s32[]{:T(128)} %bitcast), kind=kLoop, calls=%fused_computation.120 | loop fusion | flops 312 | bytes 104 | tf_op jit(solution)/shard_map/gather | solution.py:43
  24.8 0.1 gather.32
  24.9 2.6 %constant_dynamic-slice_fusion.8 = (bf16[512,1,1024]{2,0,1:T(8,128)(2,1)S(1)}, bf16[512,1,1024]{2,0,1:T(8,128)(2,1)S(1)}, bf16[512,1,1024]{2,0,1:T(8,128)(2,1)S(1)}, bf16[512,1,1024]{2,0,1:T(8,128)(2,1)S(1)}) fusion(bf16[512,1,4096]{2,0,1:T(8,128)(2,1)} %param.8, s32[]{:T(128)S(6)} %select_n.231, s32[]{:T(128)S(6)} %select_n.232, s32[]{:T(128)S(6)} %select_n.234, ...), kind=kLoop, calls=%fused_computation.87 | loop fusion | bytes 8388624 | tf_op jit(solution)/shard_map/dynamic_slice | solution.py:35
  27.6 0.7 broadcast_compare_fusion
  28.3 0.0 collective-permute-start.8
  28.3 1.6 %slice_bitcast_fusion.3 = (bf16[6,40,1024]{2,1,0:T(8,128)(2,1)}, bf16[6,40,1024]{2,1,0:T(8,128)(2,1)}, bf16[6,40,1024]{2,1,0:T(8,128)(2,1)}, bf16[6,40,1024]{2,1,0:T(8,128)(2,1)}) fusion(bf16[4,6,40,1024]{3,2,1,0:T(8,128)(2,1)S(1)} %fusion), kind=kLoop, calls=%fused_computation.36 | loop fusion | bytes 3932160 | tf_op jit(solution)/shard_map/concatenate | solution.py:73
  29.9 1.3 %collective-permute-start.12 = (bf16[6,40,1024]{2,1,0:T(8,128)(2,1)}, bf16[6,40,1024]{2,1,0:T(8,128)(2,1)}, u32[]{:S(2)}, u32[]{:S(2)}) collective-permute-start(bf16[6,40,1024]{2,1,0:T(8,128)(2,1)} %get-tuple-element.24), channel_id=1, source_target_pairs={{0,4},{4,8},{8,12},{12,0},{1,5},{5,9},{9,13},{13,1},{2,6},{6,10},{... | collective-permute-start | bytes 1474568 | tf_op jit(solution)/shard_map/ppermute | solution.py:69
  31.1 1.8 %collective-permute-start.13 = (bf16[6,40,1024]{2,1,0:T(8,128)(2,1)}, bf16[6,40,1024]{2,1,0:T(8,128)(2,1)}, u32[]{:S(2)}, u32[]{:S(2)}) collective-permute-start(bf16[6,40,1024]{2,1,0:T(8,128)(2,1)} %get-tuple-element.23), channel_id=1, source_target_pairs={{0,8},{4,12},{8,0},{12,4},{1,9},{5,13},{9,1},{13,5},{2,10},{6,14},... | collective-permute-start | bytes 1474568 | tf_op jit(solution)/shard_map/ppermute | solution.py:69
  32.9 2.3 %fusion.17 = f32[6,8,4,128]{3,1,2,0:T(8,128)S(1)} fusion(bf16[6,8,1024]{2,1,0:T(8,128)(2,1)} %collective-permute-done.2, bf16[6,8,1024]{2,1,0:T(8,128)(2,1)} %collective-permute-done.1, bf16[6,8,1024]{2,1,0:T(8,128)(2,1)} %collective-permute-done, bf16[6,8,1024]{2,1,0:T(8,128)(2,1)S(1)} %get-tuple-element.33, bf16[4,128,1024]{2,1,0:T(8,128)(2,1)S(1)} %bitcast.115, ...), kind=kOutput, calls=%fused_computation.38 | convolution fusion | flops 219676672 | bytes 4685824 | tf_op jit(solution)/shard_map/dot_general | solution.py:74
  35.3 0.7 gather_fusion.2
  36.0 0.1 broadcast_select_fusion.2
  36.1 0.7 constant_dynamic-slice_fusion.4
  36.7 3.8 %collective-permute-start.3 = (f32[6,8,128]{2,1,0:T(8,128)}, f32[6,8,128]{2,1,0:T(8,128)}, u32[]{:S(2)}, u32[]{:S(2)}) collective-permute-start(f32[6,8,128]{2,1,0:T(8,128)} %get-tuple-element.44), channel_id=1, source_target_pairs={{0,1},{1,2},{2,3},{3,0},{4,5},{5,6},{6,7},{7,4},{8,9},{9,10},{10,1... | collective-permute-start | bytes 73736 | tf_op jit(solution)/shard_map/ppermute | solution.py:90
  40.5 0.3 collective-permute-start.4
  40.8 3.3 %fusion.9 = f32[6,16,4,128]{3,1,2,0:T(8,128)S(1)} fusion(bf16[6,16,1024]{2,1,0:T(8,128)(2,1)} %collective-permute-done.8, bf16[6,16,1024]{2,1,0:T(8,128)(2,1)} %collective-permute-done.7, bf16[6,16,1024]{2,1,0:T(8,128)(2,1)} %collective-permute-done.6, bf16[6,16,1024]{2,1,0:T(8,128)(2,1)S(1)} %get-tuple-element.25, bf16[4,128,1024]{2,1,0:T(8,128)(2,1)} %bitcast.116, ...), kind=kOutput, calls=%fused_computation.21 | convolution fusion | flops 422576128 | bytes 5177344 | tf_op jit(solution)/shard_map/dot_general | solution.py:74
  44.1 0.7 gather_fusion.4
  44.8 0.1 broadcast_select_fusion.1
  44.9 19.7 %collective-permute-start.5 = (f32[6,8,128]{2,1,0:T(8,128)}, f32[6,8,128]{2,1,0:T(8,128)S(1)}, u32[]{:S(2)}, u32[]{:S(2)}) collective-permute-start(f32[6,8,128]{2,1,0:T(8,128)} %get-tuple-element.42), channel_id=1, source_target_pairs={{0,3},{1,0},{2,1},{3,2},{4,7},{5,4},{6,5},{7,6},{8,11},{9,8},{10,9... | collective-permute-start | bytes 73736 | tf_op jit(solution)/shard_map/ppermute | solution.py:90
  64.6 0.2 collective-permute-start.9
  64.8 1.6 %collective-permute-done.5 = f32[6,8,128]{2,1,0:T(8,128)S(1)} collective-permute-done((f32[6,8,128]{2,1,0:T(8,128)}, f32[6,8,128]{2,1,0:T(8,128)S(1)}, u32[]{:S(2)}, u32[]{:S(2)}) %collective-permute-start.5) | collective-permute-done | bytes 24608 | tf_op jit(solution)/shard_map/ppermute | solution.py:90
  66.4 0.9 select_reduce_fusion.4
  67.3 1.8 %collective-permute-start.10 = (f32[6,16,128]{2,1,0:T(8,128)S(1)}, f32[6,16,128]{2,1,0:T(8,128)S(1)}, u32[]{:S(2)}, u32[]{:S(2)}) collective-permute-start(f32[6,16,128]{2,1,0:T(8,128)S(1)} %get-tuple-element.39), channel_id=1, source_target_pairs={{0,2},{1,3},{2,0},{3,1},{4,6},{5,7},{6,4},{7,5},{8,10},{9,11},{10,... | collective-permute-start | bytes 147464 | tf_op jit(solution)/shard_map/ppermute | solution.py:90
  69.2 2.3 %collective-permute-done.10 = f32[6,16,128]{2,1,0:T(8,128)S(1)} collective-permute-done((f32[6,16,128]{2,1,0:T(8,128)S(1)}, f32[6,16,128]{2,1,0:T(8,128)S(1)}, u32[]{:S(2)}, u32[]{:S(2)}) %collective-permute-start.10) | collective-permute-done | bytes 49184 | tf_op jit(solution)/shard_map/ppermute | solution.py:90
  71.5 1.6 %collective-permute-done.11 = f32[6,16,128]{2,1,0:T(8,128)S(1)} collective-permute-done((f32[6,16,128]{2,1,0:T(8,128)S(1)}, f32[6,16,128]{2,1,0:T(8,128)S(1)}, u32[]{:S(2)}, u32[]{:S(2)}) %collective-permute-start.11) | collective-permute-done | bytes 49184 | tf_op jit(solution)/shard_map/ppermute | solution.py:90
  73.1 1.4 %select_reduce_fusion.2 = (f32[6,16,128]{2,1,0:T(8,128)}, f32[6,16,128]{2,1,0:T(8,128)}) fusion(f32[1,6,16,128]{3,2,1,0:T(8,128)S(1)} %bitcast.131, f32[1,6,16,128]{3,2,1,0:T(8,128)S(1)} %bitcast.130, f32[1,6,16,128]{3,2,1,0:T(8,128)S(1)} %bitcast.129, f32[1,6,16,128]{3,2,1,0:T(8,128)S(1)} %get-tuple-element.37, pred[4]{0:T(512)(128)(4,1)S(1)} %get-tuple-element.51, ...), kind=kLoop, calls=%fused_computation.52 | loop fusion | flops 319488 | bytes 294920 | tf_op jit(solution)/shard_map/reduce_sum | solution.py:94
  74.5 0.2 collective-permute-done.13
  74.7 1.5 %collective-permute-done.14 = bf16[6,40,1024]{2,1,0:T(8,128)(2,1)} collective-permute-done((bf16[6,40,1024]{2,1,0:T(8,128)(2,1)}, bf16[6,40,1024]{2,1,0:T(8,128)(2,1)}, u32[]{:S(2)}, u32[]{:S(2)}) %collective-permute-start.14) | collective-permute-done | bytes 491552 | tf_op jit(solution)/shard_map/ppermute | solution.py:69
  76.2 3.9 %fusion.1 = f32[6,40,4,128]{3,1,2,0:T(8,128)} fusion(bf16[6,40,1024]{2,1,0:T(8,128)(2,1)} %collective-permute-done.14, bf16[6,40,1024]{2,1,0:T(8,128)(2,1)} %collective-permute-done.13, bf16[6,40,1024]{2,1,0:T(8,128)(2,1)} %collective-permute-done.12, bf16[6,40,1024]{2,1,0:T(8,128)(2,1)} %get-tuple-element.21, bf16[4,128,1024]{2,1,0:T(8,128)(2,1)S(1)} %bitcast.117, ...), kind=kOutput, calls=%fused_computation.11 | convolution fusion | flops 1031274496 | bytes 6651904 | tf_op jit(solution)/shard_map/dot_general | solution.py:74
  80.2 1.7 %gather_fusion.6 = f32[24,40,128]{2,1,0:T(8,128)S(1)} fusion(f32[6,40,4,128]{3,1,2,0:T(8,128)} %fusion.1, s32[24]{0:T(128)S(1)} %fusion.39), kind=kCustom, calls=%fused_computation.6 | custom fusion | bytes 983232 | tf_op jit(solution)/shard_map/gather | solution.py:80
  81.9 0.1 broadcast_select_fusion
  82.1 3.2 %collective-permute-start.15 = (f32[6,40,128]{2,1,0:T(8,128)S(1)}, f32[6,40,128]{2,1,0:T(8,128)S(1)}, u32[]{:S(2)}, u32[]{:S(2)}) collective-permute-start(f32[6,40,128]{2,1,0:T(8,128)S(1)} %get-tuple-element.32), channel_id=1, source_target_pairs={{0,1},{1,2},{2,3},{3,0},{4,5},{5,6},{6,7},{7,4},{8,9},{9,10},{10,1... | collective-permute-start | bytes 368648 | tf_op jit(solution)/shard_map/ppermute | solution.py:90
  85.3 0.3 collective-permute-start.16
  85.5 0.2 collective-permute-start.17
  85.8 0.8 constant_dynamic-update-slice_fusion.3
  86.6 0.8 constant_dynamic-update-slice_fusion.2
  87.4 0.4 collective-permute-done.15
  87.8 3.3 %collective-permute-done.16 = f32[6,40,128]{2,1,0:T(8,128)S(1)} collective-permute-done((f32[6,40,128]{2,1,0:T(8,128)S(1)}, f32[6,40,128]{2,1,0:T(8,128)S(1)}, u32[]{:S(2)}, u32[]{:S(2)}) %collective-permute-start.16) | collective-permute-done | bytes 122912 | tf_op jit(solution)/shard_map/ppermute | solution.py:90
  91.1 0.7 collective-permute-done.17
  91.8 0.8 select_reduce_fusion
  92.6 0.0 copy-start.6
  92.6 0.7 copy-done.6
  (46 shorter events, 0.3 us)
Async XLA Ops:
  0.0 0.7 copy-start
  0.0 9.8 %copy-start.7 = (f32[1,1024]{1,0:T(1,128)S(1)}, f32[1,1024]{1,0:T(1,128)}, u32[]{:S(2)}) copy-start(f32[1,1024]{1,0:T(1,128)} %param.9) | copy-start | bytes 12292
  4.4 23.9 %collective-permute-start = (bf16[6,8,1024]{2,1,0:T(8,128)(2,1)}, bf16[6,8,1024]{2,1,0:T(8,128)(2,1)}, u32[]{:S(2)}, u32[]{:S(2)}) collective-permute-start(bf16[6,8,1024]{2,1,0:T(8,128)(2,1)} %get-tuple-element.36), channel_id=1, source_target_pairs={{0,4},{4,8},{8,12},{12,0},{1,5},{5,9},{9,13},{13,1},{2,6},{6,10},{... | collective-permute-start | bytes 294920 | tf_op jit(solution)/shard_map/ppermute | solution.py:69
  5.7 22.6 %collective-permute-start.1 = (bf16[6,8,1024]{2,1,0:T(8,128)(2,1)}, bf16[6,8,1024]{2,1,0:T(8,128)(2,1)}, u32[]{:S(2)}, u32[]{:S(2)}) collective-permute-start(bf16[6,8,1024]{2,1,0:T(8,128)(2,1)} %get-tuple-element.35), channel_id=1, source_target_pairs={{0,8},{4,12},{8,0},{12,4},{1,9},{5,13},{9,1},{13,5},{2,10},{6,14},... | collective-permute-start | bytes 294920 | tf_op jit(solution)/shard_map/ppermute | solution.py:69
  6.7 21.6 %collective-permute-start.2 = (bf16[6,8,1024]{2,1,0:T(8,128)(2,1)}, bf16[6,8,1024]{2,1,0:T(8,128)(2,1)}, u32[]{:S(2)}, u32[]{:S(2)}) collective-permute-start(bf16[6,8,1024]{2,1,0:T(8,128)(2,1)} %get-tuple-element.34), channel_id=1, source_target_pairs={{0,12},{4,0},{8,4},{12,8},{1,13},{5,1},{9,5},{13,9},{2,14},{6,2},{... | collective-permute-start | bytes 294920 | tf_op jit(solution)/shard_map/ppermute | solution.py:69
  10.9 25.9 %collective-permute-start.6 = (bf16[6,16,1024]{2,1,0:T(8,128)(2,1)}, bf16[6,16,1024]{2,1,0:T(8,128)(2,1)}, u32[]{:S(2)}, u32[]{:S(2)}) collective-permute-start(bf16[6,16,1024]{2,1,0:T(8,128)(2,1)} %get-tuple-element.28), channel_id=1, source_target_pairs={{0,4},{4,8},{8,12},{12,0},{1,5},{5,9},{9,13},{13,1},{2,6},{6,10},{... | collective-permute-start | bytes 589832 | tf_op jit(solution)/shard_map/ppermute | solution.py:69
  10.9 25.9 %collective-permute-start.7 = (bf16[6,16,1024]{2,1,0:T(8,128)(2,1)}, bf16[6,16,1024]{2,1,0:T(8,128)(2,1)}, u32[]{:S(2)}, u32[]{:S(2)}) collective-permute-start(bf16[6,16,1024]{2,1,0:T(8,128)(2,1)} %get-tuple-element.27), channel_id=1, source_target_pairs={{0,8},{4,12},{8,0},{12,4},{1,9},{5,13},{9,1},{13,5},{2,10},{6,14},... | collective-permute-start | bytes 589832 | tf_op jit(solution)/shard_map/ppermute | solution.py:69
  18.7 4.1 %copy-start.8 = (s32[1,2]{1,0:T(1,128)S(1)}, s32[1,2]{1,0:T(1,128)}, u32[]{:S(2)}) copy-start(s32[1,2]{1,0:T(1,128)} %param.13) | copy-start | bytes 28
  18.7 6.2 %copy-start.9 = (s32[1,24]{1,0:T(1,128)S(1)}, s32[1,24]{1,0:T(1,128)}, u32[]{:S(2)}) copy-start(s32[1,24]{1,0:T(1,128)} %param.12) | copy-start | bytes 292
  18.7 6.2 %copy-start.10 = (s32[1,24]{1,0:T(1,128)S(1)}, s32[1,24]{1,0:T(1,128)}, u32[]{:S(2)}) copy-start(s32[1,24]{1,0:T(1,128)} %param.11) | copy-start | bytes 292
  27.6 5.4 %copy-start.1 = (bf16[512,1,1024]{2,0,1:T(8,128)(2,1)}, bf16[512,1,1024]{2,0,1:T(8,128)(2,1)S(1)}, u32[]{:S(2)}) copy-start(bf16[512,1,1024]{2,0,1:T(8,128)(2,1)S(1)} %get-tuple-element.18) | copy-start | bytes 3145732
  27.6 5.3 %copy-start.3 = (bf16[512,1,1024]{2,0,1:T(8,128)(2,1)}, bf16[512,1,1024]{2,0,1:T(8,128)(2,1)S(1)}, u32[]{:S(2)}) copy-start(bf16[512,1,1024]{2,0,1:T(8,128)(2,1)S(1)} %get-tuple-element.19) | copy-start | bytes 3145732
  27.6 5.3 %copy-start.5 = (bf16[512,1,1024]{2,0,1:T(8,128)(2,1)}, bf16[512,1,1024]{2,0,1:T(8,128)(2,1)S(1)}, u32[]{:S(2)}) copy-start(bf16[512,1,1024]{2,0,1:T(8,128)(2,1)S(1)} %get-tuple-element.20) | copy-start | bytes 3145732
  28.3 12.3 %collective-permute-start.8 = (bf16[6,16,1024]{2,1,0:T(8,128)(2,1)S(1)}, bf16[6,16,1024]{2,1,0:T(8,128)(2,1)}, u32[]{:S(2)}, u32[]{:S(2)}) collective-permute-start(bf16[6,16,1024]{2,1,0:T(8,128)(2,1)S(1)} %get-tuple-element.26), channel_id=1, source_target_pairs={{0,12},{4,0},{8,4},{12,8},{1,13},{5,1},{9,5},{13,9},{2,14},{6,2},{... | collective-permute-start | bytes 589832 | tf_op jit(solution)/shard_map/ppermute | solution.py:69
  29.9 44.7 %collective-permute-start.12 = (bf16[6,40,1024]{2,1,0:T(8,128)(2,1)}, bf16[6,40,1024]{2,1,0:T(8,128)(2,1)}, u32[]{:S(2)}, u32[]{:S(2)}) collective-permute-start(bf16[6,40,1024]{2,1,0:T(8,128)(2,1)} %get-tuple-element.24), channel_id=1, source_target_pairs={{0,4},{4,8},{8,12},{12,0},{1,5},{5,9},{9,13},{13,1},{2,6},{6,10},{... | collective-permute-start | bytes 1474568 | tf_op jit(solution)/shard_map/ppermute | solution.py:69
  31.1 43.6 %collective-permute-start.13 = (bf16[6,40,1024]{2,1,0:T(8,128)(2,1)}, bf16[6,40,1024]{2,1,0:T(8,128)(2,1)}, u32[]{:S(2)}, u32[]{:S(2)}) collective-permute-start(bf16[6,40,1024]{2,1,0:T(8,128)(2,1)} %get-tuple-element.23), channel_id=1, source_target_pairs={{0,8},{4,12},{8,0},{12,4},{1,9},{5,13},{9,1},{13,5},{2,10},{6,14},... | collective-permute-start | bytes 1474568 | tf_op jit(solution)/shard_map/ppermute | solution.py:69
  36.7 39.5 %collective-permute-start.14 = (bf16[6,40,1024]{2,1,0:T(8,128)(2,1)}, bf16[6,40,1024]{2,1,0:T(8,128)(2,1)}, u32[]{:S(2)}, u32[]{:S(2)}) collective-permute-start(bf16[6,40,1024]{2,1,0:T(8,128)(2,1)} %get-tuple-element.22), channel_id=1, source_target_pairs={{0,12},{4,0},{8,4},{12,8},{1,13},{5,1},{9,5},{13,9},{2,14},{6,2},{... | collective-permute-start | bytes 1474568 | tf_op jit(solution)/shard_map/ppermute | solution.py:69
  36.7 8.2 %collective-permute-start.3 = (f32[6,8,128]{2,1,0:T(8,128)}, f32[6,8,128]{2,1,0:T(8,128)}, u32[]{:S(2)}, u32[]{:S(2)}) collective-permute-start(f32[6,8,128]{2,1,0:T(8,128)} %get-tuple-element.44), channel_id=1, source_target_pairs={{0,1},{1,2},{2,3},{3,0},{4,5},{5,6},{6,7},{7,4},{8,9},{9,10},{10,1... | collective-permute-start | bytes 73736 | tf_op jit(solution)/shard_map/ppermute | solution.py:90
  40.5 24.1 %collective-permute-start.4 = (f32[6,8,128]{2,1,0:T(8,128)}, f32[6,8,128]{2,1,0:T(8,128)}, u32[]{:S(2)}, u32[]{:S(2)}) collective-permute-start(f32[6,8,128]{2,1,0:T(8,128)} %get-tuple-element.43), channel_id=1, source_target_pairs={{0,2},{1,3},{2,0},{3,1},{4,6},{5,7},{6,4},{7,5},{8,10},{9,11},{10,... | collective-permute-start | bytes 73736 | tf_op jit(solution)/shard_map/ppermute | solution.py:90
  40.8 35.5 %copy-start.2 = (bf16[512,1,1024]{2,0,1:T(8,128)(2,1)S(1)}, bf16[512,1,1024]{2,0,1:T(8,128)(2,1)}, u32[]{:S(2)}) copy-start(bf16[512,1,1024]{2,0,1:T(8,128)(2,1)} %copy-done.1) | copy-start | bytes 3145732
  40.8 35.5 %copy-start.4 = (bf16[512,1,1024]{2,0,1:T(8,128)(2,1)S(1)}, bf16[512,1,1024]{2,0,1:T(8,128)(2,1)}, u32[]{:S(2)}) copy-start(bf16[512,1,1024]{2,0,1:T(8,128)(2,1)} %copy-done.3) | copy-start | bytes 3145732
  44.9 21.5 %collective-permute-start.5 = (f32[6,8,128]{2,1,0:T(8,128)}, f32[6,8,128]{2,1,0:T(8,128)S(1)}, u32[]{:S(2)}, u32[]{:S(2)}) collective-permute-start(f32[6,8,128]{2,1,0:T(8,128)} %get-tuple-element.42), channel_id=1, source_target_pairs={{0,3},{1,0},{2,1},{3,2},{4,7},{5,4},{6,5},{7,6},{8,11},{9,8},{10,9... | collective-permute-start | bytes 73736 | tf_op jit(solution)/shard_map/ppermute | solution.py:90
  64.6 4.6 %collective-permute-start.9 = (f32[6,16,128]{2,1,0:T(8,128)S(1)}, f32[6,16,128]{2,1,0:T(8,128)S(1)}, u32[]{:S(2)}, u32[]{:S(2)}) collective-permute-start(f32[6,16,128]{2,1,0:T(8,128)S(1)} %get-tuple-element.40), channel_id=1, source_target_pairs={{0,1},{1,2},{2,3},{3,0},{4,5},{5,6},{6,7},{7,4},{8,9},{9,10},{10,1... | collective-permute-start | bytes 147464 | tf_op jit(solution)/shard_map/ppermute | solution.py:90
  67.3 4.1 %collective-permute-start.10 = (f32[6,16,128]{2,1,0:T(8,128)S(1)}, f32[6,16,128]{2,1,0:T(8,128)S(1)}, u32[]{:S(2)}, u32[]{:S(2)}) collective-permute-start(f32[6,16,128]{2,1,0:T(8,128)S(1)} %get-tuple-element.39), channel_id=1, source_target_pairs={{0,2},{1,3},{2,0},{3,1},{4,6},{5,7},{6,4},{7,5},{8,10},{9,11},{10,... | collective-permute-start | bytes 147464 | tf_op jit(solution)/shard_map/ppermute | solution.py:90
  69.2 3.9 %collective-permute-start.11 = (f32[6,16,128]{2,1,0:T(8,128)S(1)}, f32[6,16,128]{2,1,0:T(8,128)S(1)}, u32[]{:S(2)}, u32[]{:S(2)}) collective-permute-start(f32[6,16,128]{2,1,0:T(8,128)S(1)} %get-tuple-element.38), channel_id=1, source_target_pairs={{0,3},{1,0},{2,1},{3,2},{4,7},{5,4},{6,5},{7,6},{8,11},{9,8},{10,9... | collective-permute-start | bytes 147464 | tf_op jit(solution)/shard_map/ppermute | solution.py:90
  82.1 5.7 %collective-permute-start.15 = (f32[6,40,128]{2,1,0:T(8,128)S(1)}, f32[6,40,128]{2,1,0:T(8,128)S(1)}, u32[]{:S(2)}, u32[]{:S(2)}) collective-permute-start(f32[6,40,128]{2,1,0:T(8,128)S(1)} %get-tuple-element.32), channel_id=1, source_target_pairs={{0,1},{1,2},{2,3},{3,0},{4,5},{5,6},{6,7},{7,4},{8,9},{9,10},{10,1... | collective-permute-start | bytes 368648 | tf_op jit(solution)/shard_map/ppermute | solution.py:90
  85.3 5.8 %collective-permute-start.16 = (f32[6,40,128]{2,1,0:T(8,128)S(1)}, f32[6,40,128]{2,1,0:T(8,128)S(1)}, u32[]{:S(2)}, u32[]{:S(2)}) collective-permute-start(f32[6,40,128]{2,1,0:T(8,128)S(1)} %get-tuple-element.31), channel_id=1, source_target_pairs={{0,2},{1,3},{2,0},{3,1},{4,6},{5,7},{6,4},{7,5},{8,10},{9,11},{10,... | collective-permute-start | bytes 368648 | tf_op jit(solution)/shard_map/ppermute | solution.py:90
  85.5 6.2 %collective-permute-start.17 = (f32[6,40,128]{2,1,0:T(8,128)S(1)}, f32[6,40,128]{2,1,0:T(8,128)S(1)}, u32[]{:S(2)}, u32[]{:S(2)}) collective-permute-start(f32[6,40,128]{2,1,0:T(8,128)S(1)} %get-tuple-element.30), channel_id=1, source_target_pairs={{0,3},{1,0},{2,1},{3,2},{4,7},{5,4},{6,5},{7,6},{8,11},{9,8},{10,9... | collective-permute-start | bytes 368648 | tf_op jit(solution)/shard_map/ppermute | solution.py:90
  92.6 0.7 copy-start.6
